TPU v7x, 512 devices: a whole 4x8x8 slice. The times are simulated.
512 devices in a mesh: section: 32 (over y, z_lo, core), tensor: 16 (over x, z_hi).
Axes of the slice: x: 4, y: 8, z: 8 (z_hi: 4, z_lo: 2; z = z_hi * 2 + z_lo), core: 2. Of those that a mesh axis runs over, the one named last changes fastest.
Arguments:
- tokens: bfloat16 [768, 8192], P('section', 'tensor'), may hold values from -6 to 6
- out_grad: bfloat16 [768, 8192], P('section', 'tensor'), may hold values from -3 to 3
- gate_weight: bfloat16 [8192, 14336], P('tensor', 'section'), may hold values from -0.0625 to 0.0625
- up_weight: bfloat16 [8192, 14336], P('tensor', 'section'), may hold values from -0.0625 to 0.0625
- down_weight: bfloat16 [14336, 8192], P('section', 'tensor'), may hold values from -0.046875 to 0.046875
Outputs:
- grad_input: bfloat16 [768, 8192], P('section', 'tensor')
- grad_gate: bfloat16 [8192, 14336], P('tensor', 'section')
- grad_up: bfloat16 [8192, 14336], P('tensor', 'section')
- grad_down: bfloat16 [14336, 8192], P('section', 'tensor')
All inputs are finite; a program needn't handle non-finite values.
Results may differ from a plain program's by a relative error of at most 0.0049.
Values may be sent and summed in bfloat16 or wider, within the bound.
No kernel may reach another device: no remote copies, remote signals or barrier semaphores. Data moves between devices by JAX's collectives and lax.ppermute only.
A program may use at most 64 MiB of HBM per device.

v0:
```python
import jax
import jax.numpy as jnp
from jax import lax
from jax.sharding import PartitionSpec as P


def swiglu_grads(gate_value, up_value, hidden_grad):
    logistic = jax.nn.sigmoid(gate_value)
    swish = gate_value * logistic
    hidden = (swish * up_value).astype(jnp.bfloat16)
    up_delta = (hidden_grad * swish).astype(jnp.bfloat16)
    gate_delta = (hidden_grad * up_value * logistic * (1.0 + gate_value * (1.0 - logistic))).astype(
        jnp.bfloat16
    )
    return (hidden, gate_delta, up_delta)


def local(tokens, out_grad, gate_weight, up_weight, down_weight):
    contract_last = (((1,), (1,)), ((), ()))
    contract_first = (((0,), (0,)), ((), ()))
    all_tokens, all_grads = (
        lax.all_gather(tokens, "section", axis=0, tiled=True),
        lax.all_gather(out_grad, "section", axis=0, tiled=True),
    )
    gate_part = jnp.dot(all_tokens, gate_weight, preferred_element_type=jnp.float32)
    up_part = jnp.dot(all_tokens, up_weight, preferred_element_type=jnp.float32)
    hidden_part = lax.dot_general(
        all_grads, down_weight, contract_last, preferred_element_type=jnp.float32
    )
    gate_value, up_value, hidden_grad = lax.psum((gate_part, up_part, hidden_part), "tensor")
    hidden, gate_delta, up_delta = swiglu_grads(gate_value, up_value, hidden_grad)
    grad_down = lax.dot_general(
        hidden, all_grads, contract_first, preferred_element_type=jnp.float32
    ).astype(jnp.bfloat16)
    grad_gate = lax.dot_general(
        all_tokens, gate_delta, contract_first, preferred_element_type=jnp.float32
    ).astype(jnp.bfloat16)
    grad_up = lax.dot_general(
        all_tokens, up_delta, contract_first, preferred_element_type=jnp.float32
    ).astype(jnp.bfloat16)
    result = lax.dot_general(
        gate_delta, gate_weight, contract_last, preferred_element_type=jnp.float32
    )
    grad_input = lax.psum_scatter(
        result
        + lax.dot_general(up_delta, up_weight, contract_last, preferred_element_type=jnp.float32),
        "section",
        scatter_dimension=0,
        tiled=True,
    ).astype(jnp.bfloat16)
    return (grad_input, grad_gate, grad_up, grad_down)


def solution(mesh):
    return jax.shard_map(
        local,
        mesh=mesh,
        in_specs=(
            P("section", "tensor"),
            P("section", "tensor"),
            P("tensor", "section"),
            P("tensor", "section"),
            P("section", "tensor"),
        ),
        out_specs=(
            P("section", "tensor"),
            P("tensor", "section"),
            P("tensor", "section"),
            P("section", "tensor"),
        ),
        check_vma=False,
    )
```

profile of v0, /device:TPU:1, one launch (start us, length us, event | category | flops | bytes accessed | tf_op | source)
XLA Modules:
  0.0 440.7 jit_solution(8860070443030646818)
XLA Ops:
  7.2 0.0 copy-start
  7.2 0.0 all-reduce.3.cloned.1.call-start
  7.2 39.7 %all_gather.7 = bf16[768,512]{1,0:T(8,128)(2,1)S(1)} all-gather(bf16[24,512]{1,0:T(8,128)(2,1)} %param.5), channel_id=1, replica_groups=mesh['section'=32,'tensor'=16] {'section'}, dimensions={0}, use_global_device_ids=true | all-gather | bytes 811008 | tf_op jit(solution)/shard_map/all_gather | solution.py:22
  46.9 34.7 %all_gather.6 = bf16[768,512]{1,0:T(8,128)(2,1)S(1)} all-gather(bf16[24,512]{1,0:T(8,128)(2,1)} %param.6), channel_id=1, replica_groups=mesh['section'=32,'tensor'=16] {'section'}, dimensions={0}, use_global_device_ids=true | all-gather | bytes 811008 | tf_op jit(solution)/shard_map/all_gather | solution.py:23
  81.6 0.0 copy-done
  81.6 0.0 copy-start.1
  81.6 1.7 fusion.7
  83.2 0.0 copy-done.1
  83.2 0.0 copy-start.5
  83.3 1.6 fusion.6
  84.9 0.0 copy-done.5
  84.9 1.7 fusion.5
  86.6 0.0 all-reduce.3.cloned.1.call-update
  86.6 0.0 reduce-scatter.2.cloned.1.call-start
  86.6 223.2 %all-reduce.3.cloned.1.call-done = (f32[768,448]{0,1:T(8,128)}, f32[768,448]{0,1:T(8,128)}, f32[768,448]{0,1:T(8,128)}) async-done(((f32[768,448]{0,1:T(8,128)}, f32[768,448]{0,1:T(8,128)}, f32[768,448]{0,1:T(8,128)}), (f32[768,448]{0,1:T(8,128)}, f32[768,448]{0,1:T(8,128)}, f32[768,448]{0,1:T(8,128)})) %all-reduce.3.cloned.1.call-update) | async-done | bytes 4128784 | tf_op jit(solution)/shard_map/psum | solution.py:30
  309.8 2.8 multiply_convert_fusion.1
  312.6 0.0 copy-start.2
  312.7 0.6 fusion.8
  313.3 0.4 copy-done.2
  313.7 1.8 convolution_add_fusion
  315.4 0.0 reduce-scatter.2.cloned.1.call-update
  315.5 0.0 copy-start.4
  315.5 1.3 fusion.2
  316.8 0.0 copy-start.3
  316.8 1.3 fusion.1
  318.1 0.0 copy-done.4
  318.1 0.1 copy-done.3
  318.1 1.3 convolution_convert_fusion
  319.4 113.0 %reduce-scatter.2.cloned.1.call-done = f32[24,512]{1,0:T(8,128)} async-done(((f32[768,512]{1,0:T(8,128)}), f32[24,512]{1,0:T(8,128)}) %reduce-scatter.2.cloned.1.call-update) | async-done | bytes 49168 | tf_op jit(solution)/shard_map/reduce_scatter | solution.py:44
  432.4 1.4 convert_element_type.29
Async XLA Ops:
  7.2 74.4 %copy-start = (bf16[512,448]{0,1:T(8,128)(2,1)S(1)}, bf16[512,448]{0,1:T(8,128)(2,1)}, u32[]{:S(2)}) copy-start(bf16[512,448]{0,1:T(8,128)(2,1)} %param.7) | copy-start | bytes 1376260
  7.2 302.6 %all-reduce.3.cloned.1.call-start = ((), (), s32[]{:S(2)}) async-start(), calls=%async_computation.2 | async-start | bytes 8257536 | tf_op jit(solution)/shard_map/psum | solution.py:30
  81.6 1.7 copy-start.1
  83.2 1.6 copy-start.5
  86.6 345.9 %reduce-scatter.2.cloned.1.call-start = ((), (), s32[]{:S(2)}) async-start(), calls=%async_computation.1 | async-start | bytes 1622016 | tf_op jit(solution)/shard_map/reduce_scatter | solution.py:44
  312.6 1.0 copy-start.2
  315.5 2.6 copy-start.4
  316.8 1.3 copy-start.3
Sparse Core Ops, SparseCore 0:
  86.7 223.0 all-reduce.2
  315.6 116.8 reduce-scatter.1
where the time goes:
time: 443 us; the launch traced here: 441 us
  waiting for transfers between devices  336 us (76%)
  blocking collectives  74.4 us (17%)
  between operations  14.1 us (3%)
  matrix products  11.2 us (3%)
    psum x1, waiting for transfers between devices, local(): lax.psum((gate_part, up_part, hidden_part), 'tensor')  223 us
    reduce_scatter x1, waiting for transfers between devices, local(): lax.psum_scatter(result + lax.dot_general(up_delta, up_weight, contract_l...  113 us
    all_gather x1, blocking collectives, local(): lax.all_gather(tokens, 'section', axis=0, tiled=True)  39.7 us
    all_gather x1, blocking collectives, local(): lax.all_gather(out_grad, 'section', axis=0, tiled=True)  34.7 us
  transfers between devices with their start and end apart: 2, of which 2 were waited for; matrix products, arithmetic and copies ran while one was open for 1% of the time, Pallas kernels for 0%

commit v1 on v0

v1 whole, which is shorter than its diff:
```python
import jax
import jax.numpy as jnp
from jax import lax
from jax.sharding import Mesh, PartitionSpec as P


def swiglu_grads(gate_value, up_value, hidden_grad):
    logistic = jax.nn.sigmoid(gate_value)
    swish = gate_value * logistic
    hidden = (swish * up_value).astype(jnp.bfloat16)
    up_delta = (hidden_grad * swish).astype(jnp.bfloat16)
    gate_delta = (hidden_grad * up_value * logistic * (1.0 + gate_value * (1.0 - logistic))).astype(
        jnp.bfloat16
    )
    return (hidden, gate_delta, up_delta)


SEC = ("y", "zl", "c")
TEN = ("x", "zh")


def scatter_sum(v, axis_name, n, dim):
    shape = v.shape
    v = v.reshape(shape[:dim] + (n, shape[dim] // n) + shape[dim + 1 :])
    v = lax.all_to_all(v, axis_name, dim, dim, tiled=True)
    return v.sum(dim)


def local(tokens, out_grad, gate_weight, up_weight, down_weight, nx, nzh, nsec):
    contract_last = (((1,), (1,)), ((), ()))
    contract_first = (((0,), (0,)), ((), ()))
    all_tokens, all_grads = (
        lax.all_gather(tokens, SEC, axis=0, tiled=True),
        lax.all_gather(out_grad, SEC, axis=0, tiled=True),
    )
    gate_part = jnp.dot(all_tokens, gate_weight, preferred_element_type=jnp.float32)
    up_part = jnp.dot(all_tokens, up_weight, preferred_element_type=jnp.float32)
    hidden_part = lax.dot_general(
        all_grads, down_weight, contract_last, preferred_element_type=jnp.float32
    )
    parts = jnp.stack([gate_part, up_part, hidden_part])
    parts = scatter_sum(parts, "x", nx, 1)
    parts = scatter_sum(parts, "zh", nzh, 1)
    hidden, gate_delta, up_delta = swiglu_grads(parts[0], parts[1], parts[2])
    deltas = lax.all_gather(jnp.stack([hidden, gate_delta, up_delta]), TEN, axis=1, tiled=True)
    hidden, gate_delta, up_delta = deltas[0], deltas[1], deltas[2]
    grad_down = lax.dot_general(
        hidden, all_grads, contract_first, preferred_element_type=jnp.float32
    ).astype(jnp.bfloat16)
    grad_gate = lax.dot_general(
        all_tokens, gate_delta, contract_first, preferred_element_type=jnp.float32
    ).astype(jnp.bfloat16)
    grad_up = lax.dot_general(
        all_tokens, up_delta, contract_first, preferred_element_type=jnp.float32
    ).astype(jnp.bfloat16)
    result = lax.dot_general(
        gate_delta, gate_weight, contract_last, preferred_element_type=jnp.float32
    ) + lax.dot_general(up_delta, up_weight, contract_last, preferred_element_type=jnp.float32)
    grad_input = scatter_sum(result, SEC, nsec, 0).astype(jnp.bfloat16)
    return (grad_input, grad_gate, grad_up, grad_down)


def solution(mesh):
    nsec, nten = mesh.shape["section"], mesh.shape["tensor"]
    nzh = 4
    nx = nten // nzh
    fine = Mesh(mesh.devices.reshape(nsec // 4, 2, 2, nx, nzh), ("y", "zl", "c", "x", "zh"))
    act = P(SEC, TEN)
    wt = P(TEN, SEC)

    def body(*args):
        return local(*args, nx=nx, nzh=nzh, nsec=nsec)

    return jax.shard_map(
        body,
        mesh=fine,
        in_specs=(act, act, wt, wt, act),
        out_specs=(act, wt, wt, act),
        check_vma=False,
    )
```

time: 443 us -> 306 us (0.69)
  waiting for transfers between devices: 336 us -> 101 us
  blocking collectives: 74.4 us -> 163 us
  starting transfers between devices: 0.08 us -> 9.06 us
    psum x1 -> x0, waiting for transfers between devices: 223 us -> none  [local(): lax.psum((gate_part, up_part, hidden_part), 'tensor')]
    reduce_scatter x1 -> x0, waiting for transfers between devices: 113 us -> none  [local(): lax.psum_scatter(result + lax.dot_general(up_delta, up_weight, contract_l...]
    all_to_all x0 -> x2, blocking collectives: none -> 88.2 us  [scatter_sum(): v = lax.all_to_all(v, axis_name, dim, dim, tiled=True)]
    all_gather x0 -> x1, waiting for transfers between devices: none -> 67 us  [local(): lax.all_gather(jnp.stack([hidden, gate_delta, up_delta]), TEN, axis=1, ti...]
    all_to_all x0 -> x1, waiting for transfers between devices: none -> 33.7 us  [scatter_sum(): v = lax.all_to_all(v, axis_name, dim, dim, tiled=True)]
    all_to_all x0 -> x1, starting transfers between devices: none -> 9.03 us  [scatter_sum(): v = lax.all_to_all(v, axis_name, dim, dim, tiled=True)]
  transfers between devices with their start and end apart: 2 -> 2, of which waited for: 2 -> 2; matrix products, arithmetic and copies ran while one was open for 1% -> 2% of each run, Pallas kernels for 0% -> 0%
where the time goes in v1:
time: 306 us; the launch traced here: 305 us
  blocking collectives  163 us (53%)
  waiting for transfers between devices  101 us (33%)
  between operations  14.1 us (5%)
  matrix products  13.1 us (4%)
  starting transfers between devices  9.06 us (3%)
  other arithmetic  5.16 us (2%)
    all_to_all x2, blocking collectives, scatter_sum(): v = lax.all_to_all(v, axis_name, dim, dim, tiled=True)  88.2 us
    all_gather x1, waiting for transfers between devices, local(): lax.all_gather(jnp.stack([hidden, gate_delta, up_delta]), TEN, axis=1, ti...  67 us
    all_gather x1, blocking collectives, local(): lax.all_gather(tokens, SEC, axis=0, tiled=True)  39.7 us
    all_gather x1, blocking collectives, local(): lax.all_gather(out_grad, SEC, axis=0, tiled=True)  34.7 us
    all_to_all x1, waiting for transfers between devices, scatter_sum(): v = lax.all_to_all(v, axis_name, dim, dim, tiled=True)  33.7 us
    all_to_all x1, starting transfers between devices, scatter_sum(): v = lax.all_to_all(v, axis_name, dim, dim, tiled=True)  9.03 us
  transfers between devices with their start and end apart: 2, of which 2 were waited for; matrix products, arithmetic and copies ran while one was open for 2% of the time, Pallas kernels for 0%

profile of v1, /device:TPU:1, one launch (start us, length us, event | category | flops | bytes accessed | tf_op | source)
XLA Modules:
  0.0 305.4 jit_solution(14879705945797379860)
XLA Ops:
  7.2 0.0 copy-start
  7.2 0.0 all-gather.2.cloned.1.call-start
  7.2 39.7 %all_gather.9 = bf16[768,512]{1,0:T(8,128)(2,1)S(1)} all-gather(bf16[24,512]{1,0:T(8,128)(2,1)} %param.5), channel_id=1, replica_groups=mesh['y'=8,'zl'=2,'c'=2,'x'=4,'zh'=4] {'y','zl','c'}, dimensions={0}, use_global_device_ids=true | all-gather | bytes 811008 | tf_op jit(solution)/shard_map/all_gather | solution.py:33
  46.9 34.7 %all_gather.10 = bf16[768,512]{1,0:T(8,128)(2,1)S(1)} all-gather(bf16[24,512]{1,0:T(8,128)(2,1)} %param.6), channel_id=1, replica_groups=mesh['y'=8,'zl'=2,'c'=2,'x'=4,'zh'=4] {'y','zl','c'}, dimensions={0}, use_global_device_ids=true | all-gather | bytes 811008 | tf_op jit(solution)/shard_map/all_gather | solution.py:34
  81.6 0.0 copy-start.1
  81.6 0.0 copy-start.4
  81.6 1.9 fusion.5
  83.5 0.0 copy-done
  83.5 0.6 fusion.4
  84.1 0.0 copy-done.1
  84.1 0.0 copy-done.4
  84.1 0.6 fusion.6
  84.7 0.5 pad_maximum_fusion
  85.3 0.5 copy.19
  85.8 57.6 %all_to_all.15 = f32[3,4,192,448]{3,2,0,1:T(8,128)} all-to-all(f32[3,4,192,448]{3,2,0,1:T(8,128)S(1)} %copy.19), channel_id=1, replica_groups=mesh['y'=8,'zl'=2,'c'=2,'x'=4,'zh'=4] {'x'}, dimensions={1} | all-to-all | bytes 8257536 | tf_op jit(solution)/shard_map/all_to_all | solution.py:25
  143.4 3.1 %reduce_sum.27 = f32[3,192,448]{2,1,0:T(8,128)S(1)} reduce(f32[3,4,192,448]{3,2,0,1:T(8,128)} %all_to_all.15, f32[]{:T(128)} %constant.0.clone.1), dimensions={1}, to_apply=%region_0.0 | reduce | flops 774144 | bytes 5160964 | tf_op jit(solution)/shard_map/reduce_sum | solution.py:26
  146.4 0.1 copy.20
  146.6 30.6 %all_to_all.16 = f32[3,4,48,448]{3,2,0,1:T(8,128)S(1)} all-to-all(f32[3,4,48,448]{3,2,0,1:T(8,128)S(1)} %copy.20), channel_id=1, replica_groups=mesh['y'=8,'zl'=2,'c'=2,'x'=4,'zh'=4] {'zh'}, dimensions={1} | all-to-all | bytes 2064384 | tf_op jit(solution)/shard_map/all_to_all | solution.py:25
  177.2 0.0 copy-start.2
  177.2 0.1 reduce_sum.28
  177.3 0.1 multiply_convert_fusion.2
  177.4 0.7 pad_maximum_fusion.1
  178.1 0.0 all-gather.2.cloned.1.call-update
  178.1 67.0 %all-gather.2.cloned.1.call-done = bf16[3,768,448]{2,1,0:T(8,128)(2,1)} async-done(((bf16[3,48,448]{2,1,0:T(8,128)(2,1)}), bf16[3,768,448]{2,1,0:T(8,128)(2,1)}) %all-gather.2.cloned.1.call-update) | async-done | bytes 2064400 | tf_op jit(solution)/shard_map/all_gather | solution.py:45
  245.1 1.7 fusion.2
  246.8 0.0 copy-done.2
  246.8 2.8 convolution_add_fusion
  249.6 9.0 %all-to-all-start.2 = ((f32[32,24,512]{2,1,0:T(8,128)}), f32[32,24,512]{2,1,0:T(8,128)S(1)}, u32[]{:S(2)}, u32[]{:S(2)}) async-start(f32[32,24,512]{2,1,0:T(8,128)} %bitcast.31), calls=%async_computation.2 | async-start | bytes 3145728 | tf_op jit(solution)/shard_map/all_to_all | solution.py:25
  258.7 0.0 copy-start.3
  258.7 2.8 convolution_convert_fusion
  261.5 0.0 copy-done.3
  261.5 1.3 fusion.1
  262.8 1.3 fusion
  264.2 33.7 %all-to-all-done.2 = f32[32,24,512]{2,1,0:T(8,128)S(1)} async-done(((f32[32,24,512]{2,1,0:T(8,128)}), f32[32,24,512]{2,1,0:T(8,128)S(1)}, u32[]{:S(2)}, u32[]{:S(2)}) %all-to-all-start.2) | async-done | bytes 1572896 | tf_op jit(solution)/shard_map/all_to_all | solution.py:25
  297.9 0.7 reduce_sum.29
Async XLA Ops:
  7.2 76.3 %copy-start = (bf16[512,448]{0,1:T(8,128)(2,1)S(1)}, bf16[512,448]{0,1:T(8,128)(2,1)}, u32[]{:S(2)}) copy-start(bf16[512,448]{0,1:T(8,128)(2,1)} %param.7) | copy-start | bytes 1376260
  7.2 237.9 %all-gather.2.cloned.1.call-start = ((), (), s32[]{:S(2)}) async-start(), calls=%async_computation.3 | async-start | bytes 2506752 | tf_op jit(solution)/shard_map/all_gather | solution.py:45
  81.6 2.5 copy-start.1
  81.6 2.5 copy-start.4
  177.2 69.6 %copy-start.2 = (bf16[512,448]{0,1:T(8,128)(2,1)S(1)}, bf16[512,448]{0,1:T(8,128)(2,1)}, u32[]{:S(2)}) copy-start(bf16[512,448]{0,1:T(8,128)(2,1)} %param.8) | copy-start | bytes 1376260
  249.6 48.2 %all-to-all-start.2 = ((f32[32,24,512]{2,1,0:T(8,128)}), f32[32,24,512]{2,1,0:T(8,128)S(1)}, u32[]{:S(2)}, u32[]{:S(2)}) async-start(f32[32,24,512]{2,1,0:T(8,128)} %bitcast.31), calls=%async_computation.2 | async-start | bytes 3145728 | tf_op jit(solution)/shard_map/all_to_all | solution.py:25
  258.7 2.9 copy-start.3
Sparse Core Ops, SparseCore 0:
  178.2 66.8 all-gather.1

commit v2 on v1

--- a/solution.py
+++ b/solution.py
@@ -26,13 +26,19 @@
     return v.sum(dim)
 
 
+def gather_a2a(v, axis_name, n, dim):
+    shape = v.shape
+    v = jnp.broadcast_to(jnp.expand_dims(v, dim), shape[:dim] + (n,) + shape[dim:])
+    v = lax.all_to_all(v, axis_name, dim, dim, tiled=True)
+    return v.reshape(shape[:dim] + (n * shape[dim],) + shape[dim + 1 :])
+
+
 def local(tokens, out_grad, gate_weight, up_weight, down_weight, nx, nzh, nsec):
     contract_last = (((1,), (1,)), ((), ()))
     contract_first = (((0,), (0,)), ((), ()))
-    all_tokens, all_grads = (
-        lax.all_gather(tokens, SEC, axis=0, tiled=True),
-        lax.all_gather(out_grad, SEC, axis=0, tiled=True),
-    )
+    both = jnp.concatenate([tokens, out_grad], 1)
+    both = gather_a2a(both, SEC, nsec, 0)
+    all_tokens, all_grads = both[:, : tokens.shape[1]], both[:, tokens.shape[1] :]
     gate_part = jnp.dot(all_tokens, gate_weight, preferred_element_type=jnp.float32)
     up_part = jnp.dot(all_tokens, up_weight, preferred_element_type=jnp.float32)
     hidden_part = lax.dot_general(
@@ -42,7 +48,9 @@
     parts = scatter_sum(parts, "x", nx, 1)
     parts = scatter_sum(parts, "zh", nzh, 1)
     hidden, gate_delta, up_delta = swiglu_grads(parts[0], parts[1], parts[2])
-    deltas = lax.all_gather(jnp.stack([hidden, gate_delta, up_delta]), TEN, axis=1, tiled=True)
+    deltas = jnp.stack([hidden, gate_delta, up_delta])
+    deltas = gather_a2a(deltas, "zh", nzh, 1)
+    deltas = gather_a2a(deltas, "x", nx, 1)
     hidden, gate_delta, up_delta = deltas[0], deltas[1], deltas[2]
     grad_down = lax.dot_general(
         hidden, all_grads, contract_first, preferred_element_type=jnp.float32

time: 306 us -> 255 us (0.83)
  waiting for transfers between devices: 101 us -> 34.1 us
  starting transfers between devices: 9.06 us -> 25.4 us
  between operations: 14.1 us -> 0.76 us
  blocking collectives: 163 us -> 175 us
  matrix products: 13.1 us -> 9.18 us
    all_to_all x0 -> x3, blocking collectives: none -> 86.5 us  [gather_a2a(): v = lax.all_to_all(v, axis_name, dim, dim, tiled=True)]
    all_gather x2 -> x0, blocking collectives: 74.4 us -> none  [the longest x1 39.7 us: local(): lax.all_gather(tokens, SEC, axis=0, tiled=True)]
    all_gather x1 -> x0, waiting for transfers between devices: 67 us -> none  [local(): lax.all_gather(jnp.stack([hidden, gate_delta, up_delta]), TEN, axis=1, ti...]
    all_to_all x1, starting transfers between devices: 9.03 us -> 25.4 us  [scatter_sum(): v = lax.all_to_all(v, axis_name, dim, dim, tiled=True)]
  transfers between devices with their start and end apart: 2 -> 1, of which waited for: 2 -> 1; matrix products, arithmetic and copies ran while one was open for 2% -> 2% of each run, Pallas kernels for 0% -> 0%
where the time goes in v2:
time: 255 us; the launch traced here: 254 us
  blocking collectives  175 us (69%)
  waiting for transfers between devices  34.1 us (13%)
  starting transfers between devices  25.4 us (10%)
  matrix products  9.18 us (4%)
  other arithmetic  6.73 us (3%)
  local copies, waits for them, and re-layouts  3.36 us (1%)
    all_to_all x2, blocking collectives, scatter_sum(): v = lax.all_to_all(v, axis_name, dim, dim, tiled=True)  88.3 us
    all_to_all x3, blocking collectives, gather_a2a(): v = lax.all_to_all(v, axis_name, dim, dim, tiled=True)  86.5 us
    all_to_all x1, waiting for transfers between devices, scatter_sum(): v = lax.all_to_all(v, axis_name, dim, dim, tiled=True)  34.1 us
    all_to_all x1, starting transfers between devices, scatter_sum(): v = lax.all_to_all(v, axis_name, dim, dim, tiled=True)  25.4 us
    reduce_sum x3, other arithmetic, scatter_sum(): return v.sum(dim)  5.31 us
  transfers between devices with their start and end apart: 1, of which 1 were waited for; matrix products, arithmetic and copies ran while one was open for 2% of the time, Pallas kernels for 0%

profile of v2, /device:TPU:1, one launch (start us, length us, event | category | flops | bytes accessed | tf_op | source)
XLA Modules:
  0.0 254.3 jit_solution(7261884260816681517)
XLA Ops:
  0.6 0.0 copy-start
  0.6 0.8 pad_maximum_fusion.2
  1.5 0.2 broadcast_in_dim.8
  1.6 0.0 copy-start.2
  1.7 50.2 %all_to_all.30 = bf16[32,24,1024]{2,1,0:T(8,128)(2,1)S(1)} all-to-all(bf16[32,24,1024]{2,1,0:T(8,128)(2,1)S(1)} %broadcast_in_dim.8), channel_id=1, replica_groups=mesh['y'=8,'zl'=2,'c'=2,'x'=4,'zh'=4] {'y','zl','c'}, dimensions={0} | all-to-all | bytes 3145728 | tf_op jit(solution)/shard_map/all_to_all | solution.py:32
  51.9 0.0 copy-start.5
  51.9 0.0 copy-done.2
  51.9 0.6 fusion.5
  52.5 0.4 copy-done.5
  52.9 0.6 fusion.1
  53.5 0.0 copy-done
  53.5 0.6 fusion.7
  54.1 0.5 pad_maximum_fusion
  54.6 0.5 copy.19
  55.1 57.2 %all_to_all.31 = f32[3,4,192,448]{3,2,0,1:T(8,128)} all-to-all(f32[3,4,192,448]{3,2,0,1:T(8,128)S(1)} %copy.19), channel_id=1, replica_groups=mesh['y'=8,'zl'=2,'c'=2,'x'=4,'zh'=4] {'x'}, dimensions={1} | all-to-all | bytes 8257536 | tf_op jit(solution)/shard_map/all_to_all | solution.py:25
  112.4 3.1 %reduce_sum.27 = f32[3,192,448]{2,1,0:T(8,128)S(1)} reduce(f32[3,4,192,448]{3,2,0,1:T(8,128)} %all_to_all.31, f32[]{:T(128)} %constant.0.clone.1), dimensions={1}, to_apply=%region_0.0 | reduce | flops 774144 | bytes 5160964 | tf_op jit(solution)/shard_map/reduce_sum | solution.py:26
  115.4 0.1 copy.20
  115.6 31.1 %all_to_all.32 = f32[3,4,48,448]{3,2,0,1:T(8,128)S(1)} all-to-all(f32[3,4,48,448]{3,2,0,1:T(8,128)S(1)} %copy.20), channel_id=1, replica_groups=mesh['y'=8,'zl'=2,'c'=2,'x'=4,'zh'=4] {'zh'}, dimensions={1} | all-to-all | bytes 2064384 | tf_op jit(solution)/shard_map/all_to_all | solution.py:25
  146.7 0.1 reduce_sum.28
  146.8 0.1 multiply_convert_fusion.2
  146.9 15.6 %all_to_all.33 = bf16[3,4,48,448]{3,2,0,1:T(8,128)(2,1)S(1)} all-to-all(bf16[3,4,48,448]{3,2,0,1:T(8,128)(2,1)S(1)} %broadcast_in_dim.9), channel_id=1, replica_groups=mesh['y'=8,'zl'=2,'c'=2,'x'=4,'zh'=4] {'zh'}, dimensions={1} | all-to-all | bytes 1032192 | tf_op jit(solution)/shard_map/all_to_all | solution.py:32
  162.5 0.2 broadcast_in_dim.22
  162.8 20.8 %all_to_all.34 = bf16[3,4,192,448]{3,2,0,1:T(8,128)(2,1)S(1)} all-to-all(bf16[3,4,192,448]{3,2,0,1:T(8,128)(2,1)S(1)} %broadcast_in_dim.22), channel_id=1, replica_groups=mesh['y'=8,'zl'=2,'c'=2,'x'=4,'zh'=4] {'x'}, dimensions={1} | all-to-all | bytes 4128768 | tf_op jit(solution)/shard_map/all_to_all | solution.py:32
  183.5 1.1 fusion.10
  184.6 0.0 copy-start.1
  184.6 0.0 copy-start.3
  184.6 0.6 fusion.11
  185.2 0.7 copy-done.3
  185.9 1.7 convolution_add_fusion
  187.6 0.0 copy-done.1
  187.6 25.4 %all-to-all-start.5 = ((f32[32,24,512]{2,1,0:T(8,128)}), f32[32,24,512]{2,1,0:T(8,128)}, u32[]{:S(2)}, u32[]{:S(2)}) async-start(f32[32,24,512]{2,1,0:T(8,128)} %bitcast.26), calls=%async_computation.5 | async-start | bytes 3145728 | tf_op jit(solution)/shard_map/all_to_all | solution.py:25
  213.0 2.5 convolution_convert_fusion.1
  215.5 0.0 copy-start.4
  215.5 1.3 convolution_convert_fusion.2
  216.8 0.0 copy-done.4
  216.8 1.3 convolution_convert_fusion
  218.1 34.1 %all-to-all-done.5 = f32[32,24,512]{2,1,0:T(8,128)} async-done(((f32[32,24,512]{2,1,0:T(8,128)}), f32[32,24,512]{2,1,0:T(8,128)}, u32[]{:S(2)}, u32[]{:S(2)}) %all-to-all-start.5) | async-done | bytes 1572896 | tf_op jit(solution)/shard_map/all_to_all | solution.py:25
  252.2 2.1 reduce_sum.29
  (3 shorter events, 0.1 us)
Async XLA Ops:
  0.6 52.9 %copy-start = (bf16[512,448]{0,1:T(8,128)(2,1)S(1)}, bf16[512,448]{0,1:T(8,128)(2,1)}, u32[]{:S(2)}) copy-start(bf16[512,448]{0,1:T(8,128)(2,1)} %param.7) | copy-start | bytes 1376260
  1.6 50.2 %copy-start.2 = (bf16[512,448]{0,1:T(8,128)(2,1)S(1)}, bf16[512,448]{0,1:T(8,128)(2,1)}, u32[]{:S(2)}) copy-start(bf16[512,448]{0,1:T(8,128)(2,1)} %param.8) | copy-start | bytes 1376260
  51.9 1.0 copy-start.5
  184.6 3.0 %copy-start.1 = (bf16[1,4,192,448]{3,2,0,1:T(8,128)(2,1)}, bf16[1,4,192,448]{3,2,0,1:T(8,128)(2,1)S(1)}, u32[]{:S(2)}) copy-start(bf16[1,4,192,448]{3,2,0,1:T(8,128)(2,1)S(1)} %get-tuple-element.5) | copy-start | bytes 2064388
  184.6 1.3 copy-start.3
  187.6 64.6 %all-to-all-start.5 = ((f32[32,24,512]{2,1,0:T(8,128)}), f32[32,24,512]{2,1,0:T(8,128)}, u32[]{:S(2)}, u32[]{:S(2)}) async-start(f32[32,24,512]{2,1,0:T(8,128)} %bitcast.26), calls=%async_computation.5 | async-start | bytes 3145728 | tf_op jit(solution)/shard_map/all_to_all | solution.py:25
  215.5 1.3 copy-start.4

commit v3 on v2

--- a/solution.py
+++ b/solution.py
@@ -36,18 +36,18 @@
 def local(tokens, out_grad, gate_weight, up_weight, down_weight, nx, nzh, nsec):
     contract_last = (((1,), (1,)), ((), ()))
     contract_first = (((0,), (0,)), ((), ()))
-    both = jnp.concatenate([tokens, out_grad], 1)
-    both = gather_a2a(both, SEC, nsec, 0)
-    all_tokens, all_grads = both[:, : tokens.shape[1]], both[:, tokens.shape[1] :]
+    all_tokens = gather_a2a(tokens, SEC, nsec, 0)
+    all_grads = gather_a2a(out_grad, SEC, nsec, 0)
     gate_part = jnp.dot(all_tokens, gate_weight, preferred_element_type=jnp.float32)
     up_part = jnp.dot(all_tokens, up_weight, preferred_element_type=jnp.float32)
     hidden_part = lax.dot_general(
         all_grads, down_weight, contract_last, preferred_element_type=jnp.float32
     )
-    parts = jnp.stack([gate_part, up_part, hidden_part])
-    parts = scatter_sum(parts, "x", nx, 1)
-    parts = scatter_sum(parts, "zh", nzh, 1)
-    hidden, gate_delta, up_delta = swiglu_grads(parts[0], parts[1], parts[2])
+    gu = scatter_sum(jnp.stack([gate_part, up_part]), "x", nx, 1)
+    hg = scatter_sum(hidden_part, "x", nx, 0)
+    gu = scatter_sum(gu, "zh", nzh, 1)
+    hg = scatter_sum(hg, "zh", nzh, 0)
+    hidden, gate_delta, up_delta = swiglu_grads(gu[0], gu[1], hg)
     deltas = jnp.stack([hidden, gate_delta, up_delta])
     deltas = gather_a2a(deltas, "zh", nzh, 1)
     deltas = gather_a2a(deltas, "x", nx, 1)

time: 255 us -> 268 us (1.051)
  blocking collectives: 175 us -> 68.2 us
  waiting for transfers between devices: 34.1 us -> 123 us
  starting transfers between devices: 25.4 us -> 54.5 us
  local copies, waits for them, and re-layouts: 3.36 us -> 6.18 us
    all_to_all x2 -> x0, blocking collectives: 88.3 us -> none  [scatter_sum(): v = lax.all_to_all(v, axis_name, dim, dim, tiled=True)]
    all_to_all x1 -> x5, waiting for transfers between devices: 34.1 us -> 102 us  [scatter_sum(): v = lax.all_to_all(v, axis_name, dim, dim, tiled=True)]
    all_to_all x1 -> x5, starting transfers between devices: 25.4 us -> 49.8 us  [scatter_sum(): v = lax.all_to_all(v, axis_name, dim, dim, tiled=True)]
    all_to_all x0 -> x1, waiting for transfers between devices: none -> 21.1 us  [gather_a2a(): v = lax.all_to_all(v, axis_name, dim, dim, tiled=True)]
    all_to_all x3, blocking collectives: 86.5 us -> 68.2 us  [gather_a2a(): v = lax.all_to_all(v, axis_name, dim, dim, tiled=True)]
    all_to_all x0 -> x1, starting transfers between devices: none -> 4.69 us  [gather_a2a(): v = lax.all_to_all(v, axis_name, dim, dim, tiled=True)]
  transfers between devices with their start and end apart: 1 -> 6, of which waited for: 1 -> 6; matrix products, arithmetic and copies ran while one was open for 2% -> 5% of each run, Pallas kernels for 0% -> 0%
where the time goes in v3:
time: 268 us; the launch traced here: 267 us
  waiting for transfers between devices  123 us (46%)
  blocking collectives  68.2 us (25%)
  starting transfers between devices  54.5 us (20%)
  matrix products  10.4 us (4%)
  local copies, waits for them, and re-layouts  6.18 us (2%)
  other arithmetic  4.52 us (2%)
    all_to_all x5, waiting for transfers between devices, scatter_sum(): v = lax.all_to_all(v, axis_name, dim, dim, tiled=True)  102 us
    all_to_all x3, blocking collectives, gather_a2a(): v = lax.all_to_all(v, axis_name, dim, dim, tiled=True)  68.2 us
    all_to_all x5, starting transfers between devices, scatter_sum(): v = lax.all_to_all(v, axis_name, dim, dim, tiled=True)  49.8 us
    all_to_all x1, waiting for transfers between devices, gather_a2a(): v = lax.all_to_all(v, axis_name, dim, dim, tiled=True)  21.1 us
  transfers between devices with their start and end apart: 6, of which 6 were waited for; matrix products, arithmetic and copies ran while one was open for 5% of the time, Pallas kernels for 0%

profile of v3, /device:TPU:1, one launch (start us, length us, event | category | flops | bytes accessed | tf_op | source)
XLA Modules:
  0.0 267.4 jit_solution(1937993596505685239)
XLA Ops:
  0.6 0.0 copy-start
  0.6 0.0 copy-start.9
  0.7 0.8 broadcast_in_dim.11
  1.5 33.0 %all_to_all.45 = bf16[32,24,512]{2,1,0:T(8,128)(2,1)S(1)} all-to-all(bf16[32,24,512]{2,1,0:T(8,128)(2,1)S(1)} %broadcast_in_dim.11), channel_id=1, replica_groups=mesh['y'=8,'zl'=2,'c'=2,'x'=4,'zh'=4] {'y','zl','c'}, dimensions={0} | all-to-all | bytes 1572864 | tf_op jit(solution)/shard_map/all_to_all | solution.py:32
  34.5 0.0 copy-done.9
  34.5 1.0 broadcast_in_dim.10
  35.5 4.7 %all-to-all-start = ((bf16[32,24,512]{2,1,0:T(8,128)(2,1)}), bf16[32,24,512]{2,1,0:T(8,128)(2,1)S(1)}, u32[]{:S(2)}, u32[]{:S(2)}) async-start(bf16[32,24,512]{2,1,0:T(8,128)(2,1)} %broadcast_in_dim.10), calls=%async_computation | async-start | bytes 1572864 | tf_op jit(solution)/shard_map/all_to_all | solution.py:32
  40.2 0.0 copy-done.8
  40.2 1.8 fusion.2
  41.9 0.0 copy-done.2
  41.9 21.1 %all-to-all-done = bf16[32,24,512]{2,1,0:T(8,128)(2,1)S(1)} async-done(((bf16[32,24,512]{2,1,0:T(8,128)(2,1)}), bf16[32,24,512]{2,1,0:T(8,128)(2,1)S(1)}, u32[]{:S(2)}, u32[]{:S(2)}) %all-to-all-start) | async-done | bytes 786464 | tf_op jit(solution)/shard_map/all_to_all | solution.py:32
  63.0 4.0 %all-to-all-start.4 = ((f32[4,192,448]{2,1,0:T(8,128)}), f32[4,192,448]{2,1,0:T(8,128)S(1)}, u32[]{:S(2)}, u32[]{:S(2)}) async-start(f32[4,192,448]{2,1,0:T(8,128)} %fusion.2), calls=%async_computation.4 | async-start | bytes 3145728 | tf_op jit(solution)/shard_map/all_to_all | solution.py:25
  67.0 0.0 copy-done.6
  67.0 0.6 convolution_bitcast_fusion
  67.6 0.0 copy-done
  67.6 0.6 convolution_bitcast_fusion.1
  68.2 0.3 pad_maximum_fusion
  68.5 1.9 copy.13
  70.5 15.8 %all-to-all-done.4 = f32[4,192,448]{2,1,0:T(8,128)S(1)} async-done(((f32[4,192,448]{2,1,0:T(8,128)}), f32[4,192,448]{2,1,0:T(8,128)S(1)}, u32[]{:S(2)}, u32[]{:S(2)}) %all-to-all-start.4) | async-done | bytes 1376288 | tf_op jit(solution)/shard_map/all_to_all | solution.py:25
  86.3 4.6 %all-to-all-start.1 = ((f32[2,4,192,448]{3,2,0,1:T(8,128)}), f32[2,4,192,448]{3,2,0,1:T(8,128)}, u32[]{:S(2)}, u32[]{:S(2)}) async-start(f32[2,4,192,448]{3,2,0,1:T(8,128)} %copy.13), calls=%async_computation.1 | async-start | bytes 6291456 | tf_op jit(solution)/shard_map/all_to_all | solution.py:25
  90.9 0.9 reduce_sum.49
  91.9 34.4 %all-to-all-done.1 = f32[2,4,192,448]{3,2,0,1:T(8,128)} async-done(((f32[2,4,192,448]{3,2,0,1:T(8,128)}), f32[2,4,192,448]{3,2,0,1:T(8,128)}, u32[]{:S(2)}, u32[]{:S(2)}) %all-to-all-start.1) | async-done | bytes 2752544 | tf_op jit(solution)/shard_map/all_to_all | solution.py:25
  126.2 9.1 %all-to-all-start.5 = ((f32[4,48,448]{2,1,0:T(8,128)}), f32[4,48,448]{2,1,0:T(8,128)S(1)}, u32[]{:S(2)}, u32[]{:S(2)}) async-start(f32[4,48,448]{2,1,0:T(8,128)} %bitcast.65), calls=%async_computation.5 | async-start | bytes 786432 | tf_op jit(solution)/shard_map/all_to_all | solution.py:25
  135.4 2.4 reduce_sum.47
  137.7 1.0 copy.14
  138.7 5.4 %all-to-all-done.5 = f32[4,48,448]{2,1,0:T(8,128)S(1)} async-done(((f32[4,48,448]{2,1,0:T(8,128)}), f32[4,48,448]{2,1,0:T(8,128)S(1)}, u32[]{:S(2)}, u32[]{:S(2)}) %all-to-all-start.5) | async-done | bytes 344096 | tf_op jit(solution)/shard_map/all_to_all | solution.py:25
  144.1 3.8 %all-to-all-start.2 = ((f32[2,4,48,448]{3,2,0,1:T(8,128)}), f32[2,4,48,448]{3,2,0,1:T(8,128)S(1)}, u32[]{:S(2)}, u32[]{:S(2)}) async-start(f32[2,4,48,448]{3,2,0,1:T(8,128)} %copy.14), calls=%async_computation.2 | async-start | bytes 1572864 | tf_op jit(solution)/shard_map/all_to_all | solution.py:25
  147.9 12.2 %all-to-all-done.2 = f32[2,4,48,448]{3,2,0,1:T(8,128)S(1)} async-done(((f32[2,4,48,448]{3,2,0,1:T(8,128)}), f32[2,4,48,448]{3,2,0,1:T(8,128)S(1)}, u32[]{:S(2)}, u32[]{:S(2)}) %all-to-all-start.2) | async-done | bytes 688160 | tf_op jit(solution)/shard_map/all_to_all | solution.py:25
  160.1 0.1 reduce_sum.48
  160.2 0.1 fusion.8
  160.4 16.0 %all_to_all.46 = bf16[3,4,48,448]{3,2,0,1:T(8,128)(2,1)S(1)} all-to-all(bf16[3,4,48,448]{3,2,0,1:T(8,128)(2,1)S(1)} %broadcast_in_dim.12), channel_id=1, replica_groups=mesh['y'=8,'zl'=2,'c'=2,'x'=4,'zh'=4] {'zh'}, dimensions={1} | all-to-all | bytes 1032192 | tf_op jit(solution)/shard_map/all_to_all | solution.py:32
  176.4 0.2 broadcast_in_dim.14
  176.7 19.2 %all_to_all.47 = bf16[3,4,192,448]{3,2,0,1:T(8,128)(2,1)S(1)} all-to-all(bf16[3,4,192,448]{3,2,0,1:T(8,128)(2,1)S(1)} %broadcast_in_dim.14), channel_id=1, replica_groups=mesh['y'=8,'zl'=2,'c'=2,'x'=4,'zh'=4] {'x'}, dimensions={1} | all-to-all | bytes 4128768 | tf_op jit(solution)/shard_map/all_to_all | solution.py:32
  195.9 1.1 fusion.11
  197.0 0.6 fusion.12
  197.5 1.7 convolution_add_fusion
  199.3 0.0 copy-done.1
  199.3 0.0 copy-done.4
  199.3 28.2 %all-to-all-start.8 = ((f32[32,24,512]{2,1,0:T(8,128)}), f32[32,24,512]{2,1,0:T(8,128)S(1)}, u32[]{:S(2)}, u32[]{:S(2)}) async-start(f32[32,24,512]{2,1,0:T(8,128)} %bitcast.56), calls=%async_computation.8 | async-start | bytes 3145728 | tf_op jit(solution)/shard_map/all_to_all | solution.py:25
  227.5 0.0 copy-start.5
  227.5 2.5 fusion
  230.0 0.0 copy-done.5
  230.0 1.3 fusion.1
  231.3 0.0 copy-done.3
  231.3 0.0 copy-done.7
  231.4 1.3 convolution_convert_fusion
  232.7 34.0 %all-to-all-done.8 = f32[32,24,512]{2,1,0:T(8,128)S(1)} async-done(((f32[32,24,512]{2,1,0:T(8,128)}), f32[32,24,512]{2,1,0:T(8,128)S(1)}, u32[]{:S(2)}, u32[]{:S(2)}) %all-to-all-start.8) | async-done | bytes 1572896 | tf_op jit(solution)/shard_map/all_to_all | solution.py:25
  266.7 0.7 reduce_sum.52
  (11 shorter events, 0.1 us)
Async XLA Ops:
  0.6 67.0 %copy-start = (bf16[512,448]{0,1:T(8,128)(2,1)S(1)}, bf16[512,448]{0,1:T(8,128)(2,1)}, u32[]{:S(2)}) copy-start(bf16[512,448]{0,1:T(8,128)(2,1)} %param.7) | copy-start | bytes 1376260
  0.6 33.8 %copy-start.9 = (bf16[24,512]{1,0:T(8,128)(2,1)S(1)}, bf16[24,512]{1,0:T(8,128)(2,1)}, u32[]{:S(2)}) copy-start(bf16[24,512]{1,0:T(8,128)(2,1)} %param.5) | copy-start | bytes 73732
  34.5 7.4 %copy-start.2 = (bf16[32,24,512]{2,1,0:T(8,128)(2,1)}, bf16[32,24,512]{2,1,0:T(8,128)(2,1)S(1)}, u32[]{:S(2)}) copy-start(bf16[32,24,512]{2,1,0:T(8,128)(2,1)S(1)} %all_to_all.45) | copy-start | bytes 2359300
  34.5 5.7 %copy-start.8 = (bf16[448,512]{1,0:T(8,128)(2,1)S(1)}, bf16[448,512]{1,0:T(8,128)(2,1)}, u32[]{:S(2)}) copy-start(bf16[448,512]{1,0:T(8,128)(2,1)} %param.9) | copy-start | bytes 1376260
  35.5 27.5 %all-to-all-start = ((bf16[32,24,512]{2,1,0:T(8,128)(2,1)}), bf16[32,24,512]{2,1,0:T(8,128)(2,1)S(1)}, u32[]{:S(2)}, u32[]{:S(2)}) async-start(bf16[32,24,512]{2,1,0:T(8,128)(2,1)} %broadcast_in_dim.10), calls=%async_computation | async-start | bytes 1572864 | tf_op jit(solution)/shard_map/all_to_all | solution.py:32
  41.9 25.1 %copy-start.6 = (bf16[512,448]{0,1:T(8,128)(2,1)S(1)}, bf16[512,448]{0,1:T(8,128)(2,1)}, u32[]{:S(2)}) copy-start(bf16[512,448]{0,1:T(8,128)(2,1)} %param.8) | copy-start | bytes 1376260
  63.0 23.3 %all-to-all-start.4 = ((f32[4,192,448]{2,1,0:T(8,128)}), f32[4,192,448]{2,1,0:T(8,128)S(1)}, u32[]{:S(2)}, u32[]{:S(2)}) async-start(f32[4,192,448]{2,1,0:T(8,128)} %fusion.2), calls=%async_computation.4 | async-start | bytes 3145728 | tf_op jit(solution)/shard_map/all_to_all | solution.py:25
  86.3 39.9 %all-to-all-start.1 = ((f32[2,4,192,448]{3,2,0,1:T(8,128)}), f32[2,4,192,448]{3,2,0,1:T(8,128)}, u32[]{:S(2)}, u32[]{:S(2)}) async-start(f32[2,4,192,448]{3,2,0,1:T(8,128)} %copy.13), calls=%async_computation.1 | async-start | bytes 6291456 | tf_op jit(solution)/shard_map/all_to_all | solution.py:25
  126.2 17.9 %all-to-all-start.5 = ((f32[4,48,448]{2,1,0:T(8,128)}), f32[4,48,448]{2,1,0:T(8,128)S(1)}, u32[]{:S(2)}, u32[]{:S(2)}) async-start(f32[4,48,448]{2,1,0:T(8,128)} %bitcast.65), calls=%async_computation.5 | async-start | bytes 786432 | tf_op jit(solution)/shard_map/all_to_all | solution.py:25
  144.1 16.0 %all-to-all-start.2 = ((f32[2,4,48,448]{3,2,0,1:T(8,128)}), f32[2,4,48,448]{3,2,0,1:T(8,128)S(1)}, u32[]{:S(2)}, u32[]{:S(2)}) async-start(f32[2,4,48,448]{3,2,0,1:T(8,128)} %copy.14), calls=%async_computation.2 | async-start | bytes 1572864 | tf_op jit(solution)/shard_map/all_to_all | solution.py:25
  197.0 2.3 copy-start.1
  197.0 2.3 copy-start.4
  199.3 67.4 %all-to-all-start.8 = ((f32[32,24,512]{2,1,0:T(8,128)}), f32[32,24,512]{2,1,0:T(8,128)S(1)}, u32[]{:S(2)}, u32[]{:S(2)}) async-start(f32[32,24,512]{2,1,0:T(8,128)} %bitcast.56), calls=%async_computation.8 | async-start | bytes 3145728 | tf_op jit(solution)/shard_map/all_to_all | solution.py:25
  227.5 2.5 copy-start.5
  230.0 1.3 copy-start.3
  230.0 1.4 copy-start.7

commit v4 on v2

--- a/solution.py
+++ b/solution.py
@@ -37,7 +37,9 @@
     contract_last = (((1,), (1,)), ((), ()))
     contract_first = (((0,), (0,)), ((), ()))
     both = jnp.concatenate([tokens, out_grad], 1)
-    both = gather_a2a(both, SEC, nsec, 0)
+    both = gather_a2a(both, ("y", "zl"), nsec // 2, 0)
+    both = both.reshape((nsec // 2, 1, -1) + both.shape[1:])
+    both = gather_a2a(both, "c", 2, 1).reshape((-1,) + both.shape[3:])
     all_tokens, all_grads = both[:, : tokens.shape[1]], both[:, tokens.shape[1] :]
     gate_part = jnp.dot(all_tokens, gate_weight, preferred_element_type=jnp.float32)
     up_part = jnp.dot(all_tokens, up_weight, preferred_element_type=jnp.float32)
@@ -64,7 +66,9 @@
     result = lax.dot_general(
         gate_delta, gate_weight, contract_last, preferred_element_type=jnp.float32
     ) + lax.dot_general(up_delta, up_weight, contract_last, preferred_element_type=jnp.float32)
-    grad_input = scatter_sum(result, SEC, nsec, 0).astype(jnp.bfloat16)
+    result = result.reshape((nsec // 2, 2, -1) + result.shape[1:])
+    result = scatter_sum(result, "c", 2, 1).reshape((-1,) + result.shape[3:])
+    grad_input = scatter_sum(result, ("y", "zl"), nsec // 2, 0).astype(jnp.bfloat16)
     return (grad_input, grad_gate, grad_up, grad_down)
 
 

time: 255 us -> 233 us (0.914)
  starting transfers between devices: 25.4 us -> 4.29 us
  waiting for transfers between devices: 34.1 us -> 15.7 us
  blocking collectives: 175 us -> 190 us
    all_to_all x1, starting transfers between devices: 25.4 us -> 4.29 us  [scatter_sum(): v = lax.all_to_all(v, axis_name, dim, dim, tiled=True)]
    all_to_all x1, waiting for transfers between devices: 34.1 us -> 15.7 us  [scatter_sum(): v = lax.all_to_all(v, axis_name, dim, dim, tiled=True)]
    all_to_all x2 -> x3, blocking collectives: 88.3 us -> 106 us  [scatter_sum(): v = lax.all_to_all(v, axis_name, dim, dim, tiled=True)]
    all_to_all x3 -> x4, blocking collectives: 86.5 us -> 83.6 us  [gather_a2a(): v = lax.all_to_all(v, axis_name, dim, dim, tiled=True)]
    reduce_sum x3 -> x4, other arithmetic: 5.31 us -> 7.5 us  [scatter_sum(): return v.sum(dim)]
where the time goes in v4:
time: 233 us; the launch traced here: 232 us
  blocking collectives  190 us (82%)
  waiting for transfers between devices  15.7 us (7%)
  other arithmetic  8.92 us (4%)
  matrix products  8.03 us (3%)
  starting transfers between devices  4.29 us (2%)
  local copies, waits for them, and re-layouts  4.2 us (2%)
    all_to_all x3, blocking collectives, scatter_sum(): v = lax.all_to_all(v, axis_name, dim, dim, tiled=True)  106 us
    all_to_all x4, blocking collectives, gather_a2a(): v = lax.all_to_all(v, axis_name, dim, dim, tiled=True)  83.6 us
    all_to_all x1, waiting for transfers between devices, scatter_sum(): v = lax.all_to_all(v, axis_name, dim, dim, tiled=True)  15.7 us
    reduce_sum x4, other arithmetic, scatter_sum(): return v.sum(dim)  7.5 us
  transfers between devices with their start and end apart: 1, of which 1 were waited for; matrix products, arithmetic and copies ran while one was open for 2% of the time, Pallas kernels for 0%

profile of v4, /device:TPU:1, one launch (start us, length us, event | category | flops | bytes accessed | tf_op | source)
XLA Modules:
  0.0 231.7 jit_solution(16476344453257823339)
XLA Ops:
  0.6 0.0 copy-start
  0.6 0.8 pad_maximum_fusion.2
  1.5 0.1 broadcast_in_dim.10
  1.5 31.3 %all_to_all.40 = bf16[16,24,1024]{2,1,0:T(8,128)(2,1)S(1)} all-to-all(bf16[16,24,1024]{2,1,0:T(8,128)(2,1)S(1)} %broadcast_in_dim.10), channel_id=1, replica_groups=mesh['y'=8,'zl'=2,'c'=2,'x'=4,'zh'=4] {'y','zl'}, dimensions={0} | all-to-all | bytes 1572864 | tf_op jit(solution)/shard_map/all_to_all | solution.py:32
  32.9 0.2 broadcast_in_dim.11
  33.1 7.0 %all_to_all.41 = bf16[16,2,1,24,1024]{4,3,2,0,1:T(8,128)(2,1)S(1)} all-to-all(bf16[16,2,1,24,1024]{4,3,2,0,1:T(8,128)(2,1)S(1)} %broadcast_in_dim.11), channel_id=1, replica_groups=mesh['y'=8,'zl'=2,'c'=2,'x'=4,'zh'=4] {'c'}, dimensions={1} | all-to-all | bytes 3145728 | tf_op jit(solution)/shard_map/all_to_all | solution.py:32
  40.1 0.0 copy-start.2
  40.1 0.1 copy.25
  40.2 0.0 copy-start.5
  40.2 0.8 copy-done.2
  41.1 0.6 fusion.5
  41.7 0.0 copy-done.5
  41.7 0.6 fusion.1
  42.3 0.0 copy-done
  42.3 0.6 fusion.7
  42.9 0.5 pad_maximum_fusion
  43.4 0.5 copy.29
  43.9 57.5 %all_to_all.42 = f32[3,4,192,448]{3,2,0,1:T(8,128)} all-to-all(f32[3,4,192,448]{3,2,0,1:T(8,128)S(1)} %copy.29), channel_id=1, replica_groups=mesh['y'=8,'zl'=2,'c'=2,'x'=4,'zh'=4] {'x'}, dimensions={1} | all-to-all | bytes 8257536 | tf_op jit(solution)/shard_map/all_to_all | solution.py:25
  101.4 3.1 %reduce_sum.36 = f32[3,192,448]{2,1,0:T(8,128)S(1)} reduce(f32[3,4,192,448]{3,2,0,1:T(8,128)} %all_to_all.42, f32[]{:T(128)} %constant.0.clone.1), dimensions={1}, to_apply=%region_0.0 | reduce | flops 774144 | bytes 5160964 | tf_op jit(solution)/shard_map/reduce_sum | solution.py:26
  104.5 0.1 copy.30
  104.6 37.8 %all_to_all.43 = f32[3,4,48,448]{3,2,0,1:T(8,128)S(1)} all-to-all(f32[3,4,48,448]{3,2,0,1:T(8,128)S(1)} %copy.30), channel_id=1, replica_groups=mesh['y'=8,'zl'=2,'c'=2,'x'=4,'zh'=4] {'zh'}, dimensions={1} | all-to-all | bytes 2064384 | tf_op jit(solution)/shard_map/all_to_all | solution.py:25
  142.4 0.1 reduce_sum.37
  142.6 0.1 multiply_convert_fusion.2
  142.7 18.0 %all_to_all.44 = bf16[3,4,48,448]{3,2,0,1:T(8,128)(2,1)S(1)} all-to-all(bf16[3,4,48,448]{3,2,0,1:T(8,128)(2,1)S(1)} %broadcast_in_dim.12), channel_id=1, replica_groups=mesh['y'=8,'zl'=2,'c'=2,'x'=4,'zh'=4] {'zh'}, dimensions={1} | all-to-all | bytes 1032192 | tf_op jit(solution)/shard_map/all_to_all | solution.py:32
  160.8 0.2 broadcast_in_dim.28
  161.0 27.2 %all_to_all.45 = bf16[3,4,192,448]{3,2,0,1:T(8,128)(2,1)S(1)} all-to-all(bf16[3,4,192,448]{3,2,0,1:T(8,128)(2,1)S(1)} %broadcast_in_dim.28), channel_id=1, replica_groups=mesh['y'=8,'zl'=2,'c'=2,'x'=4,'zh'=4] {'x'}, dimensions={1} | all-to-all | bytes 4128768 | tf_op jit(solution)/shard_map/all_to_all | solution.py:32
  188.2 1.1 fusion.10
  189.3 0.0 copy-start.1
  189.3 0.0 copy-start.3
  189.3 0.6 fusion.11
  189.9 0.7 copy-done.3
  190.6 0.6 convolution_add_fusion
  191.2 0.0 copy-done.1
  191.2 0.1 copy.32
  191.4 10.8 %all_to_all.46 = f32[16,2,1,24,512]{4,3,0,2,1:T(8,128)} all-to-all(f32[16,2,1,24,512]{4,3,0,2,1:T(8,128)S(1)} %copy.32), channel_id=1, replica_groups=mesh['y'=8,'zl'=2,'c'=2,'x'=4,'zh'=4] {'c'}, dimensions={1} | all-to-all | bytes 3145728 | tf_op jit(solution)/shard_map/all_to_all | solution.py:25
  202.2 2.5 %reduce_sum.38 = f32[16,24,512]{2,1,0:T(8,128)} reduce(f32[16,2,1,24,512]{4,3,0,2,1:T(8,128)} %all_to_all.46, f32[]{:T(128)} %constant.0.clone.1), dimensions={1,2}, to_apply=%region_2.0 | reduce | flops 196608 | bytes 2359300 | tf_op jit(solution)/shard_map/reduce_sum | solution.py:26
  204.7 4.3 %all-to-all-start.7 = ((f32[16,24,512]{2,1,0:T(8,128)}), f32[16,24,512]{2,1,0:T(8,128)}, u32[]{:S(2)}, u32[]{:S(2)}) async-start(f32[16,24,512]{2,1,0:T(8,128)} %reduce_sum.38), calls=%async_computation.7 | async-start | bytes 1572864 | tf_op jit(solution)/shard_map/all_to_all | solution.py:25
  209.0 2.5 %convolution_convert_fusion.1 = bf16[512,448]{0,1:T(8,128)(2,1)} fusion(bf16[768,448]{1,0:T(8,128)(2,1)} %bitcast.34, bf16[768,1024]{1,0:T(8,128)(2,1)S(1)} %bitcast.23), kind=kOutput, calls=%fused_computation.3 | convolution fusion | flops 352550912 | bytes 1933312 | tf_op jit(solution)/shard_map/dot_general | solution.py:63
  211.5 0.0 copy-start.4
  211.5 1.3 convolution_convert_fusion.2
  212.8 0.0 copy-done.4
  212.8 1.3 convolution_convert_fusion
  214.1 15.7 %all-to-all-done.7 = f32[16,24,512]{2,1,0:T(8,128)} async-done(((f32[16,24,512]{2,1,0:T(8,128)}), f32[16,24,512]{2,1,0:T(8,128)}, u32[]{:S(2)}, u32[]{:S(2)}) %all-to-all-start.7) | async-done | bytes 786464 | tf_op jit(solution)/shard_map/all_to_all | solution.py:25
  229.9 1.8 reduce_sum.39
  (3 shorter events, 0.1 us)
Async XLA Ops:
  0.6 41.6 %copy-start = (bf16[512,448]{0,1:T(8,128)(2,1)S(1)}, bf16[512,448]{0,1:T(8,128)(2,1)}, u32[]{:S(2)}) copy-start(bf16[512,448]{0,1:T(8,128)(2,1)} %param.7) | copy-start | bytes 1376260
  40.1 1.0 copy-start.2
  40.2 1.5 copy-start.5
  189.3 1.9 copy-start.1
  189.3 1.3 copy-start.3
  204.7 25.2 %all-to-all-start.7 = ((f32[16,24,512]{2,1,0:T(8,128)}), f32[16,24,512]{2,1,0:T(8,128)}, u32[]{:S(2)}, u32[]{:S(2)}) async-start(f32[16,24,512]{2,1,0:T(8,128)} %reduce_sum.38), calls=%async_computation.7 | async-start | bytes 1572864 | tf_op jit(solution)/shard_map/all_to_all | solution.py:25
  211.5 1.3 copy-start.4

commit v5 on v4

--- a/solution.py
+++ b/solution.py
@@ -47,12 +47,16 @@
         all_grads, down_weight, contract_last, preferred_element_type=jnp.float32
     )
     parts = jnp.stack([gate_part, up_part, hidden_part])
-    parts = scatter_sum(parts, "x", nx, 1)
-    parts = scatter_sum(parts, "zh", nzh, 1)
-    hidden, gate_delta, up_delta = swiglu_grads(parts[0], parts[1], parts[2])
-    deltas = jnp.stack([hidden, gate_delta, up_delta])
-    deltas = gather_a2a(deltas, "zh", nzh, 1)
-    deltas = gather_a2a(deltas, "x", nx, 1)
+    width = parts.shape[2] // 2
+    chunks = []
+    for c in range(2):
+        p = parts[:, :, c * width : (c + 1) * width]
+        p = scatter_sum(p, "x", nx, 1)
+        p = lax.psum_scatter(p, "zh", scatter_dimension=1, tiled=True)
+        d = jnp.stack(swiglu_grads(p[0], p[1], p[2]))
+        d = lax.all_gather(d, "zh", axis=1, tiled=True)
+        chunks.append(gather_a2a(d, "x", nx, 1))
+    deltas = jnp.concatenate(chunks, 2)
     hidden, gate_delta, up_delta = deltas[0], deltas[1], deltas[2]
     grad_down = lax.dot_general(
         hidden, all_grads, contract_first, preferred_element_type=jnp.float32

time: 233 us -> 246 us (1.056)
  blocking collectives: 190 us -> 74.6 us
  waiting for transfers between devices: 15.7 us -> 94.7 us
  starting transfers between devices: 4.29 us -> 21.8 us
  local copies, waits for them, and re-layouts: 4.2 us -> 18.6 us
  between operations: 0.81 us -> 14.2 us
    all_to_all x3 -> x1, blocking collectives: 106 us -> 10.1 us  [scatter_sum(): v = lax.all_to_all(v, axis_name, dim, dim, tiled=True)]
    all_to_all x1 -> x3, waiting for transfers between devices: 15.7 us -> 61.9 us  [scatter_sum(): v = lax.all_to_all(v, axis_name, dim, dim, tiled=True)]
    all_to_all x4 -> x2, blocking collectives: 83.6 us -> 38.3 us  [gather_a2a(): v = lax.all_to_all(v, axis_name, dim, dim, tiled=True)]
    all_gather x0 -> x2, blocking collectives: none -> 26.2 us  [local(): d = lax.all_gather(d, 'zh', axis=1, tiled=True)]
    reduce_scatter x0 -> x2, waiting for transfers between devices: none -> 20 us  [local(): p = lax.psum_scatter(p, 'zh', scatter_dimension=1, tiled=True)]
    all_to_all x0 -> x2, waiting for transfers between devices: none -> 12.8 us  [gather_a2a(): v = lax.all_to_all(v, axis_name, dim, dim, tiled=True)]
    all_to_all x1 -> x3, starting transfers between devices: 4.29 us -> 13.8 us  [scatter_sum(): v = lax.all_to_all(v, axis_name, dim, dim, tiled=True)]
    all_to_all x0 -> x2, starting transfers between devices: none -> 7.96 us  [gather_a2a(): v = lax.all_to_all(v, axis_name, dim, dim, tiled=True)]
  transfers between devices with their start and end apart: 1 -> 7, of which waited for: 1 -> 6; matrix products, arithmetic and copies ran while one was open for 2% -> 8% of each run, Pallas kernels for 0% -> 0%
where the time goes in v5:
time: 246 us; the launch traced here: 244 us
  waiting for transfers between devices  94.7 us (38%)
  blocking collectives  74.6 us (30%)
  starting transfers between devices  21.8 us (9%)
  local copies, waits for them, and re-layouts  18.6 us (8%)
  between operations  14.2 us (6%)
  other arithmetic  11 us (4%)
  matrix products  9.04 us (4%)
    all_to_all x3, waiting for transfers between devices, scatter_sum(): v = lax.all_to_all(v, axis_name, dim, dim, tiled=True)  61.9 us
    all_to_all x2, blocking collectives, gather_a2a(): v = lax.all_to_all(v, axis_name, dim, dim, tiled=True)  38.3 us
    all_gather x2, blocking collectives, local(): d = lax.all_gather(d, 'zh', axis=1, tiled=True)  26.2 us
    reduce_scatter x2, waiting for transfers between devices, local(): p = lax.psum_scatter(p, 'zh', scatter_dimension=1, tiled=True)  20 us
    all_to_all x3, starting transfers between devices, scatter_sum(): v = lax.all_to_all(v, axis_name, dim, dim, tiled=True)  13.8 us
    all_to_all x2, waiting for transfers between devices, gather_a2a(): v = lax.all_to_all(v, axis_name, dim, dim, tiled=True)  12.8 us
    all_to_all x1, blocking collectives, scatter_sum(): v = lax.all_to_all(v, axis_name, dim, dim, tiled=True)  10.1 us
    reduce_sum x4, other arithmetic, scatter_sum(): return v.sum(dim)  8.12 us
  transfers between devices with their start and end apart: 7, of which 6 were waited for; matrix products, arithmetic and copies ran while one was open for 8% of the time, Pallas kernels for 0%

profile of v5, /device:TPU:1, one launch (start us, length us, event | category | flops | bytes accessed | tf_op | source)
XLA Modules:
  0.0 244.1 jit_solution(16885144752064132307)
XLA Ops:
  7.2 0.8 pad_maximum_fusion.4
  8.0 0.1 broadcast_in_dim.8
  8.1 31.3 %all_to_all.40 = bf16[16,24,1024]{2,1,0:T(8,128)(2,1)S(1)} all-to-all(bf16[16,24,1024]{2,1,0:T(8,128)(2,1)S(1)} %broadcast_in_dim.8), channel_id=1, replica_groups=mesh['y'=8,'zl'=2,'c'=2,'x'=4,'zh'=4] {'y','zl'}, dimensions={0} | all-to-all | bytes 1572864 | tf_op jit(solution)/shard_map/all_to_all | solution.py:32
  39.4 0.2 broadcast_in_dim.9
  39.6 7.0 %all_to_all.41 = bf16[16,2,1,24,1024]{4,3,2,0,1:T(8,128)(2,1)S(1)} all-to-all(bf16[16,2,1,24,1024]{4,3,2,0,1:T(8,128)(2,1)S(1)} %broadcast_in_dim.9), channel_id=1, replica_groups=mesh['y'=8,'zl'=2,'c'=2,'x'=4,'zh'=4] {'c'}, dimensions={1} | all-to-all | bytes 3145728 | tf_op jit(solution)/shard_map/all_to_all | solution.py:32
  46.6 0.2 copy.24
  46.8 0.8 copy-done.4
  47.6 0.6 convolution_bitcast_fusion.1
  48.2 0.6 convolution_bitcast_fusion
  48.8 0.6 convolution_bitcast_fusion.2
  49.3 0.3 pad_maximum_fusion
  49.6 2.2 fusion.21
  51.8 2.0 copy.28
  53.8 1.7 copy.29
  55.5 4.0 %all-to-all-start.4 = ((f32[3,4,192,224]{3,2,0,1:T(8,128)}), f32[3,4,192,224]{3,2,0,1:T(8,128)S(1)}, u32[]{:S(2)}, u32[]{:S(2)}) async-start(f32[3,4,192,224]{3,2,0,1:T(8,128)} %copy.29), calls=%async_computation.5 | async-start | bytes 4718592 | tf_op jit(solution)/shard_map/all_to_all | solution.py:25
  59.5 3.0 %copy.25 = f32[3,768,224]{2,1,0:T(8,128)} copy(f32[3,768,224]{1,2,0:T(8,128)} %get-tuple-element.5) | data formatting | bytes 4128768 | tf_op jit(solution)/shard_map/slice | solution.py:53
  62.5 3.2 %copy.26 = f32[3,4,192,224]{3,2,0,1:T(8,128)} copy(f32[3,4,192,224]{3,2,1,0:T(8,128)} %bitcast.45) | data formatting | bytes 4128768 | tf_op jit(solution)/shard_map/reshape | solution.py:24
  65.8 22.3 %all-to-all-done.4 = f32[3,4,192,224]{3,2,0,1:T(8,128)S(1)} async-done(((f32[3,4,192,224]{3,2,0,1:T(8,128)}), f32[3,4,192,224]{3,2,0,1:T(8,128)S(1)}, u32[]{:S(2)}, u32[]{:S(2)}) %all-to-all-start.4) | async-done | bytes 2064416 | tf_op jit(solution)/shard_map/all_to_all | solution.py:25
  88.1 1.4 copy-done.3
  89.5 3.6 %all-to-all-start.2 = ((f32[3,4,192,224]{3,2,0,1:T(8,128)}), f32[3,4,192,224]{3,2,0,1:T(8,128)S(1)}, u32[]{:S(2)}, u32[]{:S(2)}) async-start(f32[3,4,192,224]{3,2,0,1:T(8,128)} %copy.26), calls=%async_computation.2 | async-start | bytes 4718592 | tf_op jit(solution)/shard_map/all_to_all | solution.py:25
  93.2 2.7 %reduce_sum.37 = f32[3,192,224]{2,1,0:T(8,128)} reduce(f32[3,4,192,224]{3,2,0,1:T(8,128)} %copy-done.3, f32[]{:T(128)} %constant.0.clone.1), dimensions={1}, to_apply=%region_2.0 | reduce | flops 387072 | bytes 2580484 | tf_op jit(solution)/shard_map/reduce_sum | solution.py:26
  96.0 0.0 reduce-scatter.3.cloned.1.call-start
  96.0 24.8 %all-to-all-done.2 = f32[3,4,192,224]{3,2,0,1:T(8,128)S(1)} async-done(((f32[3,4,192,224]{3,2,0,1:T(8,128)}), f32[3,4,192,224]{3,2,0,1:T(8,128)S(1)}, u32[]{:S(2)}, u32[]{:S(2)}) %all-to-all-start.2) | async-done | bytes 2064416 | tf_op jit(solution)/shard_map/all_to_all | solution.py:25
  120.8 1.1 reduce_sum.36
  121.9 5.7 %reduce-scatter.5.cloned.1.call-done = f32[3,48,224]{2,1,0:T(8,128)} async-done(((f32[3,192,224]{2,1,0:T(8,128)}), f32[3,48,224]{2,1,0:T(8,128)}) %reduce-scatter.5.cloned.1.call-update) | async-done | bytes 129040 | tf_op jit(solution)/shard_map/reduce_scatter | solution.py:55
  127.6 0.9 multiply_convert_fusion.2
  128.5 13.0 %all_gather.7 = bf16[3,192,224]{2,1,0:T(8,128)(2,1)S(1)} all-gather(bf16[3,48,224]{2,1,0:T(8,128)(2,1)S(1)} %pad_maximum_fusion.3), channel_id=1, replica_groups=mesh['y'=8,'zl'=2,'c'=2,'x'=4,'zh'=4] {'zh'}, dimensions={1}, use_global_device_ids=true | all-gather | bytes 322560 | tf_op jit(solution)/shard_map/all_gather | solution.py:57
  141.5 1.1 broadcast_in_dim.11
  142.7 3.7 %all-to-all-start.5 = ((bf16[3,4,192,224]{3,2,0,1:T(8,128)(2,1)}), bf16[3,4,192,224]{3,2,0,1:T(8,128)(2,1)S(1)}, u32[]{:S(2)}, u32[]{:S(2)}) async-start(bf16[3,4,192,224]{3,2,0,1:T(8,128)(2,1)} %broadcast_in_dim.11), calls=%async_computation.7 | async-start | bytes 2359296 | tf_op jit(solution)/shard_map/all_to_all | solution.py:32
  146.4 14.3 %reduce-scatter.3.cloned.1.call-done = f32[3,48,224]{2,1,0:T(8,128)} async-done(((f32[3,192,224]{2,1,0:T(8,128)}), f32[3,48,224]{2,1,0:T(8,128)}) %reduce-scatter.3.cloned.1.call-update) | async-done | bytes 129040 | tf_op jit(solution)/shard_map/reduce_scatter | solution.py:55
  160.7 0.9 multiply_convert_fusion.5
  161.6 13.2 %all_gather.6 = bf16[3,192,224]{2,1,0:T(8,128)(2,1)S(1)} all-gather(bf16[3,48,224]{2,1,0:T(8,128)(2,1)S(1)} %pad_maximum_fusion.2), channel_id=1, replica_groups=mesh['y'=8,'zl'=2,'c'=2,'x'=4,'zh'=4] {'zh'}, dimensions={1}, use_global_device_ids=true | all-gather | bytes 322560 | tf_op jit(solution)/shard_map/all_gather | solution.py:57
  174.8 1.1 broadcast_in_dim.10
  175.9 4.3 %all-to-all-start.3 = ((bf16[3,4,192,224]{3,2,0,1:T(8,128)(2,1)}), bf16[3,4,192,224]{3,2,0,1:T(8,128)(2,1)}, u32[]{:S(2)}, u32[]{:S(2)}) async-start(bf16[3,4,192,224]{3,2,0,1:T(8,128)(2,1)} %broadcast_in_dim.10), calls=%async_computation.4 | async-start | bytes 2359296 | tf_op jit(solution)/shard_map/all_to_all | solution.py:32
  180.2 0.1 copy.30
  180.3 12.8 %all-to-all-done.3 = bf16[3,4,192,224]{3,2,0,1:T(8,128)(2,1)} async-done(((bf16[3,4,192,224]{3,2,0,1:T(8,128)(2,1)}), bf16[3,4,192,224]{3,2,0,1:T(8,128)(2,1)}, u32[]{:S(2)}, u32[]{:S(2)}) %all-to-all-start.3) | async-done | bytes 1032224 | tf_op jit(solution)/shard_map/all_to_all | solution.py:32
  193.1 1.3 copy.27
  194.4 0.6 fusion.17
  195.1 0.6 convolution_add_fusion
  195.7 0.1 copy.31
  195.8 10.1 %all_to_all.42 = f32[16,2,1,24,512]{4,3,0,2,1:T(8,128)} all-to-all(f32[16,2,1,24,512]{4,3,0,2,1:T(8,128)S(1)} %copy.31), channel_id=1, replica_groups=mesh['y'=8,'zl'=2,'c'=2,'x'=4,'zh'=4] {'c'}, dimensions={1} | all-to-all | bytes 3145728 | tf_op jit(solution)/shard_map/all_to_all | solution.py:25
  205.9 2.5 %reduce_sum.38 = f32[16,24,512]{2,1,0:T(8,128)} reduce(f32[16,2,1,24,512]{4,3,0,2,1:T(8,128)} %all_to_all.42, f32[]{:T(128)} %constant.0.clone.1), dimensions={1,2}, to_apply=%region_4.0 | reduce | flops 196608 | bytes 2359300 | tf_op jit(solution)/shard_map/reduce_sum | solution.py:26
  208.4 6.1 %all-to-all-start.7 = ((f32[16,24,512]{2,1,0:T(8,128)}), f32[16,24,512]{2,1,0:T(8,128)}, u32[]{:S(2)}, u32[]{:S(2)}) async-start(f32[16,24,512]{2,1,0:T(8,128)} %reduce_sum.38), calls=%async_computation.9 | async-start | bytes 1572864 | tf_op jit(solution)/shard_map/all_to_all | solution.py:25
  214.6 2.8 %convolution_convert_fusion.1 = bf16[512,448]{0,1:T(8,128)(2,1)} fusion(bf16[768,1024]{1,0:T(8,128)(2,1)} %bitcast.41, bf16[3,768,224]{2,1,0:T(8,128)(2,1)S(1)} %bitcast.35, bf16[3,768,224]{2,1,0:T(8,128)(2,1)S(1)} %bitcast.30), kind=kOutput, calls=%fused_computation.10 | convolution fusion | flops 353927168 | bytes 3309568 | tf_op jit(solution)/shard_map/dot_general | solution.py:67
  217.4 1.6 convolution_convert_fusion.2
  218.9 1.7 convolution_convert_fusion
  220.7 14.8 %all-to-all-done.7 = f32[16,24,512]{2,1,0:T(8,128)} async-done(((f32[16,24,512]{2,1,0:T(8,128)}), f32[16,24,512]{2,1,0:T(8,128)}, u32[]{:S(2)}, u32[]{:S(2)}) %all-to-all-start.7) | async-done | bytes 786464 | tf_op jit(solution)/shard_map/all_to_all | solution.py:25
  235.4 1.8 reduce_sum.39
  (16 shorter events, 0.1 us)
Async XLA Ops:
  7.2 41.6 %copy-start = (bf16[512,448]{0,1:T(8,128)(2,1)S(1)}, bf16[512,448]{0,1:T(8,128)(2,1)}, u32[]{:S(2)}) copy-start(bf16[512,448]{0,1:T(8,128)(2,1)} %param.7) | copy-start | bytes 1376260
  46.6 1.0 copy-start.4
  46.8 2.0 copy-start.1
  46.8 1.4 copy-start.5
  55.5 32.6 %all-to-all-start.4 = ((f32[3,4,192,224]{3,2,0,1:T(8,128)}), f32[3,4,192,224]{3,2,0,1:T(8,128)S(1)}, u32[]{:S(2)}, u32[]{:S(2)}) async-start(f32[3,4,192,224]{3,2,0,1:T(8,128)} %copy.29), calls=%async_computation.5 | async-start | bytes 4718592 | tf_op jit(solution)/shard_map/all_to_all | solution.py:25
  88.1 1.4 copy-start.3
  89.5 31.3 %all-to-all-start.2 = ((f32[3,4,192,224]{3,2,0,1:T(8,128)}), f32[3,4,192,224]{3,2,0,1:T(8,128)S(1)}, u32[]{:S(2)}, u32[]{:S(2)}) async-start(f32[3,4,192,224]{3,2,0,1:T(8,128)} %copy.26), calls=%async_computation.2 | async-start | bytes 4718592 | tf_op jit(solution)/shard_map/all_to_all | solution.py:25
  93.2 34.4 %reduce-scatter.5.cloned.1.call-start = ((), (), s32[]{:S(2)}) async-start(), calls=%async_computation.11 | async-start | bytes 737280 | tf_op jit(solution)/shard_map/reduce_scatter | solution.py:55
  96.0 64.7 %reduce-scatter.3.cloned.1.call-start = ((), (), s32[]{:S(2)}) async-start(), calls=%async_computation.10 | async-start | bytes 737280 | tf_op jit(solution)/shard_map/reduce_scatter | solution.py:55
  142.7 32.1 %all-to-all-start.5 = ((bf16[3,4,192,224]{3,2,0,1:T(8,128)(2,1)}), bf16[3,4,192,224]{3,2,0,1:T(8,128)(2,1)S(1)}, u32[]{:S(2)}, u32[]{:S(2)}) async-start(bf16[3,4,192,224]{3,2,0,1:T(8,128)(2,1)} %broadcast_in_dim.11), calls=%async_computation.7 | async-start | bytes 2359296 | tf_op jit(solution)/shard_map/all_to_all | solution.py:32
  175.9 17.2 %all-to-all-start.3 = ((bf16[3,4,192,224]{3,2,0,1:T(8,128)(2,1)}), bf16[3,4,192,224]{3,2,0,1:T(8,128)(2,1)}, u32[]{:S(2)}, u32[]{:S(2)}) async-start(bf16[3,4,192,224]{3,2,0,1:T(8,128)(2,1)} %broadcast_in_dim.10), calls=%async_computation.4 | async-start | bytes 2359296 | tf_op jit(solution)/shard_map/all_to_all | solution.py:32
  208.4 27.0 %all-to-all-start.7 = ((f32[16,24,512]{2,1,0:T(8,128)}), f32[16,24,512]{2,1,0:T(8,128)}, u32[]{:S(2)}, u32[]{:S(2)}) async-start(f32[16,24,512]{2,1,0:T(8,128)} %reduce_sum.38), calls=%async_computation.9 | async-start | bytes 1572864 | tf_op jit(solution)/shard_map/all_to_all | solution.py:25
  214.6 2.8 %copy-start.2 = (bf16[16,2,1,24,1024]{4,3,1,0,2:T(8,128)(2,1)S(1)}, bf16[16,2,1,24,1024]{4,3,1,0,2:T(8,128)(2,1)}, u32[]{:S(2)}) copy-start(bf16[16,2,1,24,1024]{4,3,1,0,2:T(8,128)(2,1)} %copy-done.1) | copy-start | bytes 4718596
Sparse Core Ops, SparseCore 0:
  96.8 30.7 reduce-scatter.4
  130.4 30.2 reduce-scatter.2

commit v6 on v5

--- a/solution.py
+++ b/solution.py
@@ -33,6 +33,29 @@
     return v.reshape(shape[:dim] + (n * shape[dim],) + shape[dim + 1 :])
 
 
+def scatter_permute(v, axis_name, n, dim):
+    me = lax.axis_index(axis_name)
+    shape = v.shape
+    size = shape[dim] // n
+    total = lax.dynamic_slice_in_dim(v, me * size, size, dim)
+    for k in range(1, n):
+        part = lax.dynamic_slice_in_dim(v, ((me + k) % n) * size, size, dim)
+        total = total + lax.ppermute(part, axis_name, [(j, (j + k) % n) for j in range(n)])
+    return total
+
+
+def gather_permute(v, axis_name, n, dim):
+    me = lax.axis_index(axis_name)
+    got = [v] + [
+        lax.ppermute(v, axis_name, [(j, (j + k) % n) for j in range(n)]) for k in range(1, n)
+    ]
+    ordered = jnp.stack([got[0]] + got[:0:-1])
+    ordered = jnp.roll(ordered, me, axis=0)
+    ordered = jnp.moveaxis(ordered, 0, dim)
+    shape = v.shape
+    return ordered.reshape(shape[:dim] + (n * shape[dim],) + shape[dim + 1 :])
+
+
 def local(tokens, out_grad, gate_weight, up_weight, down_weight, nx, nzh, nsec):
     contract_last = (((1,), (1,)), ((), ()))
     contract_first = (((0,), (0,)), ((), ()))
@@ -41,22 +64,23 @@
     both = both.reshape((nsec // 2, 1, -1) + both.shape[1:])
     both = gather_a2a(both, "c", 2, 1).reshape((-1,) + both.shape[3:])
     all_tokens, all_grads = both[:, : tokens.shape[1]], both[:, tokens.shape[1] :]
-    gate_part = jnp.dot(all_tokens, gate_weight, preferred_element_type=jnp.float32)
-    up_part = jnp.dot(all_tokens, up_weight, preferred_element_type=jnp.float32)
-    hidden_part = lax.dot_general(
-        all_grads, down_weight, contract_last, preferred_element_type=jnp.float32
-    )
-    parts = jnp.stack([gate_part, up_part, hidden_part])
-    width = parts.shape[2] // 2
+    rows = all_tokens.shape[0] // 2
     chunks = []
     for c in range(2):
-        p = parts[:, :, c * width : (c + 1) * width]
+        tok = all_tokens[c * rows : (c + 1) * rows]
+        grd = all_grads[c * rows : (c + 1) * rows]
+        gate_part = jnp.dot(tok, gate_weight, preferred_element_type=jnp.float32)
+        up_part = jnp.dot(tok, up_weight, preferred_element_type=jnp.float32)
+        hidden_part = lax.dot_general(
+            grd, down_weight, contract_last, preferred_element_type=jnp.float32
+        )
+        p = jnp.stack([gate_part, up_part, hidden_part])
         p = scatter_sum(p, "x", nx, 1)
-        p = lax.psum_scatter(p, "zh", scatter_dimension=1, tiled=True)
+        p = scatter_permute(p, "zh", nzh, 1)
         d = jnp.stack(swiglu_grads(p[0], p[1], p[2]))
-        d = lax.all_gather(d, "zh", axis=1, tiled=True)
+        d = gather_permute(d, "zh", nzh, 1)
         chunks.append(gather_a2a(d, "x", nx, 1))
-    deltas = jnp.concatenate(chunks, 2)
+    deltas = jnp.concatenate(chunks, 1)
     hidden, gate_delta, up_delta = deltas[0], deltas[1], deltas[2]
     grad_down = lax.dot_general(
         hidden, all_grads, contract_first, preferred_element_type=jnp.float32

time: 246 us -> 228 us (0.927)
  starting transfers between devices: 21.8 us -> 75.9 us
  waiting for transfers between devices: 94.7 us -> 65 us
  blocking collectives: 74.6 us -> 51.6 us
  between operations: 14.2 us -> 1.09 us
  local copies, waits for them, and re-layouts: 18.6 us -> 11.5 us
    ppermute x0 -> x12, starting transfers between devices: none -> 55.5 us  [the longest x6 29.5 us: scatter_permute(): lax.ppermute(part, axis_name, [(j, (j + k) % n) for j in range(n)])]
    all_gather x2 -> x0, blocking collectives: 26.2 us -> none  [local(): d = lax.all_gather(d, 'zh', axis=1, tiled=True)]
    reduce_scatter x2 -> x0, waiting for transfers between devices: 20 us -> none  [local(): p = lax.psum_scatter(p, 'zh', scatter_dimension=1, tiled=True)]
    all_to_all x3, waiting for transfers between devices: 61.9 us -> 47.7 us  [scatter_sum(): v = lax.all_to_all(v, axis_name, dim, dim, tiled=True)]
    slice x3 -> x0, local copies, waits for them, and re-layouts: 7.21 us -> none  [local(): p = parts[:, :, c * width:(c + 1) * width]]
    ppermute x0 -> x12, waiting for transfers between devices: none -> 6.88 us  [the longest x6 5.53 us: gather_permute(): lax.ppermute(v, axis_name, [(j, (j + k) % n) for j in range(n)])]
    reshape x2 -> x0, local copies, waits for them, and re-layouts: 4.91 us -> none  [scatter_sum(): v = v.reshape(shape[:dim] + (n, shape[dim] // n) + shape[dim + 1:])]
    another operation x0 -> x2, local copies, waits for them, and re-layouts: none -> 3.29 us  [local(): p = jnp.stack([gate_part, up_part, hidden_part])]
  transfers between devices with their start and end apart: 7 -> 17, of which waited for: 6 -> 7; matrix products, arithmetic and copies ran while one was open for 8% -> 8% of each run, Pallas kernels for 0% -> 0%
where the time goes in v6:
time: 228 us; the launch traced here: 226 us
  starting transfers between devices  75.9 us (33%)
  waiting for transfers between devices  65 us (29%)
  blocking collectives  51.6 us (23%)
  other arithmetic  12.5 us (5%)
  local copies, waits for them, and re-layouts  11.5 us (5%)
  matrix products  8.71 us (4%)
    all_to_all x3, waiting for transfers between devices, scatter_sum(): v = lax.all_to_all(v, axis_name, dim, dim, tiled=True)  47.7 us
    all_to_all x2, blocking collectives, gather_a2a(): v = lax.all_to_all(v, axis_name, dim, dim, tiled=True)  38.3 us
    ppermute x6, starting transfers between devices, scatter_permute(): lax.ppermute(part, axis_name, [(j, (j + k) % n) for j in range(n)])  29.5 us
    ppermute x6, starting transfers between devices, gather_permute(): lax.ppermute(v, axis_name, [(j, (j + k) % n) for j in range(n)])  26 us
    all_to_all x1, blocking collectives, scatter_sum(): v = lax.all_to_all(v, axis_name, dim, dim, tiled=True)  13.3 us
    all_to_all x3, starting transfers between devices, scatter_sum(): v = lax.all_to_all(v, axis_name, dim, dim, tiled=True)  12.6 us
    all_to_all x2, waiting for transfers between devices, gather_a2a(): v = lax.all_to_all(v, axis_name, dim, dim, tiled=True)  10.4 us
    reduce_sum x4, other arithmetic, scatter_sum(): return v.sum(dim)  8.25 us
  transfers between devices with their start and end apart: 17, of which 7 were waited for; matrix products, arithmetic and copies ran while one was open for 8% of the time, Pallas kernels for 0%

profile of v6, /device:TPU:1, one launch (start us, length us, event | category | flops | bytes accessed | tf_op | source)
XLA Modules:
  0.0 226.3 jit_solution(17626591076731016889)
XLA Ops:
  0.6 0.8 pad_maximum_fusion.5
  1.5 31.3 %all_to_all.40 = bf16[16,24,1024]{2,1,0:T(8,128)(2,1)S(1)} all-to-all(bf16[16,24,1024]{2,1,0:T(8,128)(2,1)S(1)} %broadcast_in_dim.12), channel_id=1, replica_groups=mesh['y'=8,'zl'=2,'c'=2,'x'=4,'zh'=4] {'y','zl'}, dimensions={0} | all-to-all | bytes 1572864 | tf_op jit(solution)/shard_map/all_to_all | solution.py:32
  33.1 7.0 %all_to_all.41 = bf16[16,2,1,24,1024]{4,3,2,0,1:T(8,128)(2,1)S(1)} all-to-all(bf16[16,2,1,24,1024]{4,3,2,0,1:T(8,128)(2,1)S(1)} %broadcast_in_dim.26), channel_id=1, replica_groups=mesh['y'=8,'zl'=2,'c'=2,'x'=4,'zh'=4] {'c'}, dimensions={1} | all-to-all | bytes 3145728 | tf_op jit(solution)/shard_map/all_to_all | solution.py:32
  40.2 0.8 copy-done.3
  42.6 1.7 copy.52
  44.3 4.5 %all-to-all-start.2 = ((f32[3,4,96,448]{3,2,0,1:T(8,128)}), f32[3,4,96,448]{3,2,0,1:T(8,128)}, u32[]{:S(2)}, u32[]{:S(2)}) async-start(f32[3,4,96,448]{3,2,0,1:T(8,128)} %copy.52), calls=%async_computation.2 | async-start | bytes 4718592 | tf_op jit(solution)/shard_map/all_to_all | solution.py:25
  49.2 0.4 fusion.10
  50.2 1.6 copy.60
  51.8 25.9 %all-to-all-done.2 = f32[3,4,96,448]{3,2,0,1:T(8,128)} async-done(((f32[3,4,96,448]{3,2,0,1:T(8,128)}), f32[3,4,96,448]{3,2,0,1:T(8,128)}, u32[]{:S(2)}, u32[]{:S(2)}) %all-to-all-start.2) | async-done | bytes 2064416 | tf_op jit(solution)/shard_map/all_to_all | solution.py:25
  77.7 3.6 %all-to-all-start.4 = ((f32[3,4,96,448]{3,2,0,1:T(8,128)}), f32[3,4,96,448]{3,2,0,1:T(8,128)S(1)}, u32[]{:S(2)}, u32[]{:S(2)}) async-start(f32[3,4,96,448]{3,2,0,1:T(8,128)} %copy.60), calls=%async_computation.4 | async-start | bytes 4718592 | tf_op jit(solution)/shard_map/all_to_all | solution.py:25
  81.4 2.8 %reduce_sum.36 = f32[3,96,448]{2,1,0:T(8,128)} reduce(f32[3,4,96,448]{3,2,0,1:T(8,128)} %all-to-all-done.2, f32[]{:T(128)} %constant.52.clone.1), dimensions={1}, to_apply=%region_0.0 | reduce | flops 387072 | bytes 2580484 | tf_op jit(solution)/shard_map/reduce_sum | solution.py:26
  84.3 1.8 constant_dynamic-slice_fusion.5
  86.1 5.8 %collective-permute-start = (f32[3,24,448]{2,1,0:T(8,128)}, f32[3,24,448]{2,1,0:T(8,128)S(1)}, u32[]{:S(2)}, u32[]{:S(2)}) collective-permute-start(f32[3,24,448]{2,1,0:T(8,128)} %get-tuple-element.8), channel_id=1, source_target_pairs={{0,1},{1,2},{2,3},{3,0},{4,5},{5,6},{6,7},{7,4},{8,9},{9,10},{10,1... | collective-permute-start | bytes 387080 | tf_op jit(solution)/shard_map/ppermute | solution.py:43
  91.9 5.9 %collective-permute-start.2 = (f32[3,24,448]{2,1,0:T(8,128)}, f32[3,24,448]{2,1,0:T(8,128)}, u32[]{:S(2)}, u32[]{:S(2)}) collective-permute-start(f32[3,24,448]{2,1,0:T(8,128)} %get-tuple-element.9), channel_id=1, source_target_pairs={{0,3},{1,0},{2,1},{3,2},{4,7},{5,4},{6,5},{7,6},{8,11},{9,8},{10,9... | collective-permute-start | bytes 387080 | tf_op jit(solution)/shard_map/ppermute | solution.py:43
  97.8 5.5 %collective-permute-start.1 = (f32[3,24,448]{2,1,0:T(8,128)}, f32[3,24,448]{2,1,0:T(8,128)}, u32[]{:S(2)}, u32[]{:S(2)}) collective-permute-start(f32[3,24,448]{2,1,0:T(8,128)} %get-tuple-element.10), channel_id=1, source_target_pairs={{0,2},{1,3},{2,0},{3,1},{4,6},{5,7},{6,4},{7,5},{8,10},{9,11},{10,... | collective-permute-start | bytes 387080 | tf_op jit(solution)/shard_map/ppermute | solution.py:43
  103.2 6.2 %all-to-all-done.4 = f32[3,4,96,448]{3,2,0,1:T(8,128)S(1)} async-done(((f32[3,4,96,448]{3,2,0,1:T(8,128)}), f32[3,4,96,448]{3,2,0,1:T(8,128)S(1)}, u32[]{:S(2)}, u32[]{:S(2)}) %all-to-all-start.4) | async-done | bytes 2064416 | tf_op jit(solution)/shard_map/all_to_all | solution.py:25
  109.4 1.1 reduce_sum.37
  110.5 1.1 add_add_fusion.1
  111.7 9.6 %collective-permute-start.4 = (bf16[3,24,448]{2,1,0:T(8,128)(2,1)S(1)}, bf16[3,24,448]{2,1,0:T(8,128)(2,1)S(1)}, u32[]{:S(2)}, u32[]{:S(2)}) collective-permute-start(bf16[3,24,448]{2,1,0:T(8,128)(2,1)S(1)} %get-tuple-element.19), channel_id=1, source_target_pairs={{0,2},{1,3},{2,0},{3,1},{4,6},{5,7},{6,4},{7,5},{8,10},{9,11},{10,... | collective-permute-start | bytes 193544 | tf_op jit(solution)/shard_map/ppermute | solution.py:50
  121.4 1.9 collective-permute-start.3
  123.3 4.3 %collective-permute-start.5 = (bf16[3,24,448]{2,1,0:T(8,128)(2,1)S(1)}, bf16[3,24,448]{2,1,0:T(8,128)(2,1)S(1)}, u32[]{:S(2)}, u32[]{:S(2)}) collective-permute-start(bf16[3,24,448]{2,1,0:T(8,128)(2,1)S(1)} %get-tuple-element.19), channel_id=1, source_target_pairs={{0,1},{1,2},{2,3},{3,0},{4,5},{5,6},{6,7},{7,4},{8,9},{9,10},{10,1... | collective-permute-start | bytes 193544 | tf_op jit(solution)/shard_map/ppermute | solution.py:50
  127.6 1.1 constant_dynamic-slice_fusion.2
  128.7 5.2 %collective-permute-start.6 = (f32[3,24,448]{2,1,0:T(8,128)S(1)}, f32[3,24,448]{2,1,0:T(8,128)S(1)}, u32[]{:S(2)}, u32[]{:S(2)}) collective-permute-start(f32[3,24,448]{2,1,0:T(8,128)S(1)} %get-tuple-element.5), channel_id=1, source_target_pairs={{0,1},{1,2},{2,3},{3,0},{4,5},{5,6},{6,7},{7,4},{8,9},{9,10},{10,1... | collective-permute-start | bytes 387080 | tf_op jit(solution)/shard_map/ppermute | solution.py:43
  133.9 2.2 collective-permute-start.8
  136.1 4.9 %collective-permute-start.7 = (f32[3,24,448]{2,1,0:T(8,128)S(1)}, f32[3,24,448]{2,1,0:T(8,128)S(1)}, u32[]{:S(2)}, u32[]{:S(2)}) collective-permute-start(f32[3,24,448]{2,1,0:T(8,128)S(1)} %get-tuple-element.7), channel_id=1, source_target_pairs={{0,2},{1,3},{2,0},{3,1},{4,6},{5,7},{6,4},{7,5},{8,10},{9,11},{10,... | collective-permute-start | bytes 387080 | tf_op jit(solution)/shard_map/ppermute | solution.py:43
  141.1 0.4 fusion.33
  141.5 1.1 broadcast_in_dim.28
  142.6 3.5 %all-to-all-start.3 = ((bf16[3,4,96,448]{3,2,0,1:T(8,128)(2,1)}), bf16[3,4,96,448]{3,2,0,1:T(8,128)(2,1)S(1)}, u32[]{:S(2)}, u32[]{:S(2)}) async-start(bf16[3,4,96,448]{3,2,0,1:T(8,128)(2,1)} %broadcast_in_dim.28), calls=%async_computation.3 | async-start | bytes 2359296 | tf_op jit(solution)/shard_map/all_to_all | solution.py:32
  146.2 1.3 collective-permute-done.7
  147.5 1.0 add_add_fusion
  148.5 3.4 %collective-permute-start.10 = (bf16[3,24,448]{2,1,0:T(8,128)(2,1)S(1)}, bf16[3,24,448]{2,1,0:T(8,128)(2,1)S(1)}, u32[]{:S(2)}, u32[]{:S(2)}) collective-permute-start(bf16[3,24,448]{2,1,0:T(8,128)(2,1)S(1)} %get-tuple-element.17), channel_id=1, source_target_pairs={{0,2},{1,3},{2,0},{3,1},{4,6},{5,7},{6,4},{7,5},{8,10},{9,11},{10,... | collective-permute-start | bytes 193544 | tf_op jit(solution)/shard_map/ppermute | solution.py:50
  151.9 4.9 %collective-permute-start.9 = (bf16[3,24,448]{2,1,0:T(8,128)(2,1)S(1)}, bf16[3,24,448]{2,1,0:T(8,128)(2,1)S(1)}, u32[]{:S(2)}, u32[]{:S(2)}) collective-permute-start(bf16[3,24,448]{2,1,0:T(8,128)(2,1)S(1)} %get-tuple-element.17), channel_id=1, source_target_pairs={{0,3},{1,0},{2,1},{3,2},{4,7},{5,4},{6,5},{7,6},{8,11},{9,8},{10,9... | collective-permute-start | bytes 193544 | tf_op jit(solution)/shard_map/ppermute | solution.py:50
  156.8 1.9 collective-permute-start.11
  159.0 5.3 %collective-permute-done.11 = bf16[3,24,448]{2,1,0:T(8,128)(2,1)S(1)} collective-permute-done((bf16[3,24,448]{2,1,0:T(8,128)(2,1)S(1)}, bf16[3,24,448]{2,1,0:T(8,128)(2,1)S(1)}, u32[]{:S(2)}, u32[]{:S(2)}) %collective-permute-start.11) | collective-permute-done | bytes 64544 | tf_op jit(solution)/shard_map/ppermute | solution.py:50
  164.7 1.1 broadcast_in_dim.30
  165.8 4.3 %all-to-all-start.5 = ((bf16[3,4,96,448]{3,2,0,1:T(8,128)(2,1)}), bf16[3,4,96,448]{3,2,0,1:T(8,128)(2,1)}, u32[]{:S(2)}, u32[]{:S(2)}) async-start(bf16[3,4,96,448]{3,2,0,1:T(8,128)(2,1)} %broadcast_in_dim.30), calls=%async_computation.5 | async-start | bytes 2359296 | tf_op jit(solution)/shard_map/all_to_all | solution.py:32
  170.2 10.4 %all-to-all-done.5 = bf16[3,4,96,448]{3,2,0,1:T(8,128)(2,1)} async-done(((bf16[3,4,96,448]{3,2,0,1:T(8,128)(2,1)}), bf16[3,4,96,448]{3,2,0,1:T(8,128)(2,1)}, u32[]{:S(2)}, u32[]{:S(2)}) %all-to-all-start.5) | async-done | bytes 1032224 | tf_op jit(solution)/shard_map/all_to_all | solution.py:32
  180.6 1.4 copy.62
  182.0 0.6 fusion.43
  182.6 0.6 convolution_add_fusion
  183.3 13.3 %all_to_all.42 = f32[16,2,1,24,512]{4,3,0,2,1:T(8,128)} all-to-all(f32[16,2,1,24,512]{4,3,0,2,1:T(8,128)S(1)} %copy.63), channel_id=1, replica_groups=mesh['y'=8,'zl'=2,'c'=2,'x'=4,'zh'=4] {'c'}, dimensions={1} | all-to-all | bytes 3145728 | tf_op jit(solution)/shard_map/all_to_all | solution.py:25
  196.6 2.5 %reduce_sum.38 = f32[16,24,512]{2,1,0:T(8,128)} reduce(f32[16,2,1,24,512]{4,3,0,2,1:T(8,128)} %all_to_all.42, f32[]{:T(128)} %constant.52.clone.1), dimensions={1,2}, to_apply=%region_2.4 | reduce | flops 196608 | bytes 2359300 | tf_op jit(solution)/shard_map/reduce_sum | solution.py:26
  199.1 4.5 %all-to-all-start.7 = ((f32[16,24,512]{2,1,0:T(8,128)}), f32[16,24,512]{2,1,0:T(8,128)}, u32[]{:S(2)}, u32[]{:S(2)}) async-start(f32[16,24,512]{2,1,0:T(8,128)} %reduce_sum.38), calls=%async_computation.7 | async-start | bytes 1572864 | tf_op jit(solution)/shard_map/all_to_all | solution.py:25
  203.6 2.6 %convolution_convert_fusion.1 = bf16[512,448]{0,1:T(8,128)(2,1)} fusion(bf16[768,1024]{1,0:T(8,128)(2,1)} %bitcast.67, bf16[3,384,448]{2,1,0:T(8,128)(2,1)S(1)} %bitcast.53, bf16[3,384,448]{2,1,0:T(8,128)(2,1)S(1)} %bitcast.58), kind=kOutput, calls=%fused_computation.8 | convolution fusion | flops 353927168 | bytes 3309568 | tf_op jit(solution)/shard_map/dot_general | solution.py:91
  206.2 1.3 convolution_convert_fusion.2
  207.5 1.3 convolution_convert_fusion
  208.9 15.6 %all-to-all-done.7 = f32[16,24,512]{2,1,0:T(8,128)} async-done(((f32[16,24,512]{2,1,0:T(8,128)}), f32[16,24,512]{2,1,0:T(8,128)}, u32[]{:S(2)}, u32[]{:S(2)}) %all-to-all-start.7) | async-done | bytes 786464 | tf_op jit(solution)/shard_map/all_to_all | solution.py:25
  224.5 1.8 reduce_sum.39
  (38 shorter events, 4.0 us)
Async XLA Ops:
  0.6 41.4 %copy-start = (bf16[512,448]{0,1:T(8,128)(2,1)S(1)}, bf16[512,448]{0,1:T(8,128)(2,1)}, u32[]{:S(2)}) copy-start(bf16[512,448]{0,1:T(8,128)(2,1)} %param.9) | copy-start | bytes 1376260
  40.1 1.0 copy-start.3
  40.2 9.4 %copy-start.1 = (bf16[16,2,1,24,1024]{4,3,1,0,2:T(8,128)(2,1)}, bf16[16,2,1,24,1024]{4,3,1,0,2:T(8,128)(2,1)S(1)}, u32[]{:S(2)}) copy-start(bf16[16,2,1,24,1024]{4,3,1,0,2:T(8,128)(2,1)S(1)} %copy.48) | copy-start | bytes 4718596
  40.2 1.4 copy-start.4
  44.3 33.5 %all-to-all-start.2 = ((f32[3,4,96,448]{3,2,0,1:T(8,128)}), f32[3,4,96,448]{3,2,0,1:T(8,128)}, u32[]{:S(2)}, u32[]{:S(2)}) async-start(f32[3,4,96,448]{3,2,0,1:T(8,128)} %copy.52), calls=%async_computation.2 | async-start | bytes 4718592 | tf_op jit(solution)/shard_map/all_to_all | solution.py:25
  77.7 31.7 %all-to-all-start.4 = ((f32[3,4,96,448]{3,2,0,1:T(8,128)}), f32[3,4,96,448]{3,2,0,1:T(8,128)S(1)}, u32[]{:S(2)}, u32[]{:S(2)}) async-start(f32[3,4,96,448]{3,2,0,1:T(8,128)} %copy.60), calls=%async_computation.4 | async-start | bytes 4718592 | tf_op jit(solution)/shard_map/all_to_all | solution.py:25
  86.1 24.5 %collective-permute-start = (f32[3,24,448]{2,1,0:T(8,128)}, f32[3,24,448]{2,1,0:T(8,128)S(1)}, u32[]{:S(2)}, u32[]{:S(2)}) collective-permute-start(f32[3,24,448]{2,1,0:T(8,128)} %get-tuple-element.8), channel_id=1, source_target_pairs={{0,1},{1,2},{2,3},{3,0},{4,5},{5,6},{6,7},{7,4},{8,9},{9,10},{10,1... | collective-permute-start | bytes 387080 | tf_op jit(solution)/shard_map/ppermute | solution.py:43
  91.9 18.7 %collective-permute-start.2 = (f32[3,24,448]{2,1,0:T(8,128)}, f32[3,24,448]{2,1,0:T(8,128)}, u32[]{:S(2)}, u32[]{:S(2)}) collective-permute-start(f32[3,24,448]{2,1,0:T(8,128)} %get-tuple-element.9), channel_id=1, source_target_pairs={{0,3},{1,0},{2,1},{3,2},{4,7},{5,4},{6,5},{7,6},{8,11},{9,8},{10,9... | collective-permute-start | bytes 387080 | tf_op jit(solution)/shard_map/ppermute | solution.py:43
  97.8 12.8 %collective-permute-start.1 = (f32[3,24,448]{2,1,0:T(8,128)}, f32[3,24,448]{2,1,0:T(8,128)}, u32[]{:S(2)}, u32[]{:S(2)}) collective-permute-start(f32[3,24,448]{2,1,0:T(8,128)} %get-tuple-element.10), channel_id=1, source_target_pairs={{0,2},{1,3},{2,0},{3,1},{4,6},{5,7},{6,4},{7,5},{8,10},{9,11},{10,... | collective-permute-start | bytes 387080 | tf_op jit(solution)/shard_map/ppermute | solution.py:43
  111.7 24.4 %collective-permute-start.4 = (bf16[3,24,448]{2,1,0:T(8,128)(2,1)S(1)}, bf16[3,24,448]{2,1,0:T(8,128)(2,1)S(1)}, u32[]{:S(2)}, u32[]{:S(2)}) collective-permute-start(bf16[3,24,448]{2,1,0:T(8,128)(2,1)S(1)} %get-tuple-element.19), channel_id=1, source_target_pairs={{0,2},{1,3},{2,0},{3,1},{4,6},{5,7},{6,4},{7,5},{8,10},{9,11},{10,... | collective-permute-start | bytes 193544 | tf_op jit(solution)/shard_map/ppermute | solution.py:50
  121.4 19.7 %collective-permute-start.3 = (bf16[3,24,448]{2,1,0:T(8,128)(2,1)S(1)}, bf16[3,24,448]{2,1,0:T(8,128)(2,1)S(1)}, u32[]{:S(2)}, u32[]{:S(2)}) collective-permute-start(bf16[3,24,448]{2,1,0:T(8,128)(2,1)S(1)} %get-tuple-element.19), channel_id=1, source_target_pairs={{0,3},{1,0},{2,1},{3,2},{4,7},{5,4},{6,5},{7,6},{8,11},{9,8},{10,9... | collective-permute-start | bytes 193544 | tf_op jit(solution)/shard_map/ppermute | solution.py:50
  123.3 17.7 %collective-permute-start.5 = (bf16[3,24,448]{2,1,0:T(8,128)(2,1)S(1)}, bf16[3,24,448]{2,1,0:T(8,128)(2,1)S(1)}, u32[]{:S(2)}, u32[]{:S(2)}) collective-permute-start(bf16[3,24,448]{2,1,0:T(8,128)(2,1)S(1)} %get-tuple-element.19), channel_id=1, source_target_pairs={{0,1},{1,2},{2,3},{3,0},{4,5},{5,6},{6,7},{7,4},{8,9},{9,10},{10,1... | collective-permute-start | bytes 193544 | tf_op jit(solution)/shard_map/ppermute | solution.py:50
  128.7 17.5 %collective-permute-start.6 = (f32[3,24,448]{2,1,0:T(8,128)S(1)}, f32[3,24,448]{2,1,0:T(8,128)S(1)}, u32[]{:S(2)}, u32[]{:S(2)}) collective-permute-start(f32[3,24,448]{2,1,0:T(8,128)S(1)} %get-tuple-element.5), channel_id=1, source_target_pairs={{0,1},{1,2},{2,3},{3,0},{4,5},{5,6},{6,7},{7,4},{8,9},{9,10},{10,1... | collective-permute-start | bytes 387080 | tf_op jit(solution)/shard_map/ppermute | solution.py:43
  133.9 12.3 %collective-permute-start.8 = (f32[3,24,448]{2,1,0:T(8,128)S(1)}, f32[3,24,448]{2,1,0:T(8,128)S(1)}, u32[]{:S(2)}, u32[]{:S(2)}) collective-permute-start(f32[3,24,448]{2,1,0:T(8,128)S(1)} %get-tuple-element.6), channel_id=1, source_target_pairs={{0,3},{1,0},{2,1},{3,2},{4,7},{5,4},{6,5},{7,6},{8,11},{9,8},{10,9... | collective-permute-start | bytes 387080 | tf_op jit(solution)/shard_map/ppermute | solution.py:43
  136.1 11.4 %collective-permute-start.7 = (f32[3,24,448]{2,1,0:T(8,128)S(1)}, f32[3,24,448]{2,1,0:T(8,128)S(1)}, u32[]{:S(2)}, u32[]{:S(2)}) collective-permute-start(f32[3,24,448]{2,1,0:T(8,128)S(1)} %get-tuple-element.7), channel_id=1, source_target_pairs={{0,2},{1,3},{2,0},{3,1},{4,6},{5,7},{6,4},{7,5},{8,10},{9,11},{10,... | collective-permute-start | bytes 387080 | tf_op jit(solution)/shard_map/ppermute | solution.py:43
  142.6 22.1 %all-to-all-start.3 = ((bf16[3,4,96,448]{3,2,0,1:T(8,128)(2,1)}), bf16[3,4,96,448]{3,2,0,1:T(8,128)(2,1)S(1)}, u32[]{:S(2)}, u32[]{:S(2)}) async-start(bf16[3,4,96,448]{3,2,0,1:T(8,128)(2,1)} %broadcast_in_dim.28), calls=%async_computation.3 | async-start | bytes 2359296 | tf_op jit(solution)/shard_map/all_to_all | solution.py:32
  148.5 10.2 %collective-permute-start.10 = (bf16[3,24,448]{2,1,0:T(8,128)(2,1)S(1)}, bf16[3,24,448]{2,1,0:T(8,128)(2,1)S(1)}, u32[]{:S(2)}, u32[]{:S(2)}) collective-permute-start(bf16[3,24,448]{2,1,0:T(8,128)(2,1)S(1)} %get-tuple-element.17), channel_id=1, source_target_pairs={{0,2},{1,3},{2,0},{3,1},{4,6},{5,7},{6,4},{7,5},{8,10},{9,11},{10,... | collective-permute-start | bytes 193544 | tf_op jit(solution)/shard_map/ppermute | solution.py:50
  151.9 7.1 %collective-permute-start.9 = (bf16[3,24,448]{2,1,0:T(8,128)(2,1)S(1)}, bf16[3,24,448]{2,1,0:T(8,128)(2,1)S(1)}, u32[]{:S(2)}, u32[]{:S(2)}) collective-permute-start(bf16[3,24,448]{2,1,0:T(8,128)(2,1)S(1)} %get-tuple-element.17), channel_id=1, source_target_pairs={{0,3},{1,0},{2,1},{3,2},{4,7},{5,4},{6,5},{7,6},{8,11},{9,8},{10,9... | collective-permute-start | bytes 193544 | tf_op jit(solution)/shard_map/ppermute | solution.py:50
  156.8 7.5 %collective-permute-start.11 = (bf16[3,24,448]{2,1,0:T(8,128)(2,1)S(1)}, bf16[3,24,448]{2,1,0:T(8,128)(2,1)S(1)}, u32[]{:S(2)}, u32[]{:S(2)}) collective-permute-start(bf16[3,24,448]{2,1,0:T(8,128)(2,1)S(1)} %get-tuple-element.17), channel_id=1, source_target_pairs={{0,1},{1,2},{2,3},{3,0},{4,5},{5,6},{6,7},{7,4},{8,9},{9,10},{10,1... | collective-permute-start | bytes 193544 | tf_op jit(solution)/shard_map/ppermute | solution.py:50
  165.8 14.8 %all-to-all-start.5 = ((bf16[3,4,96,448]{3,2,0,1:T(8,128)(2,1)}), bf16[3,4,96,448]{3,2,0,1:T(8,128)(2,1)}, u32[]{:S(2)}, u32[]{:S(2)}) async-start(bf16[3,4,96,448]{3,2,0,1:T(8,128)(2,1)} %broadcast_in_dim.30), calls=%async_computation.5 | async-start | bytes 2359296 | tf_op jit(solution)/shard_map/all_to_all | solution.py:32
  199.1 25.3 %all-to-all-start.7 = ((f32[16,24,512]{2,1,0:T(8,128)}), f32[16,24,512]{2,1,0:T(8,128)}, u32[]{:S(2)}, u32[]{:S(2)}) async-start(f32[16,24,512]{2,1,0:T(8,128)} %reduce_sum.38), calls=%async_computation.7 | async-start | bytes 1572864 | tf_op jit(solution)/shard_map/all_to_all | solution.py:25
  203.6 2.6 %copy-start.2 = (bf16[16,2,1,24,1024]{4,3,1,0,2:T(8,128)(2,1)S(1)}, bf16[16,2,1,24,1024]{4,3,1,0,2:T(8,128)(2,1)}, u32[]{:S(2)}) copy-start(bf16[16,2,1,24,1024]{4,3,1,0,2:T(8,128)(2,1)} %copy-done.1) | copy-start | bytes 4718596

commit v7 on v6

--- a/solution.py
+++ b/solution.py
@@ -78,7 +78,7 @@
         p = scatter_sum(p, "x", nx, 1)
         p = scatter_permute(p, "zh", nzh, 1)
         d = jnp.stack(swiglu_grads(p[0], p[1], p[2]))
-        d = gather_permute(d, "zh", nzh, 1)
+        d = gather_a2a(d, "zh", nzh, 1)
         chunks.append(gather_a2a(d, "x", nx, 1))
     deltas = jnp.concatenate(chunks, 1)
     hidden, gate_delta, up_delta = deltas[0], deltas[1], deltas[2]

time: 228 us -> 241 us (1.057)
  waiting for transfers between devices: 65 us -> 90.8 us
  starting transfers between devices: 75.9 us -> 63.8 us
  blocking collectives: 51.6 us -> 49 us
    all_to_all x2 -> x4, waiting for transfers between devices: 10.4 us -> 43.1 us  [gather_a2a(): v = lax.all_to_all(v, axis_name, dim, dim, tiled=True)]
    ppermute x6 -> x0, starting transfers between devices: 26 us -> none  [gather_permute(): lax.ppermute(v, axis_name, [(j, (j + k) % n) for j in range(n)])]
    all_to_all x2 -> x4, starting transfers between devices: 7.8 us -> 17.2 us  [gather_a2a(): v = lax.all_to_all(v, axis_name, dim, dim, tiled=True)]
    ppermute x6 -> x0, waiting for transfers between devices: 5.53 us -> none  [gather_permute(): lax.ppermute(v, axis_name, [(j, (j + k) % n) for j in range(n)])]
    ppermute x6, starting transfers between devices: 29.5 us -> 34.2 us  [scatter_permute(): lax.ppermute(part, axis_name, [(j, (j + k) % n) for j in range(n)])]
    all_to_all x1, blocking collectives: 13.3 us -> 10.7 us  [scatter_sum(): v = lax.all_to_all(v, axis_name, dim, dim, tiled=True)]
  transfers between devices with their start and end apart: 17 -> 13, of which waited for: 7 -> 7; matrix products, arithmetic and copies ran while one was open for 8% -> 8% of each run, Pallas kernels for 0% -> 0%
where the time goes in v7:
time: 241 us; the launch traced here: 238 us
  waiting for transfers between devices  90.8 us (38%)
  starting transfers between devices  63.8 us (26%)
  blocking collectives  49 us (20%)
  local copies, waits for them, and re-layouts  13 us (5%)
  other arithmetic  11.7 us (5%)
  matrix products  8.7 us (4%)
    all_to_all x3, waiting for transfers between devices, scatter_sum(): v = lax.all_to_all(v, axis_name, dim, dim, tiled=True)  47.7 us
    all_to_all x4, waiting for transfers between devices, gather_a2a(): v = lax.all_to_all(v, axis_name, dim, dim, tiled=True)  43.1 us
    all_to_all x2, blocking collectives, gather_a2a(): v = lax.all_to_all(v, axis_name, dim, dim, tiled=True)  38.3 us
    ppermute x6, starting transfers between devices, scatter_permute(): lax.ppermute(part, axis_name, [(j, (j + k) % n) for j in range(n)])  34.2 us
    all_to_all x4, starting transfers between devices, gather_a2a(): v = lax.all_to_all(v, axis_name, dim, dim, tiled=True)  17.2 us
    all_to_all x3, starting transfers between devices, scatter_sum(): v = lax.all_to_all(v, axis_name, dim, dim, tiled=True)  12.4 us
    all_to_all x1, blocking collectives, scatter_sum(): v = lax.all_to_all(v, axis_name, dim, dim, tiled=True)  10.7 us
    reduce_sum x4, other arithmetic, scatter_sum(): return v.sum(dim)  8.24 us
  transfers between devices with their start and end apart: 13, of which 7 were waited for; matrix products, arithmetic and copies ran while one was open for 8% of the time, Pallas kernels for 0%

profile of v7, /device:TPU:1, one launch (start us, length us, event | category | flops | bytes accessed | tf_op | source)
XLA Modules:
  0.0 238.0 jit_solution(6114982947992743050)
XLA Ops:
  0.6 0.8 pad_maximum_fusion.5
  1.5 31.3 %all_to_all.50 = bf16[16,24,1024]{2,1,0:T(8,128)(2,1)S(1)} all-to-all(bf16[16,24,1024]{2,1,0:T(8,128)(2,1)S(1)} %broadcast_in_dim.16), channel_id=1, replica_groups=mesh['y'=8,'zl'=2,'c'=2,'x'=4,'zh'=4] {'y','zl'}, dimensions={0} | all-to-all | bytes 1572864 | tf_op jit(solution)/shard_map/all_to_all | solution.py:32
  33.1 7.0 %all_to_all.51 = bf16[16,2,1,24,1024]{4,3,2,0,1:T(8,128)(2,1)S(1)} all-to-all(bf16[16,2,1,24,1024]{4,3,2,0,1:T(8,128)(2,1)S(1)} %broadcast_in_dim.17), channel_id=1, replica_groups=mesh['y'=8,'zl'=2,'c'=2,'x'=4,'zh'=4] {'c'}, dimensions={1} | all-to-all | bytes 3145728 | tf_op jit(solution)/shard_map/all_to_all | solution.py:32
  40.2 0.8 copy-done.3
  42.0 0.4 fusion.20
  42.6 1.7 copy.42
  44.3 4.5 %all-to-all-start.2 = ((f32[3,4,96,448]{3,2,0,1:T(8,128)}), f32[3,4,96,448]{3,2,0,1:T(8,128)}, u32[]{:S(2)}, u32[]{:S(2)}) async-start(f32[3,4,96,448]{3,2,0,1:T(8,128)} %copy.42), calls=%async_computation.2 | async-start | bytes 4718592 | tf_op jit(solution)/shard_map/all_to_all | solution.py:25
  48.8 0.4 fusion.14
  49.2 0.4 fusion.10
  50.2 1.6 copy.48
  51.8 25.9 %all-to-all-done.2 = f32[3,4,96,448]{3,2,0,1:T(8,128)} async-done(((f32[3,4,96,448]{3,2,0,1:T(8,128)}), f32[3,4,96,448]{3,2,0,1:T(8,128)}, u32[]{:S(2)}, u32[]{:S(2)}) %all-to-all-start.2) | async-done | bytes 2064416 | tf_op jit(solution)/shard_map/all_to_all | solution.py:25
  77.7 3.6 %all-to-all-start.5 = ((f32[3,4,96,448]{3,2,0,1:T(8,128)}), f32[3,4,96,448]{3,2,0,1:T(8,128)S(1)}, u32[]{:S(2)}, u32[]{:S(2)}) async-start(f32[3,4,96,448]{3,2,0,1:T(8,128)} %copy.48), calls=%async_computation.5 | async-start | bytes 4718592 | tf_op jit(solution)/shard_map/all_to_all | solution.py:25
  81.4 2.8 %reduce_sum.36 = f32[3,96,448]{2,1,0:T(8,128)} reduce(f32[3,4,96,448]{3,2,0,1:T(8,128)} %all-to-all-done.2, f32[]{:T(128)} %constant.35.clone.1), dimensions={1}, to_apply=%region_0.0 | reduce | flops 387072 | bytes 2580484 | tf_op jit(solution)/shard_map/reduce_sum | solution.py:26
  84.2 1.8 constant_dynamic-slice_fusion.5
  86.1 5.8 %collective-permute-start = (f32[3,24,448]{2,1,0:T(8,128)}, f32[3,24,448]{2,1,0:T(8,128)S(1)}, u32[]{:S(2)}, u32[]{:S(2)}) collective-permute-start(f32[3,24,448]{2,1,0:T(8,128)} %get-tuple-element.7), channel_id=1, source_target_pairs={{0,1},{1,2},{2,3},{3,0},{4,5},{5,6},{6,7},{7,4},{8,9},{9,10},{10,1... | collective-permute-start | bytes 387080 | tf_op jit(solution)/shard_map/ppermute | solution.py:43
  91.9 5.9 %collective-permute-start.2 = (f32[3,24,448]{2,1,0:T(8,128)}, f32[3,24,448]{2,1,0:T(8,128)}, u32[]{:S(2)}, u32[]{:S(2)}) collective-permute-start(f32[3,24,448]{2,1,0:T(8,128)} %get-tuple-element.8), channel_id=1, source_target_pairs={{0,3},{1,0},{2,1},{3,2},{4,7},{5,4},{6,5},{7,6},{8,11},{9,8},{10,9... | collective-permute-start | bytes 387080 | tf_op jit(solution)/shard_map/ppermute | solution.py:43
  97.7 5.5 %collective-permute-start.1 = (f32[3,24,448]{2,1,0:T(8,128)}, f32[3,24,448]{2,1,0:T(8,128)}, u32[]{:S(2)}, u32[]{:S(2)}) collective-permute-start(f32[3,24,448]{2,1,0:T(8,128)} %get-tuple-element.9), channel_id=1, source_target_pairs={{0,2},{1,3},{2,0},{3,1},{4,6},{5,7},{6,4},{7,5},{8,10},{9,11},{10,... | collective-permute-start | bytes 387080 | tf_op jit(solution)/shard_map/ppermute | solution.py:43
  103.2 6.2 %all-to-all-done.5 = f32[3,4,96,448]{3,2,0,1:T(8,128)S(1)} async-done(((f32[3,4,96,448]{3,2,0,1:T(8,128)}), f32[3,4,96,448]{3,2,0,1:T(8,128)S(1)}, u32[]{:S(2)}, u32[]{:S(2)}) %all-to-all-start.5) | async-done | bytes 2064416 | tf_op jit(solution)/shard_map/all_to_all | solution.py:25
  109.4 1.1 reduce_sum.37
  110.5 1.1 constant_dynamic-slice_fusion.2
  111.6 5.7 %collective-permute-start.3 = (f32[3,24,448]{2,1,0:T(8,128)S(1)}, f32[3,24,448]{2,1,0:T(8,128)S(1)}, u32[]{:S(2)}, u32[]{:S(2)}) collective-permute-start(f32[3,24,448]{2,1,0:T(8,128)S(1)} %get-tuple-element.4), channel_id=1, source_target_pairs={{0,1},{1,2},{2,3},{3,0},{4,5},{5,6},{6,7},{7,4},{8,9},{9,10},{10,1... | collective-permute-start | bytes 387080 | tf_op jit(solution)/shard_map/ppermute | solution.py:43
  117.3 5.9 %collective-permute-start.5 = (f32[3,24,448]{2,1,0:T(8,128)S(1)}, f32[3,24,448]{2,1,0:T(8,128)S(1)}, u32[]{:S(2)}, u32[]{:S(2)}) collective-permute-start(f32[3,24,448]{2,1,0:T(8,128)S(1)} %get-tuple-element.5), channel_id=1, source_target_pairs={{0,3},{1,0},{2,1},{3,2},{4,7},{5,4},{6,5},{7,6},{8,11},{9,8},{10,9... | collective-permute-start | bytes 387080 | tf_op jit(solution)/shard_map/ppermute | solution.py:43
  123.2 5.5 %collective-permute-start.4 = (f32[3,24,448]{2,1,0:T(8,128)S(1)}, f32[3,24,448]{2,1,0:T(8,128)S(1)}, u32[]{:S(2)}, u32[]{:S(2)}) collective-permute-start(f32[3,24,448]{2,1,0:T(8,128)S(1)} %get-tuple-element.6), channel_id=1, source_target_pairs={{0,2},{1,3},{2,0},{3,1},{4,6},{5,7},{6,4},{7,5},{8,10},{9,11},{10,... | collective-permute-start | bytes 387080 | tf_op jit(solution)/shard_map/ppermute | solution.py:43
  128.7 1.1 add_add_fusion.1
  129.9 0.7 broadcast_in_dim.18
  130.6 3.5 %all-to-all-start.3 = ((bf16[3,4,24,448]{3,2,0,1:T(8,128)(2,1)}), bf16[3,4,24,448]{3,2,0,1:T(8,128)(2,1)S(1)}, u32[]{:S(2)}, u32[]{:S(2)}) async-start(bf16[3,4,24,448]{3,2,0,1:T(8,128)(2,1)} %broadcast_in_dim.18), calls=%async_computation.3 | async-start | bytes 589824 | tf_op jit(solution)/shard_map/all_to_all | solution.py:32
  134.1 1.0 add_add_fusion
  135.1 8.3 %all-to-all-done.3 = bf16[3,4,24,448]{3,2,0,1:T(8,128)(2,1)S(1)} async-done(((bf16[3,4,24,448]{3,2,0,1:T(8,128)(2,1)}), bf16[3,4,24,448]{3,2,0,1:T(8,128)(2,1)S(1)}, u32[]{:S(2)}, u32[]{:S(2)}) %all-to-all-start.3) | async-done | bytes 258080 | tf_op jit(solution)/shard_map/all_to_all | solution.py:32
  143.5 0.7 broadcast_in_dim.42
  144.2 5.9 %all-to-all-start.6 = ((bf16[3,4,24,448]{3,2,0,1:T(8,128)(2,1)}), bf16[3,4,24,448]{3,2,0,1:T(8,128)(2,1)S(1)}, u32[]{:S(2)}, u32[]{:S(2)}) async-start(bf16[3,4,24,448]{3,2,0,1:T(8,128)(2,1)} %broadcast_in_dim.42), calls=%async_computation.6 | async-start | bytes 589824 | tf_op jit(solution)/shard_map/all_to_all | solution.py:32
  150.2 9.2 %all-to-all-done.6 = bf16[3,4,24,448]{3,2,0,1:T(8,128)(2,1)S(1)} async-done(((bf16[3,4,24,448]{3,2,0,1:T(8,128)(2,1)}), bf16[3,4,24,448]{3,2,0,1:T(8,128)(2,1)S(1)}, u32[]{:S(2)}, u32[]{:S(2)}) %all-to-all-start.6) | async-done | bytes 258080 | tf_op jit(solution)/shard_map/all_to_all | solution.py:32
  159.3 1.1 broadcast_in_dim.20
  160.5 3.5 %all-to-all-start.4 = ((bf16[3,4,96,448]{3,2,0,1:T(8,128)(2,1)}), bf16[3,4,96,448]{3,2,0,1:T(8,128)(2,1)S(1)}, u32[]{:S(2)}, u32[]{:S(2)}) async-start(bf16[3,4,96,448]{3,2,0,1:T(8,128)(2,1)} %broadcast_in_dim.20), calls=%async_computation.4 | async-start | bytes 2359296 | tf_op jit(solution)/shard_map/all_to_all | solution.py:32
  164.0 13.4 %all-to-all-done.4 = bf16[3,4,96,448]{3,2,0,1:T(8,128)(2,1)S(1)} async-done(((bf16[3,4,96,448]{3,2,0,1:T(8,128)(2,1)}), bf16[3,4,96,448]{3,2,0,1:T(8,128)(2,1)S(1)}, u32[]{:S(2)}, u32[]{:S(2)}) %all-to-all-start.4) | async-done | bytes 1032224 | tf_op jit(solution)/shard_map/all_to_all | solution.py:32
  177.4 1.1 broadcast_in_dim.44
  178.6 4.3 %all-to-all-start.7 = ((bf16[3,4,96,448]{3,2,0,1:T(8,128)(2,1)}), bf16[3,4,96,448]{3,2,0,1:T(8,128)(2,1)}, u32[]{:S(2)}, u32[]{:S(2)}) async-start(bf16[3,4,96,448]{3,2,0,1:T(8,128)(2,1)} %broadcast_in_dim.44), calls=%async_computation.7 | async-start | bytes 2359296 | tf_op jit(solution)/shard_map/all_to_all | solution.py:32
  182.9 12.2 %all-to-all-done.7 = bf16[3,4,96,448]{3,2,0,1:T(8,128)(2,1)} async-done(((bf16[3,4,96,448]{3,2,0,1:T(8,128)(2,1)}), bf16[3,4,96,448]{3,2,0,1:T(8,128)(2,1)}, u32[]{:S(2)}, u32[]{:S(2)}) %all-to-all-start.7) | async-done | bytes 1032224 | tf_op jit(solution)/shard_map/all_to_all | solution.py:32
  195.1 1.4 copy.50
  196.5 0.6 fusion.26
  197.1 0.6 convolution_add_fusion
  197.8 10.7 %all_to_all.52 = f32[16,2,1,24,512]{4,3,0,2,1:T(8,128)} all-to-all(f32[16,2,1,24,512]{4,3,0,2,1:T(8,128)S(1)} %copy.51), channel_id=1, replica_groups=mesh['y'=8,'zl'=2,'c'=2,'x'=4,'zh'=4] {'c'}, dimensions={1} | all-to-all | bytes 3145728 | tf_op jit(solution)/shard_map/all_to_all | solution.py:25
  208.5 2.5 %reduce_sum.38 = f32[16,24,512]{2,1,0:T(8,128)} reduce(f32[16,2,1,24,512]{4,3,0,2,1:T(8,128)} %all_to_all.52, f32[]{:T(128)} %constant.35.clone.1), dimensions={1,2}, to_apply=%region_2.3 | reduce | flops 196608 | bytes 2359300 | tf_op jit(solution)/shard_map/reduce_sum | solution.py:26
  211.0 4.3 %all-to-all-start.9 = ((f32[16,24,512]{2,1,0:T(8,128)}), f32[16,24,512]{2,1,0:T(8,128)}, u32[]{:S(2)}, u32[]{:S(2)}) async-start(f32[16,24,512]{2,1,0:T(8,128)} %reduce_sum.38), calls=%async_computation.9 | async-start | bytes 1572864 | tf_op jit(solution)/shard_map/all_to_all | solution.py:25
  215.3 2.6 %convolution_convert_fusion.1 = bf16[512,448]{0,1:T(8,128)(2,1)} fusion(bf16[768,1024]{1,0:T(8,128)(2,1)} %bitcast.47, bf16[3,384,448]{2,1,0:T(8,128)(2,1)S(1)} %bitcast.33, bf16[3,384,448]{2,1,0:T(8,128)(2,1)S(1)} %bitcast.38), kind=kOutput, calls=%fused_computation.8 | convolution fusion | flops 353927168 | bytes 3309568 | tf_op jit(solution)/shard_map/dot_general | solution.py:91
  217.9 1.3 convolution_convert_fusion.2
  219.3 1.3 convolution_convert_fusion
  220.6 15.6 %all-to-all-done.9 = f32[16,24,512]{2,1,0:T(8,128)} async-done(((f32[16,24,512]{2,1,0:T(8,128)}), f32[16,24,512]{2,1,0:T(8,128)}, u32[]{:S(2)}, u32[]{:S(2)}) %all-to-all-start.9) | async-done | bytes 786464 | tf_op jit(solution)/shard_map/all_to_all | solution.py:25
  236.2 1.8 reduce_sum.39
  (31 shorter events, 2.6 us)
Async XLA Ops:
  0.6 41.4 %copy-start = (bf16[512,448]{0,1:T(8,128)(2,1)S(1)}, bf16[512,448]{0,1:T(8,128)(2,1)}, u32[]{:S(2)}) copy-start(bf16[512,448]{0,1:T(8,128)(2,1)} %param.7) | copy-start | bytes 1376260
  40.1 1.0 copy-start.3
  40.2 9.4 %copy-start.1 = (bf16[16,2,1,24,1024]{4,3,1,0,2:T(8,128)(2,1)}, bf16[16,2,1,24,1024]{4,3,1,0,2:T(8,128)(2,1)S(1)}, u32[]{:S(2)}) copy-start(bf16[16,2,1,24,1024]{4,3,1,0,2:T(8,128)(2,1)S(1)} %copy.38) | copy-start | bytes 4718596
  40.2 1.4 copy-start.4
  44.3 33.5 %all-to-all-start.2 = ((f32[3,4,96,448]{3,2,0,1:T(8,128)}), f32[3,4,96,448]{3,2,0,1:T(8,128)}, u32[]{:S(2)}, u32[]{:S(2)}) async-start(f32[3,4,96,448]{3,2,0,1:T(8,128)} %copy.42), calls=%async_computation.2 | async-start | bytes 4718592 | tf_op jit(solution)/shard_map/all_to_all | solution.py:25
  77.7 31.7 %all-to-all-start.5 = ((f32[3,4,96,448]{3,2,0,1:T(8,128)}), f32[3,4,96,448]{3,2,0,1:T(8,128)S(1)}, u32[]{:S(2)}, u32[]{:S(2)}) async-start(f32[3,4,96,448]{3,2,0,1:T(8,128)} %copy.48), calls=%async_computation.5 | async-start | bytes 4718592 | tf_op jit(solution)/shard_map/all_to_all | solution.py:25
  86.1 37.1 %collective-permute-start = (f32[3,24,448]{2,1,0:T(8,128)}, f32[3,24,448]{2,1,0:T(8,128)S(1)}, u32[]{:S(2)}, u32[]{:S(2)}) collective-permute-start(f32[3,24,448]{2,1,0:T(8,128)} %get-tuple-element.7), channel_id=1, source_target_pairs={{0,1},{1,2},{2,3},{3,0},{4,5},{5,6},{6,7},{7,4},{8,9},{9,10},{10,1... | collective-permute-start | bytes 387080 | tf_op jit(solution)/shard_map/ppermute | solution.py:43
  91.9 36.8 %collective-permute-start.2 = (f32[3,24,448]{2,1,0:T(8,128)}, f32[3,24,448]{2,1,0:T(8,128)}, u32[]{:S(2)}, u32[]{:S(2)}) collective-permute-start(f32[3,24,448]{2,1,0:T(8,128)} %get-tuple-element.8), channel_id=1, source_target_pairs={{0,3},{1,0},{2,1},{3,2},{4,7},{5,4},{6,5},{7,6},{8,11},{9,8},{10,9... | collective-permute-start | bytes 387080 | tf_op jit(solution)/shard_map/ppermute | solution.py:43
  97.7 30.9 %collective-permute-start.1 = (f32[3,24,448]{2,1,0:T(8,128)}, f32[3,24,448]{2,1,0:T(8,128)}, u32[]{:S(2)}, u32[]{:S(2)}) collective-permute-start(f32[3,24,448]{2,1,0:T(8,128)} %get-tuple-element.9), channel_id=1, source_target_pairs={{0,2},{1,3},{2,0},{3,1},{4,6},{5,7},{6,4},{7,5},{8,10},{9,11},{10,... | collective-permute-start | bytes 387080 | tf_op jit(solution)/shard_map/ppermute | solution.py:43
  111.6 22.5 %collective-permute-start.3 = (f32[3,24,448]{2,1,0:T(8,128)S(1)}, f32[3,24,448]{2,1,0:T(8,128)S(1)}, u32[]{:S(2)}, u32[]{:S(2)}) collective-permute-start(f32[3,24,448]{2,1,0:T(8,128)S(1)} %get-tuple-element.4), channel_id=1, source_target_pairs={{0,1},{1,2},{2,3},{3,0},{4,5},{5,6},{6,7},{7,4},{8,9},{9,10},{10,1... | collective-permute-start | bytes 387080 | tf_op jit(solution)/shard_map/ppermute | solution.py:43
  117.3 16.8 %collective-permute-start.5 = (f32[3,24,448]{2,1,0:T(8,128)S(1)}, f32[3,24,448]{2,1,0:T(8,128)S(1)}, u32[]{:S(2)}, u32[]{:S(2)}) collective-permute-start(f32[3,24,448]{2,1,0:T(8,128)S(1)} %get-tuple-element.5), channel_id=1, source_target_pairs={{0,3},{1,0},{2,1},{3,2},{4,7},{5,4},{6,5},{7,6},{8,11},{9,8},{10,9... | collective-permute-start | bytes 387080 | tf_op jit(solution)/shard_map/ppermute | solution.py:43
  123.2 10.9 %collective-permute-start.4 = (f32[3,24,448]{2,1,0:T(8,128)S(1)}, f32[3,24,448]{2,1,0:T(8,128)S(1)}, u32[]{:S(2)}, u32[]{:S(2)}) collective-permute-start(f32[3,24,448]{2,1,0:T(8,128)S(1)} %get-tuple-element.6), channel_id=1, source_target_pairs={{0,2},{1,3},{2,0},{3,1},{4,6},{5,7},{6,4},{7,5},{8,10},{9,11},{10,... | collective-permute-start | bytes 387080 | tf_op jit(solution)/shard_map/ppermute | solution.py:43
  130.6 12.9 %all-to-all-start.3 = ((bf16[3,4,24,448]{3,2,0,1:T(8,128)(2,1)}), bf16[3,4,24,448]{3,2,0,1:T(8,128)(2,1)S(1)}, u32[]{:S(2)}, u32[]{:S(2)}) async-start(bf16[3,4,24,448]{3,2,0,1:T(8,128)(2,1)} %broadcast_in_dim.18), calls=%async_computation.3 | async-start | bytes 589824 | tf_op jit(solution)/shard_map/all_to_all | solution.py:32
  144.2 15.1 %all-to-all-start.6 = ((bf16[3,4,24,448]{3,2,0,1:T(8,128)(2,1)}), bf16[3,4,24,448]{3,2,0,1:T(8,128)(2,1)S(1)}, u32[]{:S(2)}, u32[]{:S(2)}) async-start(bf16[3,4,24,448]{3,2,0,1:T(8,128)(2,1)} %broadcast_in_dim.42), calls=%async_computation.6 | async-start | bytes 589824 | tf_op jit(solution)/shard_map/all_to_all | solution.py:32
  160.5 17.0 %all-to-all-start.4 = ((bf16[3,4,96,448]{3,2,0,1:T(8,128)(2,1)}), bf16[3,4,96,448]{3,2,0,1:T(8,128)(2,1)S(1)}, u32[]{:S(2)}, u32[]{:S(2)}) async-start(bf16[3,4,96,448]{3,2,0,1:T(8,128)(2,1)} %broadcast_in_dim.20), calls=%async_computation.4 | async-start | bytes 2359296 | tf_op jit(solution)/shard_map/all_to_all | solution.py:32
  178.6 16.6 %all-to-all-start.7 = ((bf16[3,4,96,448]{3,2,0,1:T(8,128)(2,1)}), bf16[3,4,96,448]{3,2,0,1:T(8,128)(2,1)}, u32[]{:S(2)}, u32[]{:S(2)}) async-start(bf16[3,4,96,448]{3,2,0,1:T(8,128)(2,1)} %broadcast_in_dim.44), calls=%async_computation.7 | async-start | bytes 2359296 | tf_op jit(solution)/shard_map/all_to_all | solution.py:32
  211.0 25.2 %all-to-all-start.9 = ((f32[16,24,512]{2,1,0:T(8,128)}), f32[16,24,512]{2,1,0:T(8,128)}, u32[]{:S(2)}, u32[]{:S(2)}) async-start(f32[16,24,512]{2,1,0:T(8,128)} %reduce_sum.38), calls=%async_computation.9 | async-start | bytes 1572864 | tf_op jit(solution)/shard_map/all_to_all | solution.py:25
  215.3 2.6 %copy-start.2 = (bf16[16,2,1,24,1024]{4,3,1,0,2:T(8,128)(2,1)S(1)}, bf16[16,2,1,24,1024]{4,3,1,0,2:T(8,128)(2,1)}, u32[]{:S(2)}) copy-start(bf16[16,2,1,24,1024]{4,3,1,0,2:T(8,128)(2,1)} %copy-done.1) | copy-start | bytes 4718596

commit v8 on v6

--- a/solution.py
+++ b/solution.py
@@ -79,7 +79,7 @@
         p = scatter_permute(p, "zh", nzh, 1)
         d = jnp.stack(swiglu_grads(p[0], p[1], p[2]))
         d = gather_permute(d, "zh", nzh, 1)
-        chunks.append(gather_a2a(d, "x", nx, 1))
+        chunks.append(gather_permute(d, "x", nx, 1))
     deltas = jnp.concatenate(chunks, 1)
     hidden, gate_delta, up_delta = deltas[0], deltas[1], deltas[2]
     grad_down = lax.dot_general(

time: 228 us -> 234 us (1.026)
  starting transfers between devices: 75.9 us -> 86.4 us
  blocking collectives: 51.6 us -> 47.2 us
  local copies, waits for them, and re-layouts: 11.5 us -> 7.94 us
  other arithmetic: 12.5 us -> 15.4 us
    ppermute x6 -> x12, starting transfers between devices: 26 us -> 39.8 us  [gather_permute(): lax.ppermute(v, axis_name, [(j, (j + k) % n) for j in range(n)])]
    ppermute x6 -> x12, waiting for transfers between devices: 5.53 us -> 16 us  [gather_permute(): lax.ppermute(v, axis_name, [(j, (j + k) % n) for j in range(n)])]
    all_to_all x2 -> x0, waiting for transfers between devices: 10.4 us -> none  [gather_a2a(): v = lax.all_to_all(v, axis_name, dim, dim, tiled=True)]
    all_to_all x2 -> x0, starting transfers between devices: 7.8 us -> none  [gather_a2a(): v = lax.all_to_all(v, axis_name, dim, dim, tiled=True)]
    ppermute x6, starting transfers between devices: 29.5 us -> 34.2 us  [scatter_permute(): lax.ppermute(part, axis_name, [(j, (j + k) % n) for j in range(n)])]
    all_to_all x1, blocking collectives: 13.3 us -> 8.91 us  [scatter_sum(): v = lax.all_to_all(v, axis_name, dim, dim, tiled=True)]
    transpose x1 -> x2, other arithmetic: 0.39 us -> 3.29 us  [gather_permute(): ordered = jnp.moveaxis(ordered, 0, dim)]
  transfers between devices with their start and end apart: 17 -> 21, of which waited for: 7 -> 8; matrix products, arithmetic and copies ran while one was open for 8% -> 8% of each run, Pallas kernels for 0% -> 0%
where the time goes in v8:
time: 234 us; the launch traced here: 230 us
  starting transfers between devices  86.4 us (37%)
  waiting for transfers between devices  63.6 us (27%)
  blocking collectives  47.2 us (20%)
  other arithmetic  15.4 us (7%)
  matrix products  8.71 us (4%)
  local copies, waits for them, and re-layouts  7.94 us (3%)
    all_to_all x3, waiting for transfers between devices, scatter_sum(): v = lax.all_to_all(v, axis_name, dim, dim, tiled=True)  47.7 us
    ppermute x12, starting transfers between devices, gather_permute(): lax.ppermute(v, axis_name, [(j, (j + k) % n) for j in range(n)])  39.8 us
    all_to_all x2, blocking collectives, gather_a2a(): v = lax.all_to_all(v, axis_name, dim, dim, tiled=True)  38.3 us
    ppermute x6, starting transfers between devices, scatter_permute(): lax.ppermute(part, axis_name, [(j, (j + k) % n) for j in range(n)])  34.2 us
    ppermute x12, waiting for transfers between devices, gather_permute(): lax.ppermute(v, axis_name, [(j, (j + k) % n) for j in range(n)])  16 us
    all_to_all x3, starting transfers between devices, scatter_sum(): v = lax.all_to_all(v, axis_name, dim, dim, tiled=True)  12.4 us
    all_to_all x1, blocking collectives, scatter_sum(): v = lax.all_to_all(v, axis_name, dim, dim, tiled=True)  8.91 us
    reduce_sum x4, other arithmetic, scatter_sum(): return v.sum(dim)  8.27 us
  transfers between devices with their start and end apart: 21, of which 8 were waited for; matrix products, arithmetic and copies ran while one was open for 8% of the time, Pallas kernels for 0%

profile of v8, /device:TPU:1, one launch (start us, length us, event | category | flops | bytes accessed | tf_op | source)
XLA Modules:
  0.0 230.5 jit_solution(1715525373923314113)
XLA Ops:
  0.6 0.8 pad_maximum_fusion.5
  1.5 31.3 %all_to_all.30 = bf16[16,24,1024]{2,1,0:T(8,128)(2,1)S(1)} all-to-all(bf16[16,24,1024]{2,1,0:T(8,128)(2,1)S(1)} %broadcast_in_dim.4), channel_id=1, replica_groups=mesh['y'=8,'zl'=2,'c'=2,'x'=4,'zh'=4] {'y','zl'}, dimensions={0} | all-to-all | bytes 1572864 | tf_op jit(solution)/shard_map/all_to_all | solution.py:32
  33.1 7.0 %all_to_all.31 = bf16[16,2,1,24,1024]{4,3,2,0,1:T(8,128)(2,1)S(1)} all-to-all(bf16[16,2,1,24,1024]{4,3,2,0,1:T(8,128)(2,1)S(1)} %broadcast_in_dim.5), channel_id=1, replica_groups=mesh['y'=8,'zl'=2,'c'=2,'x'=4,'zh'=4] {'c'}, dimensions={1} | all-to-all | bytes 3145728 | tf_op jit(solution)/shard_map/all_to_all | solution.py:32
  40.2 0.8 copy-done.3
  42.6 1.6 copy.69
  44.3 4.5 %all-to-all-start.3 = ((f32[3,4,96,448]{3,2,0,1:T(8,128)}), f32[3,4,96,448]{3,2,0,1:T(8,128)}, u32[]{:S(2)}, u32[]{:S(2)}) async-start(f32[3,4,96,448]{3,2,0,1:T(8,128)} %copy.69), calls=%async_computation.3 | async-start | bytes 4718592 | tf_op jit(solution)/shard_map/all_to_all | solution.py:25
  50.2 1.6 copy.61
  51.8 25.9 %all-to-all-done.3 = f32[3,4,96,448]{3,2,0,1:T(8,128)} async-done(((f32[3,4,96,448]{3,2,0,1:T(8,128)}), f32[3,4,96,448]{3,2,0,1:T(8,128)}, u32[]{:S(2)}, u32[]{:S(2)}) %all-to-all-start.3) | async-done | bytes 2064416 | tf_op jit(solution)/shard_map/all_to_all | solution.py:25
  77.7 3.6 %all-to-all-start.2 = ((f32[3,4,96,448]{3,2,0,1:T(8,128)}), f32[3,4,96,448]{3,2,0,1:T(8,128)S(1)}, u32[]{:S(2)}, u32[]{:S(2)}) async-start(f32[3,4,96,448]{3,2,0,1:T(8,128)} %copy.61), calls=%async_computation.2 | async-start | bytes 4718592 | tf_op jit(solution)/shard_map/all_to_all | solution.py:25
  81.4 2.8 %reduce_sum.37 = f32[3,96,448]{2,1,0:T(8,128)} reduce(f32[3,4,96,448]{3,2,0,1:T(8,128)} %all-to-all-done.3, f32[]{:T(128)} %constant.69.clone.1), dimensions={1}, to_apply=%region_1.4 | reduce | flops 387072 | bytes 2580484 | tf_op jit(solution)/shard_map/reduce_sum | solution.py:26
  84.2 1.8 constant_dynamic-slice_fusion.2
  86.1 5.8 %collective-permute-start.9 = (f32[3,24,448]{2,1,0:T(8,128)}, f32[3,24,448]{2,1,0:T(8,128)S(1)}, u32[]{:S(2)}, u32[]{:S(2)}) collective-permute-start(f32[3,24,448]{2,1,0:T(8,128)} %get-tuple-element.6), channel_id=1, source_target_pairs={{0,1},{1,2},{2,3},{3,0},{4,5},{5,6},{6,7},{7,4},{8,9},{9,10},{10,1... | collective-permute-start | bytes 387080 | tf_op jit(solution)/shard_map/ppermute | solution.py:43
  91.9 5.9 %collective-permute-start.11 = (f32[3,24,448]{2,1,0:T(8,128)}, f32[3,24,448]{2,1,0:T(8,128)}, u32[]{:S(2)}, u32[]{:S(2)}) collective-permute-start(f32[3,24,448]{2,1,0:T(8,128)} %get-tuple-element.7), channel_id=1, source_target_pairs={{0,3},{1,0},{2,1},{3,2},{4,7},{5,4},{6,5},{7,6},{8,11},{9,8},{10,9... | collective-permute-start | bytes 387080 | tf_op jit(solution)/shard_map/ppermute | solution.py:43
  97.7 5.5 %collective-permute-start.10 = (f32[3,24,448]{2,1,0:T(8,128)}, f32[3,24,448]{2,1,0:T(8,128)}, u32[]{:S(2)}, u32[]{:S(2)}) collective-permute-start(f32[3,24,448]{2,1,0:T(8,128)} %get-tuple-element.8), channel_id=1, source_target_pairs={{0,2},{1,3},{2,0},{3,1},{4,6},{5,7},{6,4},{7,5},{8,10},{9,11},{10,... | collective-permute-start | bytes 387080 | tf_op jit(solution)/shard_map/ppermute | solution.py:43
  103.2 6.2 %all-to-all-done.2 = f32[3,4,96,448]{3,2,0,1:T(8,128)S(1)} async-done(((f32[3,4,96,448]{3,2,0,1:T(8,128)}), f32[3,4,96,448]{3,2,0,1:T(8,128)S(1)}, u32[]{:S(2)}, u32[]{:S(2)}) %all-to-all-start.2) | async-done | bytes 2064416 | tf_op jit(solution)/shard_map/all_to_all | solution.py:25
  109.4 1.1 reduce_sum.36
  110.5 1.1 constant_dynamic-slice_fusion.5
  111.6 5.7 %collective-permute-start = (f32[3,24,448]{2,1,0:T(8,128)S(1)}, f32[3,24,448]{2,1,0:T(8,128)S(1)}, u32[]{:S(2)}, u32[]{:S(2)}) collective-permute-start(f32[3,24,448]{2,1,0:T(8,128)S(1)} %get-tuple-element.9), channel_id=1, source_target_pairs={{0,1},{1,2},{2,3},{3,0},{4,5},{5,6},{6,7},{7,4},{8,9},{9,10},{10,1... | collective-permute-start | bytes 387080 | tf_op jit(solution)/shard_map/ppermute | solution.py:43
  117.3 5.9 %collective-permute-start.2 = (f32[3,24,448]{2,1,0:T(8,128)S(1)}, f32[3,24,448]{2,1,0:T(8,128)S(1)}, u32[]{:S(2)}, u32[]{:S(2)}) collective-permute-start(f32[3,24,448]{2,1,0:T(8,128)S(1)} %get-tuple-element.10), channel_id=1, source_target_pairs={{0,3},{1,0},{2,1},{3,2},{4,7},{5,4},{6,5},{7,6},{8,11},{9,8},{10,9... | collective-permute-start | bytes 387080 | tf_op jit(solution)/shard_map/ppermute | solution.py:43
  123.2 5.5 %collective-permute-start.1 = (f32[3,24,448]{2,1,0:T(8,128)S(1)}, f32[3,24,448]{2,1,0:T(8,128)S(1)}, u32[]{:S(2)}, u32[]{:S(2)}) collective-permute-start(f32[3,24,448]{2,1,0:T(8,128)S(1)} %get-tuple-element.11), channel_id=1, source_target_pairs={{0,2},{1,3},{2,0},{3,1},{4,6},{5,7},{6,4},{7,5},{8,10},{9,11},{10,... | collective-permute-start | bytes 387080 | tf_op jit(solution)/shard_map/ppermute | solution.py:43
  128.7 1.1 add_add_fusion
  129.9 3.7 %collective-permute-start.13 = (bf16[3,24,448]{2,1,0:T(8,128)(2,1)S(1)}, bf16[3,24,448]{2,1,0:T(8,128)(2,1)S(1)}, u32[]{:S(2)}, u32[]{:S(2)}) collective-permute-start(bf16[3,24,448]{2,1,0:T(8,128)(2,1)S(1)} %get-tuple-element.18), channel_id=1, source_target_pairs={{0,2},{1,3},{2,0},{3,1},{4,6},{5,7},{6,4},{7,5},{8,10},{9,11},{10,... | collective-permute-start | bytes 193544 | tf_op jit(solution)/shard_map/ppermute | solution.py:50
  133.6 4.3 %collective-permute-start.12 = (bf16[3,24,448]{2,1,0:T(8,128)(2,1)S(1)}, bf16[3,24,448]{2,1,0:T(8,128)(2,1)S(1)}, u32[]{:S(2)}, u32[]{:S(2)}) collective-permute-start(bf16[3,24,448]{2,1,0:T(8,128)(2,1)S(1)} %get-tuple-element.18), channel_id=1, source_target_pairs={{0,3},{1,0},{2,1},{3,2},{4,7},{5,4},{6,5},{7,6},{8,11},{9,8},{10,9... | collective-permute-start | bytes 193544 | tf_op jit(solution)/shard_map/ppermute | solution.py:50
  137.9 1.9 collective-permute-start.14
  139.8 1.0 add_add_fusion.1
  140.9 4.3 %collective-permute-done.12 = bf16[3,24,448]{2,1,0:T(8,128)(2,1)S(1)} collective-permute-done((bf16[3,24,448]{2,1,0:T(8,128)(2,1)S(1)}, bf16[3,24,448]{2,1,0:T(8,128)(2,1)S(1)}, u32[]{:S(2)}, u32[]{:S(2)}) %collective-permute-start.12) | collective-permute-done | bytes 64544 | tf_op jit(solution)/shard_map/ppermute | solution.py:50
  145.8 2.4 %collective-permute-start.17 = (bf16[3,96,448]{2,1,0:T(8,128)(2,1)S(1)}, bf16[3,96,448]{2,1,0:T(8,128)(2,1)S(1)}, u32[]{:S(2)}, u32[]{:S(2)}) collective-permute-start(bf16[3,96,448]{2,1,0:T(8,128)(2,1)S(1)} %bitcast.90), channel_id=1, source_target_pairs={{0,4},{4,8},{8,12},{12,0},{1,5},{5,9},{9,13},{13,1},{2,6},{6,10},{... | collective-permute-start | bytes 774152 | tf_op jit(solution)/shard_map/ppermute | solution.py:50
  148.2 4.4 %collective-permute-start.4 = (bf16[3,24,448]{2,1,0:T(8,128)(2,1)S(1)}, bf16[3,24,448]{2,1,0:T(8,128)(2,1)S(1)}, u32[]{:S(2)}, u32[]{:S(2)}) collective-permute-start(bf16[3,24,448]{2,1,0:T(8,128)(2,1)S(1)} %get-tuple-element.20), channel_id=1, source_target_pairs={{0,2},{1,3},{2,0},{3,1},{4,6},{5,7},{6,4},{7,5},{8,10},{9,11},{10,... | collective-permute-start | bytes 193544 | tf_op jit(solution)/shard_map/ppermute | solution.py:50
  152.6 4.8 %collective-permute-start.3 = (bf16[3,24,448]{2,1,0:T(8,128)(2,1)S(1)}, bf16[3,24,448]{2,1,0:T(8,128)(2,1)S(1)}, u32[]{:S(2)}, u32[]{:S(2)}) collective-permute-start(bf16[3,24,448]{2,1,0:T(8,128)(2,1)S(1)} %get-tuple-element.20), channel_id=1, source_target_pairs={{0,3},{1,0},{2,1},{3,2},{4,7},{5,4},{6,5},{7,6},{8,11},{9,8},{10,9... | collective-permute-start | bytes 193544 | tf_op jit(solution)/shard_map/ppermute | solution.py:50
  157.4 1.9 collective-permute-start.5
  159.3 3.7 %collective-permute-start.16 = (bf16[3,96,448]{2,1,0:T(8,128)(2,1)S(1)}, bf16[3,96,448]{2,1,0:T(8,128)(2,1)S(1)}, u32[]{:S(2)}, u32[]{:S(2)}) collective-permute-start(bf16[3,96,448]{2,1,0:T(8,128)(2,1)S(1)} %bitcast.91), channel_id=1, source_target_pairs={{0,8},{4,12},{8,0},{12,4},{1,9},{5,13},{9,1},{13,5},{2,10},{6,14},... | collective-permute-start | bytes 774152 | tf_op jit(solution)/shard_map/ppermute | solution.py:50
  163.1 2.5 %collective-permute-start.15 = (bf16[3,96,448]{2,1,0:T(8,128)(2,1)S(1)}, bf16[3,96,448]{2,1,0:T(8,128)(2,1)S(1)}, u32[]{:S(2)}, u32[]{:S(2)}) collective-permute-start(bf16[3,96,448]{2,1,0:T(8,128)(2,1)S(1)} %bitcast.92), channel_id=1, source_target_pairs={{0,12},{4,0},{8,4},{12,8},{1,13},{5,1},{9,5},{13,9},{2,14},{6,2},{... | collective-permute-start | bytes 774152 | tf_op jit(solution)/shard_map/ppermute | solution.py:50
  166.0 2.8 %collective-permute-start.8 = (bf16[3,96,448]{2,1,0:T(8,128)(2,1)S(1)}, bf16[3,96,448]{2,1,0:T(8,128)(2,1)S(1)}, u32[]{:S(2)}, u32[]{:S(2)}) collective-permute-start(bf16[3,96,448]{2,1,0:T(8,128)(2,1)S(1)} %bitcast.94), channel_id=1, source_target_pairs={{0,4},{4,8},{8,12},{12,0},{1,5},{5,9},{9,13},{13,1},{2,6},{6,10},{... | collective-permute-start | bytes 774152 | tf_op jit(solution)/shard_map/ppermute | solution.py:50
  168.8 3.7 %collective-permute-start.7 = (bf16[3,96,448]{2,1,0:T(8,128)(2,1)S(1)}, bf16[3,96,448]{2,1,0:T(8,128)(2,1)S(1)}, u32[]{:S(2)}, u32[]{:S(2)}) collective-permute-start(bf16[3,96,448]{2,1,0:T(8,128)(2,1)S(1)} %bitcast.95), channel_id=1, source_target_pairs={{0,8},{4,12},{8,0},{12,4},{1,9},{5,13},{9,1},{13,5},{2,10},{6,14},... | collective-permute-start | bytes 774152 | tf_op jit(solution)/shard_map/ppermute | solution.py:50
  172.5 3.7 %collective-permute-start.6 = (bf16[3,96,448]{2,1,0:T(8,128)(2,1)S(1)}, bf16[3,96,448]{2,1,0:T(8,128)(2,1)S(1)}, u32[]{:S(2)}, u32[]{:S(2)}) collective-permute-start(bf16[3,96,448]{2,1,0:T(8,128)(2,1)S(1)} %bitcast.96), channel_id=1, source_target_pairs={{0,12},{4,0},{8,4},{12,8},{1,13},{5,1},{9,5},{13,9},{2,14},{6,2},{... | collective-permute-start | bytes 774152 | tf_op jit(solution)/shard_map/ppermute | solution.py:50
  176.5 5.3 %collective-permute-done.7 = bf16[3,96,448]{2,1,0:T(8,128)(2,1)S(1)} collective-permute-done((bf16[3,96,448]{2,1,0:T(8,128)(2,1)S(1)}, bf16[3,96,448]{2,1,0:T(8,128)(2,1)S(1)}, u32[]{:S(2)}, u32[]{:S(2)}) %collective-permute-start.7) | collective-permute-done | bytes 258080 | tf_op jit(solution)/shard_map/ppermute | solution.py:50
  181.8 5.9 %collective-permute-done.6 = bf16[3,96,448]{2,1,0:T(8,128)(2,1)S(1)} collective-permute-done((bf16[3,96,448]{2,1,0:T(8,128)(2,1)S(1)}, bf16[3,96,448]{2,1,0:T(8,128)(2,1)S(1)}, u32[]{:S(2)}, u32[]{:S(2)}) %collective-permute-start.6) | collective-permute-done | bytes 258080 | tf_op jit(solution)/shard_map/ppermute | solution.py:50
  187.7 2.9 %fusion.4 = (bf16[3,4,96,448]{3,2,0,1:T(8,128)(2,1)S(1)}, bf16[3,4,96,448]{3,2,0,1:T(8,128)(2,1)S(1)}) fusion(s32[]{:T(128)S(6)} %select_n.67, bf16[1,3,96,448]{3,2,1,0:T(8,128)(2,1)S(1)} %bitcast.93, bf16[1,3,96,448]{3,2,1,0:T(8,128)(2,1)S(1)} %bitcast.100, bf16[1,3,96,448]{3,2,1,0:T(8,128)(2,1)S(1)} %bitcast.99, bf16[1,3,96,448]{3,2,1,0:T(8,128)(2,1)S(1)} %bitcast.98, ...), kind=kLoop, calls=%fused_computation.30 | loop fusion | flops 7225344 | bytes 4128772 | tf_op jit(solution)/shard_map/transpose | solution.py:54
  190.8 0.6 fusion.59
  191.3 0.6 convolution_add_fusion
  192.1 8.9 %all_to_all.32 = f32[16,2,1,24,512]{4,3,0,2,1:T(8,128)} all-to-all(f32[16,2,1,24,512]{4,3,0,2,1:T(8,128)S(1)} %copy.73), channel_id=1, replica_groups=mesh['y'=8,'zl'=2,'c'=2,'x'=4,'zh'=4] {'c'}, dimensions={1} | all-to-all | bytes 3145728 | tf_op jit(solution)/shard_map/all_to_all | solution.py:25
  201.0 2.5 %reduce_sum.38 = f32[16,24,512]{2,1,0:T(8,128)} reduce(f32[16,2,1,24,512]{4,3,0,2,1:T(8,128)} %all_to_all.32, f32[]{:T(128)} %constant.69.clone.1), dimensions={1,2}, to_apply=%region_2.5 | reduce | flops 196608 | bytes 2359300 | tf_op jit(solution)/shard_map/reduce_sum | solution.py:26
  203.5 4.3 %all-to-all-start.5 = ((f32[16,24,512]{2,1,0:T(8,128)}), f32[16,24,512]{2,1,0:T(8,128)}, u32[]{:S(2)}, u32[]{:S(2)}) async-start(f32[16,24,512]{2,1,0:T(8,128)} %reduce_sum.38), calls=%async_computation.5 | async-start | bytes 1572864 | tf_op jit(solution)/shard_map/all_to_all | solution.py:25
  207.8 2.6 %convolution_convert_fusion.1 = bf16[512,448]{0,1:T(8,128)(2,1)} fusion(bf16[768,1024]{1,0:T(8,128)(2,1)} %bitcast.80, bf16[3,384,448]{2,1,0:T(8,128)(2,1)S(1)} %bitcast.71, bf16[3,384,448]{2,1,0:T(8,128)(2,1)S(1)} %bitcast.66), kind=kOutput, calls=%fused_computation.24 | convolution fusion | flops 353927168 | bytes 3309568 | tf_op jit(solution)/shard_map/dot_general | solution.py:91
  210.4 1.3 convolution_convert_fusion.2
  211.7 1.3 convolution_convert_fusion
  213.0 15.6 %all-to-all-done.5 = f32[16,24,512]{2,1,0:T(8,128)} async-done(((f32[16,24,512]{2,1,0:T(8,128)}), f32[16,24,512]{2,1,0:T(8,128)}, u32[]{:S(2)}, u32[]{:S(2)}) %all-to-all-start.5) | async-done | bytes 786464 | tf_op jit(solution)/shard_map/all_to_all | solution.py:25
  228.7 1.8 reduce_sum.39
  (45 shorter events, 5.1 us)
Async XLA Ops:
  0.6 41.4 %copy-start = (bf16[512,448]{0,1:T(8,128)(2,1)S(1)}, bf16[512,448]{0,1:T(8,128)(2,1)}, u32[]{:S(2)}) copy-start(bf16[512,448]{0,1:T(8,128)(2,1)} %param.11) | copy-start | bytes 1376260
  40.1 1.0 copy-start.3
  40.2 9.3 %copy-start.1 = (bf16[16,2,1,24,1024]{4,3,1,0,2:T(8,128)(2,1)}, bf16[16,2,1,24,1024]{4,3,1,0,2:T(8,128)(2,1)S(1)}, u32[]{:S(2)}) copy-start(bf16[16,2,1,24,1024]{4,3,1,0,2:T(8,128)(2,1)S(1)} %copy.57) | copy-start | bytes 4718596
  40.2 1.4 copy-start.4
  44.3 33.5 %all-to-all-start.3 = ((f32[3,4,96,448]{3,2,0,1:T(8,128)}), f32[3,4,96,448]{3,2,0,1:T(8,128)}, u32[]{:S(2)}, u32[]{:S(2)}) async-start(f32[3,4,96,448]{3,2,0,1:T(8,128)} %copy.69), calls=%async_computation.3 | async-start | bytes 4718592 | tf_op jit(solution)/shard_map/all_to_all | solution.py:25
  77.7 31.7 %all-to-all-start.2 = ((f32[3,4,96,448]{3,2,0,1:T(8,128)}), f32[3,4,96,448]{3,2,0,1:T(8,128)S(1)}, u32[]{:S(2)}, u32[]{:S(2)}) async-start(f32[3,4,96,448]{3,2,0,1:T(8,128)} %copy.61), calls=%async_computation.2 | async-start | bytes 4718592 | tf_op jit(solution)/shard_map/all_to_all | solution.py:25
  86.1 37.2 %collective-permute-start.9 = (f32[3,24,448]{2,1,0:T(8,128)}, f32[3,24,448]{2,1,0:T(8,128)S(1)}, u32[]{:S(2)}, u32[]{:S(2)}) collective-permute-start(f32[3,24,448]{2,1,0:T(8,128)} %get-tuple-element.6), channel_id=1, source_target_pairs={{0,1},{1,2},{2,3},{3,0},{4,5},{5,6},{6,7},{7,4},{8,9},{9,10},{10,1... | collective-permute-start | bytes 387080 | tf_op jit(solution)/shard_map/ppermute | solution.py:43
  91.9 36.8 %collective-permute-start.11 = (f32[3,24,448]{2,1,0:T(8,128)}, f32[3,24,448]{2,1,0:T(8,128)}, u32[]{:S(2)}, u32[]{:S(2)}) collective-permute-start(f32[3,24,448]{2,1,0:T(8,128)} %get-tuple-element.7), channel_id=1, source_target_pairs={{0,3},{1,0},{2,1},{3,2},{4,7},{5,4},{6,5},{7,6},{8,11},{9,8},{10,9... | collective-permute-start | bytes 387080 | tf_op jit(solution)/shard_map/ppermute | solution.py:43
  97.7 31.0 %collective-permute-start.10 = (f32[3,24,448]{2,1,0:T(8,128)}, f32[3,24,448]{2,1,0:T(8,128)}, u32[]{:S(2)}, u32[]{:S(2)}) collective-permute-start(f32[3,24,448]{2,1,0:T(8,128)} %get-tuple-element.8), channel_id=1, source_target_pairs={{0,2},{1,3},{2,0},{3,1},{4,6},{5,7},{6,4},{7,5},{8,10},{9,11},{10,... | collective-permute-start | bytes 387080 | tf_op jit(solution)/shard_map/ppermute | solution.py:43
  111.6 26.3 %collective-permute-start = (f32[3,24,448]{2,1,0:T(8,128)S(1)}, f32[3,24,448]{2,1,0:T(8,128)S(1)}, u32[]{:S(2)}, u32[]{:S(2)}) collective-permute-start(f32[3,24,448]{2,1,0:T(8,128)S(1)} %get-tuple-element.9), channel_id=1, source_target_pairs={{0,1},{1,2},{2,3},{3,0},{4,5},{5,6},{6,7},{7,4},{8,9},{9,10},{10,1... | collective-permute-start | bytes 387080 | tf_op jit(solution)/shard_map/ppermute | solution.py:43
  117.3 22.5 %collective-permute-start.2 = (f32[3,24,448]{2,1,0:T(8,128)S(1)}, f32[3,24,448]{2,1,0:T(8,128)S(1)}, u32[]{:S(2)}, u32[]{:S(2)}) collective-permute-start(f32[3,24,448]{2,1,0:T(8,128)S(1)} %get-tuple-element.10), channel_id=1, source_target_pairs={{0,3},{1,0},{2,1},{3,2},{4,7},{5,4},{6,5},{7,6},{8,11},{9,8},{10,9... | collective-permute-start | bytes 387080 | tf_op jit(solution)/shard_map/ppermute | solution.py:43
  123.2 16.6 %collective-permute-start.1 = (f32[3,24,448]{2,1,0:T(8,128)S(1)}, f32[3,24,448]{2,1,0:T(8,128)S(1)}, u32[]{:S(2)}, u32[]{:S(2)}) collective-permute-start(f32[3,24,448]{2,1,0:T(8,128)S(1)} %get-tuple-element.11), channel_id=1, source_target_pairs={{0,2},{1,3},{2,0},{3,1},{4,6},{5,7},{6,4},{7,5},{8,10},{9,11},{10,... | collective-permute-start | bytes 387080 | tf_op jit(solution)/shard_map/ppermute | solution.py:43
  129.9 11.0 %collective-permute-start.13 = (bf16[3,24,448]{2,1,0:T(8,128)(2,1)S(1)}, bf16[3,24,448]{2,1,0:T(8,128)(2,1)S(1)}, u32[]{:S(2)}, u32[]{:S(2)}) collective-permute-start(bf16[3,24,448]{2,1,0:T(8,128)(2,1)S(1)} %get-tuple-element.18), channel_id=1, source_target_pairs={{0,2},{1,3},{2,0},{3,1},{4,6},{5,7},{6,4},{7,5},{8,10},{9,11},{10,... | collective-permute-start | bytes 193544 | tf_op jit(solution)/shard_map/ppermute | solution.py:50
  133.6 11.6 %collective-permute-start.12 = (bf16[3,24,448]{2,1,0:T(8,128)(2,1)S(1)}, bf16[3,24,448]{2,1,0:T(8,128)(2,1)S(1)}, u32[]{:S(2)}, u32[]{:S(2)}) collective-permute-start(bf16[3,24,448]{2,1,0:T(8,128)(2,1)S(1)} %get-tuple-element.18), channel_id=1, source_target_pairs={{0,3},{1,0},{2,1},{3,2},{4,7},{5,4},{6,5},{7,6},{8,11},{9,8},{10,9... | collective-permute-start | bytes 193544 | tf_op jit(solution)/shard_map/ppermute | solution.py:50
  137.9 7.5 %collective-permute-start.14 = (bf16[3,24,448]{2,1,0:T(8,128)(2,1)S(1)}, bf16[3,24,448]{2,1,0:T(8,128)(2,1)S(1)}, u32[]{:S(2)}, u32[]{:S(2)}) collective-permute-start(bf16[3,24,448]{2,1,0:T(8,128)(2,1)S(1)} %get-tuple-element.18), channel_id=1, source_target_pairs={{0,1},{1,2},{2,3},{3,0},{4,5},{5,6},{6,7},{7,4},{8,9},{9,10},{10,1... | collective-permute-start | bytes 193544 | tf_op jit(solution)/shard_map/ppermute | solution.py:50
  145.8 26.7 %collective-permute-start.17 = (bf16[3,96,448]{2,1,0:T(8,128)(2,1)S(1)}, bf16[3,96,448]{2,1,0:T(8,128)(2,1)S(1)}, u32[]{:S(2)}, u32[]{:S(2)}) collective-permute-start(bf16[3,96,448]{2,1,0:T(8,128)(2,1)S(1)} %bitcast.90), channel_id=1, source_target_pairs={{0,4},{4,8},{8,12},{12,0},{1,5},{5,9},{9,13},{13,1},{2,6},{6,10},{... | collective-permute-start | bytes 774152 | tf_op jit(solution)/shard_map/ppermute | solution.py:50
  148.2 14.8 %collective-permute-start.4 = (bf16[3,24,448]{2,1,0:T(8,128)(2,1)S(1)}, bf16[3,24,448]{2,1,0:T(8,128)(2,1)S(1)}, u32[]{:S(2)}, u32[]{:S(2)}) collective-permute-start(bf16[3,24,448]{2,1,0:T(8,128)(2,1)S(1)} %get-tuple-element.20), channel_id=1, source_target_pairs={{0,2},{1,3},{2,0},{3,1},{4,6},{5,7},{6,4},{7,5},{8,10},{9,11},{10,... | collective-permute-start | bytes 193544 | tf_op jit(solution)/shard_map/ppermute | solution.py:50
  152.6 13.0 %collective-permute-start.3 = (bf16[3,24,448]{2,1,0:T(8,128)(2,1)S(1)}, bf16[3,24,448]{2,1,0:T(8,128)(2,1)S(1)}, u32[]{:S(2)}, u32[]{:S(2)}) collective-permute-start(bf16[3,24,448]{2,1,0:T(8,128)(2,1)S(1)} %get-tuple-element.20), channel_id=1, source_target_pairs={{0,3},{1,0},{2,1},{3,2},{4,7},{5,4},{6,5},{7,6},{8,11},{9,8},{10,9... | collective-permute-start | bytes 193544 | tf_op jit(solution)/shard_map/ppermute | solution.py:50
  157.4 8.2 %collective-permute-start.5 = (bf16[3,24,448]{2,1,0:T(8,128)(2,1)S(1)}, bf16[3,24,448]{2,1,0:T(8,128)(2,1)S(1)}, u32[]{:S(2)}, u32[]{:S(2)}) collective-permute-start(bf16[3,24,448]{2,1,0:T(8,128)(2,1)S(1)} %get-tuple-element.20), channel_id=1, source_target_pairs={{0,1},{1,2},{2,3},{3,0},{4,5},{5,6},{6,7},{7,4},{8,9},{9,10},{10,1... | collective-permute-start | bytes 193544 | tf_op jit(solution)/shard_map/ppermute | solution.py:50
  159.3 16.9 %collective-permute-start.16 = (bf16[3,96,448]{2,1,0:T(8,128)(2,1)S(1)}, bf16[3,96,448]{2,1,0:T(8,128)(2,1)S(1)}, u32[]{:S(2)}, u32[]{:S(2)}) collective-permute-start(bf16[3,96,448]{2,1,0:T(8,128)(2,1)S(1)} %bitcast.91), channel_id=1, source_target_pairs={{0,8},{4,12},{8,0},{12,4},{1,9},{5,13},{9,1},{13,5},{2,10},{6,14},... | collective-permute-start | bytes 774152 | tf_op jit(solution)/shard_map/ppermute | solution.py:50
  163.1 13.5 %collective-permute-start.15 = (bf16[3,96,448]{2,1,0:T(8,128)(2,1)S(1)}, bf16[3,96,448]{2,1,0:T(8,128)(2,1)S(1)}, u32[]{:S(2)}, u32[]{:S(2)}) collective-permute-start(bf16[3,96,448]{2,1,0:T(8,128)(2,1)S(1)} %bitcast.92), channel_id=1, source_target_pairs={{0,12},{4,0},{8,4},{12,8},{1,13},{5,1},{9,5},{13,9},{2,14},{6,2},{... | collective-permute-start | bytes 774152 | tf_op jit(solution)/shard_map/ppermute | solution.py:50
  166.0 10.5 %collective-permute-start.8 = (bf16[3,96,448]{2,1,0:T(8,128)(2,1)S(1)}, bf16[3,96,448]{2,1,0:T(8,128)(2,1)S(1)}, u32[]{:S(2)}, u32[]{:S(2)}) collective-permute-start(bf16[3,96,448]{2,1,0:T(8,128)(2,1)S(1)} %bitcast.94), channel_id=1, source_target_pairs={{0,4},{4,8},{8,12},{12,0},{1,5},{5,9},{9,13},{13,1},{2,6},{6,10},{... | collective-permute-start | bytes 774152 | tf_op jit(solution)/shard_map/ppermute | solution.py:50
  168.8 13.0 %collective-permute-start.7 = (bf16[3,96,448]{2,1,0:T(8,128)(2,1)S(1)}, bf16[3,96,448]{2,1,0:T(8,128)(2,1)S(1)}, u32[]{:S(2)}, u32[]{:S(2)}) collective-permute-start(bf16[3,96,448]{2,1,0:T(8,128)(2,1)S(1)} %bitcast.95), channel_id=1, source_target_pairs={{0,8},{4,12},{8,0},{12,4},{1,9},{5,13},{9,1},{13,5},{2,10},{6,14},... | collective-permute-start | bytes 774152 | tf_op jit(solution)/shard_map/ppermute | solution.py:50
  172.5 15.2 %collective-permute-start.6 = (bf16[3,96,448]{2,1,0:T(8,128)(2,1)S(1)}, bf16[3,96,448]{2,1,0:T(8,128)(2,1)S(1)}, u32[]{:S(2)}, u32[]{:S(2)}) collective-permute-start(bf16[3,96,448]{2,1,0:T(8,128)(2,1)S(1)} %bitcast.96), channel_id=1, source_target_pairs={{0,12},{4,0},{8,4},{12,8},{1,13},{5,1},{9,5},{13,9},{2,14},{6,2},{... | collective-permute-start | bytes 774152 | tf_op jit(solution)/shard_map/ppermute | solution.py:50
  203.5 25.2 %all-to-all-start.5 = ((f32[16,24,512]{2,1,0:T(8,128)}), f32[16,24,512]{2,1,0:T(8,128)}, u32[]{:S(2)}, u32[]{:S(2)}) async-start(f32[16,24,512]{2,1,0:T(8,128)} %reduce_sum.38), calls=%async_computation.5 | async-start | bytes 1572864 | tf_op jit(solution)/shard_map/all_to_all | solution.py:25
  207.8 2.6 %copy-start.2 = (bf16[16,2,1,24,1024]{4,3,1,0,2:T(8,128)(2,1)S(1)}, bf16[16,2,1,24,1024]{4,3,1,0,2:T(8,128)(2,1)}, u32[]{:S(2)}) copy-start(bf16[16,2,1,24,1024]{4,3,1,0,2:T(8,128)(2,1)} %copy-done.1) | copy-start | bytes 4718596

commit v9 on v6

--- a/solution.py
+++ b/solution.py
@@ -64,9 +64,10 @@
     both = both.reshape((nsec // 2, 1, -1) + both.shape[1:])
     both = gather_a2a(both, "c", 2, 1).reshape((-1,) + both.shape[3:])
     all_tokens, all_grads = both[:, : tokens.shape[1]], both[:, tokens.shape[1] :]
-    rows = all_tokens.shape[0] // 2
+    nchunk = 3
+    rows = all_tokens.shape[0] // nchunk
     chunks = []
-    for c in range(2):
+    for c in range(nchunk):
         tok = all_tokens[c * rows : (c + 1) * rows]
         grd = all_grads[c * rows : (c + 1) * rows]
         gate_part = jnp.dot(tok, gate_weight, preferred_element_type=jnp.float32)

time: 228 us -> 273 us (1.20)
  starting transfers between devices: 75.9 us -> 102 us
  local copies, waits for them, and re-layouts: 11.5 us -> 19.2 us
  waiting for transfers between devices: 65 us -> 69 us
    ppermute x6 -> x9, starting transfers between devices: 29.5 us -> 39.3 us  [scatter_permute(): lax.ppermute(part, axis_name, [(j, (j + k) % n) for j in range(n)])]
    ppermute x6 -> x9, starting transfers between devices: 26 us -> 33.5 us  [gather_permute(): lax.ppermute(v, axis_name, [(j, (j + k) % n) for j in range(n)])]
    all_to_all x2 -> x3, starting transfers between devices: 7.8 us -> 12.8 us  [gather_a2a(): v = lax.all_to_all(v, axis_name, dim, dim, tiled=True)]
    all_to_all x3 -> x4, starting transfers between devices: 12.6 us -> 16.7 us  [scatter_sum(): v = lax.all_to_all(v, axis_name, dim, dim, tiled=True)]
    all_to_all x3 -> x4, local copies, waits for them, and re-layouts: 1.62 us -> 4.71 us  [gather_a2a(): v = lax.all_to_all(v, axis_name, dim, dim, tiled=True)]
    all_to_all x3 -> x4, waiting for transfers between devices: 47.7 us -> 50.6 us  [scatter_sum(): v = lax.all_to_all(v, axis_name, dim, dim, tiled=True)]
    all_to_all x2 -> x3, waiting for transfers between devices: 10.4 us -> 12.8 us  [gather_a2a(): v = lax.all_to_all(v, axis_name, dim, dim, tiled=True)]
    reduce_sum x4 -> x5, other arithmetic: 8.25 us -> 8.02 us  [scatter_sum(): return v.sum(dim)]
  transfers between devices with their start and end apart: 17 -> 25, of which waited for: 7 -> 7; matrix products, arithmetic and copies ran while one was open for 8% -> 11% of each run, Pallas kernels for 0% -> 0%
where the time goes in v9:
time: 273 us; the launch traced here: 270 us
  starting transfers between devices  102 us (37%)
  waiting for transfers between devices  69 us (25%)
  blocking collectives  54.2 us (20%)
  local copies, waits for them, and re-layouts  19.2 us (7%)
  other arithmetic  14.9 us (5%)
  matrix products  9.27 us (3%)
    all_to_all x4, waiting for transfers between devices, scatter_sum(): v = lax.all_to_all(v, axis_name, dim, dim, tiled=True)  50.6 us
    ppermute x9, starting transfers between devices, scatter_permute(): lax.ppermute(part, axis_name, [(j, (j + k) % n) for j in range(n)])  39.3 us
    all_to_all x2, blocking collectives, gather_a2a(): v = lax.all_to_all(v, axis_name, dim, dim, tiled=True)  38.3 us
    ppermute x9, starting transfers between devices, gather_permute(): lax.ppermute(v, axis_name, [(j, (j + k) % n) for j in range(n)])  33.5 us
    all_to_all x4, starting transfers between devices, scatter_sum(): v = lax.all_to_all(v, axis_name, dim, dim, tiled=True)  16.7 us
    all_to_all x1, blocking collectives, scatter_sum(): v = lax.all_to_all(v, axis_name, dim, dim, tiled=True)  15.9 us
    all_to_all x3, waiting for transfers between devices, gather_a2a(): v = lax.all_to_all(v, axis_name, dim, dim, tiled=True)  12.8 us
    all_to_all x3, starting transfers between devices, gather_a2a(): v = lax.all_to_all(v, axis_name, dim, dim, tiled=True)  12.8 us
  transfers between devices with their start and end apart: 25, of which 7 were waited for; matrix products, arithmetic and copies ran while one was open for 11% of the time, Pallas kernels for 0%

profile of v9, /device:TPU:1, one launch (start us, length us, event | category | flops | bytes accessed | tf_op | source)
XLA Modules:
  0.0 270.3 jit_solution(17238599689135769297)
XLA Ops:
  1.5 31.3 %all_to_all.50 = bf16[16,24,1024]{2,1,0:T(8,128)(2,1)S(1)} all-to-all(bf16[16,24,1024]{2,1,0:T(8,128)(2,1)S(1)} %broadcast_in_dim.32), channel_id=1, replica_groups=mesh['y'=8,'zl'=2,'c'=2,'x'=4,'zh'=4] {'y','zl'}, dimensions={0} | all-to-all | bytes 1572864 | tf_op jit(solution)/shard_map/all_to_all | solution.py:32
  33.1 7.0 %all_to_all.51 = bf16[16,2,1,24,1024]{4,3,2,0,1:T(8,128)(2,1)S(1)} all-to-all(bf16[16,2,1,24,1024]{4,3,2,0,1:T(8,128)(2,1)S(1)} %broadcast_in_dim.33), channel_id=1, replica_groups=mesh['y'=8,'zl'=2,'c'=2,'x'=4,'zh'=4] {'c'}, dimensions={1} | all-to-all | bytes 3145728 | tf_op jit(solution)/shard_map/all_to_all | solution.py:32
  42.2 1.4 copy.81
  43.6 4.4 %all-to-all-start.6 = ((f32[3,4,64,448]{3,2,0,1:T(8,128)}), f32[3,4,64,448]{3,2,0,1:T(8,128)}, u32[]{:S(2)}, u32[]{:S(2)}) async-start(f32[3,4,64,448]{3,2,0,1:T(8,128)} %copy.81), calls=%async_computation.6 | async-start | bytes 3145728 | tf_op jit(solution)/shard_map/all_to_all | solution.py:25
  49.1 1.4 copy.67
  50.5 18.0 %all-to-all-done.6 = f32[3,4,64,448]{3,2,0,1:T(8,128)} async-done(((f32[3,4,64,448]{3,2,0,1:T(8,128)}), f32[3,4,64,448]{3,2,0,1:T(8,128)}, u32[]{:S(2)}, u32[]{:S(2)}) %all-to-all-start.6) | async-done | bytes 1376288 | tf_op jit(solution)/shard_map/all_to_all | solution.py:25
  68.5 4.4 %all-to-all-start.2 = ((f32[3,4,64,448]{3,2,0,1:T(8,128)}), f32[3,4,64,448]{3,2,0,1:T(8,128)}, u32[]{:S(2)}, u32[]{:S(2)}) async-start(f32[3,4,64,448]{3,2,0,1:T(8,128)} %copy.67), calls=%async_computation.2 | async-start | bytes 3145728 | tf_op jit(solution)/shard_map/all_to_all | solution.py:25
  74.0 1.4 copy.75
  75.4 17.1 %all-to-all-done.2 = f32[3,4,64,448]{3,2,0,1:T(8,128)} async-done(((f32[3,4,64,448]{3,2,0,1:T(8,128)}), f32[3,4,64,448]{3,2,0,1:T(8,128)}, u32[]{:S(2)}, u32[]{:S(2)}) %all-to-all-start.2) | async-done | bytes 1376288 | tf_op jit(solution)/shard_map/all_to_all | solution.py:25
  92.5 4.3 %all-to-all-start.4 = ((f32[3,4,64,448]{3,2,0,1:T(8,128)}), f32[3,4,64,448]{3,2,0,1:T(8,128)}, u32[]{:S(2)}, u32[]{:S(2)}) async-start(f32[3,4,64,448]{3,2,0,1:T(8,128)} %copy.75), calls=%async_computation.4 | async-start | bytes 3145728 | tf_op jit(solution)/shard_map/all_to_all | solution.py:25
  96.9 1.6 reduce_sum.47
  99.2 5.8 %collective-permute-start.12 = (f32[3,16,448]{2,1,0:T(8,128)}, f32[3,16,448]{2,1,0:T(8,128)}, u32[]{:S(2)}, u32[]{:S(2)}) collective-permute-start(f32[3,16,448]{2,1,0:T(8,128)} %get-tuple-element.11), channel_id=1, source_target_pairs={{0,1},{1,2},{2,3},{3,0},{4,5},{5,6},{6,7},{7,4},{8,9},{9,10},{10,1... | collective-permute-start | bytes 258056 | tf_op jit(solution)/shard_map/ppermute | solution.py:43
  105.0 5.9 %collective-permute-start.14 = (f32[3,16,448]{2,1,0:T(8,128)}, f32[3,16,448]{2,1,0:T(8,128)}, u32[]{:S(2)}, u32[]{:S(2)}) collective-permute-start(f32[3,16,448]{2,1,0:T(8,128)} %get-tuple-element.12), channel_id=1, source_target_pairs={{0,3},{1,0},{2,1},{3,2},{4,7},{5,4},{6,5},{7,6},{8,11},{9,8},{10,9... | collective-permute-start | bytes 258056 | tf_op jit(solution)/shard_map/ppermute | solution.py:43
  110.9 1.6 reduce_sum.45
  113.4 2.2 collective-permute-start
  115.5 5.2 %collective-permute-start.2 = (f32[3,16,448]{2,1,0:T(8,128)}, f32[3,16,448]{2,1,0:T(8,128)S(1)}, u32[]{:S(2)}, u32[]{:S(2)}) collective-permute-start(f32[3,16,448]{2,1,0:T(8,128)} %get-tuple-element.6), channel_id=1, source_target_pairs={{0,3},{1,0},{2,1},{3,2},{4,7},{5,4},{6,5},{7,6},{8,11},{9,8},{10,9... | collective-permute-start | bytes 258056 | tf_op jit(solution)/shard_map/ppermute | solution.py:43
  120.8 5.5 %collective-permute-start.1 = (f32[3,16,448]{2,1,0:T(8,128)}, f32[3,16,448]{2,1,0:T(8,128)}, u32[]{:S(2)}, u32[]{:S(2)}) collective-permute-start(f32[3,16,448]{2,1,0:T(8,128)} %get-tuple-element.7), channel_id=1, source_target_pairs={{0,2},{1,3},{2,0},{3,1},{4,6},{5,7},{6,4},{7,5},{8,10},{9,11},{10,... | collective-permute-start | bytes 258056 | tf_op jit(solution)/shard_map/ppermute | solution.py:43
  126.3 1.6 reduce_sum.46
  128.7 3.7 %collective-permute-start.13 = (f32[3,16,448]{2,1,0:T(8,128)}, f32[3,16,448]{2,1,0:T(8,128)S(1)}, u32[]{:S(2)}, u32[]{:S(2)}) collective-permute-start(f32[3,16,448]{2,1,0:T(8,128)} %get-tuple-element.13), channel_id=1, source_target_pairs={{0,2},{1,3},{2,0},{3,1},{4,6},{5,7},{6,4},{7,5},{8,10},{9,11},{10,... | collective-permute-start | bytes 258056 | tf_op jit(solution)/shard_map/ppermute | solution.py:43
  132.4 2.2 collective-permute-start.6
  134.7 5.2 %collective-permute-start.8 = (f32[3,16,448]{2,1,0:T(8,128)}, f32[3,16,448]{2,1,0:T(8,128)S(1)}, u32[]{:S(2)}, u32[]{:S(2)}) collective-permute-start(f32[3,16,448]{2,1,0:T(8,128)} %get-tuple-element.9), channel_id=1, source_target_pairs={{0,3},{1,0},{2,1},{3,2},{4,7},{5,4},{6,5},{7,6},{8,11},{9,8},{10,9... | collective-permute-start | bytes 258056 | tf_op jit(solution)/shard_map/ppermute | solution.py:43
  141.0 5.5 %collective-permute-start.4 = (bf16[3,16,448]{2,1,0:T(8,128)(2,1)S(1)}, bf16[3,16,448]{2,1,0:T(8,128)(2,1)S(1)}, u32[]{:S(2)}, u32[]{:S(2)}) collective-permute-start(bf16[3,16,448]{2,1,0:T(8,128)(2,1)S(1)} %get-tuple-element.23), channel_id=1, source_target_pairs={{0,2},{1,3},{2,0},{3,1},{4,6},{5,7},{6,4},{7,5},{8,10},{9,11},{10,... | collective-permute-start | bytes 129032 | tf_op jit(solution)/shard_map/ppermute | solution.py:50
  146.5 1.9 collective-permute-start.3
  148.4 4.3 %collective-permute-start.5 = (bf16[3,16,448]{2,1,0:T(8,128)(2,1)S(1)}, bf16[3,16,448]{2,1,0:T(8,128)(2,1)S(1)}, u32[]{:S(2)}, u32[]{:S(2)}) collective-permute-start(bf16[3,16,448]{2,1,0:T(8,128)(2,1)S(1)} %get-tuple-element.23), channel_id=1, source_target_pairs={{0,1},{1,2},{2,3},{3,0},{4,5},{5,6},{6,7},{7,4},{8,9},{9,10},{10,1... | collective-permute-start | bytes 129032 | tf_op jit(solution)/shard_map/ppermute | solution.py:50
  154.4 3.7 %collective-permute-start.7 = (f32[3,16,448]{2,1,0:T(8,128)}, f32[3,16,448]{2,1,0:T(8,128)}, u32[]{:S(2)}, u32[]{:S(2)}) collective-permute-start(f32[3,16,448]{2,1,0:T(8,128)} %get-tuple-element.10), channel_id=1, source_target_pairs={{0,2},{1,3},{2,0},{3,1},{4,6},{5,7},{6,4},{7,5},{8,10},{9,11},{10,... | collective-permute-start | bytes 258056 | tf_op jit(solution)/shard_map/ppermute | solution.py:43
  158.1 5.5 %collective-permute-start.16 = (bf16[3,16,448]{2,1,0:T(8,128)(2,1)}, bf16[3,16,448]{2,1,0:T(8,128)(2,1)}, u32[]{:S(2)}, u32[]{:S(2)}) collective-permute-start(bf16[3,16,448]{2,1,0:T(8,128)(2,1)} %get-tuple-element.27), channel_id=1, source_target_pairs={{0,2},{1,3},{2,0},{3,1},{4,6},{5,7},{6,4},{7,5},{8,10},{9,11},{10,... | collective-permute-start | bytes 129032 | tf_op jit(solution)/shard_map/ppermute | solution.py:50
  163.6 3.1 %collective-permute-start.15 = (bf16[3,16,448]{2,1,0:T(8,128)(2,1)}, bf16[3,16,448]{2,1,0:T(8,128)(2,1)}, u32[]{:S(2)}, u32[]{:S(2)}) collective-permute-start(bf16[3,16,448]{2,1,0:T(8,128)(2,1)} %get-tuple-element.27), channel_id=1, source_target_pairs={{0,3},{1,0},{2,1},{3,2},{4,7},{5,4},{6,5},{7,6},{8,11},{9,8},{10,9... | collective-permute-start | bytes 129032 | tf_op jit(solution)/shard_map/ppermute | solution.py:50
  168.0 4.1 %all-to-all-start.3 = ((bf16[3,4,64,448]{3,2,0,1:T(8,128)(2,1)}), bf16[3,4,64,448]{3,2,0,1:T(8,128)(2,1)S(1)}, u32[]{:S(2)}, u32[]{:S(2)}) async-start(bf16[3,4,64,448]{3,2,0,1:T(8,128)(2,1)} %broadcast_in_dim.35), calls=%async_computation.3 | async-start | bytes 1572864 | tf_op jit(solution)/shard_map/all_to_all | solution.py:32
  172.1 3.0 %collective-permute-start.17 = (bf16[3,16,448]{2,1,0:T(8,128)(2,1)}, bf16[3,16,448]{2,1,0:T(8,128)(2,1)S(1)}, u32[]{:S(2)}, u32[]{:S(2)}) collective-permute-start(bf16[3,16,448]{2,1,0:T(8,128)(2,1)} %get-tuple-element.27), channel_id=1, source_target_pairs={{0,1},{1,2},{2,3},{3,0},{4,5},{5,6},{6,7},{7,4},{8,9},{9,10},{10,1... | collective-permute-start | bytes 129032 | tf_op jit(solution)/shard_map/ppermute | solution.py:50
  176.2 3.7 %collective-permute-start.10 = (bf16[3,16,448]{2,1,0:T(8,128)(2,1)S(1)}, bf16[3,16,448]{2,1,0:T(8,128)(2,1)S(1)}, u32[]{:S(2)}, u32[]{:S(2)}) collective-permute-start(bf16[3,16,448]{2,1,0:T(8,128)(2,1)S(1)} %get-tuple-element.25), channel_id=1, source_target_pairs={{0,2},{1,3},{2,0},{3,1},{4,6},{5,7},{6,4},{7,5},{8,10},{9,11},{10,... | collective-permute-start | bytes 129032 | tf_op jit(solution)/shard_map/ppermute | solution.py:50
  179.9 4.6 %collective-permute-start.9 = (bf16[3,16,448]{2,1,0:T(8,128)(2,1)S(1)}, bf16[3,16,448]{2,1,0:T(8,128)(2,1)S(1)}, u32[]{:S(2)}, u32[]{:S(2)}) collective-permute-start(bf16[3,16,448]{2,1,0:T(8,128)(2,1)S(1)} %get-tuple-element.25), channel_id=1, source_target_pairs={{0,3},{1,0},{2,1},{3,2},{4,7},{5,4},{6,5},{7,6},{8,11},{9,8},{10,9... | collective-permute-start | bytes 129032 | tf_op jit(solution)/shard_map/ppermute | solution.py:50
  184.6 1.9 collective-permute-start.11
  186.7 5.2 %collective-permute-done.11 = bf16[3,16,448]{2,1,0:T(8,128)(2,1)S(1)} collective-permute-done((bf16[3,16,448]{2,1,0:T(8,128)(2,1)S(1)}, bf16[3,16,448]{2,1,0:T(8,128)(2,1)S(1)}, u32[]{:S(2)}, u32[]{:S(2)}) %collective-permute-start.11) | collective-permute-done | bytes 43040 | tf_op jit(solution)/shard_map/ppermute | solution.py:50
  192.0 1.4 fusion.26
  194.0 2.1 broadcast_in_dim.37
  196.1 4.5 %all-to-all-start.5 = ((bf16[3,4,64,448]{3,2,0,1:T(8,128)(2,1)}), bf16[3,4,64,448]{3,2,0,1:T(8,128)(2,1)}, u32[]{:S(2)}, u32[]{:S(2)}) async-start(bf16[3,4,64,448]{3,2,0,1:T(8,128)(2,1)} %broadcast_in_dim.37), calls=%async_computation.5 | async-start | bytes 1572864 | tf_op jit(solution)/shard_map/all_to_all | solution.py:32
  201.3 7.8 %all-to-all-done.5 = bf16[3,4,64,448]{3,2,0,1:T(8,128)(2,1)} async-done(((bf16[3,4,64,448]{3,2,0,1:T(8,128)(2,1)}), bf16[3,4,64,448]{3,2,0,1:T(8,128)(2,1)}, u32[]{:S(2)}, u32[]{:S(2)}) %all-to-all-start.5) | async-done | bytes 688160 | tf_op jit(solution)/shard_map/all_to_all | solution.py:32
  209.1 1.9 broadcast_in_dim.39
  210.9 4.2 %all-to-all-start.7 = ((bf16[3,4,64,448]{3,2,0,1:T(8,128)(2,1)}), bf16[3,4,64,448]{3,2,0,1:T(8,128)(2,1)}, u32[]{:S(2)}, u32[]{:S(2)}) async-start(bf16[3,4,64,448]{3,2,0,1:T(8,128)(2,1)} %broadcast_in_dim.39), calls=%async_computation.7 | async-start | bytes 1572864 | tf_op jit(solution)/shard_map/all_to_all | solution.py:32
  216.4 2.1 copy.77
  218.5 5.1 %all-to-all-done.7 = bf16[3,4,64,448]{3,2,0,1:T(8,128)(2,1)} async-done(((bf16[3,4,64,448]{3,2,0,1:T(8,128)(2,1)}), bf16[3,4,64,448]{3,2,0,1:T(8,128)(2,1)}, u32[]{:S(2)}, u32[]{:S(2)}) %all-to-all-start.7) | async-done | bytes 688160 | tf_op jit(solution)/shard_map/all_to_all | solution.py:32
  226.8 15.9 %all_to_all.52 = f32[16,2,1,24,512]{4,3,0,2,1:T(8,128)} all-to-all(f32[16,2,1,24,512]{4,3,0,2,1:T(8,128)S(1)} %copy.84), channel_id=1, replica_groups=mesh['y'=8,'zl'=2,'c'=2,'x'=4,'zh'=4] {'c'}, dimensions={1} | all-to-all | bytes 3145728 | tf_op jit(solution)/shard_map/all_to_all | solution.py:25
  242.7 2.5 reduce_sum.48
  245.2 3.6 %all-to-all-start.9 = ((f32[16,24,512]{2,1,0:T(8,128)}), f32[16,24,512]{2,1,0:T(8,128)S(1)}, u32[]{:S(2)}, u32[]{:S(2)}) async-start(f32[16,24,512]{2,1,0:T(8,128)} %reduce_sum.48), calls=%async_computation.9 | async-start | bytes 1572864 | tf_op jit(solution)/shard_map/all_to_all | solution.py:25
  248.8 2.6 convolution_convert_fusion.1
  251.4 1.3 convolution_convert_fusion.2
  252.8 1.3 convolution_convert_fusion
  254.1 15.5 %all-to-all-done.9 = f32[16,24,512]{2,1,0:T(8,128)S(1)} async-done(((f32[16,24,512]{2,1,0:T(8,128)}), f32[16,24,512]{2,1,0:T(8,128)S(1)}, u32[]{:S(2)}, u32[]{:S(2)}) %all-to-all-start.9) | async-done | bytes 786464 | tf_op jit(solution)/shard_map/all_to_all | solution.py:25
  (80 shorter events, 19.5 us)
Async XLA Ops:
  0.6 41.1 %copy-start = (bf16[512,448]{0,1:T(8,128)(2,1)S(1)}, bf16[512,448]{0,1:T(8,128)(2,1)}, u32[]{:S(2)}) copy-start(bf16[512,448]{0,1:T(8,128)(2,1)} %param.9) | copy-start | bytes 1376260
  40.1 1.0 copy-start.1
  40.1 1.3 copy-start.4
  43.6 24.9 %all-to-all-start.6 = ((f32[3,4,64,448]{3,2,0,1:T(8,128)}), f32[3,4,64,448]{3,2,0,1:T(8,128)}, u32[]{:S(2)}, u32[]{:S(2)}) async-start(f32[3,4,64,448]{3,2,0,1:T(8,128)} %copy.81), calls=%async_computation.6 | async-start | bytes 3145728 | tf_op jit(solution)/shard_map/all_to_all | solution.py:25
  68.5 24.0 %all-to-all-start.2 = ((f32[3,4,64,448]{3,2,0,1:T(8,128)}), f32[3,4,64,448]{3,2,0,1:T(8,128)}, u32[]{:S(2)}, u32[]{:S(2)}) async-start(f32[3,4,64,448]{3,2,0,1:T(8,128)} %copy.67), calls=%async_computation.2 | async-start | bytes 3145728 | tf_op jit(solution)/shard_map/all_to_all | solution.py:25
  92.5 33.8 %all-to-all-start.4 = ((f32[3,4,64,448]{3,2,0,1:T(8,128)}), f32[3,4,64,448]{3,2,0,1:T(8,128)}, u32[]{:S(2)}, u32[]{:S(2)}) async-start(f32[3,4,64,448]{3,2,0,1:T(8,128)} %copy.75), calls=%async_computation.4 | async-start | bytes 3145728 | tf_op jit(solution)/shard_map/all_to_all | solution.py:25
  99.2 41.8 %collective-permute-start.12 = (f32[3,16,448]{2,1,0:T(8,128)}, f32[3,16,448]{2,1,0:T(8,128)}, u32[]{:S(2)}, u32[]{:S(2)}) collective-permute-start(f32[3,16,448]{2,1,0:T(8,128)} %get-tuple-element.11), channel_id=1, source_target_pairs={{0,1},{1,2},{2,3},{3,0},{4,5},{5,6},{6,7},{7,4},{8,9},{9,10},{10,1... | collective-permute-start | bytes 258056 | tf_op jit(solution)/shard_map/ppermute | solution.py:43
  105.0 41.4 %collective-permute-start.14 = (f32[3,16,448]{2,1,0:T(8,128)}, f32[3,16,448]{2,1,0:T(8,128)}, u32[]{:S(2)}, u32[]{:S(2)}) collective-permute-start(f32[3,16,448]{2,1,0:T(8,128)} %get-tuple-element.12), channel_id=1, source_target_pairs={{0,3},{1,0},{2,1},{3,2},{4,7},{5,4},{6,5},{7,6},{8,11},{9,8},{10,9... | collective-permute-start | bytes 258056 | tf_op jit(solution)/shard_map/ppermute | solution.py:43
  112.5 13.7 %copy-start.8 = (f32[3,64,448]{2,1,0:T(8,128)}, f32[3,64,448]{2,1,0:T(8,128)S(1)}, u32[]{:S(2)}) copy-start(f32[3,64,448]{2,1,0:T(8,128)S(1)} %reduce_sum.45) | copy-start | bytes 1032196
  113.4 15.3 %collective-permute-start = (f32[3,16,448]{2,1,0:T(8,128)}, f32[3,16,448]{2,1,0:T(8,128)S(1)}, u32[]{:S(2)}, u32[]{:S(2)}) collective-permute-start(f32[3,16,448]{2,1,0:T(8,128)} %get-tuple-element.5), channel_id=1, source_target_pairs={{0,1},{1,2},{2,3},{3,0},{4,5},{5,6},{6,7},{7,4},{8,9},{9,10},{10,1... | collective-permute-start | bytes 258056 | tf_op jit(solution)/shard_map/ppermute | solution.py:43
  115.5 16.9 %collective-permute-start.2 = (f32[3,16,448]{2,1,0:T(8,128)}, f32[3,16,448]{2,1,0:T(8,128)S(1)}, u32[]{:S(2)}, u32[]{:S(2)}) collective-permute-start(f32[3,16,448]{2,1,0:T(8,128)} %get-tuple-element.6), channel_id=1, source_target_pairs={{0,3},{1,0},{2,1},{3,2},{4,7},{5,4},{6,5},{7,6},{8,11},{9,8},{10,9... | collective-permute-start | bytes 258056 | tf_op jit(solution)/shard_map/ppermute | solution.py:43
  120.8 13.9 %collective-permute-start.1 = (f32[3,16,448]{2,1,0:T(8,128)}, f32[3,16,448]{2,1,0:T(8,128)}, u32[]{:S(2)}, u32[]{:S(2)}) collective-permute-start(f32[3,16,448]{2,1,0:T(8,128)} %get-tuple-element.7), channel_id=1, source_target_pairs={{0,2},{1,3},{2,0},{3,1},{4,6},{5,7},{6,4},{7,5},{8,10},{9,11},{10,... | collective-permute-start | bytes 258056 | tf_op jit(solution)/shard_map/ppermute | solution.py:43
  127.9 40.1 %copy-start.7 = (f32[3,64,448]{2,1,0:T(8,128)}, f32[3,64,448]{2,1,0:T(8,128)S(1)}, u32[]{:S(2)}) copy-start(f32[3,64,448]{2,1,0:T(8,128)S(1)} %reduce_sum.46) | copy-start | bytes 1032196
  128.7 3.7 %copy-start.9 = (f32[3,16,448]{2,1,0:T(8,128)}, f32[3,16,448]{2,1,0:T(8,128)S(1)}, u32[]{:S(2)}) copy-start(f32[3,16,448]{2,1,0:T(8,128)S(1)} %collective-permute-done) | copy-start | bytes 258052
  128.7 19.7 %collective-permute-start.13 = (f32[3,16,448]{2,1,0:T(8,128)}, f32[3,16,448]{2,1,0:T(8,128)S(1)}, u32[]{:S(2)}, u32[]{:S(2)}) collective-permute-start(f32[3,16,448]{2,1,0:T(8,128)} %get-tuple-element.13), channel_id=1, source_target_pairs={{0,2},{1,3},{2,0},{3,1},{4,6},{5,7},{6,4},{7,5},{8,10},{9,11},{10,... | collective-permute-start | bytes 258056 | tf_op jit(solution)/shard_map/ppermute | solution.py:43
  132.4 2.2 copy-start.10
  132.4 39.6 %collective-permute-start.6 = (f32[3,16,448]{2,1,0:T(8,128)}, f32[3,16,448]{2,1,0:T(8,128)S(1)}, u32[]{:S(2)}, u32[]{:S(2)}) collective-permute-start(f32[3,16,448]{2,1,0:T(8,128)} %get-tuple-element.8), channel_id=1, source_target_pairs={{0,1},{1,2},{2,3},{3,0},{4,5},{5,6},{6,7},{7,4},{8,9},{9,10},{10,1... | collective-permute-start | bytes 258056 | tf_op jit(solution)/shard_map/ppermute | solution.py:43
  134.7 40.5 %collective-permute-start.8 = (f32[3,16,448]{2,1,0:T(8,128)}, f32[3,16,448]{2,1,0:T(8,128)S(1)}, u32[]{:S(2)}, u32[]{:S(2)}) collective-permute-start(f32[3,16,448]{2,1,0:T(8,128)} %get-tuple-element.9), channel_id=1, source_target_pairs={{0,3},{1,0},{2,1},{3,2},{4,7},{5,4},{6,5},{7,6},{8,11},{9,8},{10,9... | collective-permute-start | bytes 258056 | tf_op jit(solution)/shard_map/ppermute | solution.py:43
  141.0 13.3 %collective-permute-start.4 = (bf16[3,16,448]{2,1,0:T(8,128)(2,1)S(1)}, bf16[3,16,448]{2,1,0:T(8,128)(2,1)S(1)}, u32[]{:S(2)}, u32[]{:S(2)}) collective-permute-start(bf16[3,16,448]{2,1,0:T(8,128)(2,1)S(1)} %get-tuple-element.23), channel_id=1, source_target_pairs={{0,2},{1,3},{2,0},{3,1},{4,6},{5,7},{6,4},{7,5},{8,10},{9,11},{10,... | collective-permute-start | bytes 129032 | tf_op jit(solution)/shard_map/ppermute | solution.py:50
  146.5 11.6 %collective-permute-start.3 = (bf16[3,16,448]{2,1,0:T(8,128)(2,1)S(1)}, bf16[3,16,448]{2,1,0:T(8,128)(2,1)S(1)}, u32[]{:S(2)}, u32[]{:S(2)}) collective-permute-start(bf16[3,16,448]{2,1,0:T(8,128)(2,1)S(1)} %get-tuple-element.23), channel_id=1, source_target_pairs={{0,3},{1,0},{2,1},{3,2},{4,7},{5,4},{6,5},{7,6},{8,11},{9,8},{10,9... | collective-permute-start | bytes 129032 | tf_op jit(solution)/shard_map/ppermute | solution.py:50
  148.4 15.1 %collective-permute-start.5 = (bf16[3,16,448]{2,1,0:T(8,128)(2,1)S(1)}, bf16[3,16,448]{2,1,0:T(8,128)(2,1)S(1)}, u32[]{:S(2)}, u32[]{:S(2)}) collective-permute-start(bf16[3,16,448]{2,1,0:T(8,128)(2,1)S(1)} %get-tuple-element.23), channel_id=1, source_target_pairs={{0,1},{1,2},{2,3},{3,0},{4,5},{5,6},{6,7},{7,4},{8,9},{9,10},{10,1... | collective-permute-start | bytes 129032 | tf_op jit(solution)/shard_map/ppermute | solution.py:50
  154.4 20.8 %collective-permute-start.7 = (f32[3,16,448]{2,1,0:T(8,128)}, f32[3,16,448]{2,1,0:T(8,128)}, u32[]{:S(2)}, u32[]{:S(2)}) collective-permute-start(f32[3,16,448]{2,1,0:T(8,128)} %get-tuple-element.10), channel_id=1, source_target_pairs={{0,2},{1,3},{2,0},{3,1},{4,6},{5,7},{6,4},{7,5},{8,10},{9,11},{10,... | collective-permute-start | bytes 258056 | tf_op jit(solution)/shard_map/ppermute | solution.py:43
  158.1 26.5 %collective-permute-start.16 = (bf16[3,16,448]{2,1,0:T(8,128)(2,1)}, bf16[3,16,448]{2,1,0:T(8,128)(2,1)}, u32[]{:S(2)}, u32[]{:S(2)}) collective-permute-start(bf16[3,16,448]{2,1,0:T(8,128)(2,1)} %get-tuple-element.27), channel_id=1, source_target_pairs={{0,2},{1,3},{2,0},{3,1},{4,6},{5,7},{6,4},{7,5},{8,10},{9,11},{10,... | collective-permute-start | bytes 129032 | tf_op jit(solution)/shard_map/ppermute | solution.py:50
  163.6 22.9 %collective-permute-start.15 = (bf16[3,16,448]{2,1,0:T(8,128)(2,1)}, bf16[3,16,448]{2,1,0:T(8,128)(2,1)}, u32[]{:S(2)}, u32[]{:S(2)}) collective-permute-start(bf16[3,16,448]{2,1,0:T(8,128)(2,1)} %get-tuple-element.27), channel_id=1, source_target_pairs={{0,3},{1,0},{2,1},{3,2},{4,7},{5,4},{6,5},{7,6},{8,11},{9,8},{10,9... | collective-permute-start | bytes 129032 | tf_op jit(solution)/shard_map/ppermute | solution.py:50
  168.0 26.1 %all-to-all-start.3 = ((bf16[3,4,64,448]{3,2,0,1:T(8,128)(2,1)}), bf16[3,4,64,448]{3,2,0,1:T(8,128)(2,1)S(1)}, u32[]{:S(2)}, u32[]{:S(2)}) async-start(bf16[3,4,64,448]{3,2,0,1:T(8,128)(2,1)} %broadcast_in_dim.35), calls=%async_computation.3 | async-start | bytes 1572864 | tf_op jit(solution)/shard_map/all_to_all | solution.py:32
  172.1 14.4 %collective-permute-start.17 = (bf16[3,16,448]{2,1,0:T(8,128)(2,1)}, bf16[3,16,448]{2,1,0:T(8,128)(2,1)S(1)}, u32[]{:S(2)}, u32[]{:S(2)}) collective-permute-start(bf16[3,16,448]{2,1,0:T(8,128)(2,1)} %get-tuple-element.27), channel_id=1, source_target_pairs={{0,1},{1,2},{2,3},{3,0},{4,5},{5,6},{6,7},{7,4},{8,9},{9,10},{10,1... | collective-permute-start | bytes 129032 | tf_op jit(solution)/shard_map/ppermute | solution.py:50
  176.2 10.3 %collective-permute-start.10 = (bf16[3,16,448]{2,1,0:T(8,128)(2,1)S(1)}, bf16[3,16,448]{2,1,0:T(8,128)(2,1)S(1)}, u32[]{:S(2)}, u32[]{:S(2)}) collective-permute-start(bf16[3,16,448]{2,1,0:T(8,128)(2,1)S(1)} %get-tuple-element.25), channel_id=1, source_target_pairs={{0,2},{1,3},{2,0},{3,1},{4,6},{5,7},{6,4},{7,5},{8,10},{9,11},{10,... | collective-permute-start | bytes 129032 | tf_op jit(solution)/shard_map/ppermute | solution.py:50
  179.9 6.8 %collective-permute-start.9 = (bf16[3,16,448]{2,1,0:T(8,128)(2,1)S(1)}, bf16[3,16,448]{2,1,0:T(8,128)(2,1)S(1)}, u32[]{:S(2)}, u32[]{:S(2)}) collective-permute-start(bf16[3,16,448]{2,1,0:T(8,128)(2,1)S(1)} %get-tuple-element.25), channel_id=1, source_target_pairs={{0,3},{1,0},{2,1},{3,2},{4,7},{5,4},{6,5},{7,6},{8,11},{9,8},{10,9... | collective-permute-start | bytes 129032 | tf_op jit(solution)/shard_map/ppermute | solution.py:50
  184.6 7.4 %collective-permute-start.11 = (bf16[3,16,448]{2,1,0:T(8,128)(2,1)S(1)}, bf16[3,16,448]{2,1,0:T(8,128)(2,1)S(1)}, u32[]{:S(2)}, u32[]{:S(2)}) collective-permute-start(bf16[3,16,448]{2,1,0:T(8,128)(2,1)S(1)} %get-tuple-element.25), channel_id=1, source_target_pairs={{0,1},{1,2},{2,3},{3,0},{4,5},{5,6},{6,7},{7,4},{8,9},{9,10},{10,1... | collective-permute-start | bytes 129032 | tf_op jit(solution)/shard_map/ppermute | solution.py:50
  194.0 16.9 %copy-start.6 = (bf16[3,4,64,448]{3,2,0,1:T(8,128)(2,1)}, bf16[3,4,64,448]{3,2,0,1:T(8,128)(2,1)S(1)}, u32[]{:S(2)}) copy-start(bf16[3,4,64,448]{3,2,0,1:T(8,128)(2,1)S(1)} %all-to-all-done.3) | copy-start | bytes 2064388
  196.1 13.0 %all-to-all-start.5 = ((bf16[3,4,64,448]{3,2,0,1:T(8,128)(2,1)}), bf16[3,4,64,448]{3,2,0,1:T(8,128)(2,1)}, u32[]{:S(2)}, u32[]{:S(2)}) async-start(bf16[3,4,64,448]{3,2,0,1:T(8,128)(2,1)} %broadcast_in_dim.37), calls=%async_computation.5 | async-start | bytes 1572864 | tf_op jit(solution)/shard_map/all_to_all | solution.py:32
  210.9 12.6 %all-to-all-start.7 = ((bf16[3,4,64,448]{3,2,0,1:T(8,128)(2,1)}), bf16[3,4,64,448]{3,2,0,1:T(8,128)(2,1)}, u32[]{:S(2)}, u32[]{:S(2)}) async-start(bf16[3,4,64,448]{3,2,0,1:T(8,128)(2,1)} %broadcast_in_dim.39), calls=%async_computation.7 | async-start | bytes 1572864 | tf_op jit(solution)/shard_map/all_to_all | solution.py:32
  223.5 1.4 copy-start.5
  225.2 1.4 copy-start.2
  245.2 24.4 %all-to-all-start.9 = ((f32[16,24,512]{2,1,0:T(8,128)}), f32[16,24,512]{2,1,0:T(8,128)S(1)}, u32[]{:S(2)}, u32[]{:S(2)}) async-start(f32[16,24,512]{2,1,0:T(8,128)} %reduce_sum.48), calls=%async_computation.9 | async-start | bytes 1572864 | tf_op jit(solution)/shard_map/all_to_all | solution.py:25
  248.8 2.6 copy-start.3

commit v10 on v6

--- a/solution.py
+++ b/solution.py
@@ -64,11 +64,12 @@
     both = both.reshape((nsec // 2, 1, -1) + both.shape[1:])
     both = gather_a2a(both, "c", 2, 1).reshape((-1,) + both.shape[3:])
     all_tokens, all_grads = both[:, : tokens.shape[1]], both[:, tokens.shape[1] :]
-    rows = all_tokens.shape[0] // 2
+    total = all_tokens.shape[0]
+    edges = [0, total * 2 // 3, total]
     chunks = []
     for c in range(2):
-        tok = all_tokens[c * rows : (c + 1) * rows]
-        grd = all_grads[c * rows : (c + 1) * rows]
+        tok = all_tokens[edges[c] : edges[c + 1]]
+        grd = all_grads[edges[c] : edges[c + 1]]
         gate_part = jnp.dot(tok, gate_weight, preferred_element_type=jnp.float32)
         up_part = jnp.dot(tok, up_weight, preferred_element_type=jnp.float32)
         hidden_part = lax.dot_general(

time: 228 us -> 235 us (1.031)
  local copies, waits for them, and re-layouts: 11.5 us -> 31.2 us
  waiting for transfers between devices: 65 us -> 53.6 us
  blocking collectives: 51.6 us -> 47 us
  matrix products: 8.71 us -> 11.2 us
    all_to_all x3, waiting for transfers between devices: 47.7 us -> 23.4 us  [scatter_sum(): v = lax.all_to_all(v, axis_name, dim, dim, tiled=True)]
    unnamed x10 -> x29, local copies, waits for them, and re-layouts: 1.01 us -> 6.75 us
    ppermute x6, waiting for transfers between devices: 1.36 us -> 6.83 us  [scatter_permute(): lax.ppermute(part, axis_name, [(j, (j + k) % n) for j in range(n)])]
    all_to_all x1, blocking collectives: 13.3 us -> 8.7 us  [scatter_sum(): v = lax.all_to_all(v, axis_name, dim, dim, tiled=True)]
    ppermute x6, waiting for transfers between devices: 5.53 us -> 10.1 us  [gather_permute(): lax.ppermute(v, axis_name, [(j, (j + k) % n) for j in range(n)])]
    another operation x2 -> x7, local copies, waits for them, and re-layouts: 3.29 us -> 7.84 us  [local(): p = jnp.stack([gate_part, up_part, hidden_part])]
    dynamic_slice x2 -> x5, local copies, waits for them, and re-layouts: 2.92 us -> 7.15 us  [scatter_permute(): part = lax.dynamic_slice_in_dim(v, (me + k) % n * size, size, dim)]
    all_to_all x3, starting transfers between devices: 12.6 us -> 16.6 us  [scatter_sum(): v = lax.all_to_all(v, axis_name, dim, dim, tiled=True)]
  transfers between devices with their start and end apart: 17 -> 17, of which waited for: 7 -> 9; matrix products, arithmetic and copies ran while one was open for 8% -> 15% of each run, Pallas kernels for 0% -> 0%
where the time goes in v10:
time: 235 us; the launch traced here: 233 us
  starting transfers between devices  75.5 us (32%)
  waiting for transfers between devices  53.6 us (23%)
  blocking collectives  47 us (20%)
  local copies, waits for them, and re-layouts  31.2 us (13%)
  other arithmetic  13.3 us (6%)
  matrix products  11.2 us (5%)
    all_to_all x2, blocking collectives, gather_a2a(): v = lax.all_to_all(v, axis_name, dim, dim, tiled=True)  38.3 us
    ppermute x6, starting transfers between devices, scatter_permute(): lax.ppermute(part, axis_name, [(j, (j + k) % n) for j in range(n)])  28.6 us
    all_to_all x3, waiting for transfers between devices, scatter_sum(): v = lax.all_to_all(v, axis_name, dim, dim, tiled=True)  23.4 us
    ppermute x6, starting transfers between devices, gather_permute(): lax.ppermute(v, axis_name, [(j, (j + k) % n) for j in range(n)])  22.5 us
    all_to_all x3, starting transfers between devices, scatter_sum(): v = lax.all_to_all(v, axis_name, dim, dim, tiled=True)  16.6 us
    all_to_all x2, waiting for transfers between devices, gather_a2a(): v = lax.all_to_all(v, axis_name, dim, dim, tiled=True)  13.2 us
    ppermute x6, waiting for transfers between devices, gather_permute(): lax.ppermute(v, axis_name, [(j, (j + k) % n) for j in range(n)])  10.1 us
    all_to_all x1, blocking collectives, scatter_sum(): v = lax.all_to_all(v, axis_name, dim, dim, tiled=True)  8.7 us
  transfers between devices with their start and end apart: 17, of which 9 were waited for; matrix products, arithmetic and copies ran while one was open for 15% of the time, Pallas kernels for 0%

profile of v10, /device:TPU:1, one launch (start us, length us, event | category | flops | bytes accessed | tf_op | source)
XLA Modules:
  0.0 233.0 jit_solution(4139713986323118103)
XLA Ops:
  1.5 31.3 %all_to_all.40 = bf16[16,24,1024]{2,1,0:T(8,128)(2,1)S(1)} all-to-all(bf16[16,24,1024]{2,1,0:T(8,128)(2,1)S(1)} %broadcast_in_dim.12), channel_id=1, replica_groups=mesh['y'=8,'zl'=2,'c'=2,'x'=4,'zh'=4] {'y','zl'}, dimensions={0} | all-to-all | bytes 1572864 | tf_op jit(solution)/shard_map/all_to_all | solution.py:32
  33.1 7.0 %all_to_all.41 = bf16[16,2,1,24,1024]{4,3,2,0,1:T(8,128)(2,1)S(1)} all-to-all(bf16[16,2,1,24,1024]{4,3,2,0,1:T(8,128)(2,1)S(1)} %broadcast_in_dim.26), channel_id=1, replica_groups=mesh['y'=8,'zl'=2,'c'=2,'x'=4,'zh'=4] {'c'}, dimensions={1} | all-to-all | bytes 3145728 | tf_op jit(solution)/shard_map/all_to_all | solution.py:32
  42.2 1.4 copy.143
  43.6 4.3 %all-to-all-start.4 = ((f32[3,4,64,448]{3,2,0,1:T(8,128)}), f32[3,4,64,448]{3,2,0,1:T(8,128)}, u32[]{:S(2)}, u32[]{:S(2)}) async-start(f32[3,4,64,448]{3,2,0,1:T(8,128)} %copy.143), calls=%async_computation.4 | async-start | bytes 3145728 | tf_op jit(solution)/shard_map/all_to_all | solution.py:25
  48.0 1.4 fusion.10
  49.3 1.5 stack.64
  51.8 1.4 fusion.12
  53.2 1.5 stack.63
  55.7 1.4 fusion.14
  57.1 1.5 stack.62
  60.0 1.7 pad_maximum_fusion
  61.8 6.7 %all-to-all-done.4 = f32[3,4,64,448]{3,2,0,1:T(8,128)} async-done(((f32[3,4,64,448]{3,2,0,1:T(8,128)}), f32[3,4,64,448]{3,2,0,1:T(8,128)}, u32[]{:S(2)}, u32[]{:S(2)}) %all-to-all-start.4) | async-done | bytes 1376288 | tf_op jit(solution)/shard_map/all_to_all | solution.py:25
  68.4 4.6 %all-to-all-start.2 = ((f32[3,4,128,448]{2,3,0,1:T(8,128)}), f32[3,4,128,448]{2,3,0,1:T(8,128)}, u32[]{:S(2)}, u32[]{:S(2)}) async-start(f32[3,4,128,448]{2,3,0,1:T(8,128)} %pad_maximum_fusion), calls=%async_computation.2 | async-start | bytes 5505024 | tf_op jit(solution)/shard_map/all_to_all | solution.py:25
  73.0 1.6 reduce_sum.37
  74.7 9.8 %collective-permute-start.8 = (f32[3,16,448]{2,1,0:T(8,128)S(1)}, f32[3,16,448]{2,1,0:T(8,128)S(1)}, u32[]{:S(2)}, u32[]{:S(2)}) collective-permute-start(f32[3,16,448]{2,1,0:T(8,128)S(1)} %get-tuple-element.9), channel_id=1, source_target_pairs={{0,3},{1,0},{2,1},{3,2},{4,7},{5,4},{6,5},{7,6},{8,11},{9,8},{10,9... | collective-permute-start | bytes 258056 | tf_op jit(solution)/shard_map/ppermute | solution.py:43
  84.4 1.9 collective-permute-start.7
  86.4 4.2 %collective-permute-start.6 = (f32[3,16,448]{2,1,0:T(8,128)S(1)}, f32[3,16,448]{2,1,0:T(8,128)S(1)}, u32[]{:S(2)}, u32[]{:S(2)}) collective-permute-start(f32[3,16,448]{2,1,0:T(8,128)S(1)} %get-tuple-element.8), channel_id=1, source_target_pairs={{0,1},{1,2},{2,3},{3,0},{4,5},{5,6},{6,7},{7,4},{8,9},{9,10},{10,1... | collective-permute-start | bytes 258056 | tf_op jit(solution)/shard_map/ppermute | solution.py:43
  90.7 1.8 collective-permute-done.8
  92.4 3.4 %collective-permute-done.7 = f32[3,16,448]{2,1,0:T(8,128)S(1)} collective-permute-done((f32[3,16,448]{2,1,0:T(8,128)S(1)}, f32[3,16,448]{2,1,0:T(8,128)S(1)}, u32[]{:S(2)}, u32[]{:S(2)}) %collective-permute-start.7) | collective-permute-done | bytes 86048 | tf_op jit(solution)/shard_map/ppermute | solution.py:43
  95.9 5.7 %collective-permute-start.9 = (bf16[3,16,448]{2,1,0:T(8,128)(2,1)S(1)}, bf16[3,16,448]{2,1,0:T(8,128)(2,1)S(1)}, u32[]{:S(2)}, u32[]{:S(2)}) collective-permute-start(bf16[3,16,448]{2,1,0:T(8,128)(2,1)S(1)} %pad_maximum_fusion.5), channel_id=1, source_target_pairs={{0,3},{1,0},{2,1},{3,2},{4,7},{5,4},{6,5},{7,6},{8,11},{9,8},{10,9... | collective-permute-start | bytes 129032 | tf_op jit(solution)/shard_map/ppermute | solution.py:50
  102.2 1.9 collective-permute-start.10
  104.2 4.2 %collective-permute-start.11 = (bf16[3,16,448]{2,1,0:T(8,128)(2,1)S(1)}, bf16[3,16,448]{2,1,0:T(8,128)(2,1)S(1)}, u32[]{:S(2)}, u32[]{:S(2)}) collective-permute-start(bf16[3,16,448]{2,1,0:T(8,128)(2,1)S(1)} %pad_maximum_fusion.5), channel_id=1, source_target_pairs={{0,1},{1,2},{2,3},{3,0},{4,5},{5,6},{6,7},{7,4},{8,9},{9,10},{10,1... | collective-permute-start | bytes 129032 | tf_op jit(solution)/shard_map/ppermute | solution.py:50
  109.0 2.6 %collective-permute-done.10 = bf16[3,16,448]{2,1,0:T(8,128)(2,1)S(1)} collective-permute-done((bf16[3,16,448]{2,1,0:T(8,128)(2,1)S(1)}, bf16[3,16,448]{2,1,0:T(8,128)(2,1)S(1)}, u32[]{:S(2)}, u32[]{:S(2)}) %collective-permute-start.10) | collective-permute-done | bytes 43040 | tf_op jit(solution)/shard_map/ppermute | solution.py:50
  114.7 2.0 reduce_sum.36
  116.7 2.1 constant_dynamic-slice_fusion.6
  118.8 2.1 copy.136
  120.9 3.3 %collective-permute-start.2 = (f32[3,32,448]{2,1,0:T(8,128)}, f32[3,32,448]{2,1,0:T(8,128)}, u32[]{:S(2)}, u32[]{:S(2)}) collective-permute-start(f32[3,32,448]{2,1,0:T(8,128)} %copy.136), channel_id=1, source_target_pairs={{0,3},{1,0},{2,1},{3,2},{4,7},{5,4},{6,5},{7,6},{8,11},{9,8},{10,9... | collective-permute-start | bytes 516104 | tf_op jit(solution)/shard_map/ppermute | solution.py:43
  124.2 2.0 copy.135
  126.2 5.2 %collective-permute-start.1 = (f32[3,32,448]{2,1,0:T(8,128)}, f32[3,32,448]{2,1,0:T(8,128)}, u32[]{:S(2)}, u32[]{:S(2)}) collective-permute-start(f32[3,32,448]{2,1,0:T(8,128)} %copy.135), channel_id=1, source_target_pairs={{0,2},{1,3},{2,0},{3,1},{4,6},{5,7},{6,4},{7,5},{8,10},{9,11},{10,... | collective-permute-start | bytes 516104 | tf_op jit(solution)/shard_map/ppermute | solution.py:43
  132.3 4.2 %collective-permute-start = (f32[3,32,448]{2,1,0:T(8,128)}, f32[3,32,448]{2,1,0:T(8,128)}, u32[]{:S(2)}, u32[]{:S(2)}) collective-permute-start(f32[3,32,448]{2,1,0:T(8,128)} %copy.134), channel_id=1, source_target_pairs={{0,1},{1,2},{2,3},{3,0},{4,5},{5,6},{6,7},{7,4},{8,9},{9,10},{10,1... | collective-permute-start | bytes 516104 | tf_op jit(solution)/shard_map/ppermute | solution.py:43
  139.1 3.5 %all-to-all-start.5 = ((bf16[3,4,64,448]{3,2,0,1:T(8,128)(2,1)}), bf16[3,4,64,448]{3,2,0,1:T(8,128)(2,1)S(1)}, u32[]{:S(2)}, u32[]{:S(2)}) async-start(bf16[3,4,64,448]{3,2,0,1:T(8,128)(2,1)} %broadcast_in_dim.30), calls=%async_computation.5 | async-start | bytes 1572864 | tf_op jit(solution)/shard_map/all_to_all | solution.py:32
  143.5 1.6 collective-permute-done
  146.5 3.1 %collective-permute-start.3 = (bf16[3,32,448]{2,1,0:T(8,128)(2,1)S(1)}, bf16[3,32,448]{2,1,0:T(8,128)(2,1)S(1)}, u32[]{:S(2)}, u32[]{:S(2)}) collective-permute-start(bf16[3,32,448]{2,1,0:T(8,128)(2,1)S(1)} %pad_maximum_fusion.3), channel_id=1, source_target_pairs={{0,3},{1,0},{2,1},{3,2},{4,7},{5,4},{6,5},{7,6},{8,11},{9,8},{10,9... | collective-permute-start | bytes 258056 | tf_op jit(solution)/shard_map/ppermute | solution.py:50
  149.6 5.7 %collective-permute-start.4 = (bf16[3,32,448]{2,1,0:T(8,128)(2,1)S(1)}, bf16[3,32,448]{2,1,0:T(8,128)(2,1)S(1)}, u32[]{:S(2)}, u32[]{:S(2)}) collective-permute-start(bf16[3,32,448]{2,1,0:T(8,128)(2,1)S(1)} %pad_maximum_fusion.3), channel_id=1, source_target_pairs={{0,2},{1,3},{2,0},{3,1},{4,6},{5,7},{6,4},{7,5},{8,10},{9,11},{10,... | collective-permute-start | bytes 258056 | tf_op jit(solution)/shard_map/ppermute | solution.py:50
  155.3 1.9 collective-permute-start.5
  157.3 1.6 collective-permute-done.4
  159.0 5.9 %collective-permute-done.5 = bf16[3,32,448]{2,1,0:T(8,128)(2,1)S(1)} collective-permute-done((bf16[3,32,448]{2,1,0:T(8,128)(2,1)S(1)}, bf16[3,32,448]{2,1,0:T(8,128)(2,1)S(1)}, u32[]{:S(2)}, u32[]{:S(2)}) %collective-permute-start.5) | collective-permute-done | bytes 86048 | tf_op jit(solution)/shard_map/ppermute | solution.py:50
  165.3 1.3 broadcast_in_dim.28
  166.6 4.3 %all-to-all-start.3 = ((bf16[3,4,128,448]{2,3,0,1:T(8,128)(2,1)}), bf16[3,4,128,448]{2,3,0,1:T(8,128)(2,1)}, u32[]{:S(2)}, u32[]{:S(2)}) async-start(bf16[3,4,128,448]{2,3,0,1:T(8,128)(2,1)} %broadcast_in_dim.28), calls=%async_computation.3 | async-start | bytes 2752512 | tf_op jit(solution)/shard_map/all_to_all | solution.py:32
  171.9 2.2 copy.151
  174.1 13.2 %all-to-all-done.3 = bf16[3,4,128,448]{2,3,0,1:T(8,128)(2,1)} async-done(((bf16[3,4,128,448]{2,3,0,1:T(8,128)(2,1)}), bf16[3,4,128,448]{2,3,0,1:T(8,128)(2,1)}, u32[]{:S(2)}, u32[]{:S(2)}) %all-to-all-start.3) | async-done | bytes 1376288 | tf_op jit(solution)/shard_map/all_to_all | solution.py:32
  187.3 1.6 copy_bitcast_fusion
  190.7 8.7 %all_to_all.42 = f32[16,2,1,24,512]{4,3,0,2,1:T(8,128)} all-to-all(f32[16,2,1,24,512]{4,3,0,2,1:T(8,128)S(1)} %copy.152), channel_id=1, replica_groups=mesh['y'=8,'zl'=2,'c'=2,'x'=4,'zh'=4] {'c'}, dimensions={1} | all-to-all | bytes 3145728 | tf_op jit(solution)/shard_map/all_to_all | solution.py:25
  199.4 2.5 %reduce_sum.38 = f32[16,24,512]{2,1,0:T(8,128)} reduce(f32[16,2,1,24,512]{4,3,0,2,1:T(8,128)} %all_to_all.42, f32[]{:T(128)} %constant.63.clone.1), dimensions={1,2}, to_apply=%region_2.3 | reduce | flops 196608 | bytes 2359300 | tf_op jit(solution)/shard_map/reduce_sum | solution.py:26
  201.9 7.7 %all-to-all-start.7 = ((f32[16,24,512]{2,1,0:T(8,128)}), f32[16,24,512]{2,1,0:T(8,128)}, u32[]{:S(2)}, u32[]{:S(2)}) async-start(f32[16,24,512]{2,1,0:T(8,128)} %reduce_sum.38), calls=%async_computation.7 | async-start | bytes 1572864 | tf_op jit(solution)/shard_map/all_to_all | solution.py:25
  209.6 2.3 convolution_convert_fusion.1
  214.5 16.8 %all-to-all-done.7 = f32[16,24,512]{2,1,0:T(8,128)} async-done(((f32[16,24,512]{2,1,0:T(8,128)}), f32[16,24,512]{2,1,0:T(8,128)}, u32[]{:S(2)}, u32[]{:S(2)}) %all-to-all-start.7) | async-done | bytes 786464 | tf_op jit(solution)/shard_map/all_to_all | solution.py:25
  231.2 1.8 reduce_sum.39
  (73 shorter events, 22.5 us)
Async XLA Ops:
  0.6 41.1 %copy-start = (bf16[512,448]{0,1:T(8,128)(2,1)S(1)}, bf16[512,448]{0,1:T(8,128)(2,1)}, u32[]{:S(2)}) copy-start(bf16[512,448]{0,1:T(8,128)(2,1)} %param.7) | copy-start | bytes 1376260
  40.1 1.0 copy-start.8
  40.1 1.3 copy-start.3
  43.6 24.9 %all-to-all-start.4 = ((f32[3,4,64,448]{3,2,0,1:T(8,128)}), f32[3,4,64,448]{3,2,0,1:T(8,128)}, u32[]{:S(2)}, u32[]{:S(2)}) async-start(f32[3,4,64,448]{3,2,0,1:T(8,128)} %copy.143), calls=%async_computation.4 | async-start | bytes 3145728 | tf_op jit(solution)/shard_map/all_to_all | solution.py:25
  58.6 1.2 copy-start.5
  58.6 1.4 copy-start.6
  68.4 46.3 %all-to-all-start.2 = ((f32[3,4,128,448]{2,3,0,1:T(8,128)}), f32[3,4,128,448]{2,3,0,1:T(8,128)}, u32[]{:S(2)}, u32[]{:S(2)}) async-start(f32[3,4,128,448]{2,3,0,1:T(8,128)} %pad_maximum_fusion), calls=%async_computation.2 | async-start | bytes 5505024 | tf_op jit(solution)/shard_map/all_to_all | solution.py:25
  74.7 17.8 %collective-permute-start.8 = (f32[3,16,448]{2,1,0:T(8,128)S(1)}, f32[3,16,448]{2,1,0:T(8,128)S(1)}, u32[]{:S(2)}, u32[]{:S(2)}) collective-permute-start(f32[3,16,448]{2,1,0:T(8,128)S(1)} %get-tuple-element.9), channel_id=1, source_target_pairs={{0,3},{1,0},{2,1},{3,2},{4,7},{5,4},{6,5},{7,6},{8,11},{9,8},{10,9... | collective-permute-start | bytes 258056 | tf_op jit(solution)/shard_map/ppermute | solution.py:43
  84.4 11.4 %collective-permute-start.7 = (f32[3,16,448]{2,1,0:T(8,128)S(1)}, f32[3,16,448]{2,1,0:T(8,128)S(1)}, u32[]{:S(2)}, u32[]{:S(2)}) collective-permute-start(f32[3,16,448]{2,1,0:T(8,128)S(1)} %get-tuple-element.10), channel_id=1, source_target_pairs={{0,2},{1,3},{2,0},{3,1},{4,6},{5,7},{6,4},{7,5},{8,10},{9,11},{10,... | collective-permute-start | bytes 258056 | tf_op jit(solution)/shard_map/ppermute | solution.py:43
  86.4 9.5 %collective-permute-start.6 = (f32[3,16,448]{2,1,0:T(8,128)S(1)}, f32[3,16,448]{2,1,0:T(8,128)S(1)}, u32[]{:S(2)}, u32[]{:S(2)}) collective-permute-start(f32[3,16,448]{2,1,0:T(8,128)S(1)} %get-tuple-element.8), channel_id=1, source_target_pairs={{0,1},{1,2},{2,3},{3,0},{4,5},{5,6},{6,7},{7,4},{8,9},{9,10},{10,1... | collective-permute-start | bytes 258056 | tf_op jit(solution)/shard_map/ppermute | solution.py:43
  95.9 12.5 %collective-permute-start.9 = (bf16[3,16,448]{2,1,0:T(8,128)(2,1)S(1)}, bf16[3,16,448]{2,1,0:T(8,128)(2,1)S(1)}, u32[]{:S(2)}, u32[]{:S(2)}) collective-permute-start(bf16[3,16,448]{2,1,0:T(8,128)(2,1)S(1)} %pad_maximum_fusion.5), channel_id=1, source_target_pairs={{0,3},{1,0},{2,1},{3,2},{4,7},{5,4},{6,5},{7,6},{8,11},{9,8},{10,9... | collective-permute-start | bytes 129032 | tf_op jit(solution)/shard_map/ppermute | solution.py:50
  102.2 9.4 %collective-permute-start.10 = (bf16[3,16,448]{2,1,0:T(8,128)(2,1)S(1)}, bf16[3,16,448]{2,1,0:T(8,128)(2,1)S(1)}, u32[]{:S(2)}, u32[]{:S(2)}) collective-permute-start(bf16[3,16,448]{2,1,0:T(8,128)(2,1)S(1)} %pad_maximum_fusion.5), channel_id=1, source_target_pairs={{0,2},{1,3},{2,0},{3,1},{4,6},{5,7},{6,4},{7,5},{8,10},{9,11},{10,... | collective-permute-start | bytes 129032 | tf_op jit(solution)/shard_map/ppermute | solution.py:50
  104.2 8.1 %collective-permute-start.11 = (bf16[3,16,448]{2,1,0:T(8,128)(2,1)S(1)}, bf16[3,16,448]{2,1,0:T(8,128)(2,1)S(1)}, u32[]{:S(2)}, u32[]{:S(2)}) collective-permute-start(bf16[3,16,448]{2,1,0:T(8,128)(2,1)S(1)} %pad_maximum_fusion.5), channel_id=1, source_target_pairs={{0,1},{1,2},{2,3},{3,0},{4,5},{5,6},{6,7},{7,4},{8,9},{9,10},{10,1... | collective-permute-start | bytes 129032 | tf_op jit(solution)/shard_map/ppermute | solution.py:50
  118.8 12.5 %copy-start.7 = (f32[3,32,448]{1,2,0:T(8,128)S(1)}, f32[3,32,448]{1,2,0:T(8,128)}, u32[]{:S(2)}) copy-start(f32[3,32,448]{1,2,0:T(8,128)} %get-tuple-element.4) | copy-start | bytes 516100
  120.9 22.6 %collective-permute-start.2 = (f32[3,32,448]{2,1,0:T(8,128)}, f32[3,32,448]{2,1,0:T(8,128)}, u32[]{:S(2)}, u32[]{:S(2)}) collective-permute-start(f32[3,32,448]{2,1,0:T(8,128)} %copy.136), channel_id=1, source_target_pairs={{0,3},{1,0},{2,1},{3,2},{4,7},{5,4},{6,5},{7,6},{8,11},{9,8},{10,9... | collective-permute-start | bytes 516104 | tf_op jit(solution)/shard_map/ppermute | solution.py:43
  126.2 17.3 %collective-permute-start.1 = (f32[3,32,448]{2,1,0:T(8,128)}, f32[3,32,448]{2,1,0:T(8,128)}, u32[]{:S(2)}, u32[]{:S(2)}) collective-permute-start(f32[3,32,448]{2,1,0:T(8,128)} %copy.135), channel_id=1, source_target_pairs={{0,2},{1,3},{2,0},{3,1},{4,6},{5,7},{6,4},{7,5},{8,10},{9,11},{10,... | collective-permute-start | bytes 516104 | tf_op jit(solution)/shard_map/ppermute | solution.py:43
  132.3 12.9 %collective-permute-start = (f32[3,32,448]{2,1,0:T(8,128)}, f32[3,32,448]{2,1,0:T(8,128)}, u32[]{:S(2)}, u32[]{:S(2)}) collective-permute-start(f32[3,32,448]{2,1,0:T(8,128)} %copy.134), channel_id=1, source_target_pairs={{0,1},{1,2},{2,3},{3,0},{4,5},{5,6},{6,7},{7,4},{8,9},{9,10},{10,1... | collective-permute-start | bytes 516104 | tf_op jit(solution)/shard_map/ppermute | solution.py:43
  139.1 26.2 %all-to-all-start.5 = ((bf16[3,4,64,448]{3,2,0,1:T(8,128)(2,1)}), bf16[3,4,64,448]{3,2,0,1:T(8,128)(2,1)S(1)}, u32[]{:S(2)}, u32[]{:S(2)}) async-start(bf16[3,4,64,448]{3,2,0,1:T(8,128)(2,1)} %broadcast_in_dim.30), calls=%async_computation.5 | async-start | bytes 1572864 | tf_op jit(solution)/shard_map/all_to_all | solution.py:32
  146.5 10.8 %collective-permute-start.3 = (bf16[3,32,448]{2,1,0:T(8,128)(2,1)S(1)}, bf16[3,32,448]{2,1,0:T(8,128)(2,1)S(1)}, u32[]{:S(2)}, u32[]{:S(2)}) collective-permute-start(bf16[3,32,448]{2,1,0:T(8,128)(2,1)S(1)} %pad_maximum_fusion.3), channel_id=1, source_target_pairs={{0,3},{1,0},{2,1},{3,2},{4,7},{5,4},{6,5},{7,6},{8,11},{9,8},{10,9... | collective-permute-start | bytes 258056 | tf_op jit(solution)/shard_map/ppermute | solution.py:50
  149.6 9.4 %collective-permute-start.4 = (bf16[3,32,448]{2,1,0:T(8,128)(2,1)S(1)}, bf16[3,32,448]{2,1,0:T(8,128)(2,1)S(1)}, u32[]{:S(2)}, u32[]{:S(2)}) collective-permute-start(bf16[3,32,448]{2,1,0:T(8,128)(2,1)S(1)} %pad_maximum_fusion.3), channel_id=1, source_target_pairs={{0,2},{1,3},{2,0},{3,1},{4,6},{5,7},{6,4},{7,5},{8,10},{9,11},{10,... | collective-permute-start | bytes 258056 | tf_op jit(solution)/shard_map/ppermute | solution.py:50
  155.3 9.6 %collective-permute-start.5 = (bf16[3,32,448]{2,1,0:T(8,128)(2,1)S(1)}, bf16[3,32,448]{2,1,0:T(8,128)(2,1)S(1)}, u32[]{:S(2)}, u32[]{:S(2)}) collective-permute-start(bf16[3,32,448]{2,1,0:T(8,128)(2,1)S(1)} %pad_maximum_fusion.3), channel_id=1, source_target_pairs={{0,1},{1,2},{2,3},{3,0},{4,5},{5,6},{6,7},{7,4},{8,9},{9,10},{10,1... | collective-permute-start | bytes 258056 | tf_op jit(solution)/shard_map/ppermute | solution.py:50
  166.6 20.7 %all-to-all-start.3 = ((bf16[3,4,128,448]{2,3,0,1:T(8,128)(2,1)}), bf16[3,4,128,448]{2,3,0,1:T(8,128)(2,1)}, u32[]{:S(2)}, u32[]{:S(2)}) async-start(bf16[3,4,128,448]{2,3,0,1:T(8,128)(2,1)} %broadcast_in_dim.28), calls=%async_computation.3 | async-start | bytes 2752512 | tf_op jit(solution)/shard_map/all_to_all | solution.py:32
  187.3 1.6 copy-start.1
  188.9 1.0 copy-start.4
  201.9 29.3 %all-to-all-start.7 = ((f32[16,24,512]{2,1,0:T(8,128)}), f32[16,24,512]{2,1,0:T(8,128)}, u32[]{:S(2)}, u32[]{:S(2)}) async-start(f32[16,24,512]{2,1,0:T(8,128)} %reduce_sum.38), calls=%async_computation.7 | async-start | bytes 1572864 | tf_op jit(solution)/shard_map/all_to_all | solution.py:25
  209.6 2.3 copy-start.2

commit v11 on v6

--- a/solution.py
+++ b/solution.py
@@ -76,7 +76,10 @@
         )
         p = jnp.stack([gate_part, up_part, hidden_part])
         p = scatter_sum(p, "x", nx, 1)
-        p = scatter_permute(p, "zh", nzh, 1)
+        if c == 0:
+            p = scatter_permute(p, "zh", nzh, 1)
+        else:
+            p = scatter_sum(p, "zh", nzh, 1)
         d = jnp.stack(swiglu_grads(p[0], p[1], p[2]))
         d = gather_permute(d, "zh", nzh, 1)
         chunks.append(gather_a2a(d, "x", nx, 1))

time: 228 us -> 231 us (1.013)
  waiting for transfers between devices: 65 us -> 76.6 us
  blocking collectives: 51.6 us -> 46.6 us
  starting transfers between devices: 75.9 us -> 71.8 us
    ppermute x6 -> x3, starting transfers between devices: 29.5 us -> 17.1 us  [scatter_permute(): lax.ppermute(part, axis_name, [(j, (j + k) % n) for j in range(n)])]
    all_to_all x3 -> x4, starting transfers between devices: 12.6 us -> 21.4 us  [scatter_sum(): v = lax.all_to_all(v, axis_name, dim, dim, tiled=True)]
    ppermute x6, waiting for transfers between devices: 5.53 us -> 14.2 us  [gather_permute(): lax.ppermute(v, axis_name, [(j, (j + k) % n) for j in range(n)])]
    all_to_all x1, blocking collectives: 13.3 us -> 8.27 us  [scatter_sum(): v = lax.all_to_all(v, axis_name, dim, dim, tiled=True)]
    all_to_all x2, waiting for transfers between devices: 10.4 us -> 14.6 us  [gather_a2a(): v = lax.all_to_all(v, axis_name, dim, dim, tiled=True)]
    reduce_sum x4 -> x5, other arithmetic: 8.25 us -> 8.31 us  [scatter_sum(): return v.sum(dim)]
    all_to_all x3 -> x4, waiting for transfers between devices: 47.7 us -> 47.7 us  [scatter_sum(): v = lax.all_to_all(v, axis_name, dim, dim, tiled=True)]
  transfers between devices with their start and end apart: 17 -> 15, of which waited for: 7 -> 8; matrix products, arithmetic and copies ran while one was open for 8% -> 8% of each run, Pallas kernels for 0% -> 0%
where the time goes in v11:
time: 231 us; the launch traced here: 229 us
  waiting for transfers between devices  76.6 us (33%)
  starting transfers between devices  71.8 us (31%)
  blocking collectives  46.6 us (20%)
  local copies, waits for them, and re-layouts  12.4 us (5%)
  other arithmetic  11.6 us (5%)
  matrix products  8.71 us (4%)
    all_to_all x4, waiting for transfers between devices, scatter_sum(): v = lax.all_to_all(v, axis_name, dim, dim, tiled=True)  47.7 us
    all_to_all x2, blocking collectives, gather_a2a(): v = lax.all_to_all(v, axis_name, dim, dim, tiled=True)  38.3 us
    ppermute x6, starting transfers between devices, gather_permute(): lax.ppermute(v, axis_name, [(j, (j + k) % n) for j in range(n)])  25.5 us
    all_to_all x4, starting transfers between devices, scatter_sum(): v = lax.all_to_all(v, axis_name, dim, dim, tiled=True)  21.4 us
    ppermute x3, starting transfers between devices, scatter_permute(): lax.ppermute(part, axis_name, [(j, (j + k) % n) for j in range(n)])  17.1 us
    all_to_all x2, waiting for transfers between devices, gather_a2a(): v = lax.all_to_all(v, axis_name, dim, dim, tiled=True)  14.6 us
    ppermute x6, waiting for transfers between devices, gather_permute(): lax.ppermute(v, axis_name, [(j, (j + k) % n) for j in range(n)])  14.2 us
    reduce_sum x5, other arithmetic, scatter_sum(): return v.sum(dim)  8.31 us
  transfers between devices with their start and end apart: 15, of which 8 were waited for; matrix products, arithmetic and copies ran while one was open for 8% of the time, Pallas kernels for 0%

profile of v11, /device:TPU:1, one launch (start us, length us, event | category | flops | bytes accessed | tf_op | source)
XLA Modules:
  0.0 228.7 jit_solution(1012276916446110095)
XLA Ops:
  0.6 0.8 pad_maximum_fusion.5
  1.5 31.3 %all_to_all.45 = bf16[16,24,1024]{2,1,0:T(8,128)(2,1)S(1)} all-to-all(bf16[16,24,1024]{2,1,0:T(8,128)(2,1)S(1)} %broadcast_in_dim.12), channel_id=1, replica_groups=mesh['y'=8,'zl'=2,'c'=2,'x'=4,'zh'=4] {'y','zl'}, dimensions={0} | all-to-all | bytes 1572864 | tf_op jit(solution)/shard_map/all_to_all | solution.py:32
  33.1 7.0 %all_to_all.46 = bf16[16,2,1,24,1024]{4,3,2,0,1:T(8,128)(2,1)S(1)} all-to-all(bf16[16,2,1,24,1024]{4,3,2,0,1:T(8,128)(2,1)S(1)} %broadcast_in_dim.26), channel_id=1, replica_groups=mesh['y'=8,'zl'=2,'c'=2,'x'=4,'zh'=4] {'c'}, dimensions={1} | all-to-all | bytes 3145728 | tf_op jit(solution)/shard_map/all_to_all | solution.py:32
  40.2 0.8 copy-done.3
  42.6 1.6 copy.53
  44.3 4.5 %all-to-all-start.2 = ((f32[3,4,96,448]{3,2,0,1:T(8,128)}), f32[3,4,96,448]{3,2,0,1:T(8,128)}, u32[]{:S(2)}, u32[]{:S(2)}) async-start(f32[3,4,96,448]{3,2,0,1:T(8,128)} %copy.53), calls=%async_computation.2 | async-start | bytes 4718592 | tf_op jit(solution)/shard_map/all_to_all | solution.py:25
  49.2 0.4 fusion.10
  50.2 1.6 copy.61
  51.8 25.9 %all-to-all-done.2 = f32[3,4,96,448]{3,2,0,1:T(8,128)} async-done(((f32[3,4,96,448]{3,2,0,1:T(8,128)}), f32[3,4,96,448]{3,2,0,1:T(8,128)}, u32[]{:S(2)}, u32[]{:S(2)}) %all-to-all-start.2) | async-done | bytes 2064416 | tf_op jit(solution)/shard_map/all_to_all | solution.py:25
  77.7 3.6 %all-to-all-start.4 = ((f32[3,4,96,448]{3,2,0,1:T(8,128)}), f32[3,4,96,448]{3,2,0,1:T(8,128)S(1)}, u32[]{:S(2)}, u32[]{:S(2)}) async-start(f32[3,4,96,448]{3,2,0,1:T(8,128)} %copy.61), calls=%async_computation.4 | async-start | bytes 4718592 | tf_op jit(solution)/shard_map/all_to_all | solution.py:25
  81.4 2.8 %reduce_sum.45 = f32[3,96,448]{2,1,0:T(8,128)} reduce(f32[3,4,96,448]{3,2,0,1:T(8,128)} %all-to-all-done.2, f32[]{:T(128)} %constant.46.clone.1), dimensions={1}, to_apply=%region_0.0 | reduce | flops 387072 | bytes 2580484 | tf_op jit(solution)/shard_map/reduce_sum | solution.py:26
  84.2 1.8 constant_dynamic-slice_fusion.2
  86.1 5.8 %collective-permute-start = (f32[3,24,448]{2,1,0:T(8,128)}, f32[3,24,448]{2,1,0:T(8,128)S(1)}, u32[]{:S(2)}, u32[]{:S(2)}) collective-permute-start(f32[3,24,448]{2,1,0:T(8,128)} %get-tuple-element.5), channel_id=1, source_target_pairs={{0,1},{1,2},{2,3},{3,0},{4,5},{5,6},{6,7},{7,4},{8,9},{9,10},{10,1... | collective-permute-start | bytes 387080 | tf_op jit(solution)/shard_map/ppermute | solution.py:43
  91.9 5.9 %collective-permute-start.2 = (f32[3,24,448]{2,1,0:T(8,128)}, f32[3,24,448]{2,1,0:T(8,128)}, u32[]{:S(2)}, u32[]{:S(2)}) collective-permute-start(f32[3,24,448]{2,1,0:T(8,128)} %get-tuple-element.6), channel_id=1, source_target_pairs={{0,3},{1,0},{2,1},{3,2},{4,7},{5,4},{6,5},{7,6},{8,11},{9,8},{10,9... | collective-permute-start | bytes 387080 | tf_op jit(solution)/shard_map/ppermute | solution.py:43
  97.7 5.5 %collective-permute-start.1 = (f32[3,24,448]{2,1,0:T(8,128)}, f32[3,24,448]{2,1,0:T(8,128)}, u32[]{:S(2)}, u32[]{:S(2)}) collective-permute-start(f32[3,24,448]{2,1,0:T(8,128)} %get-tuple-element.7), channel_id=1, source_target_pairs={{0,2},{1,3},{2,0},{3,1},{4,6},{5,7},{6,4},{7,5},{8,10},{9,11},{10,... | collective-permute-start | bytes 387080 | tf_op jit(solution)/shard_map/ppermute | solution.py:43
  103.2 6.2 %all-to-all-done.4 = f32[3,4,96,448]{3,2,0,1:T(8,128)S(1)} async-done(((f32[3,4,96,448]{3,2,0,1:T(8,128)}), f32[3,4,96,448]{3,2,0,1:T(8,128)S(1)}, u32[]{:S(2)}, u32[]{:S(2)}) %all-to-all-start.4) | async-done | bytes 2064416 | tf_op jit(solution)/shard_map/all_to_all | solution.py:25
  109.4 1.1 reduce_sum.46
  110.5 1.9 copy.62
  112.5 9.0 %all-to-all-start.5 = ((f32[3,4,24,448]{3,2,0,1:T(8,128)}), f32[3,4,24,448]{3,2,0,1:T(8,128)S(1)}, u32[]{:S(2)}, u32[]{:S(2)}) async-start(f32[3,4,24,448]{3,2,0,1:T(8,128)} %copy.62), calls=%async_computation.5 | async-start | bytes 1179648 | tf_op jit(solution)/shard_map/all_to_all | solution.py:25
  121.5 1.1 add_add_fusion
  122.7 7.3 %collective-permute-start.4 = (bf16[3,24,448]{2,1,0:T(8,128)(2,1)S(1)}, bf16[3,24,448]{2,1,0:T(8,128)(2,1)S(1)}, u32[]{:S(2)}, u32[]{:S(2)}) collective-permute-start(bf16[3,24,448]{2,1,0:T(8,128)(2,1)S(1)} %get-tuple-element.16), channel_id=1, source_target_pairs={{0,2},{1,3},{2,0},{3,1},{4,6},{5,7},{6,4},{7,5},{8,10},{9,11},{10,... | collective-permute-start | bytes 193544 | tf_op jit(solution)/shard_map/ppermute | solution.py:50
  130.0 2.2 collective-permute-start.3
  132.2 4.0 %collective-permute-start.5 = (bf16[3,24,448]{2,1,0:T(8,128)(2,1)S(1)}, bf16[3,24,448]{2,1,0:T(8,128)(2,1)S(1)}, u32[]{:S(2)}, u32[]{:S(2)}) collective-permute-start(bf16[3,24,448]{2,1,0:T(8,128)(2,1)S(1)} %get-tuple-element.16), channel_id=1, source_target_pairs={{0,1},{1,2},{2,3},{3,0},{4,5},{5,6},{6,7},{7,4},{8,9},{9,10},{10,1... | collective-permute-start | bytes 193544 | tf_op jit(solution)/shard_map/ppermute | solution.py:50
  136.2 0.9 collective-permute-done.4
  137.1 7.1 %collective-permute-done.3 = bf16[3,24,448]{2,1,0:T(8,128)(2,1)S(1)} collective-permute-done((bf16[3,24,448]{2,1,0:T(8,128)(2,1)S(1)}, bf16[3,24,448]{2,1,0:T(8,128)(2,1)S(1)}, u32[]{:S(2)}, u32[]{:S(2)}) %collective-permute-start.3) | collective-permute-done | bytes 64544 | tf_op jit(solution)/shard_map/ppermute | solution.py:50
  144.2 0.4 fusion.33
  144.6 1.1 broadcast_in_dim.28
  145.7 3.5 %all-to-all-start.3 = ((bf16[3,4,96,448]{3,2,0,1:T(8,128)(2,1)}), bf16[3,4,96,448]{3,2,0,1:T(8,128)(2,1)S(1)}, u32[]{:S(2)}, u32[]{:S(2)}) async-start(bf16[3,4,96,448]{3,2,0,1:T(8,128)(2,1)} %broadcast_in_dim.28), calls=%async_computation.3 | async-start | bytes 2359296 | tf_op jit(solution)/shard_map/all_to_all | solution.py:32
  149.3 4.9 %collective-permute-start.7 = (bf16[3,24,448]{2,1,0:T(8,128)(2,1)S(1)}, bf16[3,24,448]{2,1,0:T(8,128)(2,1)S(1)}, u32[]{:S(2)}, u32[]{:S(2)}) collective-permute-start(bf16[3,24,448]{2,1,0:T(8,128)(2,1)S(1)} %get-tuple-element.14), channel_id=1, source_target_pairs={{0,2},{1,3},{2,0},{3,1},{4,6},{5,7},{6,4},{7,5},{8,10},{9,11},{10,... | collective-permute-start | bytes 193544 | tf_op jit(solution)/shard_map/ppermute | solution.py:50
  154.2 5.2 %collective-permute-start.6 = (bf16[3,24,448]{2,1,0:T(8,128)(2,1)S(1)}, bf16[3,24,448]{2,1,0:T(8,128)(2,1)S(1)}, u32[]{:S(2)}, u32[]{:S(2)}) collective-permute-start(bf16[3,24,448]{2,1,0:T(8,128)(2,1)S(1)} %get-tuple-element.14), channel_id=1, source_target_pairs={{0,3},{1,0},{2,1},{3,2},{4,7},{5,4},{6,5},{7,6},{8,11},{9,8},{10,9... | collective-permute-start | bytes 193544 | tf_op jit(solution)/shard_map/ppermute | solution.py:50
  159.5 1.9 collective-permute-start.8
  161.4 2.1 collective-permute-done.6
  163.5 4.2 %collective-permute-done.8 = bf16[3,24,448]{2,1,0:T(8,128)(2,1)S(1)} collective-permute-done((bf16[3,24,448]{2,1,0:T(8,128)(2,1)S(1)}, bf16[3,24,448]{2,1,0:T(8,128)(2,1)S(1)}, u32[]{:S(2)}, u32[]{:S(2)}) %collective-permute-start.8) | collective-permute-done | bytes 64544 | tf_op jit(solution)/shard_map/ppermute | solution.py:50
  167.7 0.4 fusion.26
  168.1 1.1 broadcast_in_dim.30
  169.2 4.3 %all-to-all-start.6 = ((bf16[3,4,96,448]{3,2,0,1:T(8,128)(2,1)}), bf16[3,4,96,448]{3,2,0,1:T(8,128)(2,1)}, u32[]{:S(2)}, u32[]{:S(2)}) async-start(bf16[3,4,96,448]{3,2,0,1:T(8,128)(2,1)} %broadcast_in_dim.30), calls=%async_computation.6 | async-start | bytes 2359296 | tf_op jit(solution)/shard_map/all_to_all | solution.py:32
  173.6 14.6 %all-to-all-done.6 = bf16[3,4,96,448]{3,2,0,1:T(8,128)(2,1)} async-done(((bf16[3,4,96,448]{3,2,0,1:T(8,128)(2,1)}), bf16[3,4,96,448]{3,2,0,1:T(8,128)(2,1)}, u32[]{:S(2)}, u32[]{:S(2)}) %all-to-all-start.6) | async-done | bytes 1032224 | tf_op jit(solution)/shard_map/all_to_all | solution.py:32
  188.2 1.4 copy.64
  189.6 0.6 fusion.43
  190.2 0.6 convolution_add_fusion
  190.9 8.3 %all_to_all.47 = f32[16,2,1,24,512]{4,3,0,2,1:T(8,128)} all-to-all(f32[16,2,1,24,512]{4,3,0,2,1:T(8,128)S(1)} %copy.65), channel_id=1, replica_groups=mesh['y'=8,'zl'=2,'c'=2,'x'=4,'zh'=4] {'c'}, dimensions={1} | all-to-all | bytes 3145728 | tf_op jit(solution)/shard_map/all_to_all | solution.py:25
  199.2 2.5 %reduce_sum.48 = f32[16,24,512]{2,1,0:T(8,128)} reduce(f32[16,2,1,24,512]{4,3,0,2,1:T(8,128)} %all_to_all.47, f32[]{:T(128)} %constant.46.clone.1), dimensions={1,2}, to_apply=%region_3.5 | reduce | flops 196608 | bytes 2359300 | tf_op jit(solution)/shard_map/reduce_sum | solution.py:26
  201.7 4.3 %all-to-all-start.8 = ((f32[16,24,512]{2,1,0:T(8,128)}), f32[16,24,512]{2,1,0:T(8,128)}, u32[]{:S(2)}, u32[]{:S(2)}) async-start(f32[16,24,512]{2,1,0:T(8,128)} %reduce_sum.48), calls=%async_computation.8 | async-start | bytes 1572864 | tf_op jit(solution)/shard_map/all_to_all | solution.py:25
  206.0 2.6 %convolution_convert_fusion.1 = bf16[512,448]{0,1:T(8,128)(2,1)} fusion(bf16[768,1024]{1,0:T(8,128)(2,1)} %bitcast.68, bf16[3,384,448]{2,1,0:T(8,128)(2,1)S(1)} %bitcast.54, bf16[3,384,448]{2,1,0:T(8,128)(2,1)S(1)} %bitcast.59), kind=kOutput, calls=%fused_computation.8 | convolution fusion | flops 353927168 | bytes 3309568 | tf_op jit(solution)/shard_map/dot_general | solution.py:94
  208.6 1.3 convolution_convert_fusion.2
  209.9 1.3 convolution_convert_fusion
  211.3 15.6 %all-to-all-done.8 = f32[16,24,512]{2,1,0:T(8,128)} async-done(((f32[16,24,512]{2,1,0:T(8,128)}), f32[16,24,512]{2,1,0:T(8,128)}, u32[]{:S(2)}, u32[]{:S(2)}) %all-to-all-start.8) | async-done | bytes 786464 | tf_op jit(solution)/shard_map/all_to_all | solution.py:25
  226.9 1.8 reduce_sum.49
  (34 shorter events, 3.4 us)
Async XLA Ops:
  0.6 41.4 %copy-start = (bf16[512,448]{0,1:T(8,128)(2,1)S(1)}, bf16[512,448]{0,1:T(8,128)(2,1)}, u32[]{:S(2)}) copy-start(bf16[512,448]{0,1:T(8,128)(2,1)} %param.9) | copy-start | bytes 1376260
  40.1 1.0 copy-start.3
  40.2 9.4 %copy-start.1 = (bf16[16,2,1,24,1024]{4,3,1,0,2:T(8,128)(2,1)}, bf16[16,2,1,24,1024]{4,3,1,0,2:T(8,128)(2,1)S(1)}, u32[]{:S(2)}) copy-start(bf16[16,2,1,24,1024]{4,3,1,0,2:T(8,128)(2,1)S(1)} %copy.49) | copy-start | bytes 4718596
  40.2 1.4 copy-start.4
  44.3 33.5 %all-to-all-start.2 = ((f32[3,4,96,448]{3,2,0,1:T(8,128)}), f32[3,4,96,448]{3,2,0,1:T(8,128)}, u32[]{:S(2)}, u32[]{:S(2)}) async-start(f32[3,4,96,448]{3,2,0,1:T(8,128)} %copy.53), calls=%async_computation.2 | async-start | bytes 4718592 | tf_op jit(solution)/shard_map/all_to_all | solution.py:25
  77.7 31.7 %all-to-all-start.4 = ((f32[3,4,96,448]{3,2,0,1:T(8,128)}), f32[3,4,96,448]{3,2,0,1:T(8,128)S(1)}, u32[]{:S(2)}, u32[]{:S(2)}) async-start(f32[3,4,96,448]{3,2,0,1:T(8,128)} %copy.61), calls=%async_computation.4 | async-start | bytes 4718592 | tf_op jit(solution)/shard_map/all_to_all | solution.py:25
  86.1 35.4 %collective-permute-start = (f32[3,24,448]{2,1,0:T(8,128)}, f32[3,24,448]{2,1,0:T(8,128)S(1)}, u32[]{:S(2)}, u32[]{:S(2)}) collective-permute-start(f32[3,24,448]{2,1,0:T(8,128)} %get-tuple-element.5), channel_id=1, source_target_pairs={{0,1},{1,2},{2,3},{3,0},{4,5},{5,6},{6,7},{7,4},{8,9},{9,10},{10,1... | collective-permute-start | bytes 387080 | tf_op jit(solution)/shard_map/ppermute | solution.py:43
  91.9 29.6 %collective-permute-start.2 = (f32[3,24,448]{2,1,0:T(8,128)}, f32[3,24,448]{2,1,0:T(8,128)}, u32[]{:S(2)}, u32[]{:S(2)}) collective-permute-start(f32[3,24,448]{2,1,0:T(8,128)} %get-tuple-element.6), channel_id=1, source_target_pairs={{0,3},{1,0},{2,1},{3,2},{4,7},{5,4},{6,5},{7,6},{8,11},{9,8},{10,9... | collective-permute-start | bytes 387080 | tf_op jit(solution)/shard_map/ppermute | solution.py:43
  97.7 23.8 %collective-permute-start.1 = (f32[3,24,448]{2,1,0:T(8,128)}, f32[3,24,448]{2,1,0:T(8,128)}, u32[]{:S(2)}, u32[]{:S(2)}) collective-permute-start(f32[3,24,448]{2,1,0:T(8,128)} %get-tuple-element.7), channel_id=1, source_target_pairs={{0,2},{1,3},{2,0},{3,1},{4,6},{5,7},{6,4},{7,5},{8,10},{9,11},{10,... | collective-permute-start | bytes 387080 | tf_op jit(solution)/shard_map/ppermute | solution.py:43
  112.5 32.1 %all-to-all-start.5 = ((f32[3,4,24,448]{3,2,0,1:T(8,128)}), f32[3,4,24,448]{3,2,0,1:T(8,128)S(1)}, u32[]{:S(2)}, u32[]{:S(2)}) async-start(f32[3,4,24,448]{3,2,0,1:T(8,128)} %copy.62), calls=%async_computation.5 | async-start | bytes 1179648 | tf_op jit(solution)/shard_map/all_to_all | solution.py:25
  122.7 14.4 %collective-permute-start.4 = (bf16[3,24,448]{2,1,0:T(8,128)(2,1)S(1)}, bf16[3,24,448]{2,1,0:T(8,128)(2,1)S(1)}, u32[]{:S(2)}, u32[]{:S(2)}) collective-permute-start(bf16[3,24,448]{2,1,0:T(8,128)(2,1)S(1)} %get-tuple-element.16), channel_id=1, source_target_pairs={{0,2},{1,3},{2,0},{3,1},{4,6},{5,7},{6,4},{7,5},{8,10},{9,11},{10,... | collective-permute-start | bytes 193544 | tf_op jit(solution)/shard_map/ppermute | solution.py:50
  130.0 14.2 %collective-permute-start.3 = (bf16[3,24,448]{2,1,0:T(8,128)(2,1)S(1)}, bf16[3,24,448]{2,1,0:T(8,128)(2,1)S(1)}, u32[]{:S(2)}, u32[]{:S(2)}) collective-permute-start(bf16[3,24,448]{2,1,0:T(8,128)(2,1)S(1)} %get-tuple-element.16), channel_id=1, source_target_pairs={{0,3},{1,0},{2,1},{3,2},{4,7},{5,4},{6,5},{7,6},{8,11},{9,8},{10,9... | collective-permute-start | bytes 193544 | tf_op jit(solution)/shard_map/ppermute | solution.py:50
  132.2 12.0 %collective-permute-start.5 = (bf16[3,24,448]{2,1,0:T(8,128)(2,1)S(1)}, bf16[3,24,448]{2,1,0:T(8,128)(2,1)S(1)}, u32[]{:S(2)}, u32[]{:S(2)}) collective-permute-start(bf16[3,24,448]{2,1,0:T(8,128)(2,1)S(1)} %get-tuple-element.16), channel_id=1, source_target_pairs={{0,1},{1,2},{2,3},{3,0},{4,5},{5,6},{6,7},{7,4},{8,9},{9,10},{10,1... | collective-permute-start | bytes 193544 | tf_op jit(solution)/shard_map/ppermute | solution.py:50
  145.7 22.4 %all-to-all-start.3 = ((bf16[3,4,96,448]{3,2,0,1:T(8,128)(2,1)}), bf16[3,4,96,448]{3,2,0,1:T(8,128)(2,1)S(1)}, u32[]{:S(2)}, u32[]{:S(2)}) async-start(bf16[3,4,96,448]{3,2,0,1:T(8,128)(2,1)} %broadcast_in_dim.28), calls=%async_computation.3 | async-start | bytes 2359296 | tf_op jit(solution)/shard_map/all_to_all | solution.py:32
  149.3 12.0 %collective-permute-start.7 = (bf16[3,24,448]{2,1,0:T(8,128)(2,1)S(1)}, bf16[3,24,448]{2,1,0:T(8,128)(2,1)S(1)}, u32[]{:S(2)}, u32[]{:S(2)}) collective-permute-start(bf16[3,24,448]{2,1,0:T(8,128)(2,1)S(1)} %get-tuple-element.14), channel_id=1, source_target_pairs={{0,2},{1,3},{2,0},{3,1},{4,6},{5,7},{6,4},{7,5},{8,10},{9,11},{10,... | collective-permute-start | bytes 193544 | tf_op jit(solution)/shard_map/ppermute | solution.py:50
  154.2 9.2 %collective-permute-start.6 = (bf16[3,24,448]{2,1,0:T(8,128)(2,1)S(1)}, bf16[3,24,448]{2,1,0:T(8,128)(2,1)S(1)}, u32[]{:S(2)}, u32[]{:S(2)}) collective-permute-start(bf16[3,24,448]{2,1,0:T(8,128)(2,1)S(1)} %get-tuple-element.14), channel_id=1, source_target_pairs={{0,3},{1,0},{2,1},{3,2},{4,7},{5,4},{6,5},{7,6},{8,11},{9,8},{10,9... | collective-permute-start | bytes 193544 | tf_op jit(solution)/shard_map/ppermute | solution.py:50
  159.5 8.2 %collective-permute-start.8 = (bf16[3,24,448]{2,1,0:T(8,128)(2,1)S(1)}, bf16[3,24,448]{2,1,0:T(8,128)(2,1)S(1)}, u32[]{:S(2)}, u32[]{:S(2)}) collective-permute-start(bf16[3,24,448]{2,1,0:T(8,128)(2,1)S(1)} %get-tuple-element.14), channel_id=1, source_target_pairs={{0,1},{1,2},{2,3},{3,0},{4,5},{5,6},{6,7},{7,4},{8,9},{9,10},{10,1... | collective-permute-start | bytes 193544 | tf_op jit(solution)/shard_map/ppermute | solution.py:50
  169.2 19.0 %all-to-all-start.6 = ((bf16[3,4,96,448]{3,2,0,1:T(8,128)(2,1)}), bf16[3,4,96,448]{3,2,0,1:T(8,128)(2,1)}, u32[]{:S(2)}, u32[]{:S(2)}) async-start(bf16[3,4,96,448]{3,2,0,1:T(8,128)(2,1)} %broadcast_in_dim.30), calls=%async_computation.6 | async-start | bytes 2359296 | tf_op jit(solution)/shard_map/all_to_all | solution.py:32
  201.7 25.2 %all-to-all-start.8 = ((f32[16,24,512]{2,1,0:T(8,128)}), f32[16,24,512]{2,1,0:T(8,128)}, u32[]{:S(2)}, u32[]{:S(2)}) async-start(f32[16,24,512]{2,1,0:T(8,128)} %reduce_sum.48), calls=%async_computation.8 | async-start | bytes 1572864 | tf_op jit(solution)/shard_map/all_to_all | solution.py:25
  206.0 2.6 %copy-start.2 = (bf16[16,2,1,24,1024]{4,3,1,0,2:T(8,128)(2,1)S(1)}, bf16[16,2,1,24,1024]{4,3,1,0,2:T(8,128)(2,1)}, u32[]{:S(2)}) copy-start(bf16[16,2,1,24,1024]{4,3,1,0,2:T(8,128)(2,1)} %copy-done.1) | copy-start | bytes 4718596

commit v12 on v6

--- a/solution.py
+++ b/solution.py
@@ -60,15 +60,13 @@
     contract_last = (((1,), (1,)), ((), ()))
     contract_first = (((0,), (0,)), ((), ()))
     both = jnp.concatenate([tokens, out_grad], 1)
-    both = gather_a2a(both, ("y", "zl"), nsec // 2, 0)
-    both = both.reshape((nsec // 2, 1, -1) + both.shape[1:])
-    both = gather_a2a(both, "c", 2, 1).reshape((-1,) + both.shape[3:])
-    all_tokens, all_grads = both[:, : tokens.shape[1]], both[:, tokens.shape[1] :]
-    rows = all_tokens.shape[0] // 2
+    mine = gather_a2a(both, ("y", "zl"), nsec // 2, 0)
+    swap = [(0, 1), (1, 0)]
+    parts_in = [mine, lax.ppermute(mine, "c", swap)]
+    width = tokens.shape[1]
     chunks = []
-    for c in range(2):
-        tok = all_tokens[c * rows : (c + 1) * rows]
-        grd = all_grads[c * rows : (c + 1) * rows]
+    for rows in parts_in:
+        tok, grd = rows[:, :width], rows[:, width:]
         gate_part = jnp.dot(tok, gate_weight, preferred_element_type=jnp.float32)
         up_part = jnp.dot(tok, up_weight, preferred_element_type=jnp.float32)
         hidden_part = lax.dot_general(
@@ -81,6 +79,8 @@
         d = gather_permute(d, "zh", nzh, 1)
         chunks.append(gather_a2a(d, "x", nx, 1))
     deltas = jnp.concatenate(chunks, 1)
+    both = jnp.concatenate(parts_in, 0)
+    all_tokens, all_grads = both[:, :width], both[:, width:]
     hidden, gate_delta, up_delta = deltas[0], deltas[1], deltas[2]
     grad_down = lax.dot_general(
         hidden, all_grads, contract_first, preferred_element_type=jnp.float32
@@ -94,8 +94,8 @@
     result = lax.dot_general(
         gate_delta, gate_weight, contract_last, preferred_element_type=jnp.float32
     ) + lax.dot_general(up_delta, up_weight, contract_last, preferred_element_type=jnp.float32)
-    result = result.reshape((nsec // 2, 2, -1) + result.shape[1:])
-    result = scatter_sum(result, "c", 2, 1).reshape((-1,) + result.shape[3:])
+    half = result.shape[0] // 2
+    result = result[:half] + lax.ppermute(result[half:], "c", swap)
     grad_input = scatter_sum(result, ("y", "zl"), nsec // 2, 0).astype(jnp.bfloat16)
     return (grad_input, grad_gate, grad_up, grad_down)
 

time: 228 us -> 222 us (0.974)
  blocking collectives: 51.6 us -> 31.5 us
  starting transfers between devices: 75.9 us -> 90.5 us
    all_to_all x1 -> x0, blocking collectives: 13.3 us -> none  [scatter_sum(): v = lax.all_to_all(v, axis_name, dim, dim, tiled=True)]
    ppermute x0 -> x2, starting transfers between devices: none -> 13.3 us  [the longest x1 9.07 us: local(): result = result[:half] + lax.ppermute(result[half:], 'c', swap)]
    ppermute x6, waiting for transfers between devices: 1.36 us -> 8.39 us  [scatter_permute(): lax.ppermute(part, axis_name, [(j, (j + k) % n) for j in range(n)])]
    all_to_all x2 -> x1, blocking collectives: 38.3 us -> 31.5 us  [gather_a2a(): v = lax.all_to_all(v, axis_name, dim, dim, tiled=True)]
    all_to_all x3, waiting for transfers between devices: 47.7 us -> 42.3 us  [scatter_sum(): v = lax.all_to_all(v, axis_name, dim, dim, tiled=True)]
    all_to_all x3, starting transfers between devices: 12.6 us -> 17 us  [scatter_sum(): v = lax.all_to_all(v, axis_name, dim, dim, tiled=True)]
    ppermute x6, starting transfers between devices: 29.5 us -> 26.4 us  [scatter_permute(): lax.ppermute(part, axis_name, [(j, (j + k) % n) for j in range(n)])]
    reduce_sum x4 -> x3, other arithmetic: 8.25 us -> 5.75 us  [scatter_sum(): return v.sum(dim)]
  transfers between devices with their start and end apart: 17 -> 19, of which waited for: 7 -> 9; matrix products, arithmetic and copies ran while one was open for 8% -> 11% of each run, Pallas kernels for 0% -> 0%
where the time goes in v12:
time: 222 us; the launch traced here: 220 us
  starting transfers between devices  90.5 us (41%)
  waiting for transfers between devices  66.2 us (30%)
  blocking collectives  31.5 us (14%)
  other arithmetic  12 us (5%)
  local copies, waits for them, and re-layouts  10.3 us (5%)
  matrix products  8.7 us (4%)
    all_to_all x3, waiting for transfers between devices, scatter_sum(): v = lax.all_to_all(v, axis_name, dim, dim, tiled=True)  42.3 us
    all_to_all x1, blocking collectives, gather_a2a(): v = lax.all_to_all(v, axis_name, dim, dim, tiled=True)  31.5 us
    ppermute x6, starting transfers between devices, scatter_permute(): lax.ppermute(part, axis_name, [(j, (j + k) % n) for j in range(n)])  26.4 us
    ppermute x6, starting transfers between devices, gather_permute(): lax.ppermute(v, axis_name, [(j, (j + k) % n) for j in range(n)])  25.9 us
    all_to_all x3, starting transfers between devices, scatter_sum(): v = lax.all_to_all(v, axis_name, dim, dim, tiled=True)  17 us
    all_to_all x2, waiting for transfers between devices, gather_a2a(): v = lax.all_to_all(v, axis_name, dim, dim, tiled=True)  10.4 us
    ppermute x1, starting transfers between devices, local(): result = result[:half] + lax.ppermute(result[half:], 'c', swap)  9.07 us
    ppermute x6, waiting for transfers between devices, scatter_permute(): lax.ppermute(part, axis_name, [(j, (j + k) % n) for j in range(n)])  8.39 us
  transfers between devices with their start and end apart: 19, of which 9 were waited for; matrix products, arithmetic and copies ran while one was open for 11% of the time, Pallas kernels for 0%

profile of v12, /device:TPU:1, one launch (start us, length us, event | category | flops | bytes accessed | tf_op | source)
XLA Modules:
  0.0 220.2 jit_solution(9879473696155994555)
XLA Ops:
  0.7 0.8 pad_maximum_fusion.7
  1.6 31.5 %all_to_all.30 = bf16[16,24,1024]{2,1,0:T(8,128)(2,1)S(1)} all-to-all(bf16[16,24,1024]{2,1,0:T(8,128)(2,1)S(1)} %broadcast_in_dim.20), channel_id=1, replica_groups=mesh['y'=8,'zl'=2,'c'=2,'x'=4,'zh'=4] {'y','zl'}, dimensions={0} | all-to-all | bytes 1572864 | tf_op jit(solution)/shard_map/all_to_all | solution.py:32
  33.1 4.3 %collective-permute-start.6 = (bf16[384,1024]{1,0:T(8,128)(2,1)S(1)}, bf16[384,1024]{1,0:T(8,128)(2,1)S(1)}, u32[]{:S(2)}, u32[]{:S(2)}) collective-permute-start(bf16[384,1024]{1,0:T(8,128)(2,1)S(1)} %bitcast.61), channel_id=1, source_target_pairs={{0,16},{16,0},{1,17},{17,1},{2,18},{18,2},{3,19},{19,3},{4,20},{20... | collective-permute-start | bytes 2359304 | tf_op jit(solution)/shard_map/ppermute | solution.py:65
  38.8 1.7 copy.34
  40.4 4.5 %all-to-all-start.1 = ((f32[3,4,96,448]{3,2,0,1:T(8,128)}), f32[3,4,96,448]{3,2,0,1:T(8,128)}, u32[]{:S(2)}, u32[]{:S(2)}) async-start(f32[3,4,96,448]{3,2,0,1:T(8,128)} %copy.34), calls=%async_computation.1 | async-start | bytes 4718592 | tf_op jit(solution)/shard_map/all_to_all | solution.py:25
  46.5 1.6 copy.42
  48.1 26.2 %all-to-all-done.1 = f32[3,4,96,448]{3,2,0,1:T(8,128)} async-done(((f32[3,4,96,448]{3,2,0,1:T(8,128)}), f32[3,4,96,448]{3,2,0,1:T(8,128)}, u32[]{:S(2)}, u32[]{:S(2)}) %all-to-all-start.1) | async-done | bytes 2064416 | tf_op jit(solution)/shard_map/all_to_all | solution.py:25
  74.3 3.6 %all-to-all-start.3 = ((f32[3,4,96,448]{3,2,0,1:T(8,128)}), f32[3,4,96,448]{3,2,0,1:T(8,128)S(1)}, u32[]{:S(2)}, u32[]{:S(2)}) async-start(f32[3,4,96,448]{3,2,0,1:T(8,128)} %copy.42), calls=%async_computation.3 | async-start | bytes 4718592 | tf_op jit(solution)/shard_map/all_to_all | solution.py:25
  78.0 2.8 %reduce_sum.27 = f32[3,96,448]{2,1,0:T(8,128)} reduce(f32[3,4,96,448]{3,2,0,1:T(8,128)} %all-to-all-done.1, f32[]{:T(128)} %constant.52.clone.1), dimensions={1}, to_apply=%region_0.0 | reduce | flops 387072 | bytes 2580484 | tf_op jit(solution)/shard_map/reduce_sum | solution.py:26
  80.8 1.8 constant_dynamic-slice_fusion.5
  82.6 5.8 %collective-permute-start = (f32[3,24,448]{2,1,0:T(8,128)}, f32[3,24,448]{2,1,0:T(8,128)S(1)}, u32[]{:S(2)}, u32[]{:S(2)}) collective-permute-start(f32[3,24,448]{2,1,0:T(8,128)} %get-tuple-element.8), channel_id=1, source_target_pairs={{0,1},{1,2},{2,3},{3,0},{4,5},{5,6},{6,7},{7,4},{8,9},{9,10},{10,1... | collective-permute-start | bytes 387080 | tf_op jit(solution)/shard_map/ppermute | solution.py:43
  88.4 5.9 %collective-permute-start.2 = (f32[3,24,448]{2,1,0:T(8,128)}, f32[3,24,448]{2,1,0:T(8,128)}, u32[]{:S(2)}, u32[]{:S(2)}) collective-permute-start(f32[3,24,448]{2,1,0:T(8,128)} %get-tuple-element.9), channel_id=1, source_target_pairs={{0,3},{1,0},{2,1},{3,2},{4,7},{5,4},{6,5},{7,6},{8,11},{9,8},{10,9... | collective-permute-start | bytes 387080 | tf_op jit(solution)/shard_map/ppermute | solution.py:43
  94.3 5.5 %collective-permute-start.1 = (f32[3,24,448]{2,1,0:T(8,128)}, f32[3,24,448]{2,1,0:T(8,128)}, u32[]{:S(2)}, u32[]{:S(2)}) collective-permute-start(f32[3,24,448]{2,1,0:T(8,128)} %get-tuple-element.10), channel_id=1, source_target_pairs={{0,2},{1,3},{2,0},{3,1},{4,6},{5,7},{6,4},{7,5},{8,10},{9,11},{10,... | collective-permute-start | bytes 387080 | tf_op jit(solution)/shard_map/ppermute | solution.py:43
  99.8 3.0 %collective-permute-done.2 = f32[3,24,448]{2,1,0:T(8,128)} collective-permute-done((f32[3,24,448]{2,1,0:T(8,128)}, f32[3,24,448]{2,1,0:T(8,128)}, u32[]{:S(2)}, u32[]{:S(2)}) %collective-permute-start.2) | collective-permute-done | bytes 129056 | tf_op jit(solution)/shard_map/ppermute | solution.py:43
  102.8 3.5 %collective-permute-done.1 = f32[3,24,448]{2,1,0:T(8,128)} collective-permute-done((f32[3,24,448]{2,1,0:T(8,128)}, f32[3,24,448]{2,1,0:T(8,128)}, u32[]{:S(2)}, u32[]{:S(2)}) %collective-permute-start.1) | collective-permute-done | bytes 129056 | tf_op jit(solution)/shard_map/ppermute | solution.py:43
  106.3 1.1 add_add_fusion.1
  107.5 8.2 %collective-permute-start.4 = (bf16[3,24,448]{2,1,0:T(8,128)(2,1)S(1)}, bf16[3,24,448]{2,1,0:T(8,128)(2,1)S(1)}, u32[]{:S(2)}, u32[]{:S(2)}) collective-permute-start(bf16[3,24,448]{2,1,0:T(8,128)(2,1)S(1)} %get-tuple-element.19), channel_id=1, source_target_pairs={{0,2},{1,3},{2,0},{3,1},{4,6},{5,7},{6,4},{7,5},{8,10},{9,11},{10,... | collective-permute-start | bytes 193544 | tf_op jit(solution)/shard_map/ppermute | solution.py:50
  115.6 1.9 collective-permute-start.3
  117.6 4.3 %collective-permute-start.5 = (bf16[3,24,448]{2,1,0:T(8,128)(2,1)S(1)}, bf16[3,24,448]{2,1,0:T(8,128)(2,1)}, u32[]{:S(2)}, u32[]{:S(2)}) collective-permute-start(bf16[3,24,448]{2,1,0:T(8,128)(2,1)S(1)} %get-tuple-element.19), channel_id=1, source_target_pairs={{0,1},{1,2},{2,3},{3,0},{4,5},{5,6},{6,7},{7,4},{8,9},{9,10},{10,1... | collective-permute-start | bytes 193544 | tf_op jit(solution)/shard_map/ppermute | solution.py:50
  121.8 1.1 reduce_sum.28
  123.0 1.1 constant_dynamic-slice_fusion.2
  124.0 1.9 collective-permute-start.7
  126.0 5.5 %collective-permute-start.9 = (f32[3,24,448]{2,1,0:T(8,128)S(1)}, f32[3,24,448]{2,1,0:T(8,128)S(1)}, u32[]{:S(2)}, u32[]{:S(2)}) collective-permute-start(f32[3,24,448]{2,1,0:T(8,128)S(1)} %get-tuple-element.6), channel_id=1, source_target_pairs={{0,3},{1,0},{2,1},{3,2},{4,7},{5,4},{6,5},{7,6},{8,11},{9,8},{10,9... | collective-permute-start | bytes 387080 | tf_op jit(solution)/shard_map/ppermute | solution.py:43
  131.5 1.9 collective-permute-start.8
  133.4 1.4 fusion.32
  134.8 1.2 broadcast_in_dim.22
  136.0 3.6 %all-to-all-start.2 = ((bf16[3,4,96,448]{3,2,0,1:T(8,128)(2,1)}), bf16[3,4,96,448]{3,2,0,1:T(8,128)(2,1)S(1)}, u32[]{:S(2)}, u32[]{:S(2)}) async-start(bf16[3,4,96,448]{3,2,0,1:T(8,128)(2,1)} %broadcast_in_dim.22), calls=%async_computation.2 | async-start | bytes 2359296 | tf_op jit(solution)/shard_map/all_to_all | solution.py:32
  139.5 1.9 collective-permute-done.8
  141.4 1.0 add_add_fusion
  142.4 5.4 %collective-permute-start.11 = (bf16[3,24,448]{2,1,0:T(8,128)(2,1)S(1)}, bf16[3,24,448]{2,1,0:T(8,128)(2,1)S(1)}, u32[]{:S(2)}, u32[]{:S(2)}) collective-permute-start(bf16[3,24,448]{2,1,0:T(8,128)(2,1)S(1)} %get-tuple-element.17), channel_id=1, source_target_pairs={{0,2},{1,3},{2,0},{3,1},{4,6},{5,7},{6,4},{7,5},{8,10},{9,11},{10,... | collective-permute-start | bytes 193544 | tf_op jit(solution)/shard_map/ppermute | solution.py:50
  147.9 1.9 collective-permute-start.10
  149.8 4.3 %collective-permute-start.12 = (bf16[3,24,448]{2,1,0:T(8,128)(2,1)S(1)}, bf16[3,24,448]{2,1,0:T(8,128)(2,1)S(1)}, u32[]{:S(2)}, u32[]{:S(2)}) collective-permute-start(bf16[3,24,448]{2,1,0:T(8,128)(2,1)S(1)} %get-tuple-element.17), channel_id=1, source_target_pairs={{0,1},{1,2},{2,3},{3,0},{4,5},{5,6},{6,7},{7,4},{8,9},{9,10},{10,1... | collective-permute-start | bytes 193544 | tf_op jit(solution)/shard_map/ppermute | solution.py:50
  154.1 3.1 %collective-permute-done.12 = bf16[3,24,448]{2,1,0:T(8,128)(2,1)S(1)} collective-permute-done((bf16[3,24,448]{2,1,0:T(8,128)(2,1)S(1)}, bf16[3,24,448]{2,1,0:T(8,128)(2,1)S(1)}, u32[]{:S(2)}, u32[]{:S(2)}) %collective-permute-start.12) | collective-permute-done | bytes 64544 | tf_op jit(solution)/shard_map/ppermute | solution.py:50
  157.7 1.1 broadcast_in_dim.24
  158.8 4.3 %all-to-all-start.4 = ((bf16[3,4,96,448]{3,2,0,1:T(8,128)(2,1)}), bf16[3,4,96,448]{3,2,0,1:T(8,128)(2,1)}, u32[]{:S(2)}, u32[]{:S(2)}) async-start(bf16[3,4,96,448]{3,2,0,1:T(8,128)(2,1)} %broadcast_in_dim.24), calls=%async_computation.4 | async-start | bytes 2359296 | tf_op jit(solution)/shard_map/all_to_all | solution.py:32
  163.2 10.4 %all-to-all-done.4 = bf16[3,4,96,448]{3,2,0,1:T(8,128)(2,1)} async-done(((bf16[3,4,96,448]{3,2,0,1:T(8,128)(2,1)}), bf16[3,4,96,448]{3,2,0,1:T(8,128)(2,1)}, u32[]{:S(2)}, u32[]{:S(2)}) %all-to-all-start.4) | async-done | bytes 1032224 | tf_op jit(solution)/shard_map/all_to_all | solution.py:32
  173.6 1.4 copy.44
  175.0 0.6 fusion.44
  175.6 0.6 convolution_add_fusion
  176.2 9.1 %collective-permute-start.13 = (f32[384,512]{1,0:T(8,128)S(1)}, f32[384,512]{1,0:T(8,128)S(1)}, u32[]{:S(2)}, u32[]{:S(2)}) collective-permute-start(f32[384,512]{1,0:T(8,128)S(1)} %slice.83), channel_id=1, source_target_pairs={{0,16},{16,0},{1,17},{17,1},{2,18},{18,2},{3,19},{19,3},{4,20},{20... | collective-permute-start | bytes 2359304 | tf_op jit(solution)/shard_map/ppermute | solution.py:98
  185.3 1.9 collective-permute-done.13
  187.2 1.1 slice_add_fusion
  188.3 8.8 %all-to-all-start.5 = ((f32[16,24,512]{2,1,0:T(8,128)}), f32[16,24,512]{2,1,0:T(8,128)}, u32[]{:S(2)}, u32[]{:S(2)}) async-start(f32[16,24,512]{2,1,0:T(8,128)} %bitcast.74), calls=%async_computation.5 | async-start | bytes 1572864 | tf_op jit(solution)/shard_map/all_to_all | solution.py:25
  197.1 2.6 %convolution_convert_fusion = bf16[448,512]{1,0:T(8,128)(2,1)} fusion(bf16[384,1024]{1,0:T(8,128)(2,1)} %copy-done.3, bf16[384,1024]{1,0:T(8,128)(2,1)} %bitcast.65, bf16[3,384,448]{2,1,0:T(8,128)(2,1)S(1)} %bitcast.58, bf16[3,384,448]{2,1,0:T(8,128)(2,1)S(1)} %bitcast.53), kind=kOutput, calls=%fused_computation.9 | convolution fusion | flops 355500032 | bytes 4096000 | tf_op jit(solution)/shard_map/dot_general | solution.py:85
  199.7 1.3 convolution_convert_fusion.1
  201.0 1.3 convolution_convert_fusion.2
  202.3 16.1 %all-to-all-done.5 = f32[16,24,512]{2,1,0:T(8,128)} async-done(((f32[16,24,512]{2,1,0:T(8,128)}), f32[16,24,512]{2,1,0:T(8,128)}, u32[]{:S(2)}, u32[]{:S(2)}) %all-to-all-start.5) | async-done | bytes 786464 | tf_op jit(solution)/shard_map/all_to_all | solution.py:25
  218.4 1.8 reduce_sum.29
  (42 shorter events, 3.8 us)
Async XLA Ops:
  0.6 37.5 %copy-start = (bf16[512,448]{0,1:T(8,128)(2,1)S(1)}, bf16[512,448]{0,1:T(8,128)(2,1)}, u32[]{:S(2)}) copy-start(bf16[512,448]{0,1:T(8,128)(2,1)} %param.9) | copy-start | bytes 1376260
  0.6 36.7 %copy-start.5 = (bf16[512,448]{0,1:T(8,128)(2,1)S(1)}, bf16[512,448]{0,1:T(8,128)(2,1)}, u32[]{:S(2)}) copy-start(bf16[512,448]{0,1:T(8,128)(2,1)} %param.10) | copy-start | bytes 1376260
  1.6 36.1 %copy-start.6 = (bf16[448,512]{1,0:T(8,128)(2,1)S(1)}, bf16[448,512]{1,0:T(8,128)(2,1)}, u32[]{:S(2)}) copy-start(bf16[448,512]{1,0:T(8,128)(2,1)} %param.11) | copy-start | bytes 1376260
  33.1 5.1 %copy-start.1 = (bf16[16,24,1024]{2,1,0:T(8,128)(2,1)}, bf16[16,24,1024]{2,1,0:T(8,128)(2,1)S(1)}, u32[]{:S(2)}) copy-start(bf16[16,24,1024]{2,1,0:T(8,128)(2,1)S(1)} %all_to_all.30) | copy-start | bytes 2359300
  33.1 11.9 %collective-permute-start.6 = (bf16[384,1024]{1,0:T(8,128)(2,1)S(1)}, bf16[384,1024]{1,0:T(8,128)(2,1)S(1)}, u32[]{:S(2)}, u32[]{:S(2)}) collective-permute-start(bf16[384,1024]{1,0:T(8,128)(2,1)S(1)} %bitcast.61), channel_id=1, source_target_pairs={{0,16},{16,0},{1,17},{17,1},{2,18},{18,2},{3,19},{19,3},{4,20},{20... | collective-permute-start | bytes 2359304 | tf_op jit(solution)/shard_map/ppermute | solution.py:65
  40.4 33.9 %all-to-all-start.1 = ((f32[3,4,96,448]{3,2,0,1:T(8,128)}), f32[3,4,96,448]{3,2,0,1:T(8,128)}, u32[]{:S(2)}, u32[]{:S(2)}) async-start(f32[3,4,96,448]{3,2,0,1:T(8,128)} %copy.34), calls=%async_computation.1 | async-start | bytes 4718592 | tf_op jit(solution)/shard_map/all_to_all | solution.py:25
  44.9 0.9 copy-start.3
  74.3 47.6 %all-to-all-start.3 = ((f32[3,4,96,448]{3,2,0,1:T(8,128)}), f32[3,4,96,448]{3,2,0,1:T(8,128)S(1)}, u32[]{:S(2)}, u32[]{:S(2)}) async-start(f32[3,4,96,448]{3,2,0,1:T(8,128)} %copy.42), calls=%async_computation.3 | async-start | bytes 4718592 | tf_op jit(solution)/shard_map/all_to_all | solution.py:25
  82.6 17.2 %collective-permute-start = (f32[3,24,448]{2,1,0:T(8,128)}, f32[3,24,448]{2,1,0:T(8,128)S(1)}, u32[]{:S(2)}, u32[]{:S(2)}) collective-permute-start(f32[3,24,448]{2,1,0:T(8,128)} %get-tuple-element.8), channel_id=1, source_target_pairs={{0,1},{1,2},{2,3},{3,0},{4,5},{5,6},{6,7},{7,4},{8,9},{9,10},{10,1... | collective-permute-start | bytes 387080 | tf_op jit(solution)/shard_map/ppermute | solution.py:43
  88.4 14.4 %collective-permute-start.2 = (f32[3,24,448]{2,1,0:T(8,128)}, f32[3,24,448]{2,1,0:T(8,128)}, u32[]{:S(2)}, u32[]{:S(2)}) collective-permute-start(f32[3,24,448]{2,1,0:T(8,128)} %get-tuple-element.9), channel_id=1, source_target_pairs={{0,3},{1,0},{2,1},{3,2},{4,7},{5,4},{6,5},{7,6},{8,11},{9,8},{10,9... | collective-permute-start | bytes 387080 | tf_op jit(solution)/shard_map/ppermute | solution.py:43
  94.3 12.0 %collective-permute-start.1 = (f32[3,24,448]{2,1,0:T(8,128)}, f32[3,24,448]{2,1,0:T(8,128)}, u32[]{:S(2)}, u32[]{:S(2)}) collective-permute-start(f32[3,24,448]{2,1,0:T(8,128)} %get-tuple-element.10), channel_id=1, source_target_pairs={{0,2},{1,3},{2,0},{3,1},{4,6},{5,7},{6,4},{7,5},{8,10},{9,11},{10,... | collective-permute-start | bytes 387080 | tf_op jit(solution)/shard_map/ppermute | solution.py:43
  107.5 24.0 %collective-permute-start.4 = (bf16[3,24,448]{2,1,0:T(8,128)(2,1)S(1)}, bf16[3,24,448]{2,1,0:T(8,128)(2,1)S(1)}, u32[]{:S(2)}, u32[]{:S(2)}) collective-permute-start(bf16[3,24,448]{2,1,0:T(8,128)(2,1)S(1)} %get-tuple-element.19), channel_id=1, source_target_pairs={{0,2},{1,3},{2,0},{3,1},{4,6},{5,7},{6,4},{7,5},{8,10},{9,11},{10,... | collective-permute-start | bytes 193544 | tf_op jit(solution)/shard_map/ppermute | solution.py:50
  115.6 17.8 %collective-permute-start.3 = (bf16[3,24,448]{2,1,0:T(8,128)(2,1)S(1)}, bf16[3,24,448]{2,1,0:T(8,128)(2,1)}, u32[]{:S(2)}, u32[]{:S(2)}) collective-permute-start(bf16[3,24,448]{2,1,0:T(8,128)(2,1)S(1)} %get-tuple-element.19), channel_id=1, source_target_pairs={{0,3},{1,0},{2,1},{3,2},{4,7},{5,4},{6,5},{7,6},{8,11},{9,8},{10,9... | collective-permute-start | bytes 193544 | tf_op jit(solution)/shard_map/ppermute | solution.py:50
  117.6 15.8 %collective-permute-start.5 = (bf16[3,24,448]{2,1,0:T(8,128)(2,1)S(1)}, bf16[3,24,448]{2,1,0:T(8,128)(2,1)}, u32[]{:S(2)}, u32[]{:S(2)}) collective-permute-start(bf16[3,24,448]{2,1,0:T(8,128)(2,1)S(1)} %get-tuple-element.19), channel_id=1, source_target_pairs={{0,1},{1,2},{2,3},{3,0},{4,5},{5,6},{6,7},{7,4},{8,9},{9,10},{10,1... | collective-permute-start | bytes 193544 | tf_op jit(solution)/shard_map/ppermute | solution.py:50
  124.0 15.5 %collective-permute-start.7 = (f32[3,24,448]{2,1,0:T(8,128)S(1)}, f32[3,24,448]{2,1,0:T(8,128)S(1)}, u32[]{:S(2)}, u32[]{:S(2)}) collective-permute-start(f32[3,24,448]{2,1,0:T(8,128)S(1)} %get-tuple-element.5), channel_id=1, source_target_pairs={{0,1},{1,2},{2,3},{3,0},{4,5},{5,6},{6,7},{7,4},{8,9},{9,10},{10,1... | collective-permute-start | bytes 387080 | tf_op jit(solution)/shard_map/ppermute | solution.py:43
  126.0 13.6 %collective-permute-start.9 = (f32[3,24,448]{2,1,0:T(8,128)S(1)}, f32[3,24,448]{2,1,0:T(8,128)S(1)}, u32[]{:S(2)}, u32[]{:S(2)}) collective-permute-start(f32[3,24,448]{2,1,0:T(8,128)S(1)} %get-tuple-element.6), channel_id=1, source_target_pairs={{0,3},{1,0},{2,1},{3,2},{4,7},{5,4},{6,5},{7,6},{8,11},{9,8},{10,9... | collective-permute-start | bytes 387080 | tf_op jit(solution)/shard_map/ppermute | solution.py:43
  131.5 9.9 %collective-permute-start.8 = (f32[3,24,448]{2,1,0:T(8,128)S(1)}, f32[3,24,448]{2,1,0:T(8,128)S(1)}, u32[]{:S(2)}, u32[]{:S(2)}) collective-permute-start(f32[3,24,448]{2,1,0:T(8,128)S(1)} %get-tuple-element.7), channel_id=1, source_target_pairs={{0,2},{1,3},{2,0},{3,1},{4,6},{5,7},{6,4},{7,5},{8,10},{9,11},{10,... | collective-permute-start | bytes 387080 | tf_op jit(solution)/shard_map/ppermute | solution.py:43
  136.0 21.7 %all-to-all-start.2 = ((bf16[3,4,96,448]{3,2,0,1:T(8,128)(2,1)}), bf16[3,4,96,448]{3,2,0,1:T(8,128)(2,1)S(1)}, u32[]{:S(2)}, u32[]{:S(2)}) async-start(bf16[3,4,96,448]{3,2,0,1:T(8,128)(2,1)} %broadcast_in_dim.22), calls=%async_computation.2 | async-start | bytes 2359296 | tf_op jit(solution)/shard_map/all_to_all | solution.py:32
  142.4 11.6 %collective-permute-start.11 = (bf16[3,24,448]{2,1,0:T(8,128)(2,1)S(1)}, bf16[3,24,448]{2,1,0:T(8,128)(2,1)S(1)}, u32[]{:S(2)}, u32[]{:S(2)}) collective-permute-start(bf16[3,24,448]{2,1,0:T(8,128)(2,1)S(1)} %get-tuple-element.17), channel_id=1, source_target_pairs={{0,2},{1,3},{2,0},{3,1},{4,6},{5,7},{6,4},{7,5},{8,10},{9,11},{10,... | collective-permute-start | bytes 193544 | tf_op jit(solution)/shard_map/ppermute | solution.py:50
  147.9 6.3 %collective-permute-start.10 = (bf16[3,24,448]{2,1,0:T(8,128)(2,1)S(1)}, bf16[3,24,448]{2,1,0:T(8,128)(2,1)S(1)}, u32[]{:S(2)}, u32[]{:S(2)}) collective-permute-start(bf16[3,24,448]{2,1,0:T(8,128)(2,1)S(1)} %get-tuple-element.17), channel_id=1, source_target_pairs={{0,3},{1,0},{2,1},{3,2},{4,7},{5,4},{6,5},{7,6},{8,11},{9,8},{10,9... | collective-permute-start | bytes 193544 | tf_op jit(solution)/shard_map/ppermute | solution.py:50
  149.8 7.5 %collective-permute-start.12 = (bf16[3,24,448]{2,1,0:T(8,128)(2,1)S(1)}, bf16[3,24,448]{2,1,0:T(8,128)(2,1)S(1)}, u32[]{:S(2)}, u32[]{:S(2)}) collective-permute-start(bf16[3,24,448]{2,1,0:T(8,128)(2,1)S(1)} %get-tuple-element.17), channel_id=1, source_target_pairs={{0,1},{1,2},{2,3},{3,0},{4,5},{5,6},{6,7},{7,4},{8,9},{9,10},{10,1... | collective-permute-start | bytes 193544 | tf_op jit(solution)/shard_map/ppermute | solution.py:50
  158.8 14.8 %all-to-all-start.4 = ((bf16[3,4,96,448]{3,2,0,1:T(8,128)(2,1)}), bf16[3,4,96,448]{3,2,0,1:T(8,128)(2,1)}, u32[]{:S(2)}, u32[]{:S(2)}) async-start(bf16[3,4,96,448]{3,2,0,1:T(8,128)(2,1)} %broadcast_in_dim.24), calls=%async_computation.4 | async-start | bytes 2359296 | tf_op jit(solution)/shard_map/all_to_all | solution.py:32
  176.2 11.0 %collective-permute-start.13 = (f32[384,512]{1,0:T(8,128)S(1)}, f32[384,512]{1,0:T(8,128)S(1)}, u32[]{:S(2)}, u32[]{:S(2)}) collective-permute-start(f32[384,512]{1,0:T(8,128)S(1)} %slice.83), channel_id=1, source_target_pairs={{0,16},{16,0},{1,17},{17,1},{2,18},{18,2},{3,19},{19,3},{4,20},{20... | collective-permute-start | bytes 2359304 | tf_op jit(solution)/shard_map/ppermute | solution.py:98
  188.3 30.2 %all-to-all-start.5 = ((f32[16,24,512]{2,1,0:T(8,128)}), f32[16,24,512]{2,1,0:T(8,128)}, u32[]{:S(2)}, u32[]{:S(2)}) async-start(f32[16,24,512]{2,1,0:T(8,128)} %bitcast.74), calls=%async_computation.5 | async-start | bytes 1572864 | tf_op jit(solution)/shard_map/all_to_all | solution.py:25
  197.1 2.6 %copy-start.2 = (bf16[16,24,1024]{2,1,0:T(8,128)(2,1)S(1)}, bf16[16,24,1024]{2,1,0:T(8,128)(2,1)}, u32[]{:S(2)}) copy-start(bf16[16,24,1024]{2,1,0:T(8,128)(2,1)} %copy-done.1) | copy-start | bytes 2359300
  197.1 2.6 %copy-start.4 = (bf16[384,1024]{1,0:T(8,128)(2,1)S(1)}, bf16[384,1024]{1,0:T(8,128)(2,1)}, u32[]{:S(2)}) copy-start(bf16[384,1024]{1,0:T(8,128)(2,1)} %copy-done.3) | copy-start | bytes 2359300

commit v13 on v12

--- a/solution.py
+++ b/solution.py
@@ -66,14 +66,13 @@
     width = tokens.shape[1]
     chunks = []
     for rows in parts_in:
-        tok, grd = rows[:, :width], rows[:, width:]
-        gate_part = jnp.dot(tok, gate_weight, preferred_element_type=jnp.float32)
-        up_part = jnp.dot(tok, up_weight, preferred_element_type=jnp.float32)
-        hidden_part = lax.dot_general(
-            grd, down_weight, contract_last, preferred_element_type=jnp.float32
-        )
-        p = jnp.stack([gate_part, up_part, hidden_part])
-        p = scatter_sum(p, "x", nx, 1)
+        rows = rows.reshape((nx, -1) + rows.shape[1:])
+        tok, grd = rows[..., :width], rows[..., width:]
+        gate_part = jnp.einsum("brd,dh->brh", tok, gate_weight, preferred_element_type=jnp.float32)
+        up_part = jnp.einsum("brd,dh->brh", tok, up_weight, preferred_element_type=jnp.float32)
+        hidden_part = jnp.einsum("brd,hd->brh", grd, down_weight, preferred_element_type=jnp.float32)
+        p = jnp.stack([gate_part, up_part, hidden_part], 1)
+        p = lax.all_to_all(p, "x", 0, 0, tiled=True).sum(0)
         p = scatter_permute(p, "zh", nzh, 1)
         d = jnp.stack(swiglu_grads(p[0], p[1], p[2]))
         d = gather_permute(d, "zh", nzh, 1)

time: 222 us -> 216 us (0.973)
  waiting for transfers between devices: 66.2 us -> 60.6 us
    all_to_all x3 -> x1, waiting for transfers between devices: 42.3 us -> 15.6 us  [scatter_sum(): v = lax.all_to_all(v, axis_name, dim, dim, tiled=True)]
    all_to_all x0 -> x2, waiting for transfers between devices: none -> 17.5 us  [local(): p = lax.all_to_all(p, 'x', 0, 0, tiled=True).sum(0)]
    all_to_all x0 -> x2, starting transfers between devices: none -> 8.14 us  [local(): p = lax.all_to_all(p, 'x', 0, 0, tiled=True).sum(0)]
    all_to_all x3 -> x1, starting transfers between devices: 17 us -> 10.2 us  [scatter_sum(): v = lax.all_to_all(v, axis_name, dim, dim, tiled=True)]
    reduce_sum x0 -> x2, other arithmetic: none -> 3.95 us  [local(): p = lax.all_to_all(p, 'x', 0, 0, tiled=True).sum(0)]
    reduce_sum x3 -> x1, other arithmetic: 5.75 us -> 1.8 us  [scatter_sum(): return v.sum(dim)]
    ppermute x6, starting transfers between devices: 25.9 us -> 22.5 us  [gather_permute(): lax.ppermute(v, axis_name, [(j, (j + k) % n) for j in range(n)])]
  transfers between devices with their start and end apart: 19 -> 19, of which waited for: 9 -> 9; matrix products, arithmetic and copies ran while one was open for 11% -> 9% of each run, Pallas kernels for 0% -> 0%
where the time goes in v13:
time: 216 us; the launch traced here: 214 us
  starting transfers between devices  90.1 us (42%)
  waiting for transfers between devices  60.6 us (28%)
  blocking collectives  31.5 us (15%)
  other arithmetic  12 us (6%)
  local copies, waits for them, and re-layouts  10.3 us (5%)
  matrix products  8.71 us (4%)
    all_to_all x1, blocking collectives, gather_a2a(): v = lax.all_to_all(v, axis_name, dim, dim, tiled=True)  31.5 us
    ppermute x6, starting transfers between devices, scatter_permute(): lax.ppermute(part, axis_name, [(j, (j + k) % n) for j in range(n)])  27.1 us
    ppermute x6, starting transfers between devices, gather_permute(): lax.ppermute(v, axis_name, [(j, (j + k) % n) for j in range(n)])  22.5 us
    all_to_all x2, waiting for transfers between devices, local(): p = lax.all_to_all(p, 'x', 0, 0, tiled=True).sum(0)  17.5 us
    all_to_all x1, waiting for transfers between devices, scatter_sum(): v = lax.all_to_all(v, axis_name, dim, dim, tiled=True)  15.6 us
    all_to_all x2, waiting for transfers between devices, gather_a2a(): v = lax.all_to_all(v, axis_name, dim, dim, tiled=True)  10.5 us
    all_to_all x1, starting transfers between devices, scatter_sum(): v = lax.all_to_all(v, axis_name, dim, dim, tiled=True)  10.2 us
    all_to_all x2, starting transfers between devices, gather_a2a(): v = lax.all_to_all(v, axis_name, dim, dim, tiled=True)  9.02 us
  transfers between devices with their start and end apart: 19, of which 9 were waited for; matrix products, arithmetic and copies ran while one was open for 9% of the time, Pallas kernels for 0%

profile of v13, /device:TPU:1, one launch (start us, length us, event | category | flops | bytes accessed | tf_op | source)
XLA Modules:
  0.0 214.3 jit_solution(3490428760256146318)
XLA Ops:
  0.7 0.8 pad_maximum_fusion.7
  1.6 31.5 %all_to_all.30 = bf16[16,24,1024]{2,1,0:T(8,128)(2,1)S(1)} all-to-all(bf16[16,24,1024]{2,1,0:T(8,128)(2,1)S(1)} %broadcast_in_dim.20), channel_id=1, replica_groups=mesh['y'=8,'zl'=2,'c'=2,'x'=4,'zh'=4] {'y','zl'}, dimensions={0} | all-to-all | bytes 1572864 | tf_op jit(solution)/shard_map/all_to_all | solution.py:32
  34.5 1.7 copy.19
  36.1 4.5 %all-to-all-start.1 = ((f32[4,3,96,448]{3,2,1,0:T(8,128)}), f32[4,3,96,448]{3,2,1,0:T(8,128)}, u32[]{:S(2)}, u32[]{:S(2)}) async-start(f32[4,3,96,448]{3,2,1,0:T(8,128)} %copy.19), calls=%async_computation.1 | async-start | bytes 4718592 | tf_op jit(solution)/shard_map/all_to_all | solution.py:75
  40.7 4.3 %collective-permute-start.6 = (bf16[384,1024]{1,0:T(8,128)(2,1)S(1)}, bf16[384,1024]{1,0:T(8,128)(2,1)S(1)}, u32[]{:S(2)}, u32[]{:S(2)}) collective-permute-start(bf16[384,1024]{1,0:T(8,128)(2,1)S(1)} %bitcast.81), channel_id=1, source_target_pairs={{0,16},{16,0},{1,17},{17,1},{2,18},{18,2},{3,19},{19,3},{4,20},{20... | collective-permute-start | bytes 2359304 | tf_op jit(solution)/shard_map/ppermute | solution.py:65
  44.9 1.9 collective-permute-done.6
  48.4 1.6 copy.24
  50.0 17.5 %all-to-all-done.1 = f32[4,3,96,448]{3,2,1,0:T(8,128)} async-done(((f32[4,3,96,448]{3,2,1,0:T(8,128)}), f32[4,3,96,448]{3,2,1,0:T(8,128)}, u32[]{:S(2)}, u32[]{:S(2)}) %all-to-all-start.1) | async-done | bytes 2064416 | tf_op jit(solution)/shard_map/all_to_all | solution.py:75
  67.5 3.6 %all-to-all-start.3 = ((f32[4,3,96,448]{3,2,1,0:T(8,128)}), f32[4,3,96,448]{3,2,1,0:T(8,128)S(1)}, u32[]{:S(2)}, u32[]{:S(2)}) async-start(f32[4,3,96,448]{3,2,1,0:T(8,128)} %copy.24), calls=%async_computation.3 | async-start | bytes 4718592 | tf_op jit(solution)/shard_map/all_to_all | solution.py:75
  71.2 2.8 %reduce_sum.27 = f32[3,96,448]{2,1,0:T(8,128)} reduce(f32[4,3,96,448]{3,2,1,0:T(8,128)} %all-to-all-done.1, f32[]{:T(128)} %constant.52.clone.1), dimensions={0}, to_apply=%region_0.0 | reduce | flops 387072 | bytes 2580484 | tf_op jit(solution)/shard_map/reduce_sum | solution.py:75
  74.0 1.8 constant_dynamic-slice_fusion.5
  75.9 5.8 %collective-permute-start = (f32[3,24,448]{2,1,0:T(8,128)}, f32[3,24,448]{2,1,0:T(8,128)S(1)}, u32[]{:S(2)}, u32[]{:S(2)}) collective-permute-start(f32[3,24,448]{2,1,0:T(8,128)} %get-tuple-element.8), channel_id=1, source_target_pairs={{0,1},{1,2},{2,3},{3,0},{4,5},{5,6},{6,7},{7,4},{8,9},{9,10},{10,1... | collective-permute-start | bytes 387080 | tf_op jit(solution)/shard_map/ppermute | solution.py:43
  81.7 5.9 %collective-permute-start.2 = (f32[3,24,448]{2,1,0:T(8,128)}, f32[3,24,448]{2,1,0:T(8,128)}, u32[]{:S(2)}, u32[]{:S(2)}) collective-permute-start(f32[3,24,448]{2,1,0:T(8,128)} %get-tuple-element.9), channel_id=1, source_target_pairs={{0,3},{1,0},{2,1},{3,2},{4,7},{5,4},{6,5},{7,6},{8,11},{9,8},{10,9... | collective-permute-start | bytes 387080 | tf_op jit(solution)/shard_map/ppermute | solution.py:43
  87.6 5.5 %collective-permute-start.1 = (f32[3,24,448]{2,1,0:T(8,128)}, f32[3,24,448]{2,1,0:T(8,128)}, u32[]{:S(2)}, u32[]{:S(2)}) collective-permute-start(f32[3,24,448]{2,1,0:T(8,128)} %get-tuple-element.10), channel_id=1, source_target_pairs={{0,2},{1,3},{2,0},{3,1},{4,6},{5,7},{6,4},{7,5},{8,10},{9,11},{10,... | collective-permute-start | bytes 387080 | tf_op jit(solution)/shard_map/ppermute | solution.py:43
  93.0 4.7 %collective-permute-done.1 = f32[3,24,448]{2,1,0:T(8,128)} collective-permute-done((f32[3,24,448]{2,1,0:T(8,128)}, f32[3,24,448]{2,1,0:T(8,128)}, u32[]{:S(2)}, u32[]{:S(2)}) %collective-permute-start.1) | collective-permute-done | bytes 129056 | tf_op jit(solution)/shard_map/ppermute | solution.py:43
  97.8 1.1 add_add_fusion.1
  99.0 6.6 %collective-permute-start.4 = (bf16[3,24,448]{2,1,0:T(8,128)(2,1)S(1)}, bf16[3,24,448]{2,1,0:T(8,128)(2,1)S(1)}, u32[]{:S(2)}, u32[]{:S(2)}) collective-permute-start(bf16[3,24,448]{2,1,0:T(8,128)(2,1)S(1)} %get-tuple-element.19), channel_id=1, source_target_pairs={{0,2},{1,3},{2,0},{3,1},{4,6},{5,7},{6,4},{7,5},{8,10},{9,11},{10,... | collective-permute-start | bytes 193544 | tf_op jit(solution)/shard_map/ppermute | solution.py:50
  105.6 1.9 collective-permute-start.3
  107.5 4.3 %collective-permute-start.5 = (bf16[3,24,448]{2,1,0:T(8,128)(2,1)S(1)}, bf16[3,24,448]{2,1,0:T(8,128)(2,1)}, u32[]{:S(2)}, u32[]{:S(2)}) collective-permute-start(bf16[3,24,448]{2,1,0:T(8,128)(2,1)S(1)} %get-tuple-element.19), channel_id=1, source_target_pairs={{0,1},{1,2},{2,3},{3,0},{4,5},{5,6},{6,7},{7,4},{8,9},{9,10},{10,1... | collective-permute-start | bytes 193544 | tf_op jit(solution)/shard_map/ppermute | solution.py:50
  111.8 1.1 reduce_sum.28
  112.9 1.1 constant_dynamic-slice_fusion.2
  114.0 2.7 %collective-permute-start.7 = (f32[3,24,448]{2,1,0:T(8,128)S(1)}, f32[3,24,448]{2,1,0:T(8,128)S(1)}, u32[]{:S(2)}, u32[]{:S(2)}) collective-permute-start(f32[3,24,448]{2,1,0:T(8,128)S(1)} %get-tuple-element.5), channel_id=1, source_target_pairs={{0,1},{1,2},{2,3},{3,0},{4,5},{5,6},{6,7},{7,4},{8,9},{9,10},{10,1... | collective-permute-start | bytes 387080 | tf_op jit(solution)/shard_map/ppermute | solution.py:43
  116.7 4.6 %collective-permute-start.9 = (f32[3,24,448]{2,1,0:T(8,128)S(1)}, f32[3,24,448]{2,1,0:T(8,128)S(1)}, u32[]{:S(2)}, u32[]{:S(2)}) collective-permute-start(f32[3,24,448]{2,1,0:T(8,128)S(1)} %get-tuple-element.6), channel_id=1, source_target_pairs={{0,3},{1,0},{2,1},{3,2},{4,7},{5,4},{6,5},{7,6},{8,11},{9,8},{10,9... | collective-permute-start | bytes 387080 | tf_op jit(solution)/shard_map/ppermute | solution.py:43
  121.4 2.6 %collective-permute-start.8 = (f32[3,24,448]{2,1,0:T(8,128)S(1)}, f32[3,24,448]{2,1,0:T(8,128)S(1)}, u32[]{:S(2)}, u32[]{:S(2)}) collective-permute-start(f32[3,24,448]{2,1,0:T(8,128)S(1)} %get-tuple-element.7), channel_id=1, source_target_pairs={{0,2},{1,3},{2,0},{3,1},{4,6},{5,7},{6,4},{7,5},{8,10},{9,11},{10,... | collective-permute-start | bytes 387080 | tf_op jit(solution)/shard_map/ppermute | solution.py:43
  124.0 1.4 fusion.32
  125.4 1.2 broadcast_in_dim.22
  126.5 4.1 %all-to-all-start.2 = ((bf16[3,4,96,448]{3,2,0,1:T(8,128)(2,1)}), bf16[3,4,96,448]{3,2,0,1:T(8,128)(2,1)S(1)}, u32[]{:S(2)}, u32[]{:S(2)}) async-start(bf16[3,4,96,448]{3,2,0,1:T(8,128)(2,1)} %broadcast_in_dim.22), calls=%async_computation.2 | async-start | bytes 2359296 | tf_op jit(solution)/shard_map/all_to_all | solution.py:32
  130.6 3.2 %collective-permute-done.8 = f32[3,24,448]{2,1,0:T(8,128)S(1)} collective-permute-done((f32[3,24,448]{2,1,0:T(8,128)S(1)}, f32[3,24,448]{2,1,0:T(8,128)S(1)}, u32[]{:S(2)}, u32[]{:S(2)}) %collective-permute-start.8) | collective-permute-done | bytes 129056 | tf_op jit(solution)/shard_map/ppermute | solution.py:43
  133.8 1.0 add_add_fusion
  134.8 3.5 %collective-permute-start.11 = (bf16[3,24,448]{2,1,0:T(8,128)(2,1)S(1)}, bf16[3,24,448]{2,1,0:T(8,128)(2,1)S(1)}, u32[]{:S(2)}, u32[]{:S(2)}) collective-permute-start(bf16[3,24,448]{2,1,0:T(8,128)(2,1)S(1)} %get-tuple-element.17), channel_id=1, source_target_pairs={{0,2},{1,3},{2,0},{3,1},{4,6},{5,7},{6,4},{7,5},{8,10},{9,11},{10,... | collective-permute-start | bytes 193544 | tf_op jit(solution)/shard_map/ppermute | solution.py:50
  138.4 3.5 %collective-permute-start.10 = (bf16[3,24,448]{2,1,0:T(8,128)(2,1)S(1)}, bf16[3,24,448]{2,1,0:T(8,128)(2,1)S(1)}, u32[]{:S(2)}, u32[]{:S(2)}) collective-permute-start(bf16[3,24,448]{2,1,0:T(8,128)(2,1)S(1)} %get-tuple-element.17), channel_id=1, source_target_pairs={{0,3},{1,0},{2,1},{3,2},{4,7},{5,4},{6,5},{7,6},{8,11},{9,8},{10,9... | collective-permute-start | bytes 193544 | tf_op jit(solution)/shard_map/ppermute | solution.py:50
  141.9 2.7 %collective-permute-start.12 = (bf16[3,24,448]{2,1,0:T(8,128)(2,1)S(1)}, bf16[3,24,448]{2,1,0:T(8,128)(2,1)S(1)}, u32[]{:S(2)}, u32[]{:S(2)}) collective-permute-start(bf16[3,24,448]{2,1,0:T(8,128)(2,1)S(1)} %get-tuple-element.17), channel_id=1, source_target_pairs={{0,1},{1,2},{2,3},{3,0},{4,5},{5,6},{6,7},{7,4},{8,9},{9,10},{10,1... | collective-permute-start | bytes 193544 | tf_op jit(solution)/shard_map/ppermute | solution.py:50
  144.6 0.7 collective-permute-done.10
  145.3 4.6 %collective-permute-done.12 = bf16[3,24,448]{2,1,0:T(8,128)(2,1)S(1)} collective-permute-done((bf16[3,24,448]{2,1,0:T(8,128)(2,1)S(1)}, bf16[3,24,448]{2,1,0:T(8,128)(2,1)S(1)}, u32[]{:S(2)}, u32[]{:S(2)}) %collective-permute-start.12) | collective-permute-done | bytes 64544 | tf_op jit(solution)/shard_map/ppermute | solution.py:50
  150.3 1.1 broadcast_in_dim.24
  151.4 4.9 %all-to-all-start.4 = ((bf16[3,4,96,448]{3,2,0,1:T(8,128)(2,1)}), bf16[3,4,96,448]{3,2,0,1:T(8,128)(2,1)}, u32[]{:S(2)}, u32[]{:S(2)}) async-start(bf16[3,4,96,448]{3,2,0,1:T(8,128)(2,1)} %broadcast_in_dim.24), calls=%async_computation.4 | async-start | bytes 2359296 | tf_op jit(solution)/shard_map/all_to_all | solution.py:32
  156.4 10.5 %all-to-all-done.4 = bf16[3,4,96,448]{3,2,0,1:T(8,128)(2,1)} async-done(((bf16[3,4,96,448]{3,2,0,1:T(8,128)(2,1)}), bf16[3,4,96,448]{3,2,0,1:T(8,128)(2,1)}, u32[]{:S(2)}, u32[]{:S(2)}) %all-to-all-start.4) | async-done | bytes 1032224 | tf_op jit(solution)/shard_map/all_to_all | solution.py:32
  166.9 1.4 copy.26
  168.3 0.6 fusion.44
  169.6 8.9 %collective-permute-start.13 = (f32[384,512]{1,0:T(8,128)S(1)}, f32[384,512]{1,0:T(8,128)S(1)}, u32[]{:S(2)}, u32[]{:S(2)}) collective-permute-start(f32[384,512]{1,0:T(8,128)S(1)} %slice.83), channel_id=1, source_target_pairs={{0,16},{16,0},{1,17},{17,1},{2,18},{18,2},{3,19},{19,3},{4,20},{20... | collective-permute-start | bytes 2359304 | tf_op jit(solution)/shard_map/ppermute | solution.py:97
  178.5 1.9 collective-permute-done.13
  180.4 1.1 slice_add_fusion
  181.4 10.2 %all-to-all-start.5 = ((f32[16,24,512]{2,1,0:T(8,128)}), f32[16,24,512]{2,1,0:T(8,128)}, u32[]{:S(2)}, u32[]{:S(2)}) async-start(f32[16,24,512]{2,1,0:T(8,128)} %bitcast.88), calls=%async_computation.5 | async-start | bytes 1572864 | tf_op jit(solution)/shard_map/all_to_all | solution.py:25
  191.6 2.6 %convolution_convert_fusion = bf16[448,512]{1,0:T(8,128)(2,1)} fusion(bf16[384,1024]{1,0:T(8,128)(2,1)} %copy-done.3, bf16[384,1024]{1,0:T(8,128)(2,1)} %bitcast.82, bf16[3,384,448]{2,1,0:T(8,128)(2,1)S(1)} %bitcast.75, bf16[3,384,448]{2,1,0:T(8,128)(2,1)S(1)} %bitcast.70), kind=kOutput, calls=%fused_computation.15 | convolution fusion | flops 355500032 | bytes 4096000 | tf_op jit(solution)/shard_map/dot_general | solution.py:84
  194.2 1.3 convolution_convert_fusion.1
  195.5 1.3 convolution_convert_fusion.2
  196.9 15.6 %all-to-all-done.5 = f32[16,24,512]{2,1,0:T(8,128)} async-done(((f32[16,24,512]{2,1,0:T(8,128)}), f32[16,24,512]{2,1,0:T(8,128)}, u32[]{:S(2)}, u32[]{:S(2)}) %all-to-all-start.5) | async-done | bytes 786464 | tf_op jit(solution)/shard_map/all_to_all | solution.py:25
  212.5 1.8 reduce_sum.29
  (42 shorter events, 4.3 us)
Async XLA Ops:
  0.6 33.2 %copy-start = (bf16[512,448]{0,1:T(8,128)(2,1)S(1)}, bf16[512,448]{0,1:T(8,128)(2,1)}, u32[]{:S(2)}) copy-start(bf16[512,448]{0,1:T(8,128)(2,1)} %param.9) | copy-start | bytes 1376260
  0.6 32.4 %copy-start.5 = (bf16[512,448]{0,1:T(8,128)(2,1)S(1)}, bf16[512,448]{0,1:T(8,128)(2,1)}, u32[]{:S(2)}) copy-start(bf16[512,448]{0,1:T(8,128)(2,1)} %param.10) | copy-start | bytes 1376260
  1.6 31.9 %copy-start.6 = (bf16[448,512]{1,0:T(8,128)(2,1)S(1)}, bf16[448,512]{1,0:T(8,128)(2,1)}, u32[]{:S(2)}) copy-start(bf16[448,512]{1,0:T(8,128)(2,1)} %param.11) | copy-start | bytes 1376260
  33.1 7.6 %copy-start.1 = (bf16[16,24,1024]{2,1,0:T(8,128)(2,1)}, bf16[16,24,1024]{2,1,0:T(8,128)(2,1)S(1)}, u32[]{:S(2)}) copy-start(bf16[16,24,1024]{2,1,0:T(8,128)(2,1)S(1)} %all_to_all.30) | copy-start | bytes 2359300
  36.1 31.4 %all-to-all-start.1 = ((f32[4,3,96,448]{3,2,1,0:T(8,128)}), f32[4,3,96,448]{3,2,1,0:T(8,128)}, u32[]{:S(2)}, u32[]{:S(2)}) async-start(f32[4,3,96,448]{3,2,1,0:T(8,128)} %copy.19), calls=%async_computation.1 | async-start | bytes 4718592 | tf_op jit(solution)/shard_map/all_to_all | solution.py:75
  40.7 6.2 %collective-permute-start.6 = (bf16[384,1024]{1,0:T(8,128)(2,1)S(1)}, bf16[384,1024]{1,0:T(8,128)(2,1)S(1)}, u32[]{:S(2)}, u32[]{:S(2)}) collective-permute-start(bf16[384,1024]{1,0:T(8,128)(2,1)S(1)} %bitcast.81), channel_id=1, source_target_pairs={{0,16},{16,0},{1,17},{17,1},{2,18},{18,2},{3,19},{19,3},{4,20},{20... | collective-permute-start | bytes 2359304 | tf_op jit(solution)/shard_map/ppermute | solution.py:65
  46.8 0.9 copy-start.3
  67.5 44.3 %all-to-all-start.3 = ((f32[4,3,96,448]{3,2,1,0:T(8,128)}), f32[4,3,96,448]{3,2,1,0:T(8,128)S(1)}, u32[]{:S(2)}, u32[]{:S(2)}) async-start(f32[4,3,96,448]{3,2,1,0:T(8,128)} %copy.24), calls=%async_computation.3 | async-start | bytes 4718592 | tf_op jit(solution)/shard_map/all_to_all | solution.py:75
  75.9 17.2 %collective-permute-start = (f32[3,24,448]{2,1,0:T(8,128)}, f32[3,24,448]{2,1,0:T(8,128)S(1)}, u32[]{:S(2)}, u32[]{:S(2)}) collective-permute-start(f32[3,24,448]{2,1,0:T(8,128)} %get-tuple-element.8), channel_id=1, source_target_pairs={{0,1},{1,2},{2,3},{3,0},{4,5},{5,6},{6,7},{7,4},{8,9},{9,10},{10,1... | collective-permute-start | bytes 387080 | tf_op jit(solution)/shard_map/ppermute | solution.py:43
  81.7 11.4 %collective-permute-start.2 = (f32[3,24,448]{2,1,0:T(8,128)}, f32[3,24,448]{2,1,0:T(8,128)}, u32[]{:S(2)}, u32[]{:S(2)}) collective-permute-start(f32[3,24,448]{2,1,0:T(8,128)} %get-tuple-element.9), channel_id=1, source_target_pairs={{0,3},{1,0},{2,1},{3,2},{4,7},{5,4},{6,5},{7,6},{8,11},{9,8},{10,9... | collective-permute-start | bytes 387080 | tf_op jit(solution)/shard_map/ppermute | solution.py:43
  87.6 10.2 %collective-permute-start.1 = (f32[3,24,448]{2,1,0:T(8,128)}, f32[3,24,448]{2,1,0:T(8,128)}, u32[]{:S(2)}, u32[]{:S(2)}) collective-permute-start(f32[3,24,448]{2,1,0:T(8,128)} %get-tuple-element.10), channel_id=1, source_target_pairs={{0,2},{1,3},{2,0},{3,1},{4,6},{5,7},{6,4},{7,5},{8,10},{9,11},{10,... | collective-permute-start | bytes 387080 | tf_op jit(solution)/shard_map/ppermute | solution.py:43
  99.0 22.5 %collective-permute-start.4 = (bf16[3,24,448]{2,1,0:T(8,128)(2,1)S(1)}, bf16[3,24,448]{2,1,0:T(8,128)(2,1)S(1)}, u32[]{:S(2)}, u32[]{:S(2)}) collective-permute-start(bf16[3,24,448]{2,1,0:T(8,128)(2,1)S(1)} %get-tuple-element.19), channel_id=1, source_target_pairs={{0,2},{1,3},{2,0},{3,1},{4,6},{5,7},{6,4},{7,5},{8,10},{9,11},{10,... | collective-permute-start | bytes 193544 | tf_op jit(solution)/shard_map/ppermute | solution.py:50
  105.6 18.4 %collective-permute-start.3 = (bf16[3,24,448]{2,1,0:T(8,128)(2,1)S(1)}, bf16[3,24,448]{2,1,0:T(8,128)(2,1)}, u32[]{:S(2)}, u32[]{:S(2)}) collective-permute-start(bf16[3,24,448]{2,1,0:T(8,128)(2,1)S(1)} %get-tuple-element.19), channel_id=1, source_target_pairs={{0,3},{1,0},{2,1},{3,2},{4,7},{5,4},{6,5},{7,6},{8,11},{9,8},{10,9... | collective-permute-start | bytes 193544 | tf_op jit(solution)/shard_map/ppermute | solution.py:50
  107.5 16.5 %collective-permute-start.5 = (bf16[3,24,448]{2,1,0:T(8,128)(2,1)S(1)}, bf16[3,24,448]{2,1,0:T(8,128)(2,1)}, u32[]{:S(2)}, u32[]{:S(2)}) collective-permute-start(bf16[3,24,448]{2,1,0:T(8,128)(2,1)S(1)} %get-tuple-element.19), channel_id=1, source_target_pairs={{0,1},{1,2},{2,3},{3,0},{4,5},{5,6},{6,7},{7,4},{8,9},{9,10},{10,1... | collective-permute-start | bytes 193544 | tf_op jit(solution)/shard_map/ppermute | solution.py:50
  114.0 16.6 %collective-permute-start.7 = (f32[3,24,448]{2,1,0:T(8,128)S(1)}, f32[3,24,448]{2,1,0:T(8,128)S(1)}, u32[]{:S(2)}, u32[]{:S(2)}) collective-permute-start(f32[3,24,448]{2,1,0:T(8,128)S(1)} %get-tuple-element.5), channel_id=1, source_target_pairs={{0,1},{1,2},{2,3},{3,0},{4,5},{5,6},{6,7},{7,4},{8,9},{9,10},{10,1... | collective-permute-start | bytes 387080 | tf_op jit(solution)/shard_map/ppermute | solution.py:43
  116.7 13.9 %collective-permute-start.9 = (f32[3,24,448]{2,1,0:T(8,128)S(1)}, f32[3,24,448]{2,1,0:T(8,128)S(1)}, u32[]{:S(2)}, u32[]{:S(2)}) collective-permute-start(f32[3,24,448]{2,1,0:T(8,128)S(1)} %get-tuple-element.6), channel_id=1, source_target_pairs={{0,3},{1,0},{2,1},{3,2},{4,7},{5,4},{6,5},{7,6},{8,11},{9,8},{10,9... | collective-permute-start | bytes 387080 | tf_op jit(solution)/shard_map/ppermute | solution.py:43
  121.4 12.4 %collective-permute-start.8 = (f32[3,24,448]{2,1,0:T(8,128)S(1)}, f32[3,24,448]{2,1,0:T(8,128)S(1)}, u32[]{:S(2)}, u32[]{:S(2)}) collective-permute-start(f32[3,24,448]{2,1,0:T(8,128)S(1)} %get-tuple-element.7), channel_id=1, source_target_pairs={{0,2},{1,3},{2,0},{3,1},{4,6},{5,7},{6,4},{7,5},{8,10},{9,11},{10,... | collective-permute-start | bytes 387080 | tf_op jit(solution)/shard_map/ppermute | solution.py:43
  126.5 23.8 %all-to-all-start.2 = ((bf16[3,4,96,448]{3,2,0,1:T(8,128)(2,1)}), bf16[3,4,96,448]{3,2,0,1:T(8,128)(2,1)S(1)}, u32[]{:S(2)}, u32[]{:S(2)}) async-start(bf16[3,4,96,448]{3,2,0,1:T(8,128)(2,1)} %broadcast_in_dim.22), calls=%async_computation.2 | async-start | bytes 2359296 | tf_op jit(solution)/shard_map/all_to_all | solution.py:32
  134.8 9.7 %collective-permute-start.11 = (bf16[3,24,448]{2,1,0:T(8,128)(2,1)S(1)}, bf16[3,24,448]{2,1,0:T(8,128)(2,1)S(1)}, u32[]{:S(2)}, u32[]{:S(2)}) collective-permute-start(bf16[3,24,448]{2,1,0:T(8,128)(2,1)S(1)} %get-tuple-element.17), channel_id=1, source_target_pairs={{0,2},{1,3},{2,0},{3,1},{4,6},{5,7},{6,4},{7,5},{8,10},{9,11},{10,... | collective-permute-start | bytes 193544 | tf_op jit(solution)/shard_map/ppermute | solution.py:50
  138.4 6.9 %collective-permute-start.10 = (bf16[3,24,448]{2,1,0:T(8,128)(2,1)S(1)}, bf16[3,24,448]{2,1,0:T(8,128)(2,1)S(1)}, u32[]{:S(2)}, u32[]{:S(2)}) collective-permute-start(bf16[3,24,448]{2,1,0:T(8,128)(2,1)S(1)} %get-tuple-element.17), channel_id=1, source_target_pairs={{0,3},{1,0},{2,1},{3,2},{4,7},{5,4},{6,5},{7,6},{8,11},{9,8},{10,9... | collective-permute-start | bytes 193544 | tf_op jit(solution)/shard_map/ppermute | solution.py:50
  141.9 8.0 %collective-permute-start.12 = (bf16[3,24,448]{2,1,0:T(8,128)(2,1)S(1)}, bf16[3,24,448]{2,1,0:T(8,128)(2,1)S(1)}, u32[]{:S(2)}, u32[]{:S(2)}) collective-permute-start(bf16[3,24,448]{2,1,0:T(8,128)(2,1)S(1)} %get-tuple-element.17), channel_id=1, source_target_pairs={{0,1},{1,2},{2,3},{3,0},{4,5},{5,6},{6,7},{7,4},{8,9},{9,10},{10,1... | collective-permute-start | bytes 193544 | tf_op jit(solution)/shard_map/ppermute | solution.py:50
  151.4 15.5 %all-to-all-start.4 = ((bf16[3,4,96,448]{3,2,0,1:T(8,128)(2,1)}), bf16[3,4,96,448]{3,2,0,1:T(8,128)(2,1)}, u32[]{:S(2)}, u32[]{:S(2)}) async-start(bf16[3,4,96,448]{3,2,0,1:T(8,128)(2,1)} %broadcast_in_dim.24), calls=%async_computation.4 | async-start | bytes 2359296 | tf_op jit(solution)/shard_map/all_to_all | solution.py:32
  169.6 10.8 %collective-permute-start.13 = (f32[384,512]{1,0:T(8,128)S(1)}, f32[384,512]{1,0:T(8,128)S(1)}, u32[]{:S(2)}, u32[]{:S(2)}) collective-permute-start(f32[384,512]{1,0:T(8,128)S(1)} %slice.83), channel_id=1, source_target_pairs={{0,16},{16,0},{1,17},{17,1},{2,18},{18,2},{3,19},{19,3},{4,20},{20... | collective-permute-start | bytes 2359304 | tf_op jit(solution)/shard_map/ppermute | solution.py:97
  181.4 31.0 %all-to-all-start.5 = ((f32[16,24,512]{2,1,0:T(8,128)}), f32[16,24,512]{2,1,0:T(8,128)}, u32[]{:S(2)}, u32[]{:S(2)}) async-start(f32[16,24,512]{2,1,0:T(8,128)} %bitcast.88), calls=%async_computation.5 | async-start | bytes 1572864 | tf_op jit(solution)/shard_map/all_to_all | solution.py:25
  191.6 2.6 %copy-start.2 = (bf16[16,24,1024]{2,1,0:T(8,128)(2,1)S(1)}, bf16[16,24,1024]{2,1,0:T(8,128)(2,1)}, u32[]{:S(2)}) copy-start(bf16[16,24,1024]{2,1,0:T(8,128)(2,1)} %copy-done.1) | copy-start | bytes 2359300
  191.6 2.6 %copy-start.4 = (bf16[384,1024]{1,0:T(8,128)(2,1)S(1)}, bf16[384,1024]{1,0:T(8,128)(2,1)}, u32[]{:S(2)}) copy-start(bf16[384,1024]{1,0:T(8,128)(2,1)} %copy-done.3) | copy-start | bytes 2359300

commit v14 on v13

--- a/solution.py
+++ b/solution.py
@@ -76,8 +76,11 @@
         p = scatter_permute(p, "zh", nzh, 1)
         d = jnp.stack(swiglu_grads(p[0], p[1], p[2]))
         d = gather_permute(d, "zh", nzh, 1)
-        chunks.append(gather_a2a(d, "x", nx, 1))
-    deltas = jnp.concatenate(chunks, 1)
+        d = jnp.broadcast_to(d[None], (nx,) + d.shape)
+        chunks.append(lax.all_to_all(d, "x", 0, 0, tiled=True))
+    deltas = jnp.stack(
+        [jnp.concatenate([c[:, k].reshape((-1,) + c.shape[3:]) for c in chunks], 0) for k in range(3)]
+    )
     both = jnp.concatenate(parts_in, 0)
     all_tokens, all_grads = both[:, :width], both[:, width:]
     hidden, gate_delta, up_delta = deltas[0], deltas[1], deltas[2]

time: 216 us -> 215 us (level)
  local copies, waits for them, and re-layouts: 10.3 us -> 12.9 us
    broadcast_in_dim x0 -> x2, local copies, waits for them, and re-layouts: none -> 2.28 us  [local(): d = jnp.broadcast_to(d[None], (nx,) + d.shape)]
    broadcast_in_dim x3 -> x1, local copies, waits for them, and re-layouts: 2.36 us -> 0.08 us  [gather_a2a(): jnp.broadcast_to(jnp.expand_dims(v, dim), shape[:dim] + (n,) + shape[dim:])]
    unnamed x14 -> x36, local copies, waits for them, and re-layouts: 0.18 us -> 2.39 us
  transfers between devices with their start and end apart: 19 -> 19, of which waited for: 9 -> 9; matrix products, arithmetic and copies ran while one was open for 9% -> 10% of each run, Pallas kernels for 0% -> 0%
where the time goes in v14:
time: 215 us; the launch traced here: 213 us
  starting transfers between devices  89 us (41%)
  waiting for transfers between devices  59.4 us (28%)
  blocking collectives  31.5 us (15%)
  local copies, waits for them, and re-layouts  12.9 us (6%)
  other arithmetic  10.8 us (5%)
  matrix products  8.54 us (4%)
    all_to_all x1, blocking collectives, gather_a2a(): v = lax.all_to_all(v, axis_name, dim, dim, tiled=True)  31.5 us
    ppermute x6, starting transfers between devices, scatter_permute(): lax.ppermute(part, axis_name, [(j, (j + k) % n) for j in range(n)])  27 us
    ppermute x6, starting transfers between devices, gather_permute(): lax.ppermute(v, axis_name, [(j, (j + k) % n) for j in range(n)])  22.6 us
    all_to_all x2, waiting for transfers between devices, local(): p = lax.all_to_all(p, 'x', 0, 0, tiled=True).sum(0)  16.6 us
    all_to_all x1, waiting for transfers between devices, scatter_sum(): v = lax.all_to_all(v, axis_name, dim, dim, tiled=True)  15.7 us
    all_to_all x2, waiting for transfers between devices, local(): chunks.append(lax.all_to_all(d, 'x', 0, 0, tiled=True))  9.45 us
    all_to_all x1, starting transfers between devices, scatter_sum(): v = lax.all_to_all(v, axis_name, dim, dim, tiled=True)  9.13 us
    ppermute x1, starting transfers between devices, local(): result = result[:half] + lax.ppermute(result[half:], 'c', swap)  9.01 us
  transfers between devices with their start and end apart: 19, of which 9 were waited for; matrix products, arithmetic and copies ran while one was open for 10% of the time, Pallas kernels for 0%

profile of v14, /device:TPU:1, one launch (start us, length us, event | category | flops | bytes accessed | tf_op | source)
XLA Modules:
  0.0 213.3 jit_solution(8519286092106938892)
XLA Ops:
  0.7 0.8 pad_maximum_fusion.12
  1.6 31.5 %all_to_all.30 = bf16[16,24,1024]{2,1,0:T(8,128)(2,1)S(1)} all-to-all(bf16[16,24,1024]{2,1,0:T(8,128)(2,1)S(1)} %broadcast_in_dim.20), channel_id=1, replica_groups=mesh['y'=8,'zl'=2,'c'=2,'x'=4,'zh'=4] {'y','zl'}, dimensions={0} | all-to-all | bytes 1572864 | tf_op jit(solution)/shard_map/all_to_all | solution.py:32
  34.6 1.6 copy.19
  36.2 4.0 %all-to-all-start.1 = ((f32[4,3,96,448]{3,2,1,0:T(8,128)}), f32[4,3,96,448]{3,2,1,0:T(8,128)S(1)}, u32[]{:S(2)}, u32[]{:S(2)}) async-start(f32[4,3,96,448]{3,2,1,0:T(8,128)} %copy.19), calls=%async_computation.1 | async-start | bytes 4718592 | tf_op jit(solution)/shard_map/all_to_all | solution.py:75
  40.2 4.7 %collective-permute-start.6 = (bf16[384,1024]{1,0:T(8,128)(2,1)}, bf16[384,1024]{1,0:T(8,128)(2,1)S(1)}, u32[]{:S(2)}, u32[]{:S(2)}) collective-permute-start(bf16[384,1024]{1,0:T(8,128)(2,1)} %bitcast.64), channel_id=1, source_target_pairs={{0,16},{16,0},{1,17},{17,1},{2,18},{18,2},{3,19},{19,3},{4,20},{20... | collective-permute-start | bytes 2359304 | tf_op jit(solution)/shard_map/ppermute | solution.py:65
  44.9 2.1 collective-permute-done.6
  48.5 1.6 copy.23
  50.2 16.6 %all-to-all-done.1 = f32[4,3,96,448]{3,2,1,0:T(8,128)S(1)} async-done(((f32[4,3,96,448]{3,2,1,0:T(8,128)}), f32[4,3,96,448]{3,2,1,0:T(8,128)S(1)}, u32[]{:S(2)}, u32[]{:S(2)}) %all-to-all-start.1) | async-done | bytes 2064416 | tf_op jit(solution)/shard_map/all_to_all | solution.py:75
  66.8 1.4 copy-done.1
  68.2 3.6 %all-to-all-start.3 = ((f32[4,3,96,448]{3,2,1,0:T(8,128)}), f32[4,3,96,448]{3,2,1,0:T(8,128)S(1)}, u32[]{:S(2)}, u32[]{:S(2)}) async-start(f32[4,3,96,448]{3,2,1,0:T(8,128)} %copy.23), calls=%async_computation.3 | async-start | bytes 4718592 | tf_op jit(solution)/shard_map/all_to_all | solution.py:75
  71.9 2.8 %reduce_sum.27 = f32[3,96,448]{2,1,0:T(8,128)} reduce(f32[4,3,96,448]{3,2,1,0:T(8,128)} %copy-done.1, f32[]{:T(128)} %constant.52.clone.1), dimensions={0}, to_apply=%region_0.0 | reduce | flops 387072 | bytes 2580484 | tf_op jit(solution)/shard_map/reduce_sum | solution.py:75
  74.7 1.8 constant_dynamic-slice_fusion.5
  76.5 5.8 %collective-permute-start = (f32[3,24,448]{2,1,0:T(8,128)}, f32[3,24,448]{2,1,0:T(8,128)S(1)}, u32[]{:S(2)}, u32[]{:S(2)}) collective-permute-start(f32[3,24,448]{2,1,0:T(8,128)} %get-tuple-element.11), channel_id=1, source_target_pairs={{0,1},{1,2},{2,3},{3,0},{4,5},{5,6},{6,7},{7,4},{8,9},{9,10},{10,1... | collective-permute-start | bytes 387080 | tf_op jit(solution)/shard_map/ppermute | solution.py:43
  82.3 5.9 %collective-permute-start.2 = (f32[3,24,448]{2,1,0:T(8,128)}, f32[3,24,448]{2,1,0:T(8,128)}, u32[]{:S(2)}, u32[]{:S(2)}) collective-permute-start(f32[3,24,448]{2,1,0:T(8,128)} %get-tuple-element.12), channel_id=1, source_target_pairs={{0,3},{1,0},{2,1},{3,2},{4,7},{5,4},{6,5},{7,6},{8,11},{9,8},{10,9... | collective-permute-start | bytes 387080 | tf_op jit(solution)/shard_map/ppermute | solution.py:43
  88.2 5.4 %collective-permute-start.1 = (f32[3,24,448]{2,1,0:T(8,128)}, f32[3,24,448]{2,1,0:T(8,128)}, u32[]{:S(2)}, u32[]{:S(2)}) collective-permute-start(f32[3,24,448]{2,1,0:T(8,128)} %get-tuple-element.13), channel_id=1, source_target_pairs={{0,2},{1,3},{2,0},{3,1},{4,6},{5,7},{6,4},{7,5},{8,10},{9,11},{10,... | collective-permute-start | bytes 387080 | tf_op jit(solution)/shard_map/ppermute | solution.py:43
  93.7 4.7 %collective-permute-done.1 = f32[3,24,448]{2,1,0:T(8,128)} collective-permute-done((f32[3,24,448]{2,1,0:T(8,128)}, f32[3,24,448]{2,1,0:T(8,128)}, u32[]{:S(2)}, u32[]{:S(2)}) %collective-permute-start.1) | collective-permute-done | bytes 129056 | tf_op jit(solution)/shard_map/ppermute | solution.py:43
  98.4 1.1 add_add_fusion.1
  99.5 6.7 %collective-permute-start.4 = (bf16[3,24,448]{2,1,0:T(8,128)(2,1)S(1)}, bf16[3,24,448]{2,1,0:T(8,128)(2,1)S(1)}, u32[]{:S(2)}, u32[]{:S(2)}) collective-permute-start(bf16[3,24,448]{2,1,0:T(8,128)(2,1)S(1)} %get-tuple-element.23), channel_id=1, source_target_pairs={{0,2},{1,3},{2,0},{3,1},{4,6},{5,7},{6,4},{7,5},{8,10},{9,11},{10,... | collective-permute-start | bytes 193544 | tf_op jit(solution)/shard_map/ppermute | solution.py:50
  106.2 1.9 collective-permute-start.3
  108.2 4.3 %collective-permute-start.5 = (bf16[3,24,448]{2,1,0:T(8,128)(2,1)S(1)}, bf16[3,24,448]{2,1,0:T(8,128)(2,1)}, u32[]{:S(2)}, u32[]{:S(2)}) collective-permute-start(bf16[3,24,448]{2,1,0:T(8,128)(2,1)S(1)} %get-tuple-element.23), channel_id=1, source_target_pairs={{0,1},{1,2},{2,3},{3,0},{4,5},{5,6},{6,7},{7,4},{8,9},{9,10},{10,1... | collective-permute-start | bytes 193544 | tf_op jit(solution)/shard_map/ppermute | solution.py:50
  112.4 1.1 reduce_sum.28
  113.6 1.1 constant_dynamic-slice_fusion.2
  114.7 2.7 %collective-permute-start.7 = (f32[3,24,448]{2,1,0:T(8,128)S(1)}, f32[3,24,448]{2,1,0:T(8,128)S(1)}, u32[]{:S(2)}, u32[]{:S(2)}) collective-permute-start(f32[3,24,448]{2,1,0:T(8,128)S(1)} %get-tuple-element.14), channel_id=1, source_target_pairs={{0,1},{1,2},{2,3},{3,0},{4,5},{5,6},{6,7},{7,4},{8,9},{9,10},{10,1... | collective-permute-start | bytes 387080 | tf_op jit(solution)/shard_map/ppermute | solution.py:43
  117.4 4.6 %collective-permute-start.9 = (f32[3,24,448]{2,1,0:T(8,128)S(1)}, f32[3,24,448]{2,1,0:T(8,128)S(1)}, u32[]{:S(2)}, u32[]{:S(2)}) collective-permute-start(f32[3,24,448]{2,1,0:T(8,128)S(1)} %get-tuple-element.15), channel_id=1, source_target_pairs={{0,3},{1,0},{2,1},{3,2},{4,7},{5,4},{6,5},{7,6},{8,11},{9,8},{10,9... | collective-permute-start | bytes 387080 | tf_op jit(solution)/shard_map/ppermute | solution.py:43
  122.1 2.5 %collective-permute-start.8 = (f32[3,24,448]{2,1,0:T(8,128)S(1)}, f32[3,24,448]{2,1,0:T(8,128)S(1)}, u32[]{:S(2)}, u32[]{:S(2)}) collective-permute-start(f32[3,24,448]{2,1,0:T(8,128)S(1)} %get-tuple-element.16), channel_id=1, source_target_pairs={{0,2},{1,3},{2,0},{3,1},{4,6},{5,7},{6,4},{7,5},{8,10},{9,11},{10,... | collective-permute-start | bytes 387080 | tf_op jit(solution)/shard_map/ppermute | solution.py:43
  124.6 1.4 fusion.29
  126.0 1.1 broadcast_in_dim.22
  127.2 4.4 %all-to-all-start.2 = ((bf16[4,3,96,448]{3,2,1,0:T(8,128)(2,1)}), bf16[4,3,96,448]{3,2,1,0:T(8,128)(2,1)S(1)}, u32[]{:S(2)}, u32[]{:S(2)}) async-start(bf16[4,3,96,448]{3,2,1,0:T(8,128)(2,1)} %broadcast_in_dim.22), calls=%async_computation.2 | async-start | bytes 2359296 | tf_op jit(solution)/shard_map/all_to_all | solution.py:80
  131.5 3.0 %collective-permute-done.8 = f32[3,24,448]{2,1,0:T(8,128)S(1)} collective-permute-done((f32[3,24,448]{2,1,0:T(8,128)S(1)}, f32[3,24,448]{2,1,0:T(8,128)S(1)}, u32[]{:S(2)}, u32[]{:S(2)}) %collective-permute-start.8) | collective-permute-done | bytes 129056 | tf_op jit(solution)/shard_map/ppermute | solution.py:43
  134.5 1.0 add_add_fusion
  135.5 3.5 %collective-permute-start.11 = (bf16[3,24,448]{2,1,0:T(8,128)(2,1)S(1)}, bf16[3,24,448]{2,1,0:T(8,128)(2,1)S(1)}, u32[]{:S(2)}, u32[]{:S(2)}) collective-permute-start(bf16[3,24,448]{2,1,0:T(8,128)(2,1)S(1)} %get-tuple-element.25), channel_id=1, source_target_pairs={{0,2},{1,3},{2,0},{3,1},{4,6},{5,7},{6,4},{7,5},{8,10},{9,11},{10,... | collective-permute-start | bytes 193544 | tf_op jit(solution)/shard_map/ppermute | solution.py:50
  139.0 4.1 %collective-permute-start.10 = (bf16[3,24,448]{2,1,0:T(8,128)(2,1)S(1)}, bf16[3,24,448]{2,1,0:T(8,128)(2,1)S(1)}, u32[]{:S(2)}, u32[]{:S(2)}) collective-permute-start(bf16[3,24,448]{2,1,0:T(8,128)(2,1)S(1)} %get-tuple-element.25), channel_id=1, source_target_pairs={{0,3},{1,0},{2,1},{3,2},{4,7},{5,4},{6,5},{7,6},{8,11},{9,8},{10,9... | collective-permute-start | bytes 193544 | tf_op jit(solution)/shard_map/ppermute | solution.py:50
  143.1 2.1 collective-permute-start.12
  145.3 0.9 collective-permute-done.10
  146.1 5.1 %collective-permute-done.12 = bf16[3,24,448]{2,1,0:T(8,128)(2,1)S(1)} collective-permute-done((bf16[3,24,448]{2,1,0:T(8,128)(2,1)S(1)}, bf16[3,24,448]{2,1,0:T(8,128)(2,1)S(1)}, u32[]{:S(2)}, u32[]{:S(2)}) %collective-permute-start.12) | collective-permute-done | bytes 64544 | tf_op jit(solution)/shard_map/ppermute | solution.py:50
  151.7 1.1 broadcast_in_dim.24
  152.9 4.6 %all-to-all-start.4 = ((bf16[4,3,96,448]{3,2,1,0:T(8,128)(2,1)}), bf16[4,3,96,448]{3,2,1,0:T(8,128)(2,1)S(1)}, u32[]{:S(2)}, u32[]{:S(2)}) async-start(bf16[4,3,96,448]{3,2,1,0:T(8,128)(2,1)} %broadcast_in_dim.24), calls=%async_computation.4 | async-start | bytes 2359296 | tf_op jit(solution)/shard_map/all_to_all | solution.py:80
  157.5 1.0 fusion.44
  158.5 9.4 %all-to-all-done.4 = bf16[4,3,96,448]{3,2,1,0:T(8,128)(2,1)S(1)} async-done(((bf16[4,3,96,448]{3,2,1,0:T(8,128)(2,1)}), bf16[4,3,96,448]{3,2,1,0:T(8,128)(2,1)S(1)}, u32[]{:S(2)}, u32[]{:S(2)}) %all-to-all-start.4) | async-done | bytes 1032224 | tf_op jit(solution)/shard_map/all_to_all | solution.py:80
  168.0 0.8 fusion.45
  170.8 9.0 %collective-permute-start.13 = (f32[384,512]{1,0:T(8,128)S(1)}, f32[384,512]{1,0:T(8,128)S(1)}, u32[]{:S(2)}, u32[]{:S(2)}) collective-permute-start(f32[384,512]{1,0:T(8,128)S(1)} %slice.95), channel_id=1, source_target_pairs={{0,16},{16,0},{1,17},{17,1},{2,18},{18,2},{3,19},{19,3},{4,20},{20... | collective-permute-start | bytes 2359304 | tf_op jit(solution)/shard_map/ppermute | solution.py:100
  179.8 1.9 collective-permute-done.13
  181.7 1.0 slice_add_fusion
  182.7 9.1 %all-to-all-start.5 = ((f32[16,24,512]{2,1,0:T(8,128)}), f32[16,24,512]{2,1,0:T(8,128)S(1)}, u32[]{:S(2)}, u32[]{:S(2)}) async-start(f32[16,24,512]{2,1,0:T(8,128)} %bitcast.31), calls=%async_computation.5 | async-start | bytes 1572864 | tf_op jit(solution)/shard_map/all_to_all | solution.py:25
  191.9 2.4 %convolution_convert_fusion.1 = bf16[512,448]{0,1:T(8,128)(2,1)} fusion(bf16[384,448]{1,0:T(8,128)(2,1)} %bitcast.74, bf16[384,448]{1,0:T(8,128)(2,1)S(1)} %bitcast.72, bf16[384,1024]{1,0:T(8,128)(2,1)S(1)} %bitcast.65, bf16[384,1024]{1,0:T(8,128)(2,1)S(1)} %copy-done.8), kind=kOutput, calls=%fused_computation.12 | convolution fusion | flops 355500032 | bytes 2719744 | tf_op jit(solution)/shard_map/dot_general | solution.py:93
  194.3 1.3 convolution_convert_fusion.2
  195.7 1.3 convolution_convert_fusion
  197.0 15.7 %all-to-all-done.5 = f32[16,24,512]{2,1,0:T(8,128)S(1)} async-done(((f32[16,24,512]{2,1,0:T(8,128)}), f32[16,24,512]{2,1,0:T(8,128)S(1)}, u32[]{:S(2)}, u32[]{:S(2)}) %all-to-all-start.5) | async-done | bytes 786464 | tf_op jit(solution)/shard_map/all_to_all | solution.py:25
  (64 shorter events, 6.2 us)
Async XLA Ops:
  0.6 33.3 %copy-start = (bf16[512,448]{0,1:T(8,128)(2,1)S(1)}, bf16[512,448]{0,1:T(8,128)(2,1)}, u32[]{:S(2)}) copy-start(bf16[512,448]{0,1:T(8,128)(2,1)} %param.9) | copy-start | bytes 1376260
  0.6 32.4 %copy-start.4 = (bf16[512,448]{0,1:T(8,128)(2,1)S(1)}, bf16[512,448]{0,1:T(8,128)(2,1)}, u32[]{:S(2)}) copy-start(bf16[512,448]{0,1:T(8,128)(2,1)} %param.10) | copy-start | bytes 1376260
  1.6 31.9 %copy-start.5 = (bf16[448,512]{1,0:T(8,128)(2,1)S(1)}, bf16[448,512]{1,0:T(8,128)(2,1)}, u32[]{:S(2)}) copy-start(bf16[448,512]{1,0:T(8,128)(2,1)} %param.11) | copy-start | bytes 1376260
  33.1 0.9 copy-start.2
  36.2 30.6 %all-to-all-start.1 = ((f32[4,3,96,448]{3,2,1,0:T(8,128)}), f32[4,3,96,448]{3,2,1,0:T(8,128)S(1)}, u32[]{:S(2)}, u32[]{:S(2)}) async-start(f32[4,3,96,448]{3,2,1,0:T(8,128)} %copy.19), calls=%async_computation.1 | async-start | bytes 4718592 | tf_op jit(solution)/shard_map/all_to_all | solution.py:75
  40.2 7.2 %copy-start.6 = (bf16[448,512]{1,0:T(8,128)(2,1)S(1)}, bf16[448,512]{1,0:T(8,128)(2,1)}, u32[]{:S(2)}) copy-start(bf16[448,512]{1,0:T(8,128)(2,1)} %param.11) | copy-start | bytes 1376260
  40.2 6.8 %collective-permute-start.6 = (bf16[384,1024]{1,0:T(8,128)(2,1)}, bf16[384,1024]{1,0:T(8,128)(2,1)S(1)}, u32[]{:S(2)}, u32[]{:S(2)}) collective-permute-start(bf16[384,1024]{1,0:T(8,128)(2,1)} %bitcast.64), channel_id=1, source_target_pairs={{0,16},{16,0},{1,17},{17,1},{2,18},{18,2},{3,19},{19,3},{4,20},{20... | collective-permute-start | bytes 2359304 | tf_op jit(solution)/shard_map/ppermute | solution.py:65
  47.0 0.9 copy-start.7
  66.8 1.4 copy-start.1
  68.2 44.2 %all-to-all-start.3 = ((f32[4,3,96,448]{3,2,1,0:T(8,128)}), f32[4,3,96,448]{3,2,1,0:T(8,128)S(1)}, u32[]{:S(2)}, u32[]{:S(2)}) async-start(f32[4,3,96,448]{3,2,1,0:T(8,128)} %copy.23), calls=%async_computation.3 | async-start | bytes 4718592 | tf_op jit(solution)/shard_map/all_to_all | solution.py:75
  76.5 17.2 %collective-permute-start = (f32[3,24,448]{2,1,0:T(8,128)}, f32[3,24,448]{2,1,0:T(8,128)S(1)}, u32[]{:S(2)}, u32[]{:S(2)}) collective-permute-start(f32[3,24,448]{2,1,0:T(8,128)} %get-tuple-element.11), channel_id=1, source_target_pairs={{0,1},{1,2},{2,3},{3,0},{4,5},{5,6},{6,7},{7,4},{8,9},{9,10},{10,1... | collective-permute-start | bytes 387080 | tf_op jit(solution)/shard_map/ppermute | solution.py:43
  82.3 11.4 %collective-permute-start.2 = (f32[3,24,448]{2,1,0:T(8,128)}, f32[3,24,448]{2,1,0:T(8,128)}, u32[]{:S(2)}, u32[]{:S(2)}) collective-permute-start(f32[3,24,448]{2,1,0:T(8,128)} %get-tuple-element.12), channel_id=1, source_target_pairs={{0,3},{1,0},{2,1},{3,2},{4,7},{5,4},{6,5},{7,6},{8,11},{9,8},{10,9... | collective-permute-start | bytes 387080 | tf_op jit(solution)/shard_map/ppermute | solution.py:43
  88.2 10.2 %collective-permute-start.1 = (f32[3,24,448]{2,1,0:T(8,128)}, f32[3,24,448]{2,1,0:T(8,128)}, u32[]{:S(2)}, u32[]{:S(2)}) collective-permute-start(f32[3,24,448]{2,1,0:T(8,128)} %get-tuple-element.13), channel_id=1, source_target_pairs={{0,2},{1,3},{2,0},{3,1},{4,6},{5,7},{6,4},{7,5},{8,10},{9,11},{10,... | collective-permute-start | bytes 387080 | tf_op jit(solution)/shard_map/ppermute | solution.py:43
  99.5 22.5 %collective-permute-start.4 = (bf16[3,24,448]{2,1,0:T(8,128)(2,1)S(1)}, bf16[3,24,448]{2,1,0:T(8,128)(2,1)S(1)}, u32[]{:S(2)}, u32[]{:S(2)}) collective-permute-start(bf16[3,24,448]{2,1,0:T(8,128)(2,1)S(1)} %get-tuple-element.23), channel_id=1, source_target_pairs={{0,2},{1,3},{2,0},{3,1},{4,6},{5,7},{6,4},{7,5},{8,10},{9,11},{10,... | collective-permute-start | bytes 193544 | tf_op jit(solution)/shard_map/ppermute | solution.py:50
  106.2 18.4 %collective-permute-start.3 = (bf16[3,24,448]{2,1,0:T(8,128)(2,1)S(1)}, bf16[3,24,448]{2,1,0:T(8,128)(2,1)}, u32[]{:S(2)}, u32[]{:S(2)}) collective-permute-start(bf16[3,24,448]{2,1,0:T(8,128)(2,1)S(1)} %get-tuple-element.23), channel_id=1, source_target_pairs={{0,3},{1,0},{2,1},{3,2},{4,7},{5,4},{6,5},{7,6},{8,11},{9,8},{10,9... | collective-permute-start | bytes 193544 | tf_op jit(solution)/shard_map/ppermute | solution.py:50
  108.2 16.4 %collective-permute-start.5 = (bf16[3,24,448]{2,1,0:T(8,128)(2,1)S(1)}, bf16[3,24,448]{2,1,0:T(8,128)(2,1)}, u32[]{:S(2)}, u32[]{:S(2)}) collective-permute-start(bf16[3,24,448]{2,1,0:T(8,128)(2,1)S(1)} %get-tuple-element.23), channel_id=1, source_target_pairs={{0,1},{1,2},{2,3},{3,0},{4,5},{5,6},{6,7},{7,4},{8,9},{9,10},{10,1... | collective-permute-start | bytes 193544 | tf_op jit(solution)/shard_map/ppermute | solution.py:50
  114.7 16.8 %collective-permute-start.7 = (f32[3,24,448]{2,1,0:T(8,128)S(1)}, f32[3,24,448]{2,1,0:T(8,128)S(1)}, u32[]{:S(2)}, u32[]{:S(2)}) collective-permute-start(f32[3,24,448]{2,1,0:T(8,128)S(1)} %get-tuple-element.14), channel_id=1, source_target_pairs={{0,1},{1,2},{2,3},{3,0},{4,5},{5,6},{6,7},{7,4},{8,9},{9,10},{10,1... | collective-permute-start | bytes 387080 | tf_op jit(solution)/shard_map/ppermute | solution.py:43
  117.4 14.1 %collective-permute-start.9 = (f32[3,24,448]{2,1,0:T(8,128)S(1)}, f32[3,24,448]{2,1,0:T(8,128)S(1)}, u32[]{:S(2)}, u32[]{:S(2)}) collective-permute-start(f32[3,24,448]{2,1,0:T(8,128)S(1)} %get-tuple-element.15), channel_id=1, source_target_pairs={{0,3},{1,0},{2,1},{3,2},{4,7},{5,4},{6,5},{7,6},{8,11},{9,8},{10,9... | collective-permute-start | bytes 387080 | tf_op jit(solution)/shard_map/ppermute | solution.py:43
  122.1 12.4 %collective-permute-start.8 = (f32[3,24,448]{2,1,0:T(8,128)S(1)}, f32[3,24,448]{2,1,0:T(8,128)S(1)}, u32[]{:S(2)}, u32[]{:S(2)}) collective-permute-start(f32[3,24,448]{2,1,0:T(8,128)S(1)} %get-tuple-element.16), channel_id=1, source_target_pairs={{0,2},{1,3},{2,0},{3,1},{4,6},{5,7},{6,4},{7,5},{8,10},{9,11},{10,... | collective-permute-start | bytes 387080 | tf_op jit(solution)/shard_map/ppermute | solution.py:43
  127.2 24.5 %all-to-all-start.2 = ((bf16[4,3,96,448]{3,2,1,0:T(8,128)(2,1)}), bf16[4,3,96,448]{3,2,1,0:T(8,128)(2,1)S(1)}, u32[]{:S(2)}, u32[]{:S(2)}) async-start(bf16[4,3,96,448]{3,2,1,0:T(8,128)(2,1)} %broadcast_in_dim.22), calls=%async_computation.2 | async-start | bytes 2359296 | tf_op jit(solution)/shard_map/all_to_all | solution.py:80
  135.5 9.7 %collective-permute-start.11 = (bf16[3,24,448]{2,1,0:T(8,128)(2,1)S(1)}, bf16[3,24,448]{2,1,0:T(8,128)(2,1)S(1)}, u32[]{:S(2)}, u32[]{:S(2)}) collective-permute-start(bf16[3,24,448]{2,1,0:T(8,128)(2,1)S(1)} %get-tuple-element.25), channel_id=1, source_target_pairs={{0,2},{1,3},{2,0},{3,1},{4,6},{5,7},{6,4},{7,5},{8,10},{9,11},{10,... | collective-permute-start | bytes 193544 | tf_op jit(solution)/shard_map/ppermute | solution.py:50
  139.0 7.1 %collective-permute-start.10 = (bf16[3,24,448]{2,1,0:T(8,128)(2,1)S(1)}, bf16[3,24,448]{2,1,0:T(8,128)(2,1)S(1)}, u32[]{:S(2)}, u32[]{:S(2)}) collective-permute-start(bf16[3,24,448]{2,1,0:T(8,128)(2,1)S(1)} %get-tuple-element.25), channel_id=1, source_target_pairs={{0,3},{1,0},{2,1},{3,2},{4,7},{5,4},{6,5},{7,6},{8,11},{9,8},{10,9... | collective-permute-start | bytes 193544 | tf_op jit(solution)/shard_map/ppermute | solution.py:50
  143.1 8.1 %collective-permute-start.12 = (bf16[3,24,448]{2,1,0:T(8,128)(2,1)S(1)}, bf16[3,24,448]{2,1,0:T(8,128)(2,1)S(1)}, u32[]{:S(2)}, u32[]{:S(2)}) collective-permute-start(bf16[3,24,448]{2,1,0:T(8,128)(2,1)S(1)} %get-tuple-element.25), channel_id=1, source_target_pairs={{0,1},{1,2},{2,3},{3,0},{4,5},{5,6},{6,7},{7,4},{8,9},{9,10},{10,1... | collective-permute-start | bytes 193544 | tf_op jit(solution)/shard_map/ppermute | solution.py:50
  152.9 15.1 %all-to-all-start.4 = ((bf16[4,3,96,448]{3,2,1,0:T(8,128)(2,1)}), bf16[4,3,96,448]{3,2,1,0:T(8,128)(2,1)S(1)}, u32[]{:S(2)}, u32[]{:S(2)}) async-start(bf16[4,3,96,448]{3,2,1,0:T(8,128)(2,1)} %broadcast_in_dim.24), calls=%async_computation.4 | async-start | bytes 2359296 | tf_op jit(solution)/shard_map/all_to_all | solution.py:80
  158.5 10.3 %copy-start.12 = (bf16[4,1,96,448]{3,2,1,0:T(8,128)(2,1)S(1)}, bf16[4,1,96,448]{3,2,1,0:T(8,128)(2,1)}, u32[]{:S(2)}) copy-start(bf16[4,1,96,448]{3,2,1,0:T(8,128)(2,1)} %get-tuple-element.7) | copy-start | bytes 1032196
  168.8 1.8 copy-start.11
  168.8 1.8 copy-start.14
  168.8 1.3 copy-start.9
  170.7 21.1 %copy-start.3 = (bf16[16,24,1024]{2,1,0:T(8,128)(2,1)S(1)}, bf16[16,24,1024]{2,1,0:T(8,128)(2,1)}, u32[]{:S(2)}) copy-start(bf16[16,24,1024]{2,1,0:T(8,128)(2,1)} %copy-done.2) | copy-start | bytes 2359300
  170.7 21.1 %copy-start.8 = (bf16[384,1024]{1,0:T(8,128)(2,1)S(1)}, bf16[384,1024]{1,0:T(8,128)(2,1)}, u32[]{:S(2)}) copy-start(bf16[384,1024]{1,0:T(8,128)(2,1)} %copy-done.7) | copy-start | bytes 2359300
  170.8 21.1 %copy-start.10 = (bf16[4,1,96,448]{3,2,1,0:T(8,128)(2,1)S(1)}, bf16[4,1,96,448]{3,2,1,0:T(8,128)(2,1)}, u32[]{:S(2)}) copy-start(bf16[4,1,96,448]{3,2,1,0:T(8,128)(2,1)} %get-tuple-element.6) | copy-start | bytes 1032196
  170.8 10.9 %collective-permute-start.13 = (f32[384,512]{1,0:T(8,128)S(1)}, f32[384,512]{1,0:T(8,128)S(1)}, u32[]{:S(2)}, u32[]{:S(2)}) collective-permute-start(f32[384,512]{1,0:T(8,128)S(1)} %slice.95), channel_id=1, source_target_pairs={{0,16},{16,0},{1,17},{17,1},{2,18},{18,2},{3,19},{19,3},{4,20},{20... | collective-permute-start | bytes 2359304 | tf_op jit(solution)/shard_map/ppermute | solution.py:100
  182.7 30.0 %all-to-all-start.5 = ((f32[16,24,512]{2,1,0:T(8,128)}), f32[16,24,512]{2,1,0:T(8,128)S(1)}, u32[]{:S(2)}, u32[]{:S(2)}) async-start(f32[16,24,512]{2,1,0:T(8,128)} %bitcast.31), calls=%async_computation.5 | async-start | bytes 1572864 | tf_op jit(solution)/shard_map/all_to_all | solution.py:25
  191.9 2.4 %copy-start.13 = (bf16[4,1,96,448]{3,2,1,0:T(8,128)(2,1)S(1)}, bf16[4,1,96,448]{3,2,1,0:T(8,128)(2,1)}, u32[]{:S(2)}) copy-start(bf16[4,1,96,448]{3,2,1,0:T(8,128)(2,1)} %get-tuple-element.7) | copy-start | bytes 1032196
  191.9 2.4 %copy-start.15 = (bf16[4,1,96,448]{3,2,1,0:T(8,128)(2,1)S(1)}, bf16[4,1,96,448]{3,2,1,0:T(8,128)(2,1)}, u32[]{:S(2)}) copy-start(bf16[4,1,96,448]{3,2,1,0:T(8,128)(2,1)} %copy-done.14) | copy-start | bytes 1032196
  194.3 1.4 copy-start.16
  194.3 1.4 copy-start.17

commit v15 on v13

--- a/solution.py
+++ b/solution.py
@@ -66,14 +66,14 @@
     width = tokens.shape[1]
     chunks = []
     for rows in parts_in:
-        rows = rows.reshape((nx, -1) + rows.shape[1:])
+        rows = rows.reshape((nx, nzh, -1) + rows.shape[1:])
         tok, grd = rows[..., :width], rows[..., width:]
-        gate_part = jnp.einsum("brd,dh->brh", tok, gate_weight, preferred_element_type=jnp.float32)
-        up_part = jnp.einsum("brd,dh->brh", tok, up_weight, preferred_element_type=jnp.float32)
-        hidden_part = jnp.einsum("brd,hd->brh", grd, down_weight, preferred_element_type=jnp.float32)
-        p = jnp.stack([gate_part, up_part, hidden_part], 1)
+        gate_part = jnp.einsum("bzrd,dh->bzrh", tok, gate_weight, preferred_element_type=jnp.float32)
+        up_part = jnp.einsum("bzrd,dh->bzrh", tok, up_weight, preferred_element_type=jnp.float32)
+        hidden_part = jnp.einsum("bzrd,hd->bzrh", grd, down_weight, preferred_element_type=jnp.float32)
+        p = jnp.stack([gate_part, up_part, hidden_part], 2)
         p = lax.all_to_all(p, "x", 0, 0, tiled=True).sum(0)
-        p = scatter_permute(p, "zh", nzh, 1)
+        p = scatter_permute(p, "zh", nzh, 0)[0]
         d = jnp.stack(swiglu_grads(p[0], p[1], p[2]))
         d = gather_permute(d, "zh", nzh, 1)
         chunks.append(gather_a2a(d, "x", nx, 1))

time: 216 us -> 232 us (1.074)
  waiting for transfers between devices: 60.6 us -> 77.1 us
    all_to_all x2, waiting for transfers between devices: 10.5 us -> 25.2 us  [gather_a2a(): v = lax.all_to_all(v, axis_name, dim, dim, tiled=True)]
    ppermute x6, waiting for transfers between devices: 7.93 us -> 11 us  [scatter_permute(): lax.ppermute(part, axis_name, [(j, (j + k) % n) for j in range(n)])]
    ppermute x6, starting transfers between devices: 27.1 us -> 29.6 us  [scatter_permute(): lax.ppermute(part, axis_name, [(j, (j + k) % n) for j in range(n)])]
  transfers between devices with their start and end apart: 19 -> 19, of which waited for: 9 -> 11; matrix products, arithmetic and copies ran while one was open for 9% -> 7% of each run, Pallas kernels for 0% -> 0%
where the time goes in v15:
time: 232 us; the launch traced here: 230 us
  starting transfers between devices  89.7 us (39%)
  waiting for transfers between devices  77.1 us (33%)
  blocking collectives  31.5 us (14%)
  other arithmetic  11.2 us (5%)
  local copies, waits for them, and re-layouts  10.4 us (4%)
  matrix products  8.71 us (4%)
    all_to_all x1, blocking collectives, gather_a2a(): v = lax.all_to_all(v, axis_name, dim, dim, tiled=True)  31.5 us
    ppermute x6, starting transfers between devices, scatter_permute(): lax.ppermute(part, axis_name, [(j, (j + k) % n) for j in range(n)])  29.6 us
    all_to_all x2, waiting for transfers between devices, gather_a2a(): v = lax.all_to_all(v, axis_name, dim, dim, tiled=True)  25.2 us
    ppermute x6, starting transfers between devices, gather_permute(): lax.ppermute(v, axis_name, [(j, (j + k) % n) for j in range(n)])  21.3 us
    all_to_all x2, waiting for transfers between devices, local(): p = lax.all_to_all(p, 'x', 0, 0, tiled=True).sum(0)  17.4 us
    all_to_all x1, waiting for transfers between devices, scatter_sum(): v = lax.all_to_all(v, axis_name, dim, dim, tiled=True)  15.6 us
    ppermute x6, waiting for transfers between devices, scatter_permute(): lax.ppermute(part, axis_name, [(j, (j + k) % n) for j in range(n)])  11 us
    all_to_all x2, starting transfers between devices, gather_a2a(): v = lax.all_to_all(v, axis_name, dim, dim, tiled=True)  9.86 us
  transfers between devices with their start and end apart: 19, of which 11 were waited for; matrix products, arithmetic and copies ran while one was open for 7% of the time, Pallas kernels for 0%

profile of v15, /device:TPU:1, one launch (start us, length us, event | category | flops | bytes accessed | tf_op | source)
XLA Modules:
  0.0 229.7 jit_solution(11490918146610501602)
XLA Ops:
  0.7 0.8 pad_maximum_fusion.7
  1.6 31.5 %all_to_all.30 = bf16[16,24,1024]{2,1,0:T(8,128)(2,1)S(1)} all-to-all(bf16[16,24,1024]{2,1,0:T(8,128)(2,1)S(1)} %broadcast_in_dim.20), channel_id=1, replica_groups=mesh['y'=8,'zl'=2,'c'=2,'x'=4,'zh'=4] {'y','zl'}, dimensions={0} | all-to-all | bytes 1572864 | tf_op jit(solution)/shard_map/all_to_all | solution.py:32
  34.5 1.7 copy.25
  36.3 4.5 %all-to-all-start.1 = ((f32[4,4,3,24,448]{4,3,1,2,0:T(8,128)}), f32[4,4,3,24,448]{4,3,1,2,0:T(8,128)}, u32[]{:S(2)}, u32[]{:S(2)}) async-start(f32[4,4,3,24,448]{4,3,1,2,0:T(8,128)} %copy.25), calls=%async_computation.1 | async-start | bytes 4718592 | tf_op jit(solution)/shard_map/all_to_all | solution.py:75
  40.8 4.3 %collective-permute-start.6 = (bf16[384,1024]{1,0:T(8,128)(2,1)S(1)}, bf16[384,1024]{1,0:T(8,128)(2,1)S(1)}, u32[]{:S(2)}, u32[]{:S(2)}) collective-permute-start(bf16[384,1024]{1,0:T(8,128)(2,1)S(1)} %bitcast.139), channel_id=1, source_target_pairs={{0,16},{16,0},{1,17},{17,1},{2,18},{18,2},{3,19},{19,3},{4,20},{20... | collective-permute-start | bytes 2359304 | tf_op jit(solution)/shard_map/ppermute | solution.py:65
  45.0 1.9 collective-permute-done.6
  48.5 1.7 copy.31
  50.2 17.4 %all-to-all-done.1 = f32[4,4,3,24,448]{4,3,1,2,0:T(8,128)} async-done(((f32[4,4,3,24,448]{4,3,1,2,0:T(8,128)}), f32[4,4,3,24,448]{4,3,1,2,0:T(8,128)}, u32[]{:S(2)}, u32[]{:S(2)}) %all-to-all-start.1) | async-done | bytes 2064416 | tf_op jit(solution)/shard_map/all_to_all | solution.py:75
  67.6 3.6 %all-to-all-start.3 = ((f32[4,4,3,24,448]{4,3,1,2,0:T(8,128)}), f32[4,4,3,24,448]{4,3,1,2,0:T(8,128)S(1)}, u32[]{:S(2)}, u32[]{:S(2)}) async-start(f32[4,4,3,24,448]{4,3,1,2,0:T(8,128)} %copy.31), calls=%async_computation.3 | async-start | bytes 4718592 | tf_op jit(solution)/shard_map/all_to_all | solution.py:75
  71.3 2.8 %reduce_sum.27 = f32[4,3,24,448]{3,2,0,1:T(8,128)} reduce(f32[4,4,3,24,448]{4,3,1,2,0:T(8,128)} %all-to-all-done.1, f32[]{:T(128)} %constant.50.clone.1), dimensions={0}, to_apply=%region_0.0 | reduce | flops 387072 | bytes 2580484 | tf_op jit(solution)/shard_map/reduce_sum | solution.py:75
  74.2 1.8 constant_dynamic-slice_fusion.2
  76.0 5.8 %collective-permute-start = (f32[1,3,24,448]{3,2,0,1:T(8,128)}, f32[1,3,24,448]{3,2,0,1:T(8,128)S(1)}, u32[]{:S(2)}, u32[]{:S(2)}) collective-permute-start(f32[1,3,24,448]{3,2,0,1:T(8,128)} %get-tuple-element.8), channel_id=1, source_target_pairs={{0,1},{1,2},{2,3},{3,0},{4,5},{5,6},{6,7},{7,4},{8,9},{9,10},{10,1... | collective-permute-start | bytes 387080 | tf_op jit(solution)/shard_map/ppermute | solution.py:43
  81.8 7.9 %collective-permute-start.1 = (f32[1,3,24,448]{3,2,0,1:T(8,128)}, f32[1,3,24,448]{3,2,0,1:T(8,128)}, u32[]{:S(2)}, u32[]{:S(2)}) collective-permute-start(f32[1,3,24,448]{3,2,0,1:T(8,128)} %get-tuple-element.9), channel_id=1, source_target_pairs={{0,2},{1,3},{2,0},{3,1},{4,6},{5,7},{6,4},{7,5},{8,10},{9,11},{10,... | collective-permute-start | bytes 387080 | tf_op jit(solution)/shard_map/ppermute | solution.py:43
  89.7 3.4 %collective-permute-start.2 = (f32[1,3,24,448]{3,2,0,1:T(8,128)}, f32[1,3,24,448]{3,2,0,1:T(8,128)}, u32[]{:S(2)}, u32[]{:S(2)}) collective-permute-start(f32[1,3,24,448]{3,2,0,1:T(8,128)} %get-tuple-element.10), channel_id=1, source_target_pairs={{0,3},{1,0},{2,1},{3,2},{4,7},{5,4},{6,5},{7,6},{8,11},{9,8},{10,9... | collective-permute-start | bytes 387080 | tf_op jit(solution)/shard_map/ppermute | solution.py:43
  93.2 2.9 %collective-permute-done.1 = f32[1,3,24,448]{3,2,0,1:T(8,128)} collective-permute-done((f32[1,3,24,448]{3,2,0,1:T(8,128)}, f32[1,3,24,448]{3,2,0,1:T(8,128)}, u32[]{:S(2)}, u32[]{:S(2)}) %collective-permute-start.1) | collective-permute-done | bytes 129056 | tf_op jit(solution)/shard_map/ppermute | solution.py:43
  96.1 7.7 %collective-permute-done.2 = f32[1,3,24,448]{3,2,0,1:T(8,128)} collective-permute-done((f32[1,3,24,448]{3,2,0,1:T(8,128)}, f32[1,3,24,448]{3,2,0,1:T(8,128)}, u32[]{:S(2)}, u32[]{:S(2)}) %collective-permute-start.2) | collective-permute-done | bytes 129056 | tf_op jit(solution)/shard_map/ppermute | solution.py:43
  103.8 1.2 add_add_fusion
  105.0 1.1 reduce_sum.28
  106.1 1.1 dynamic-slice_bitcast_fusion.2
  107.2 3.0 %collective-permute-start.7 = (f32[1,3,24,448]{3,2,1,0:T(8,128)S(1)}, f32[1,3,24,448]{3,2,1,0:T(8,128)S(1)}, u32[]{:S(2)}, u32[]{:S(2)}) collective-permute-start(f32[1,3,24,448]{3,2,1,0:T(8,128)S(1)} %get-tuple-element.5), channel_id=1, source_target_pairs={{0,1},{1,2},{2,3},{3,0},{4,5},{5,6},{6,7},{7,4},{8,9},{9,10},{10,1... | collective-permute-start | bytes 387080 | tf_op jit(solution)/shard_map/ppermute | solution.py:43
  110.2 6.1 %collective-permute-start.8 = (f32[1,3,24,448]{3,2,1,0:T(8,128)S(1)}, f32[1,3,24,448]{3,2,1,0:T(8,128)S(1)}, u32[]{:S(2)}, u32[]{:S(2)}) collective-permute-start(f32[1,3,24,448]{3,2,1,0:T(8,128)S(1)} %get-tuple-element.6), channel_id=1, source_target_pairs={{0,2},{1,3},{2,0},{3,1},{4,6},{5,7},{6,4},{7,5},{8,10},{9,11},{10,... | collective-permute-start | bytes 387080 | tf_op jit(solution)/shard_map/ppermute | solution.py:43
  116.3 3.4 %collective-permute-start.9 = (f32[1,3,24,448]{3,2,1,0:T(8,128)S(1)}, f32[1,3,24,448]{3,2,1,0:T(8,128)S(1)}, u32[]{:S(2)}, u32[]{:S(2)}) collective-permute-start(f32[1,3,24,448]{3,2,1,0:T(8,128)S(1)} %get-tuple-element.7), channel_id=1, source_target_pairs={{0,3},{1,0},{2,1},{3,2},{4,7},{5,4},{6,5},{7,6},{8,11},{9,8},{10,9... | collective-permute-start | bytes 387080 | tf_op jit(solution)/shard_map/ppermute | solution.py:43
  119.8 4.1 %collective-permute-start.4 = (bf16[3,24,448]{2,1,0:T(8,128)(2,1)S(1)}, bf16[3,24,448]{2,1,0:T(8,128)(2,1)S(1)}, u32[]{:S(2)}, u32[]{:S(2)}) collective-permute-start(bf16[3,24,448]{2,1,0:T(8,128)(2,1)S(1)} %get-tuple-element.19), channel_id=1, source_target_pairs={{0,2},{1,3},{2,0},{3,1},{4,6},{5,7},{6,4},{7,5},{8,10},{9,11},{10,... | collective-permute-start | bytes 193544 | tf_op jit(solution)/shard_map/ppermute | solution.py:50
  123.9 3.9 %collective-permute-start.3 = (bf16[3,24,448]{2,1,0:T(8,128)(2,1)S(1)}, bf16[3,24,448]{2,1,0:T(8,128)(2,1)S(1)}, u32[]{:S(2)}, u32[]{:S(2)}) collective-permute-start(bf16[3,24,448]{2,1,0:T(8,128)(2,1)S(1)} %get-tuple-element.19), channel_id=1, source_target_pairs={{0,3},{1,0},{2,1},{3,2},{4,7},{5,4},{6,5},{7,6},{8,11},{9,8},{10,9... | collective-permute-start | bytes 193544 | tf_op jit(solution)/shard_map/ppermute | solution.py:50
  127.8 2.3 %collective-permute-start.5 = (bf16[3,24,448]{2,1,0:T(8,128)(2,1)S(1)}, bf16[3,24,448]{2,1,0:T(8,128)(2,1)S(1)}, u32[]{:S(2)}, u32[]{:S(2)}) collective-permute-start(bf16[3,24,448]{2,1,0:T(8,128)(2,1)S(1)} %get-tuple-element.19), channel_id=1, source_target_pairs={{0,1},{1,2},{2,3},{3,0},{4,5},{5,6},{6,7},{7,4},{8,9},{9,10},{10,1... | collective-permute-start | bytes 193544 | tf_op jit(solution)/shard_map/ppermute | solution.py:50
  130.4 1.0 fusion.38
  131.4 4.9 %collective-permute-start.11 = (bf16[3,24,448]{2,1,0:T(8,128)(2,1)S(1)}, bf16[3,24,448]{2,1,0:T(8,128)(2,1)S(1)}, u32[]{:S(2)}, u32[]{:S(2)}) collective-permute-start(bf16[3,24,448]{2,1,0:T(8,128)(2,1)S(1)} %get-tuple-element.17), channel_id=1, source_target_pairs={{0,2},{1,3},{2,0},{3,1},{4,6},{5,7},{6,4},{7,5},{8,10},{9,11},{10,... | collective-permute-start | bytes 193544 | tf_op jit(solution)/shard_map/ppermute | solution.py:50
  136.3 3.1 %collective-permute-start.10 = (bf16[3,24,448]{2,1,0:T(8,128)(2,1)S(1)}, bf16[3,24,448]{2,1,0:T(8,128)(2,1)S(1)}, u32[]{:S(2)}, u32[]{:S(2)}) collective-permute-start(bf16[3,24,448]{2,1,0:T(8,128)(2,1)S(1)} %get-tuple-element.17), channel_id=1, source_target_pairs={{0,3},{1,0},{2,1},{3,2},{4,7},{5,4},{6,5},{7,6},{8,11},{9,8},{10,9... | collective-permute-start | bytes 193544 | tf_op jit(solution)/shard_map/ppermute | solution.py:50
  139.4 3.1 %collective-permute-start.12 = (bf16[3,24,448]{2,1,0:T(8,128)(2,1)S(1)}, bf16[3,24,448]{2,1,0:T(8,128)(2,1)S(1)}, u32[]{:S(2)}, u32[]{:S(2)}) collective-permute-start(bf16[3,24,448]{2,1,0:T(8,128)(2,1)S(1)} %get-tuple-element.17), channel_id=1, source_target_pairs={{0,1},{1,2},{2,3},{3,0},{4,5},{5,6},{6,7},{7,4},{8,9},{9,10},{10,1... | collective-permute-start | bytes 193544 | tf_op jit(solution)/shard_map/ppermute | solution.py:50
  142.6 1.2 collective-permute-done.10
  143.8 2.9 %collective-permute-done.12 = bf16[3,24,448]{2,1,0:T(8,128)(2,1)S(1)} collective-permute-done((bf16[3,24,448]{2,1,0:T(8,128)(2,1)S(1)}, bf16[3,24,448]{2,1,0:T(8,128)(2,1)S(1)}, u32[]{:S(2)}, u32[]{:S(2)}) %collective-permute-start.12) | collective-permute-done | bytes 64544 | tf_op jit(solution)/shard_map/ppermute | solution.py:50
  146.6 0.7 fusion.25
  147.4 1.1 broadcast_in_dim.22
  148.5 5.6 %all-to-all-start.2 = ((bf16[3,4,96,448]{3,2,0,1:T(8,128)(2,1)}), bf16[3,4,96,448]{3,2,0,1:T(8,128)(2,1)S(1)}, u32[]{:S(2)}, u32[]{:S(2)}) async-start(bf16[3,4,96,448]{3,2,0,1:T(8,128)(2,1)} %broadcast_in_dim.22), calls=%async_computation.2 | async-start | bytes 2359296 | tf_op jit(solution)/shard_map/all_to_all | solution.py:32
  154.2 13.2 %all-to-all-done.2 = bf16[3,4,96,448]{3,2,0,1:T(8,128)(2,1)S(1)} async-done(((bf16[3,4,96,448]{3,2,0,1:T(8,128)(2,1)}), bf16[3,4,96,448]{3,2,0,1:T(8,128)(2,1)S(1)}, u32[]{:S(2)}, u32[]{:S(2)}) %all-to-all-start.2) | async-done | bytes 1032224 | tf_op jit(solution)/shard_map/all_to_all | solution.py:32
  167.4 1.1 broadcast_in_dim.24
  168.5 4.3 %all-to-all-start.4 = ((bf16[3,4,96,448]{3,2,0,1:T(8,128)(2,1)}), bf16[3,4,96,448]{3,2,0,1:T(8,128)(2,1)}, u32[]{:S(2)}, u32[]{:S(2)}) async-start(bf16[3,4,96,448]{3,2,0,1:T(8,128)(2,1)} %broadcast_in_dim.24), calls=%async_computation.4 | async-start | bytes 2359296 | tf_op jit(solution)/shard_map/all_to_all | solution.py:32
  172.9 12.0 %all-to-all-done.4 = bf16[3,4,96,448]{3,2,0,1:T(8,128)(2,1)} async-done(((bf16[3,4,96,448]{3,2,0,1:T(8,128)(2,1)}), bf16[3,4,96,448]{3,2,0,1:T(8,128)(2,1)}, u32[]{:S(2)}, u32[]{:S(2)}) %all-to-all-start.4) | async-done | bytes 1032224 | tf_op jit(solution)/shard_map/all_to_all | solution.py:32
  184.9 1.4 copy.38
  187.5 7.3 %collective-permute-start.13 = (f32[384,512]{1,0:T(8,128)S(1)}, f32[384,512]{1,0:T(8,128)S(1)}, u32[]{:S(2)}, u32[]{:S(2)}) collective-permute-start(f32[384,512]{1,0:T(8,128)S(1)} %slice.89), channel_id=1, source_target_pairs={{0,16},{16,0},{1,17},{17,1},{2,18},{18,2},{3,19},{19,3},{4,20},{20... | collective-permute-start | bytes 2359304 | tf_op jit(solution)/shard_map/ppermute | solution.py:97
  194.8 1.9 collective-permute-done.13
  196.7 1.1 slice_add_fusion
  197.8 9.2 %all-to-all-start.5 = ((f32[16,24,512]{2,1,0:T(8,128)}), f32[16,24,512]{2,1,0:T(8,128)}, u32[]{:S(2)}, u32[]{:S(2)}) async-start(f32[16,24,512]{2,1,0:T(8,128)} %bitcast.146), calls=%async_computation.5 | async-start | bytes 1572864 | tf_op jit(solution)/shard_map/all_to_all | solution.py:25
  207.0 2.6 %convolution_convert_fusion = bf16[448,512]{1,0:T(8,128)(2,1)} fusion(bf16[384,1024]{1,0:T(8,128)(2,1)} %copy-done.3, bf16[384,1024]{1,0:T(8,128)(2,1)} %bitcast.140, bf16[3,384,448]{2,1,0:T(8,128)(2,1)S(1)} %bitcast.133, bf16[3,384,448]{2,1,0:T(8,128)(2,1)S(1)} %bitcast.128), kind=kOutput, calls=%fused_computation.15 | convolution fusion | flops 355500032 | bytes 4096000 | tf_op jit(solution)/shard_map/dot_general | solution.py:84
  209.6 1.3 convolution_convert_fusion.1
  210.9 1.3 convolution_convert_fusion.2
  212.2 15.6 %all-to-all-done.5 = f32[16,24,512]{2,1,0:T(8,128)} async-done(((f32[16,24,512]{2,1,0:T(8,128)}), f32[16,24,512]{2,1,0:T(8,128)}, u32[]{:S(2)}, u32[]{:S(2)}) %all-to-all-start.5) | async-done | bytes 786464 | tf_op jit(solution)/shard_map/all_to_all | solution.py:25
  227.9 1.8 reduce_sum.29
  (44 shorter events, 4.9 us)
Async XLA Ops:
  0.6 33.2 %copy-start = (bf16[512,448]{0,1:T(8,128)(2,1)S(1)}, bf16[512,448]{0,1:T(8,128)(2,1)}, u32[]{:S(2)}) copy-start(bf16[512,448]{0,1:T(8,128)(2,1)} %param.9) | copy-start | bytes 1376260
  0.6 32.4 %copy-start.5 = (bf16[512,448]{0,1:T(8,128)(2,1)S(1)}, bf16[512,448]{0,1:T(8,128)(2,1)}, u32[]{:S(2)}) copy-start(bf16[512,448]{0,1:T(8,128)(2,1)} %param.10) | copy-start | bytes 1376260
  1.6 31.9 %copy-start.6 = (bf16[448,512]{1,0:T(8,128)(2,1)S(1)}, bf16[448,512]{1,0:T(8,128)(2,1)}, u32[]{:S(2)}) copy-start(bf16[448,512]{1,0:T(8,128)(2,1)} %param.11) | copy-start | bytes 1376260
  33.1 7.7 %copy-start.1 = (bf16[16,24,1024]{2,1,0:T(8,128)(2,1)}, bf16[16,24,1024]{2,1,0:T(8,128)(2,1)S(1)}, u32[]{:S(2)}) copy-start(bf16[16,24,1024]{2,1,0:T(8,128)(2,1)S(1)} %all_to_all.30) | copy-start | bytes 2359300
  36.3 31.4 %all-to-all-start.1 = ((f32[4,4,3,24,448]{4,3,1,2,0:T(8,128)}), f32[4,4,3,24,448]{4,3,1,2,0:T(8,128)}, u32[]{:S(2)}, u32[]{:S(2)}) async-start(f32[4,4,3,24,448]{4,3,1,2,0:T(8,128)} %copy.25), calls=%async_computation.1 | async-start | bytes 4718592 | tf_op jit(solution)/shard_map/all_to_all | solution.py:75
  40.8 6.2 %collective-permute-start.6 = (bf16[384,1024]{1,0:T(8,128)(2,1)S(1)}, bf16[384,1024]{1,0:T(8,128)(2,1)S(1)}, u32[]{:S(2)}, u32[]{:S(2)}) collective-permute-start(bf16[384,1024]{1,0:T(8,128)(2,1)S(1)} %bitcast.139), channel_id=1, source_target_pairs={{0,16},{16,0},{1,17},{17,1},{2,18},{18,2},{3,19},{19,3},{4,20},{20... | collective-permute-start | bytes 2359304 | tf_op jit(solution)/shard_map/ppermute | solution.py:65
  46.9 0.9 copy-start.3
  67.6 37.4 %all-to-all-start.3 = ((f32[4,4,3,24,448]{4,3,1,2,0:T(8,128)}), f32[4,4,3,24,448]{4,3,1,2,0:T(8,128)S(1)}, u32[]{:S(2)}, u32[]{:S(2)}) async-start(f32[4,4,3,24,448]{4,3,1,2,0:T(8,128)} %copy.31), calls=%async_computation.3 | async-start | bytes 4718592 | tf_op jit(solution)/shard_map/all_to_all | solution.py:75
  76.0 17.2 %collective-permute-start = (f32[1,3,24,448]{3,2,0,1:T(8,128)}, f32[1,3,24,448]{3,2,0,1:T(8,128)S(1)}, u32[]{:S(2)}, u32[]{:S(2)}) collective-permute-start(f32[1,3,24,448]{3,2,0,1:T(8,128)} %get-tuple-element.8), channel_id=1, source_target_pairs={{0,1},{1,2},{2,3},{3,0},{4,5},{5,6},{6,7},{7,4},{8,9},{9,10},{10,1... | collective-permute-start | bytes 387080 | tf_op jit(solution)/shard_map/ppermute | solution.py:43
  81.8 14.3 %collective-permute-start.1 = (f32[1,3,24,448]{3,2,0,1:T(8,128)}, f32[1,3,24,448]{3,2,0,1:T(8,128)}, u32[]{:S(2)}, u32[]{:S(2)}) collective-permute-start(f32[1,3,24,448]{3,2,0,1:T(8,128)} %get-tuple-element.9), channel_id=1, source_target_pairs={{0,2},{1,3},{2,0},{3,1},{4,6},{5,7},{6,4},{7,5},{8,10},{9,11},{10,... | collective-permute-start | bytes 387080 | tf_op jit(solution)/shard_map/ppermute | solution.py:43
  89.7 14.1 %collective-permute-start.2 = (f32[1,3,24,448]{3,2,0,1:T(8,128)}, f32[1,3,24,448]{3,2,0,1:T(8,128)}, u32[]{:S(2)}, u32[]{:S(2)}) collective-permute-start(f32[1,3,24,448]{3,2,0,1:T(8,128)} %get-tuple-element.10), channel_id=1, source_target_pairs={{0,3},{1,0},{2,1},{3,2},{4,7},{5,4},{6,5},{7,6},{8,11},{9,8},{10,9... | collective-permute-start | bytes 387080 | tf_op jit(solution)/shard_map/ppermute | solution.py:43
  93.1 3.0 %copy-start.7 = (f32[1,3,24,448]{3,2,0,1:T(8,128)}, f32[1,3,24,448]{3,2,0,1:T(8,128)S(1)}, u32[]{:S(2)}) copy-start(f32[1,3,24,448]{3,2,0,1:T(8,128)S(1)} %collective-permute-done) | copy-start | bytes 387076
  107.2 20.6 %collective-permute-start.7 = (f32[1,3,24,448]{3,2,1,0:T(8,128)S(1)}, f32[1,3,24,448]{3,2,1,0:T(8,128)S(1)}, u32[]{:S(2)}, u32[]{:S(2)}) collective-permute-start(f32[1,3,24,448]{3,2,1,0:T(8,128)S(1)} %get-tuple-element.5), channel_id=1, source_target_pairs={{0,1},{1,2},{2,3},{3,0},{4,5},{5,6},{6,7},{7,4},{8,9},{9,10},{10,1... | collective-permute-start | bytes 387080 | tf_op jit(solution)/shard_map/ppermute | solution.py:43
  110.2 19.9 %collective-permute-start.8 = (f32[1,3,24,448]{3,2,1,0:T(8,128)S(1)}, f32[1,3,24,448]{3,2,1,0:T(8,128)S(1)}, u32[]{:S(2)}, u32[]{:S(2)}) collective-permute-start(f32[1,3,24,448]{3,2,1,0:T(8,128)S(1)} %get-tuple-element.6), channel_id=1, source_target_pairs={{0,2},{1,3},{2,0},{3,1},{4,6},{5,7},{6,4},{7,5},{8,10},{9,11},{10,... | collective-permute-start | bytes 387080 | tf_op jit(solution)/shard_map/ppermute | solution.py:43
  116.3 14.1 %collective-permute-start.9 = (f32[1,3,24,448]{3,2,1,0:T(8,128)S(1)}, f32[1,3,24,448]{3,2,1,0:T(8,128)S(1)}, u32[]{:S(2)}, u32[]{:S(2)}) collective-permute-start(f32[1,3,24,448]{3,2,1,0:T(8,128)S(1)} %get-tuple-element.7), channel_id=1, source_target_pairs={{0,3},{1,0},{2,1},{3,2},{4,7},{5,4},{6,5},{7,6},{8,11},{9,8},{10,9... | collective-permute-start | bytes 387080 | tf_op jit(solution)/shard_map/ppermute | solution.py:43
  119.8 19.6 %collective-permute-start.4 = (bf16[3,24,448]{2,1,0:T(8,128)(2,1)S(1)}, bf16[3,24,448]{2,1,0:T(8,128)(2,1)S(1)}, u32[]{:S(2)}, u32[]{:S(2)}) collective-permute-start(bf16[3,24,448]{2,1,0:T(8,128)(2,1)S(1)} %get-tuple-element.19), channel_id=1, source_target_pairs={{0,2},{1,3},{2,0},{3,1},{4,6},{5,7},{6,4},{7,5},{8,10},{9,11},{10,... | collective-permute-start | bytes 193544 | tf_op jit(solution)/shard_map/ppermute | solution.py:50
  123.9 18.7 %collective-permute-start.3 = (bf16[3,24,448]{2,1,0:T(8,128)(2,1)S(1)}, bf16[3,24,448]{2,1,0:T(8,128)(2,1)S(1)}, u32[]{:S(2)}, u32[]{:S(2)}) collective-permute-start(bf16[3,24,448]{2,1,0:T(8,128)(2,1)S(1)} %get-tuple-element.19), channel_id=1, source_target_pairs={{0,3},{1,0},{2,1},{3,2},{4,7},{5,4},{6,5},{7,6},{8,11},{9,8},{10,9... | collective-permute-start | bytes 193544 | tf_op jit(solution)/shard_map/ppermute | solution.py:50
  127.8 14.8 %collective-permute-start.5 = (bf16[3,24,448]{2,1,0:T(8,128)(2,1)S(1)}, bf16[3,24,448]{2,1,0:T(8,128)(2,1)S(1)}, u32[]{:S(2)}, u32[]{:S(2)}) collective-permute-start(bf16[3,24,448]{2,1,0:T(8,128)(2,1)S(1)} %get-tuple-element.19), channel_id=1, source_target_pairs={{0,1},{1,2},{2,3},{3,0},{4,5},{5,6},{6,7},{7,4},{8,9},{9,10},{10,1... | collective-permute-start | bytes 193544 | tf_op jit(solution)/shard_map/ppermute | solution.py:50
  131.4 11.1 %collective-permute-start.11 = (bf16[3,24,448]{2,1,0:T(8,128)(2,1)S(1)}, bf16[3,24,448]{2,1,0:T(8,128)(2,1)S(1)}, u32[]{:S(2)}, u32[]{:S(2)}) collective-permute-start(bf16[3,24,448]{2,1,0:T(8,128)(2,1)S(1)} %get-tuple-element.17), channel_id=1, source_target_pairs={{0,2},{1,3},{2,0},{3,1},{4,6},{5,7},{6,4},{7,5},{8,10},{9,11},{10,... | collective-permute-start | bytes 193544 | tf_op jit(solution)/shard_map/ppermute | solution.py:50
  136.3 7.4 %collective-permute-start.10 = (bf16[3,24,448]{2,1,0:T(8,128)(2,1)S(1)}, bf16[3,24,448]{2,1,0:T(8,128)(2,1)S(1)}, u32[]{:S(2)}, u32[]{:S(2)}) collective-permute-start(bf16[3,24,448]{2,1,0:T(8,128)(2,1)S(1)} %get-tuple-element.17), channel_id=1, source_target_pairs={{0,3},{1,0},{2,1},{3,2},{4,7},{5,4},{6,5},{7,6},{8,11},{9,8},{10,9... | collective-permute-start | bytes 193544 | tf_op jit(solution)/shard_map/ppermute | solution.py:50
  139.4 7.2 %collective-permute-start.12 = (bf16[3,24,448]{2,1,0:T(8,128)(2,1)S(1)}, bf16[3,24,448]{2,1,0:T(8,128)(2,1)S(1)}, u32[]{:S(2)}, u32[]{:S(2)}) collective-permute-start(bf16[3,24,448]{2,1,0:T(8,128)(2,1)S(1)} %get-tuple-element.17), channel_id=1, source_target_pairs={{0,1},{1,2},{2,3},{3,0},{4,5},{5,6},{6,7},{7,4},{8,9},{9,10},{10,1... | collective-permute-start | bytes 193544 | tf_op jit(solution)/shard_map/ppermute | solution.py:50
  148.5 18.9 %all-to-all-start.2 = ((bf16[3,4,96,448]{3,2,0,1:T(8,128)(2,1)}), bf16[3,4,96,448]{3,2,0,1:T(8,128)(2,1)S(1)}, u32[]{:S(2)}, u32[]{:S(2)}) async-start(bf16[3,4,96,448]{3,2,0,1:T(8,128)(2,1)} %broadcast_in_dim.22), calls=%async_computation.2 | async-start | bytes 2359296 | tf_op jit(solution)/shard_map/all_to_all | solution.py:32
  168.5 16.4 %all-to-all-start.4 = ((bf16[3,4,96,448]{3,2,0,1:T(8,128)(2,1)}), bf16[3,4,96,448]{3,2,0,1:T(8,128)(2,1)}, u32[]{:S(2)}, u32[]{:S(2)}) async-start(bf16[3,4,96,448]{3,2,0,1:T(8,128)(2,1)} %broadcast_in_dim.24), calls=%async_computation.4 | async-start | bytes 2359296 | tf_op jit(solution)/shard_map/all_to_all | solution.py:32
  187.5 9.2 %collective-permute-start.13 = (f32[384,512]{1,0:T(8,128)S(1)}, f32[384,512]{1,0:T(8,128)S(1)}, u32[]{:S(2)}, u32[]{:S(2)}) collective-permute-start(f32[384,512]{1,0:T(8,128)S(1)} %slice.89), channel_id=1, source_target_pairs={{0,16},{16,0},{1,17},{17,1},{2,18},{18,2},{3,19},{19,3},{4,20},{20... | collective-permute-start | bytes 2359304 | tf_op jit(solution)/shard_map/ppermute | solution.py:97
  197.8 30.1 %all-to-all-start.5 = ((f32[16,24,512]{2,1,0:T(8,128)}), f32[16,24,512]{2,1,0:T(8,128)}, u32[]{:S(2)}, u32[]{:S(2)}) async-start(f32[16,24,512]{2,1,0:T(8,128)} %bitcast.146), calls=%async_computation.5 | async-start | bytes 1572864 | tf_op jit(solution)/shard_map/all_to_all | solution.py:25
  207.0 2.6 %copy-start.2 = (bf16[16,24,1024]{2,1,0:T(8,128)(2,1)S(1)}, bf16[16,24,1024]{2,1,0:T(8,128)(2,1)}, u32[]{:S(2)}) copy-start(bf16[16,24,1024]{2,1,0:T(8,128)(2,1)} %copy-done.1) | copy-start | bytes 2359300
  207.0 2.6 %copy-start.4 = (bf16[384,1024]{1,0:T(8,128)(2,1)S(1)}, bf16[384,1024]{1,0:T(8,128)(2,1)}, u32[]{:S(2)}) copy-start(bf16[384,1024]{1,0:T(8,128)(2,1)} %copy-done.3) | copy-start | bytes 2359300

commit v16 on v13

--- a/solution.py
+++ b/solution.py
@@ -64,14 +64,14 @@
     swap = [(0, 1), (1, 0)]
     parts_in = [mine, lax.ppermute(mine, "c", swap)]
     width = tokens.shape[1]
+    gate_up_weight = jnp.stack([gate_weight, up_weight])
     chunks = []
     for rows in parts_in:
         rows = rows.reshape((nx, -1) + rows.shape[1:])
         tok, grd = rows[..., :width], rows[..., width:]
-        gate_part = jnp.einsum("brd,dh->brh", tok, gate_weight, preferred_element_type=jnp.float32)
-        up_part = jnp.einsum("brd,dh->brh", tok, up_weight, preferred_element_type=jnp.float32)
+        gate_up = jnp.einsum("brd,kdh->bkrh", tok, gate_up_weight, preferred_element_type=jnp.float32)
         hidden_part = jnp.einsum("brd,hd->brh", grd, down_weight, preferred_element_type=jnp.float32)
-        p = jnp.stack([gate_part, up_part, hidden_part], 1)
+        p = jnp.concatenate([gate_up, hidden_part[:, None]], 1)
         p = lax.all_to_all(p, "x", 0, 0, tiled=True).sum(0)
         p = scatter_permute(p, "zh", nzh, 1)
         d = jnp.stack(swiglu_grads(p[0], p[1], p[2]))

time: 216 us -> 213 us (0.986)
  other arithmetic: 12 us -> 9.45 us
    another operation x2 -> x0, local copies, waits for them, and re-layouts: 3.29 us -> none  [local(): p = jnp.stack([gate_part, up_part, hidden_part], 1)]
    concatenate x0 -> x2, local copies, waits for them, and re-layouts: none -> 3.27 us  [local(): p = jnp.concatenate([gate_up, hidden_part[:, None]], 1)]
    unnamed x14 -> x22, local copies, waits for them, and re-layouts: 0.18 us -> 2.95 us
  transfers between devices with their start and end apart: 19 -> 19, of which waited for: 9 -> 9; matrix products, arithmetic and copies ran while one was open for 9% -> 7% of each run, Pallas kernels for 0% -> 0%
where the time goes in v16:
time: 213 us; the launch traced here: 210 us
  starting transfers between devices  88.6 us (42%)
  waiting for transfers between devices  60.5 us (28%)
  blocking collectives  31.5 us (15%)
  local copies, waits for them, and re-layouts  10.9 us (5%)
  other arithmetic  9.45 us (4%)
  matrix products  8.31 us (4%)
    all_to_all x1, blocking collectives, gather_a2a(): v = lax.all_to_all(v, axis_name, dim, dim, tiled=True)  31.5 us
    ppermute x6, starting transfers between devices, scatter_permute(): lax.ppermute(part, axis_name, [(j, (j + k) % n) for j in range(n)])  27 us
    ppermute x6, starting transfers between devices, gather_permute(): lax.ppermute(v, axis_name, [(j, (j + k) % n) for j in range(n)])  22.5 us
    all_to_all x2, waiting for transfers between devices, local(): p = lax.all_to_all(p, 'x', 0, 0, tiled=True).sum(0)  16.4 us
    all_to_all x1, waiting for transfers between devices, scatter_sum(): v = lax.all_to_all(v, axis_name, dim, dim, tiled=True)  15.6 us
    all_to_all x2, waiting for transfers between devices, gather_a2a(): v = lax.all_to_all(v, axis_name, dim, dim, tiled=True)  10.4 us
    all_to_all x1, starting transfers between devices, scatter_sum(): v = lax.all_to_all(v, axis_name, dim, dim, tiled=True)  9.2 us
    ppermute x1, starting transfers between devices, local(): result = result[:half] + lax.ppermute(result[half:], 'c', swap)  9.06 us
  transfers between devices with their start and end apart: 19, of which 9 were waited for; matrix products, arithmetic and copies ran while one was open for 7% of the time, Pallas kernels for 0%

profile of v16, /device:TPU:1, one launch (start us, length us, event | category | flops | bytes accessed | tf_op | source)
XLA Modules:
  0.0 210.4 jit_solution(13834597502396038324)
XLA Ops:
  0.6 0.8 pad_maximum_fusion.7
  1.6 31.5 %all_to_all.30 = bf16[16,24,1024]{2,1,0:T(8,128)(2,1)S(1)} all-to-all(bf16[16,24,1024]{2,1,0:T(8,128)(2,1)S(1)} %broadcast_in_dim.26), channel_id=1, replica_groups=mesh['y'=8,'zl'=2,'c'=2,'x'=4,'zh'=4] {'y','zl'}, dimensions={0} | all-to-all | bytes 1572864 | tf_op jit(solution)/shard_map/all_to_all | solution.py:32
  33.9 0.6 convolution_bitcast_fusion.1
  34.8 1.7 copy.19
  36.4 4.0 %all-to-all-start.1 = ((f32[4,3,96,448]{3,2,1,0:T(8,128)}), f32[4,3,96,448]{3,2,1,0:T(8,128)S(1)}, u32[]{:S(2)}, u32[]{:S(2)}) async-start(f32[4,3,96,448]{3,2,1,0:T(8,128)} %copy.19), calls=%async_computation.1 | async-start | bytes 4718592 | tf_op jit(solution)/shard_map/all_to_all | solution.py:75
  40.4 4.7 %collective-permute-start.6 = (bf16[384,1024]{1,0:T(8,128)(2,1)}, bf16[384,1024]{1,0:T(8,128)(2,1)S(1)}, u32[]{:S(2)}, u32[]{:S(2)}) collective-permute-start(bf16[384,1024]{1,0:T(8,128)(2,1)} %bitcast.80), channel_id=1, source_target_pairs={{0,16},{16,0},{1,17},{17,1},{2,18},{18,2},{3,19},{19,3},{4,20},{20... | collective-permute-start | bytes 2359304 | tf_op jit(solution)/shard_map/ppermute | solution.py:65
  45.1 2.1 collective-permute-done.6
  48.1 0.6 convolution_bitcast_fusion
  48.9 1.6 copy.24
  50.5 16.4 %all-to-all-done.1 = f32[4,3,96,448]{3,2,1,0:T(8,128)S(1)} async-done(((f32[4,3,96,448]{3,2,1,0:T(8,128)}), f32[4,3,96,448]{3,2,1,0:T(8,128)S(1)}, u32[]{:S(2)}, u32[]{:S(2)}) %all-to-all-start.1) | async-done | bytes 2064416 | tf_op jit(solution)/shard_map/all_to_all | solution.py:75
  67.0 1.4 copy-done.1
  68.4 3.6 %all-to-all-start.3 = ((f32[4,3,96,448]{3,2,1,0:T(8,128)}), f32[4,3,96,448]{3,2,1,0:T(8,128)S(1)}, u32[]{:S(2)}, u32[]{:S(2)}) async-start(f32[4,3,96,448]{3,2,1,0:T(8,128)} %copy.24), calls=%async_computation.3 | async-start | bytes 4718592 | tf_op jit(solution)/shard_map/all_to_all | solution.py:75
  72.1 2.0 reduce_sum.27
  74.1 0.8 constant_dynamic-slice_fusion.5
  74.9 5.8 %collective-permute-start = (f32[3,24,448]{2,1,0:T(8,128)}, f32[3,24,448]{2,1,0:T(8,128)S(1)}, u32[]{:S(2)}, u32[]{:S(2)}) collective-permute-start(f32[3,24,448]{2,1,0:T(8,128)} %get-tuple-element.8), channel_id=1, source_target_pairs={{0,1},{1,2},{2,3},{3,0},{4,5},{5,6},{6,7},{7,4},{8,9},{9,10},{10,1... | collective-permute-start | bytes 387080 | tf_op jit(solution)/shard_map/ppermute | solution.py:43
  80.7 5.9 %collective-permute-start.2 = (f32[3,24,448]{2,1,0:T(8,128)}, f32[3,24,448]{2,1,0:T(8,128)}, u32[]{:S(2)}, u32[]{:S(2)}) collective-permute-start(f32[3,24,448]{2,1,0:T(8,128)} %get-tuple-element.9), channel_id=1, source_target_pairs={{0,3},{1,0},{2,1},{3,2},{4,7},{5,4},{6,5},{7,6},{8,11},{9,8},{10,9... | collective-permute-start | bytes 387080 | tf_op jit(solution)/shard_map/ppermute | solution.py:43
  86.6 5.4 %collective-permute-start.1 = (f32[3,24,448]{2,1,0:T(8,128)}, f32[3,24,448]{2,1,0:T(8,128)}, u32[]{:S(2)}, u32[]{:S(2)}) collective-permute-start(f32[3,24,448]{2,1,0:T(8,128)} %get-tuple-element.10), channel_id=1, source_target_pairs={{0,2},{1,3},{2,0},{3,1},{4,6},{5,7},{6,4},{7,5},{8,10},{9,11},{10,... | collective-permute-start | bytes 387080 | tf_op jit(solution)/shard_map/ppermute | solution.py:43
  92.1 4.7 %collective-permute-done.1 = f32[3,24,448]{2,1,0:T(8,128)} collective-permute-done((f32[3,24,448]{2,1,0:T(8,128)}, f32[3,24,448]{2,1,0:T(8,128)}, u32[]{:S(2)}, u32[]{:S(2)}) %collective-permute-start.1) | collective-permute-done | bytes 129056 | tf_op jit(solution)/shard_map/ppermute | solution.py:43
  96.8 1.0 add_add_fusion.1
  97.9 6.7 %collective-permute-start.4 = (bf16[3,24,448]{2,1,0:T(8,128)(2,1)S(1)}, bf16[3,24,448]{2,1,0:T(8,128)(2,1)}, u32[]{:S(2)}, u32[]{:S(2)}) collective-permute-start(bf16[3,24,448]{2,1,0:T(8,128)(2,1)S(1)} %get-tuple-element.19), channel_id=1, source_target_pairs={{0,2},{1,3},{2,0},{3,1},{4,6},{5,7},{6,4},{7,5},{8,10},{9,11},{10,... | collective-permute-start | bytes 193544 | tf_op jit(solution)/shard_map/ppermute | solution.py:50
  104.5 1.9 collective-permute-start.3
  106.5 4.3 %collective-permute-start.5 = (bf16[3,24,448]{2,1,0:T(8,128)(2,1)S(1)}, bf16[3,24,448]{2,1,0:T(8,128)(2,1)}, u32[]{:S(2)}, u32[]{:S(2)}) collective-permute-start(bf16[3,24,448]{2,1,0:T(8,128)(2,1)S(1)} %get-tuple-element.19), channel_id=1, source_target_pairs={{0,1},{1,2},{2,3},{3,0},{4,5},{5,6},{6,7},{7,4},{8,9},{9,10},{10,1... | collective-permute-start | bytes 193544 | tf_op jit(solution)/shard_map/ppermute | solution.py:50
  111.1 2.7 %collective-permute-start.7 = (f32[3,24,448]{2,1,0:T(8,128)S(1)}, f32[3,24,448]{2,1,0:T(8,128)S(1)}, u32[]{:S(2)}, u32[]{:S(2)}) collective-permute-start(f32[3,24,448]{2,1,0:T(8,128)S(1)} %get-tuple-element.5), channel_id=1, source_target_pairs={{0,1},{1,2},{2,3},{3,0},{4,5},{5,6},{6,7},{7,4},{8,9},{9,10},{10,1... | collective-permute-start | bytes 387080 | tf_op jit(solution)/shard_map/ppermute | solution.py:43
  113.9 4.6 %collective-permute-start.9 = (f32[3,24,448]{2,1,0:T(8,128)S(1)}, f32[3,24,448]{2,1,0:T(8,128)S(1)}, u32[]{:S(2)}, u32[]{:S(2)}) collective-permute-start(f32[3,24,448]{2,1,0:T(8,128)S(1)} %get-tuple-element.6), channel_id=1, source_target_pairs={{0,3},{1,0},{2,1},{3,2},{4,7},{5,4},{6,5},{7,6},{8,11},{9,8},{10,9... | collective-permute-start | bytes 387080 | tf_op jit(solution)/shard_map/ppermute | solution.py:43
  118.5 2.5 %collective-permute-start.8 = (f32[3,24,448]{2,1,0:T(8,128)S(1)}, f32[3,24,448]{2,1,0:T(8,128)S(1)}, u32[]{:S(2)}, u32[]{:S(2)}) collective-permute-start(f32[3,24,448]{2,1,0:T(8,128)S(1)} %get-tuple-element.7), channel_id=1, source_target_pairs={{0,2},{1,3},{2,0},{3,1},{4,6},{5,7},{6,4},{7,5},{8,10},{9,11},{10,... | collective-permute-start | bytes 387080 | tf_op jit(solution)/shard_map/ppermute | solution.py:43
  121.1 1.5 fusion.24
  122.5 1.1 broadcast_in_dim.29
  123.7 4.3 %all-to-all-start.2 = ((bf16[3,4,96,448]{3,2,0,1:T(8,128)(2,1)}), bf16[3,4,96,448]{3,2,0,1:T(8,128)(2,1)S(1)}, u32[]{:S(2)}, u32[]{:S(2)}) async-start(bf16[3,4,96,448]{3,2,0,1:T(8,128)(2,1)} %broadcast_in_dim.29), calls=%async_computation.2 | async-start | bytes 2359296 | tf_op jit(solution)/shard_map/all_to_all | solution.py:32
  128.0 3.4 %collective-permute-done.8 = f32[3,24,448]{2,1,0:T(8,128)S(1)} collective-permute-done((f32[3,24,448]{2,1,0:T(8,128)S(1)}, f32[3,24,448]{2,1,0:T(8,128)S(1)}, u32[]{:S(2)}, u32[]{:S(2)}) %collective-permute-start.8) | collective-permute-done | bytes 129056 | tf_op jit(solution)/shard_map/ppermute | solution.py:43
  131.5 3.4 %collective-permute-start.11 = (bf16[3,24,448]{2,1,0:T(8,128)(2,1)S(1)}, bf16[3,24,448]{2,1,0:T(8,128)(2,1)S(1)}, u32[]{:S(2)}, u32[]{:S(2)}) collective-permute-start(bf16[3,24,448]{2,1,0:T(8,128)(2,1)S(1)} %get-tuple-element.17), channel_id=1, source_target_pairs={{0,2},{1,3},{2,0},{3,1},{4,6},{5,7},{6,4},{7,5},{8,10},{9,11},{10,... | collective-permute-start | bytes 193544 | tf_op jit(solution)/shard_map/ppermute | solution.py:50
  134.9 4.0 %collective-permute-start.10 = (bf16[3,24,448]{2,1,0:T(8,128)(2,1)S(1)}, bf16[3,24,448]{2,1,0:T(8,128)(2,1)S(1)}, u32[]{:S(2)}, u32[]{:S(2)}) collective-permute-start(bf16[3,24,448]{2,1,0:T(8,128)(2,1)S(1)} %get-tuple-element.17), channel_id=1, source_target_pairs={{0,3},{1,0},{2,1},{3,2},{4,7},{5,4},{6,5},{7,6},{8,11},{9,8},{10,9... | collective-permute-start | bytes 193544 | tf_op jit(solution)/shard_map/ppermute | solution.py:50
  138.9 2.2 %collective-permute-start.12 = (bf16[3,24,448]{2,1,0:T(8,128)(2,1)S(1)}, bf16[3,24,448]{2,1,0:T(8,128)(2,1)S(1)}, u32[]{:S(2)}, u32[]{:S(2)}) collective-permute-start(bf16[3,24,448]{2,1,0:T(8,128)(2,1)S(1)} %get-tuple-element.17), channel_id=1, source_target_pairs={{0,1},{1,2},{2,3},{3,0},{4,5},{5,6},{6,7},{7,4},{8,9},{9,10},{10,1... | collective-permute-start | bytes 193544 | tf_op jit(solution)/shard_map/ppermute | solution.py:50
  141.1 0.8 collective-permute-done.10
  141.9 5.2 %collective-permute-done.12 = bf16[3,24,448]{2,1,0:T(8,128)(2,1)S(1)} collective-permute-done((bf16[3,24,448]{2,1,0:T(8,128)(2,1)S(1)}, bf16[3,24,448]{2,1,0:T(8,128)(2,1)S(1)}, u32[]{:S(2)}, u32[]{:S(2)}) %collective-permute-start.12) | collective-permute-done | bytes 64544 | tf_op jit(solution)/shard_map/ppermute | solution.py:50
  147.5 1.1 broadcast_in_dim.32
  148.7 4.3 %all-to-all-start.4 = ((bf16[3,4,96,448]{3,2,0,1:T(8,128)(2,1)}), bf16[3,4,96,448]{3,2,0,1:T(8,128)(2,1)}, u32[]{:S(2)}, u32[]{:S(2)}) async-start(bf16[3,4,96,448]{3,2,0,1:T(8,128)(2,1)} %broadcast_in_dim.32), calls=%async_computation.4 | async-start | bytes 2359296 | tf_op jit(solution)/shard_map/all_to_all | solution.py:32
  153.0 10.4 %all-to-all-done.4 = bf16[3,4,96,448]{3,2,0,1:T(8,128)(2,1)} async-done(((bf16[3,4,96,448]{3,2,0,1:T(8,128)(2,1)}), bf16[3,4,96,448]{3,2,0,1:T(8,128)(2,1)}, u32[]{:S(2)}, u32[]{:S(2)}) %all-to-all-start.4) | async-done | bytes 1032224 | tf_op jit(solution)/shard_map/all_to_all | solution.py:32
  163.4 1.4 copy.26
  165.9 0.6 convolution_add_fusion
  166.5 9.1 %collective-permute-start.13 = (f32[384,512]{1,0:T(8,128)S(1)}, f32[384,512]{1,0:T(8,128)S(1)}, u32[]{:S(2)}, u32[]{:S(2)}) collective-permute-start(f32[384,512]{1,0:T(8,128)S(1)} %slice.83), channel_id=1, source_target_pairs={{0,16},{16,0},{1,17},{17,1},{2,18},{18,2},{3,19},{19,3},{4,20},{20... | collective-permute-start | bytes 2359304 | tf_op jit(solution)/shard_map/ppermute | solution.py:97
  175.6 1.9 collective-permute-done.13
  177.5 1.1 slice_add_fusion
  178.5 9.2 %all-to-all-start.5 = ((f32[16,24,512]{2,1,0:T(8,128)}), f32[16,24,512]{2,1,0:T(8,128)}, u32[]{:S(2)}, u32[]{:S(2)}) async-start(f32[16,24,512]{2,1,0:T(8,128)} %bitcast.84), calls=%async_computation.5 | async-start | bytes 1572864 | tf_op jit(solution)/shard_map/all_to_all | solution.py:25
  187.8 2.6 %convolution_convert_fusion = bf16[448,512]{1,0:T(8,128)(2,1)} fusion(bf16[384,1024]{1,0:T(8,128)(2,1)} %copy-done.4, bf16[384,1024]{1,0:T(8,128)(2,1)} %bitcast.81, bf16[3,384,448]{2,1,0:T(8,128)(2,1)S(1)} %bitcast.75, bf16[3,384,448]{2,1,0:T(8,128)(2,1)S(1)} %bitcast.70), kind=kOutput, calls=%fused_computation.13 | convolution fusion | flops 355500032 | bytes 4096000 | tf_op jit(solution)/shard_map/dot_general | solution.py:84
  190.3 1.3 convolution_convert_fusion.1
  191.7 1.3 convolution_convert_fusion.2
  193.0 15.6 %all-to-all-done.5 = f32[16,24,512]{2,1,0:T(8,128)} async-done(((f32[16,24,512]{2,1,0:T(8,128)}), f32[16,24,512]{2,1,0:T(8,128)}, u32[]{:S(2)}, u32[]{:S(2)}) %all-to-all-start.5) | async-done | bytes 786464 | tf_op jit(solution)/shard_map/all_to_all | solution.py:25
  208.6 1.8 reduce_sum.29
  (48 shorter events, 4.4 us)
Async XLA Ops:
  0.6 32.4 %copy-start = (bf16[448,512]{1,0:T(8,128)(2,1)S(1)}, bf16[448,512]{1,0:T(8,128)(2,1)}, u32[]{:S(2)}) copy-start(bf16[448,512]{1,0:T(8,128)(2,1)} %param.11) | copy-start | bytes 1376260
  1.5 32.4 %copy-start.6 = (bf16[512,448]{0,1:T(8,128)(2,1)S(1)}, bf16[512,448]{0,1:T(8,128)(2,1)}, u32[]{:S(2)}) copy-start(bf16[512,448]{0,1:T(8,128)(2,1)} %param.9) | copy-start | bytes 1376260
  1.6 32.4 %copy-start.8 = (bf16[512,448]{0,1:T(8,128)(2,1)S(1)}, bf16[512,448]{0,1:T(8,128)(2,1)}, u32[]{:S(2)}) copy-start(bf16[512,448]{0,1:T(8,128)(2,1)} %param.10) | copy-start | bytes 1376260
  33.0 0.9 copy-start.2
  36.4 30.6 %all-to-all-start.1 = ((f32[4,3,96,448]{3,2,1,0:T(8,128)}), f32[4,3,96,448]{3,2,1,0:T(8,128)S(1)}, u32[]{:S(2)}, u32[]{:S(2)}) async-start(f32[4,3,96,448]{3,2,1,0:T(8,128)} %copy.19), calls=%async_computation.1 | async-start | bytes 4718592 | tf_op jit(solution)/shard_map/all_to_all | solution.py:75
  40.4 7.7 %copy-start.9 = (bf16[512,448]{0,1:T(8,128)(2,1)S(1)}, bf16[512,448]{0,1:T(8,128)(2,1)}, u32[]{:S(2)}) copy-start(bf16[512,448]{0,1:T(8,128)(2,1)} %param.10) | copy-start | bytes 1376260
  40.4 6.8 %collective-permute-start.6 = (bf16[384,1024]{1,0:T(8,128)(2,1)}, bf16[384,1024]{1,0:T(8,128)(2,1)S(1)}, u32[]{:S(2)}, u32[]{:S(2)}) collective-permute-start(bf16[384,1024]{1,0:T(8,128)(2,1)} %bitcast.80), channel_id=1, source_target_pairs={{0,16},{16,0},{1,17},{17,1},{2,18},{18,2},{3,19},{19,3},{4,20},{20... | collective-permute-start | bytes 2359304 | tf_op jit(solution)/shard_map/ppermute | solution.py:65
  47.2 0.9 copy-start.4
  67.0 1.4 copy-start.1
  68.4 42.3 %all-to-all-start.3 = ((f32[4,3,96,448]{3,2,1,0:T(8,128)}), f32[4,3,96,448]{3,2,1,0:T(8,128)S(1)}, u32[]{:S(2)}, u32[]{:S(2)}) async-start(f32[4,3,96,448]{3,2,1,0:T(8,128)} %copy.24), calls=%async_computation.3 | async-start | bytes 4718592 | tf_op jit(solution)/shard_map/all_to_all | solution.py:75
  74.9 17.2 %collective-permute-start = (f32[3,24,448]{2,1,0:T(8,128)}, f32[3,24,448]{2,1,0:T(8,128)S(1)}, u32[]{:S(2)}, u32[]{:S(2)}) collective-permute-start(f32[3,24,448]{2,1,0:T(8,128)} %get-tuple-element.8), channel_id=1, source_target_pairs={{0,1},{1,2},{2,3},{3,0},{4,5},{5,6},{6,7},{7,4},{8,9},{9,10},{10,1... | collective-permute-start | bytes 387080 | tf_op jit(solution)/shard_map/ppermute | solution.py:43
  80.7 11.4 %collective-permute-start.2 = (f32[3,24,448]{2,1,0:T(8,128)}, f32[3,24,448]{2,1,0:T(8,128)}, u32[]{:S(2)}, u32[]{:S(2)}) collective-permute-start(f32[3,24,448]{2,1,0:T(8,128)} %get-tuple-element.9), channel_id=1, source_target_pairs={{0,3},{1,0},{2,1},{3,2},{4,7},{5,4},{6,5},{7,6},{8,11},{9,8},{10,9... | collective-permute-start | bytes 387080 | tf_op jit(solution)/shard_map/ppermute | solution.py:43
  86.6 10.2 %collective-permute-start.1 = (f32[3,24,448]{2,1,0:T(8,128)}, f32[3,24,448]{2,1,0:T(8,128)}, u32[]{:S(2)}, u32[]{:S(2)}) collective-permute-start(f32[3,24,448]{2,1,0:T(8,128)} %get-tuple-element.10), channel_id=1, source_target_pairs={{0,2},{1,3},{2,0},{3,1},{4,6},{5,7},{6,4},{7,5},{8,10},{9,11},{10,... | collective-permute-start | bytes 387080 | tf_op jit(solution)/shard_map/ppermute | solution.py:43
  97.9 20.7 %collective-permute-start.4 = (bf16[3,24,448]{2,1,0:T(8,128)(2,1)S(1)}, bf16[3,24,448]{2,1,0:T(8,128)(2,1)}, u32[]{:S(2)}, u32[]{:S(2)}) collective-permute-start(bf16[3,24,448]{2,1,0:T(8,128)(2,1)S(1)} %get-tuple-element.19), channel_id=1, source_target_pairs={{0,2},{1,3},{2,0},{3,1},{4,6},{5,7},{6,4},{7,5},{8,10},{9,11},{10,... | collective-permute-start | bytes 193544 | tf_op jit(solution)/shard_map/ppermute | solution.py:50
  104.5 16.5 %collective-permute-start.3 = (bf16[3,24,448]{2,1,0:T(8,128)(2,1)S(1)}, bf16[3,24,448]{2,1,0:T(8,128)(2,1)}, u32[]{:S(2)}, u32[]{:S(2)}) collective-permute-start(bf16[3,24,448]{2,1,0:T(8,128)(2,1)S(1)} %get-tuple-element.19), channel_id=1, source_target_pairs={{0,3},{1,0},{2,1},{3,2},{4,7},{5,4},{6,5},{7,6},{8,11},{9,8},{10,9... | collective-permute-start | bytes 193544 | tf_op jit(solution)/shard_map/ppermute | solution.py:50
  106.5 14.6 %collective-permute-start.5 = (bf16[3,24,448]{2,1,0:T(8,128)(2,1)S(1)}, bf16[3,24,448]{2,1,0:T(8,128)(2,1)}, u32[]{:S(2)}, u32[]{:S(2)}) collective-permute-start(bf16[3,24,448]{2,1,0:T(8,128)(2,1)S(1)} %get-tuple-element.19), channel_id=1, source_target_pairs={{0,1},{1,2},{2,3},{3,0},{4,5},{5,6},{6,7},{7,4},{8,9},{9,10},{10,1... | collective-permute-start | bytes 193544 | tf_op jit(solution)/shard_map/ppermute | solution.py:50
  111.1 16.9 %collective-permute-start.7 = (f32[3,24,448]{2,1,0:T(8,128)S(1)}, f32[3,24,448]{2,1,0:T(8,128)S(1)}, u32[]{:S(2)}, u32[]{:S(2)}) collective-permute-start(f32[3,24,448]{2,1,0:T(8,128)S(1)} %get-tuple-element.5), channel_id=1, source_target_pairs={{0,1},{1,2},{2,3},{3,0},{4,5},{5,6},{6,7},{7,4},{8,9},{9,10},{10,1... | collective-permute-start | bytes 387080 | tf_op jit(solution)/shard_map/ppermute | solution.py:43
  113.9 14.1 %collective-permute-start.9 = (f32[3,24,448]{2,1,0:T(8,128)S(1)}, f32[3,24,448]{2,1,0:T(8,128)S(1)}, u32[]{:S(2)}, u32[]{:S(2)}) collective-permute-start(f32[3,24,448]{2,1,0:T(8,128)S(1)} %get-tuple-element.6), channel_id=1, source_target_pairs={{0,3},{1,0},{2,1},{3,2},{4,7},{5,4},{6,5},{7,6},{8,11},{9,8},{10,9... | collective-permute-start | bytes 387080 | tf_op jit(solution)/shard_map/ppermute | solution.py:43
  118.5 12.9 %collective-permute-start.8 = (f32[3,24,448]{2,1,0:T(8,128)S(1)}, f32[3,24,448]{2,1,0:T(8,128)S(1)}, u32[]{:S(2)}, u32[]{:S(2)}) collective-permute-start(f32[3,24,448]{2,1,0:T(8,128)S(1)} %get-tuple-element.7), channel_id=1, source_target_pairs={{0,2},{1,3},{2,0},{3,1},{4,6},{5,7},{6,4},{7,5},{8,10},{9,11},{10,... | collective-permute-start | bytes 387080 | tf_op jit(solution)/shard_map/ppermute | solution.py:43
  123.7 23.9 %all-to-all-start.2 = ((bf16[3,4,96,448]{3,2,0,1:T(8,128)(2,1)}), bf16[3,4,96,448]{3,2,0,1:T(8,128)(2,1)S(1)}, u32[]{:S(2)}, u32[]{:S(2)}) async-start(bf16[3,4,96,448]{3,2,0,1:T(8,128)(2,1)} %broadcast_in_dim.29), calls=%async_computation.2 | async-start | bytes 2359296 | tf_op jit(solution)/shard_map/all_to_all | solution.py:32
  131.5 9.6 %collective-permute-start.11 = (bf16[3,24,448]{2,1,0:T(8,128)(2,1)S(1)}, bf16[3,24,448]{2,1,0:T(8,128)(2,1)S(1)}, u32[]{:S(2)}, u32[]{:S(2)}) collective-permute-start(bf16[3,24,448]{2,1,0:T(8,128)(2,1)S(1)} %get-tuple-element.17), channel_id=1, source_target_pairs={{0,2},{1,3},{2,0},{3,1},{4,6},{5,7},{6,4},{7,5},{8,10},{9,11},{10,... | collective-permute-start | bytes 193544 | tf_op jit(solution)/shard_map/ppermute | solution.py:50
  134.9 7.0 %collective-permute-start.10 = (bf16[3,24,448]{2,1,0:T(8,128)(2,1)S(1)}, bf16[3,24,448]{2,1,0:T(8,128)(2,1)S(1)}, u32[]{:S(2)}, u32[]{:S(2)}) collective-permute-start(bf16[3,24,448]{2,1,0:T(8,128)(2,1)S(1)} %get-tuple-element.17), channel_id=1, source_target_pairs={{0,3},{1,0},{2,1},{3,2},{4,7},{5,4},{6,5},{7,6},{8,11},{9,8},{10,9... | collective-permute-start | bytes 193544 | tf_op jit(solution)/shard_map/ppermute | solution.py:50
  138.9 8.2 %collective-permute-start.12 = (bf16[3,24,448]{2,1,0:T(8,128)(2,1)S(1)}, bf16[3,24,448]{2,1,0:T(8,128)(2,1)S(1)}, u32[]{:S(2)}, u32[]{:S(2)}) collective-permute-start(bf16[3,24,448]{2,1,0:T(8,128)(2,1)S(1)} %get-tuple-element.17), channel_id=1, source_target_pairs={{0,1},{1,2},{2,3},{3,0},{4,5},{5,6},{6,7},{7,4},{8,9},{9,10},{10,1... | collective-permute-start | bytes 193544 | tf_op jit(solution)/shard_map/ppermute | solution.py:50
  148.7 14.8 %all-to-all-start.4 = ((bf16[3,4,96,448]{3,2,0,1:T(8,128)(2,1)}), bf16[3,4,96,448]{3,2,0,1:T(8,128)(2,1)}, u32[]{:S(2)}, u32[]{:S(2)}) async-start(bf16[3,4,96,448]{3,2,0,1:T(8,128)(2,1)} %broadcast_in_dim.32), calls=%async_computation.4 | async-start | bytes 2359296 | tf_op jit(solution)/shard_map/all_to_all | solution.py:32
  153.0 11.8 %copy-start.7 = (bf16[512,448]{0,1:T(8,128)(2,1)S(1)}, bf16[512,448]{0,1:T(8,128)(2,1)}, u32[]{:S(2)}) copy-start(bf16[512,448]{0,1:T(8,128)(2,1)} %param.9) | copy-start | bytes 1376260
  164.9 1.0 copy-start.10
  166.5 11.0 %collective-permute-start.13 = (f32[384,512]{1,0:T(8,128)S(1)}, f32[384,512]{1,0:T(8,128)S(1)}, u32[]{:S(2)}, u32[]{:S(2)}) collective-permute-start(f32[384,512]{1,0:T(8,128)S(1)} %slice.83), channel_id=1, source_target_pairs={{0,16},{16,0},{1,17},{17,1},{2,18},{18,2},{3,19},{19,3},{4,20},{20... | collective-permute-start | bytes 2359304 | tf_op jit(solution)/shard_map/ppermute | solution.py:97
  178.5 30.1 %all-to-all-start.5 = ((f32[16,24,512]{2,1,0:T(8,128)}), f32[16,24,512]{2,1,0:T(8,128)}, u32[]{:S(2)}, u32[]{:S(2)}) async-start(f32[16,24,512]{2,1,0:T(8,128)} %bitcast.84), calls=%async_computation.5 | async-start | bytes 1572864 | tf_op jit(solution)/shard_map/all_to_all | solution.py:25
  187.7 2.6 %copy-start.3 = (bf16[16,24,1024]{2,1,0:T(8,128)(2,1)S(1)}, bf16[16,24,1024]{2,1,0:T(8,128)(2,1)}, u32[]{:S(2)}) copy-start(bf16[16,24,1024]{2,1,0:T(8,128)(2,1)} %copy-done.2) | copy-start | bytes 2359300
  187.8 2.6 %copy-start.5 = (bf16[384,1024]{1,0:T(8,128)(2,1)S(1)}, bf16[384,1024]{1,0:T(8,128)(2,1)}, u32[]{:S(2)}) copy-start(bf16[384,1024]{1,0:T(8,128)(2,1)} %copy-done.4) | copy-start | bytes 2359300

commit v17 on v16

--- a/solution.py
+++ b/solution.py
@@ -84,12 +84,10 @@
     grad_down = lax.dot_general(
         hidden, all_grads, contract_first, preferred_element_type=jnp.float32
     ).astype(jnp.bfloat16)
-    grad_gate = lax.dot_general(
-        all_tokens, gate_delta, contract_first, preferred_element_type=jnp.float32
+    grad_gate_up = jnp.einsum(
+        "rd,krh->kdh", all_tokens, deltas[1:], preferred_element_type=jnp.float32
     ).astype(jnp.bfloat16)
-    grad_up = lax.dot_general(
-        all_tokens, up_delta, contract_first, preferred_element_type=jnp.float32
-    ).astype(jnp.bfloat16)
+    grad_gate, grad_up = grad_gate_up[0], grad_gate_up[1]
     result = lax.dot_general(
         gate_delta, gate_weight, contract_last, preferred_element_type=jnp.float32
     ) + lax.dot_general(up_delta, up_weight, contract_last, preferred_element_type=jnp.float32)

time: 213 us -> 213 us (level)
  local copies, waits for them, and re-layouts: 10.9 us -> 16.4 us
  waiting for transfers between devices: 60.5 us -> 58.3 us
    reshape x0 -> x2, local copies, waits for them, and re-layouts: none -> 3.66 us  [gather_a2a(): return v.reshape(shape[:dim] + (n * shape[dim],) + shape[dim + 1:])]
    all_to_all x2, waiting for transfers between devices: 10.4 us -> 7.46 us  [gather_a2a(): v = lax.all_to_all(v, axis_name, dim, dim, tiled=True)]
  transfers between devices with their start and end apart: 19 -> 19, of which waited for: 9 -> 9; matrix products, arithmetic and copies ran while one was open for 7% -> 8% of each run, Pallas kernels for 0% -> 0%
where the time goes in v17:
time: 213 us; the launch traced here: 211 us
  starting transfers between devices  88.6 us (42%)
  waiting for transfers between devices  58.3 us (27%)
  blocking collectives  31.5 us (15%)
  local copies, waits for them, and re-layouts  16.4 us (8%)
  other arithmetic  8.28 us (4%)
  matrix products  6.54 us (3%)
    all_to_all x1, blocking collectives, gather_a2a(): v = lax.all_to_all(v, axis_name, dim, dim, tiled=True)  31.5 us
    ppermute x6, starting transfers between devices, scatter_permute(): lax.ppermute(part, axis_name, [(j, (j + k) % n) for j in range(n)])  27 us
    ppermute x6, starting transfers between devices, gather_permute(): lax.ppermute(v, axis_name, [(j, (j + k) % n) for j in range(n)])  22.4 us
    all_to_all x2, waiting for transfers between devices, local(): p = lax.all_to_all(p, 'x', 0, 0, tiled=True).sum(0)  16.4 us
    all_to_all x1, waiting for transfers between devices, scatter_sum(): v = lax.all_to_all(v, axis_name, dim, dim, tiled=True)  16.4 us
    ppermute x1, starting transfers between devices, local(): result = result[:half] + lax.ppermute(result[half:], 'c', swap)  9.32 us
    all_to_all x1, starting transfers between devices, scatter_sum(): v = lax.all_to_all(v, axis_name, dim, dim, tiled=True)  9.15 us
    all_to_all x2, starting transfers between devices, gather_a2a(): v = lax.all_to_all(v, axis_name, dim, dim, tiled=True)  8.35 us
  transfers between devices with their start and end apart: 19, of which 9 were waited for; matrix products, arithmetic and copies ran while one was open for 8% of the time, Pallas kernels for 0%

profile of v17, /device:TPU:1, one launch (start us, length us, event | category | flops | bytes accessed | tf_op | source)
XLA Modules:
  0.0 210.7 jit_solution(1945634114410057588)
XLA Ops:
  0.6 0.8 pad_maximum_fusion.12
  1.6 31.5 %all_to_all.30 = bf16[16,24,1024]{2,1,0:T(8,128)(2,1)S(1)} all-to-all(bf16[16,24,1024]{2,1,0:T(8,128)(2,1)S(1)} %broadcast_in_dim.26), channel_id=1, replica_groups=mesh['y'=8,'zl'=2,'c'=2,'x'=4,'zh'=4] {'y','zl'}, dimensions={0} | all-to-all | bytes 1572864 | tf_op jit(solution)/shard_map/all_to_all | solution.py:32
  34.8 1.6 copy.19
  36.4 4.0 %all-to-all-start.1 = ((f32[4,3,96,448]{3,2,1,0:T(8,128)}), f32[4,3,96,448]{3,2,1,0:T(8,128)S(1)}, u32[]{:S(2)}, u32[]{:S(2)}) async-start(f32[4,3,96,448]{3,2,1,0:T(8,128)} %copy.19), calls=%async_computation.1 | async-start | bytes 4718592 | tf_op jit(solution)/shard_map/all_to_all | solution.py:75
  40.4 4.7 %collective-permute-start.6 = (bf16[384,1024]{1,0:T(8,128)(2,1)}, bf16[384,1024]{1,0:T(8,128)(2,1)S(1)}, u32[]{:S(2)}, u32[]{:S(2)}) collective-permute-start(bf16[384,1024]{1,0:T(8,128)(2,1)} %bitcast.80), channel_id=1, source_target_pairs={{0,16},{16,0},{1,17},{17,1},{2,18},{18,2},{3,19},{19,3},{4,20},{20... | collective-permute-start | bytes 2359304 | tf_op jit(solution)/shard_map/ppermute | solution.py:65
  45.1 2.1 collective-permute-done.6
  48.9 1.6 copy.24
  50.5 16.4 %all-to-all-done.1 = f32[4,3,96,448]{3,2,1,0:T(8,128)S(1)} async-done(((f32[4,3,96,448]{3,2,1,0:T(8,128)}), f32[4,3,96,448]{3,2,1,0:T(8,128)S(1)}, u32[]{:S(2)}, u32[]{:S(2)}) %all-to-all-start.1) | async-done | bytes 2064416 | tf_op jit(solution)/shard_map/all_to_all | solution.py:75
  67.0 1.4 copy-done.1
  68.4 3.6 %all-to-all-start.3 = ((f32[4,3,96,448]{3,2,1,0:T(8,128)}), f32[4,3,96,448]{3,2,1,0:T(8,128)S(1)}, u32[]{:S(2)}, u32[]{:S(2)}) async-start(f32[4,3,96,448]{3,2,1,0:T(8,128)} %copy.24), calls=%async_computation.3 | async-start | bytes 4718592 | tf_op jit(solution)/shard_map/all_to_all | solution.py:75
  72.1 2.0 reduce_sum.27
  74.1 0.8 constant_dynamic-slice_fusion.5
  74.9 5.8 %collective-permute-start = (f32[3,24,448]{2,1,0:T(8,128)}, f32[3,24,448]{2,1,0:T(8,128)S(1)}, u32[]{:S(2)}, u32[]{:S(2)}) collective-permute-start(f32[3,24,448]{2,1,0:T(8,128)} %get-tuple-element.10), channel_id=1, source_target_pairs={{0,1},{1,2},{2,3},{3,0},{4,5},{5,6},{6,7},{7,4},{8,9},{9,10},{10,1... | collective-permute-start | bytes 387080 | tf_op jit(solution)/shard_map/ppermute | solution.py:43
  80.7 5.9 %collective-permute-start.2 = (f32[3,24,448]{2,1,0:T(8,128)}, f32[3,24,448]{2,1,0:T(8,128)}, u32[]{:S(2)}, u32[]{:S(2)}) collective-permute-start(f32[3,24,448]{2,1,0:T(8,128)} %get-tuple-element.11), channel_id=1, source_target_pairs={{0,3},{1,0},{2,1},{3,2},{4,7},{5,4},{6,5},{7,6},{8,11},{9,8},{10,9... | collective-permute-start | bytes 387080 | tf_op jit(solution)/shard_map/ppermute | solution.py:43
  86.6 5.5 %collective-permute-start.1 = (f32[3,24,448]{2,1,0:T(8,128)}, f32[3,24,448]{2,1,0:T(8,128)}, u32[]{:S(2)}, u32[]{:S(2)}) collective-permute-start(f32[3,24,448]{2,1,0:T(8,128)} %get-tuple-element.12), channel_id=1, source_target_pairs={{0,2},{1,3},{2,0},{3,1},{4,6},{5,7},{6,4},{7,5},{8,10},{9,11},{10,... | collective-permute-start | bytes 387080 | tf_op jit(solution)/shard_map/ppermute | solution.py:43
  92.1 4.7 %collective-permute-done.1 = f32[3,24,448]{2,1,0:T(8,128)} collective-permute-done((f32[3,24,448]{2,1,0:T(8,128)}, f32[3,24,448]{2,1,0:T(8,128)}, u32[]{:S(2)}, u32[]{:S(2)}) %collective-permute-start.1) | collective-permute-done | bytes 129056 | tf_op jit(solution)/shard_map/ppermute | solution.py:43
  96.8 1.0 add_add_fusion.1
  97.8 6.7 %collective-permute-start.4 = (bf16[3,24,448]{2,1,0:T(8,128)(2,1)S(1)}, bf16[3,24,448]{2,1,0:T(8,128)(2,1)}, u32[]{:S(2)}, u32[]{:S(2)}) collective-permute-start(bf16[3,24,448]{2,1,0:T(8,128)(2,1)S(1)} %get-tuple-element.21), channel_id=1, source_target_pairs={{0,2},{1,3},{2,0},{3,1},{4,6},{5,7},{6,4},{7,5},{8,10},{9,11},{10,... | collective-permute-start | bytes 193544 | tf_op jit(solution)/shard_map/ppermute | solution.py:50
  104.5 1.9 collective-permute-start.3
  106.5 4.3 %collective-permute-start.5 = (bf16[3,24,448]{2,1,0:T(8,128)(2,1)S(1)}, bf16[3,24,448]{2,1,0:T(8,128)(2,1)}, u32[]{:S(2)}, u32[]{:S(2)}) collective-permute-start(bf16[3,24,448]{2,1,0:T(8,128)(2,1)S(1)} %get-tuple-element.21), channel_id=1, source_target_pairs={{0,1},{1,2},{2,3},{3,0},{4,5},{5,6},{6,7},{7,4},{8,9},{9,10},{10,1... | collective-permute-start | bytes 193544 | tf_op jit(solution)/shard_map/ppermute | solution.py:50
  111.1 2.7 %collective-permute-start.7 = (f32[3,24,448]{2,1,0:T(8,128)S(1)}, f32[3,24,448]{2,1,0:T(8,128)S(1)}, u32[]{:S(2)}, u32[]{:S(2)}) collective-permute-start(f32[3,24,448]{2,1,0:T(8,128)S(1)} %get-tuple-element.7), channel_id=1, source_target_pairs={{0,1},{1,2},{2,3},{3,0},{4,5},{5,6},{6,7},{7,4},{8,9},{9,10},{10,1... | collective-permute-start | bytes 387080 | tf_op jit(solution)/shard_map/ppermute | solution.py:43
  113.9 4.7 %collective-permute-start.9 = (f32[3,24,448]{2,1,0:T(8,128)S(1)}, f32[3,24,448]{2,1,0:T(8,128)S(1)}, u32[]{:S(2)}, u32[]{:S(2)}) collective-permute-start(f32[3,24,448]{2,1,0:T(8,128)S(1)} %get-tuple-element.8), channel_id=1, source_target_pairs={{0,3},{1,0},{2,1},{3,2},{4,7},{5,4},{6,5},{7,6},{8,11},{9,8},{10,9... | collective-permute-start | bytes 387080 | tf_op jit(solution)/shard_map/ppermute | solution.py:43
  118.5 2.5 %collective-permute-start.8 = (f32[3,24,448]{2,1,0:T(8,128)S(1)}, f32[3,24,448]{2,1,0:T(8,128)S(1)}, u32[]{:S(2)}, u32[]{:S(2)}) collective-permute-start(f32[3,24,448]{2,1,0:T(8,128)S(1)} %get-tuple-element.9), channel_id=1, source_target_pairs={{0,2},{1,3},{2,0},{3,1},{4,6},{5,7},{6,4},{7,5},{8,10},{9,11},{10,... | collective-permute-start | bytes 387080 | tf_op jit(solution)/shard_map/ppermute | solution.py:43
  121.1 1.5 fusion.32
  122.5 1.1 broadcast_in_dim.29
  123.7 4.4 %all-to-all-start.2 = ((bf16[3,4,96,448]{3,2,0,1:T(8,128)(2,1)}), bf16[3,4,96,448]{3,2,0,1:T(8,128)(2,1)S(1)}, u32[]{:S(2)}, u32[]{:S(2)}) async-start(bf16[3,4,96,448]{3,2,0,1:T(8,128)(2,1)} %broadcast_in_dim.29), calls=%async_computation.2 | async-start | bytes 2359296 | tf_op jit(solution)/shard_map/all_to_all | solution.py:32
  128.0 3.4 %collective-permute-done.8 = f32[3,24,448]{2,1,0:T(8,128)S(1)} collective-permute-done((f32[3,24,448]{2,1,0:T(8,128)S(1)}, f32[3,24,448]{2,1,0:T(8,128)S(1)}, u32[]{:S(2)}, u32[]{:S(2)}) %collective-permute-start.8) | collective-permute-done | bytes 129056 | tf_op jit(solution)/shard_map/ppermute | solution.py:43
  131.5 3.4 %collective-permute-start.11 = (bf16[3,24,448]{2,1,0:T(8,128)(2,1)S(1)}, bf16[3,24,448]{2,1,0:T(8,128)(2,1)S(1)}, u32[]{:S(2)}, u32[]{:S(2)}) collective-permute-start(bf16[3,24,448]{2,1,0:T(8,128)(2,1)S(1)} %get-tuple-element.19), channel_id=1, source_target_pairs={{0,2},{1,3},{2,0},{3,1},{4,6},{5,7},{6,4},{7,5},{8,10},{9,11},{10,... | collective-permute-start | bytes 193544 | tf_op jit(solution)/shard_map/ppermute | solution.py:50
  134.9 4.1 %collective-permute-start.10 = (bf16[3,24,448]{2,1,0:T(8,128)(2,1)S(1)}, bf16[3,24,448]{2,1,0:T(8,128)(2,1)S(1)}, u32[]{:S(2)}, u32[]{:S(2)}) collective-permute-start(bf16[3,24,448]{2,1,0:T(8,128)(2,1)S(1)} %get-tuple-element.19), channel_id=1, source_target_pairs={{0,3},{1,0},{2,1},{3,2},{4,7},{5,4},{6,5},{7,6},{8,11},{9,8},{10,9... | collective-permute-start | bytes 193544 | tf_op jit(solution)/shard_map/ppermute | solution.py:50
  139.0 2.1 %collective-permute-start.12 = (bf16[3,24,448]{2,1,0:T(8,128)(2,1)S(1)}, bf16[3,24,448]{2,1,0:T(8,128)(2,1)S(1)}, u32[]{:S(2)}, u32[]{:S(2)}) collective-permute-start(bf16[3,24,448]{2,1,0:T(8,128)(2,1)S(1)} %get-tuple-element.19), channel_id=1, source_target_pairs={{0,1},{1,2},{2,3},{3,0},{4,5},{5,6},{6,7},{7,4},{8,9},{9,10},{10,1... | collective-permute-start | bytes 193544 | tf_op jit(solution)/shard_map/ppermute | solution.py:50
  141.1 0.8 collective-permute-done.10
  141.9 5.2 %collective-permute-done.12 = bf16[3,24,448]{2,1,0:T(8,128)(2,1)S(1)} collective-permute-done((bf16[3,24,448]{2,1,0:T(8,128)(2,1)S(1)}, bf16[3,24,448]{2,1,0:T(8,128)(2,1)S(1)}, u32[]{:S(2)}, u32[]{:S(2)}) %collective-permute-start.12) | collective-permute-done | bytes 64544 | tf_op jit(solution)/shard_map/ppermute | solution.py:50
  147.5 1.1 broadcast_in_dim.32
  148.6 4.0 %all-to-all-start.4 = ((bf16[3,4,96,448]{3,2,0,1:T(8,128)(2,1)}), bf16[3,4,96,448]{3,2,0,1:T(8,128)(2,1)S(1)}, u32[]{:S(2)}, u32[]{:S(2)}) async-start(bf16[3,4,96,448]{3,2,0,1:T(8,128)(2,1)} %broadcast_in_dim.32), calls=%async_computation.4 | async-start | bytes 2359296 | tf_op jit(solution)/shard_map/all_to_all | solution.py:32
  152.6 1.2 copy.23
  153.8 1.8 copy.27
  155.6 7.5 %all-to-all-done.4 = bf16[3,4,96,448]{3,2,0,1:T(8,128)(2,1)S(1)} async-done(((bf16[3,4,96,448]{3,2,0,1:T(8,128)(2,1)}), bf16[3,4,96,448]{3,2,0,1:T(8,128)(2,1)S(1)}, u32[]{:S(2)}, u32[]{:S(2)}) %all-to-all-start.4) | async-done | bytes 1032224 | tf_op jit(solution)/shard_map/all_to_all | solution.py:32
  163.1 1.2 copy.26
  164.2 1.9 copy.28
  167.8 9.3 %collective-permute-start.13 = (f32[384,512]{1,0:T(8,128)S(1)}, f32[384,512]{1,0:T(8,128)S(1)}, u32[]{:S(2)}, u32[]{:S(2)}) collective-permute-start(f32[384,512]{1,0:T(8,128)S(1)} %slice.95), channel_id=1, source_target_pairs={{0,16},{16,0},{1,17},{17,1},{2,18},{18,2},{3,19},{19,3},{4,20},{20... | collective-permute-start | bytes 2359304 | tf_op jit(solution)/shard_map/ppermute | solution.py:95
  177.1 1.9 collective-permute-done.13
  179.0 1.0 slice_add_fusion
  180.1 9.1 %all-to-all-start.5 = ((f32[16,24,512]{2,1,0:T(8,128)}), f32[16,24,512]{2,1,0:T(8,128)S(1)}, u32[]{:S(2)}, u32[]{:S(2)}) async-start(f32[16,24,512]{2,1,0:T(8,128)} %bitcast.77), calls=%async_computation.5 | async-start | bytes 1572864 | tf_op jit(solution)/shard_map/all_to_all | solution.py:25
  189.2 2.5 %convolution_convert_fusion = bf16[448,512]{1,0:T(8,128)(2,1)} fusion(bf16[384,1024]{1,0:T(8,128)(2,1)} %copy-done.9, bf16[384,1024]{1,0:T(8,128)(2,1)} %bitcast.81, bf16[3,384,448]{1,2,0:T(8,128)(2,1)S(1)} %copy.27, bf16[3,384,448]{1,2,0:T(8,128)(2,1)S(1)} %copy.28), kind=kOutput, calls=%fused_computation.19 | convolution fusion | flops 355500032 | bytes 4096000 | tf_op jit(solution)/shard_map/dot_general | solution.py:84
  191.8 0.9 fusion.2
  192.7 1.0 slice_bitcast_fusion
  193.6 16.4 %all-to-all-done.5 = f32[16,24,512]{2,1,0:T(8,128)S(1)} async-done(((f32[16,24,512]{2,1,0:T(8,128)}), f32[16,24,512]{2,1,0:T(8,128)S(1)}, u32[]{:S(2)}, u32[]{:S(2)}) %all-to-all-start.5) | async-done | bytes 786464 | tf_op jit(solution)/shard_map/all_to_all | solution.py:25
  210.0 0.7 reduce_sum.29
  (50 shorter events, 6.1 us)
Async XLA Ops:
  0.6 32.4 %copy-start = (bf16[448,512]{1,0:T(8,128)(2,1)S(1)}, bf16[448,512]{1,0:T(8,128)(2,1)}, u32[]{:S(2)}) copy-start(bf16[448,512]{1,0:T(8,128)(2,1)} %param.11) | copy-start | bytes 1376260
  1.5 32.4 %copy-start.4 = (bf16[512,448]{0,1:T(8,128)(2,1)S(1)}, bf16[512,448]{0,1:T(8,128)(2,1)}, u32[]{:S(2)}) copy-start(bf16[512,448]{0,1:T(8,128)(2,1)} %param.9) | copy-start | bytes 1376260
  1.6 32.4 %copy-start.6 = (bf16[512,448]{0,1:T(8,128)(2,1)S(1)}, bf16[512,448]{0,1:T(8,128)(2,1)}, u32[]{:S(2)}) copy-start(bf16[512,448]{0,1:T(8,128)(2,1)} %param.10) | copy-start | bytes 1376260
  33.0 0.9 copy-start.2
  36.4 30.5 %all-to-all-start.1 = ((f32[4,3,96,448]{3,2,1,0:T(8,128)}), f32[4,3,96,448]{3,2,1,0:T(8,128)S(1)}, u32[]{:S(2)}, u32[]{:S(2)}) async-start(f32[4,3,96,448]{3,2,1,0:T(8,128)} %copy.19), calls=%async_computation.1 | async-start | bytes 4718592 | tf_op jit(solution)/shard_map/all_to_all | solution.py:75
  40.4 7.7 %copy-start.7 = (bf16[512,448]{0,1:T(8,128)(2,1)S(1)}, bf16[512,448]{0,1:T(8,128)(2,1)}, u32[]{:S(2)}) copy-start(bf16[512,448]{0,1:T(8,128)(2,1)} %param.10) | copy-start | bytes 1376260
  40.4 6.8 %collective-permute-start.6 = (bf16[384,1024]{1,0:T(8,128)(2,1)}, bf16[384,1024]{1,0:T(8,128)(2,1)S(1)}, u32[]{:S(2)}, u32[]{:S(2)}) collective-permute-start(bf16[384,1024]{1,0:T(8,128)(2,1)} %bitcast.80), channel_id=1, source_target_pairs={{0,16},{16,0},{1,17},{17,1},{2,18},{18,2},{3,19},{19,3},{4,20},{20... | collective-permute-start | bytes 2359304 | tf_op jit(solution)/shard_map/ppermute | solution.py:65
  47.2 0.9 copy-start.9
  67.0 1.4 copy-start.1
  68.4 42.3 %all-to-all-start.3 = ((f32[4,3,96,448]{3,2,1,0:T(8,128)}), f32[4,3,96,448]{3,2,1,0:T(8,128)S(1)}, u32[]{:S(2)}, u32[]{:S(2)}) async-start(f32[4,3,96,448]{3,2,1,0:T(8,128)} %copy.24), calls=%async_computation.3 | async-start | bytes 4718592 | tf_op jit(solution)/shard_map/all_to_all | solution.py:75
  74.9 17.2 %collective-permute-start = (f32[3,24,448]{2,1,0:T(8,128)}, f32[3,24,448]{2,1,0:T(8,128)S(1)}, u32[]{:S(2)}, u32[]{:S(2)}) collective-permute-start(f32[3,24,448]{2,1,0:T(8,128)} %get-tuple-element.10), channel_id=1, source_target_pairs={{0,1},{1,2},{2,3},{3,0},{4,5},{5,6},{6,7},{7,4},{8,9},{9,10},{10,1... | collective-permute-start | bytes 387080 | tf_op jit(solution)/shard_map/ppermute | solution.py:43
  80.7 11.4 %collective-permute-start.2 = (f32[3,24,448]{2,1,0:T(8,128)}, f32[3,24,448]{2,1,0:T(8,128)}, u32[]{:S(2)}, u32[]{:S(2)}) collective-permute-start(f32[3,24,448]{2,1,0:T(8,128)} %get-tuple-element.11), channel_id=1, source_target_pairs={{0,3},{1,0},{2,1},{3,2},{4,7},{5,4},{6,5},{7,6},{8,11},{9,8},{10,9... | collective-permute-start | bytes 387080 | tf_op jit(solution)/shard_map/ppermute | solution.py:43
  86.6 10.2 %collective-permute-start.1 = (f32[3,24,448]{2,1,0:T(8,128)}, f32[3,24,448]{2,1,0:T(8,128)}, u32[]{:S(2)}, u32[]{:S(2)}) collective-permute-start(f32[3,24,448]{2,1,0:T(8,128)} %get-tuple-element.12), channel_id=1, source_target_pairs={{0,2},{1,3},{2,0},{3,1},{4,6},{5,7},{6,4},{7,5},{8,10},{9,11},{10,... | collective-permute-start | bytes 387080 | tf_op jit(solution)/shard_map/ppermute | solution.py:43
  97.8 20.7 %collective-permute-start.4 = (bf16[3,24,448]{2,1,0:T(8,128)(2,1)S(1)}, bf16[3,24,448]{2,1,0:T(8,128)(2,1)}, u32[]{:S(2)}, u32[]{:S(2)}) collective-permute-start(bf16[3,24,448]{2,1,0:T(8,128)(2,1)S(1)} %get-tuple-element.21), channel_id=1, source_target_pairs={{0,2},{1,3},{2,0},{3,1},{4,6},{5,7},{6,4},{7,5},{8,10},{9,11},{10,... | collective-permute-start | bytes 193544 | tf_op jit(solution)/shard_map/ppermute | solution.py:50
  104.5 16.5 %collective-permute-start.3 = (bf16[3,24,448]{2,1,0:T(8,128)(2,1)S(1)}, bf16[3,24,448]{2,1,0:T(8,128)(2,1)}, u32[]{:S(2)}, u32[]{:S(2)}) collective-permute-start(bf16[3,24,448]{2,1,0:T(8,128)(2,1)S(1)} %get-tuple-element.21), channel_id=1, source_target_pairs={{0,3},{1,0},{2,1},{3,2},{4,7},{5,4},{6,5},{7,6},{8,11},{9,8},{10,9... | collective-permute-start | bytes 193544 | tf_op jit(solution)/shard_map/ppermute | solution.py:50
  106.5 14.6 %collective-permute-start.5 = (bf16[3,24,448]{2,1,0:T(8,128)(2,1)S(1)}, bf16[3,24,448]{2,1,0:T(8,128)(2,1)}, u32[]{:S(2)}, u32[]{:S(2)}) collective-permute-start(bf16[3,24,448]{2,1,0:T(8,128)(2,1)S(1)} %get-tuple-element.21), channel_id=1, source_target_pairs={{0,1},{1,2},{2,3},{3,0},{4,5},{5,6},{6,7},{7,4},{8,9},{9,10},{10,1... | collective-permute-start | bytes 193544 | tf_op jit(solution)/shard_map/ppermute | solution.py:50
  111.1 16.9 %collective-permute-start.7 = (f32[3,24,448]{2,1,0:T(8,128)S(1)}, f32[3,24,448]{2,1,0:T(8,128)S(1)}, u32[]{:S(2)}, u32[]{:S(2)}) collective-permute-start(f32[3,24,448]{2,1,0:T(8,128)S(1)} %get-tuple-element.7), channel_id=1, source_target_pairs={{0,1},{1,2},{2,3},{3,0},{4,5},{5,6},{6,7},{7,4},{8,9},{9,10},{10,1... | collective-permute-start | bytes 387080 | tf_op jit(solution)/shard_map/ppermute | solution.py:43
  113.9 14.2 %collective-permute-start.9 = (f32[3,24,448]{2,1,0:T(8,128)S(1)}, f32[3,24,448]{2,1,0:T(8,128)S(1)}, u32[]{:S(2)}, u32[]{:S(2)}) collective-permute-start(f32[3,24,448]{2,1,0:T(8,128)S(1)} %get-tuple-element.8), channel_id=1, source_target_pairs={{0,3},{1,0},{2,1},{3,2},{4,7},{5,4},{6,5},{7,6},{8,11},{9,8},{10,9... | collective-permute-start | bytes 387080 | tf_op jit(solution)/shard_map/ppermute | solution.py:43
  118.5 12.9 %collective-permute-start.8 = (f32[3,24,448]{2,1,0:T(8,128)S(1)}, f32[3,24,448]{2,1,0:T(8,128)S(1)}, u32[]{:S(2)}, u32[]{:S(2)}) collective-permute-start(f32[3,24,448]{2,1,0:T(8,128)S(1)} %get-tuple-element.9), channel_id=1, source_target_pairs={{0,2},{1,3},{2,0},{3,1},{4,6},{5,7},{6,4},{7,5},{8,10},{9,11},{10,... | collective-permute-start | bytes 387080 | tf_op jit(solution)/shard_map/ppermute | solution.py:43
  123.7 23.8 %all-to-all-start.2 = ((bf16[3,4,96,448]{3,2,0,1:T(8,128)(2,1)}), bf16[3,4,96,448]{3,2,0,1:T(8,128)(2,1)S(1)}, u32[]{:S(2)}, u32[]{:S(2)}) async-start(bf16[3,4,96,448]{3,2,0,1:T(8,128)(2,1)} %broadcast_in_dim.29), calls=%async_computation.2 | async-start | bytes 2359296 | tf_op jit(solution)/shard_map/all_to_all | solution.py:32
  131.5 9.6 %collective-permute-start.11 = (bf16[3,24,448]{2,1,0:T(8,128)(2,1)S(1)}, bf16[3,24,448]{2,1,0:T(8,128)(2,1)S(1)}, u32[]{:S(2)}, u32[]{:S(2)}) collective-permute-start(bf16[3,24,448]{2,1,0:T(8,128)(2,1)S(1)} %get-tuple-element.19), channel_id=1, source_target_pairs={{0,2},{1,3},{2,0},{3,1},{4,6},{5,7},{6,4},{7,5},{8,10},{9,11},{10,... | collective-permute-start | bytes 193544 | tf_op jit(solution)/shard_map/ppermute | solution.py:50
  134.9 7.0 %collective-permute-start.10 = (bf16[3,24,448]{2,1,0:T(8,128)(2,1)S(1)}, bf16[3,24,448]{2,1,0:T(8,128)(2,1)S(1)}, u32[]{:S(2)}, u32[]{:S(2)}) collective-permute-start(bf16[3,24,448]{2,1,0:T(8,128)(2,1)S(1)} %get-tuple-element.19), channel_id=1, source_target_pairs={{0,3},{1,0},{2,1},{3,2},{4,7},{5,4},{6,5},{7,6},{8,11},{9,8},{10,9... | collective-permute-start | bytes 193544 | tf_op jit(solution)/shard_map/ppermute | solution.py:50
  139.0 8.1 %collective-permute-start.12 = (bf16[3,24,448]{2,1,0:T(8,128)(2,1)S(1)}, bf16[3,24,448]{2,1,0:T(8,128)(2,1)S(1)}, u32[]{:S(2)}, u32[]{:S(2)}) collective-permute-start(bf16[3,24,448]{2,1,0:T(8,128)(2,1)S(1)} %get-tuple-element.19), channel_id=1, source_target_pairs={{0,1},{1,2},{2,3},{3,0},{4,5},{5,6},{6,7},{7,4},{8,9},{9,10},{10,1... | collective-permute-start | bytes 193544 | tf_op jit(solution)/shard_map/ppermute | solution.py:50
  148.6 14.4 %all-to-all-start.4 = ((bf16[3,4,96,448]{3,2,0,1:T(8,128)(2,1)}), bf16[3,4,96,448]{3,2,0,1:T(8,128)(2,1)S(1)}, u32[]{:S(2)}, u32[]{:S(2)}) async-start(bf16[3,4,96,448]{3,2,0,1:T(8,128)(2,1)} %broadcast_in_dim.32), calls=%async_computation.4 | async-start | bytes 2359296 | tf_op jit(solution)/shard_map/all_to_all | solution.py:32
  164.2 1.9 copy-start.5
  166.1 1.0 copy-start.8
  167.8 11.2 %collective-permute-start.13 = (f32[384,512]{1,0:T(8,128)S(1)}, f32[384,512]{1,0:T(8,128)S(1)}, u32[]{:S(2)}, u32[]{:S(2)}) collective-permute-start(f32[384,512]{1,0:T(8,128)S(1)} %slice.95), channel_id=1, source_target_pairs={{0,16},{16,0},{1,17},{17,1},{2,18},{18,2},{3,19},{19,3},{4,20},{20... | collective-permute-start | bytes 2359304 | tf_op jit(solution)/shard_map/ppermute | solution.py:95
  180.1 30.0 %all-to-all-start.5 = ((f32[16,24,512]{2,1,0:T(8,128)}), f32[16,24,512]{2,1,0:T(8,128)S(1)}, u32[]{:S(2)}, u32[]{:S(2)}) async-start(f32[16,24,512]{2,1,0:T(8,128)} %bitcast.77), calls=%async_computation.5 | async-start | bytes 1572864 | tf_op jit(solution)/shard_map/all_to_all | solution.py:25
  189.2 2.5 %copy-start.3 = (bf16[16,24,1024]{2,1,0:T(8,128)(2,1)S(1)}, bf16[16,24,1024]{2,1,0:T(8,128)(2,1)}, u32[]{:S(2)}) copy-start(bf16[16,24,1024]{2,1,0:T(8,128)(2,1)} %copy-done.2) | copy-start | bytes 2359300
  189.2 2.5 %copy-start.10 = (bf16[384,1024]{1,0:T(8,128)(2,1)S(1)}, bf16[384,1024]{1,0:T(8,128)(2,1)}, u32[]{:S(2)}) copy-start(bf16[384,1024]{1,0:T(8,128)(2,1)} %copy-done.9) | copy-start | bytes 2359300
